TPU v7x, 32 devices: a whole 2x2x4 slice. The times are simulated.
32 devices in a mesh: section: 2 (over x), dp: 16 (over z, y, core).
Axes of the slice: x: 2, y: 2, z: 4, core: 2. Of those that a mesh axis runs over, the one named last changes fastest.
Arguments:
- hidden_states: bfloat16 [2, 2048, 6144], P('section', 'dp'), may hold values from -27 to 27
- norm_gain: bfloat16 [2, 6144], P('section'), may hold values from 0.099609375 to 1.8984375
- gate_weight: bfloat16 [2, 6144, 32768], P('section', None, 'dp'), may hold values from -0.078125 to 0.078125
- up_weight: bfloat16 [2, 6144, 32768], P('section', None, 'dp'), may hold values from -0.078125 to 0.078125
- down_weight: bfloat16 [2, 32768, 6144], P('section', 'dp'), may hold values from -0.1875 to 0.1875
- route_rows: int32 [2, 16, 2, 16], P('section', 'dp'), may hold values from 0 to 127, as said below
- route_count: int32 [2, 16, 2], P('section', 'dp'), may hold values from 4 to 16, as said below
- route_gate: float32 [2, 16, 2, 16], P('section', 'dp'), may hold values from 0.2 to 1
Outputs:
- handed: bfloat16 [2, 2048, 6144], P('section', 'dp')
Inputs may be any that keep to these rules, and one draw needn't show every extreme that they name: `route_rows`: within one section, rank and expert the 16 numbers are distinct rows of that rank's micro-batch; only the first route_count of them are live. `route_count`: in every section one of the 2 experts receives 16 live rows from every rank.
All inputs are finite; a program needn't handle non-finite values.
Results may differ from a plain program's by a relative error of at most 0.0034.
Values may be sent and summed in bfloat16 or wider, within the bound.
No kernel may reach another device: no remote copies, remote signals or barrier semaphores. Data moves between devices by JAX's collectives and lax.ppermute only.
A program may use at most 192 MiB of HBM per device.

v0:
```python
import jax
import jax.numpy as jnp
from jax import lax
from jax.sharding import PartitionSpec as P


def passed_along(block, axis, distance):
    devices = range(lax.axis_size(axis))
    route = [((i - distance) % len(devices), i) for i in devices]
    return lax.ppermute(block, axis, route)


def body(
    hidden_states,
    norm_gain,
    gate_weight,
    up_weight,
    down_weight,
    route_rows,
    route_count,
    route_gate,
):
    states = hidden_states[0]
    scale_gain = norm_gain[0]
    gate_cols = gate_weight[0]
    up_cols = up_weight[0]
    down_rows = down_weight[0]
    slot_rows = route_rows[0, 0]
    live_count = route_count[0, 0]
    slot_gates = route_gate[0, 0]
    width = states.shape[1]
    tok_count = states.shape[0]
    experts = slot_rows.shape[0]
    capacity = slot_rows.shape[1]
    ranks = lax.axis_size("dp")
    owners = ranks // experts
    my_expert = lax.axis_index("dp") // owners
    widened = states.astype(jnp.float32)
    normed = (
        widened
        * lax.rsqrt(jnp.mean(widened * widened, axis=-1, keepdims=True) + 1e-05)
        * scale_gain.astype(jnp.float32)
    ).astype(jnp.bfloat16)
    picked = jnp.take(normed, slot_rows, axis=0)
    chosen = lax.dynamic_index_in_dim(
        lax.all_gather(picked[None], "dp", axis=0, tiled=True), my_expert, 1, keepdims=False
    )
    flat_rows = chosen.reshape(-1, width)
    gate_part = jnp.dot(flat_rows, gate_cols, preferred_element_type=jnp.float32)
    up_part = jnp.dot(flat_rows, up_cols, preferred_element_type=jnp.float32)
    activated = (jax.nn.silu(gate_part) * up_part).astype(jnp.bfloat16)
    partial_out = jnp.dot(activated, down_rows, preferred_element_type=jnp.float32).astype(
        jnp.bfloat16
    )
    partials = partial_out.reshape(chosen.shape)
    returned_rows = lax.all_to_all(partials, "dp", split_axis=0, concat_axis=0, tiled=True)
    summed = returned_rows.reshape(experts, owners, capacity, width).astype(jnp.float32).sum(axis=1)
    live_mask = jnp.arange(capacity)[None, :] < live_count[:, None]
    weighting = jnp.where(live_mask, slot_gates, 0.0)
    one_hot = (slot_rows[..., None] == jnp.arange(tok_count)[None, None, :]).astype(
        jnp.float32
    ) * weighting[..., None]
    branch = jnp.einsum("ect,ecd->td", one_hot, summed, precision=lax.Precision.HIGHEST)
    layer_out = (widened + branch).astype(jnp.bfloat16)
    return passed_along(layer_out[None], "section", 1)


def solution(mesh):
    placed = (
        P("section", "dp", None),
        P("section", None),
        P("section", None, "dp"),
        P("section", None, "dp"),
        P("section", "dp", None),
        P("section", "dp", None, None),
        P("section", "dp", None),
        P("section", "dp", None, None),
    )
    return jax.shard_map(
        body, mesh=mesh, in_specs=placed, out_specs=P("section", "dp", None), check_vma=False
    )
```

profile of v0, /device:TPU:12, one launch (start us, length us, event | category | flops | bytes accessed | tf_op | source)
XLA Modules:
  0.0 239.6 jit_solution(12485191722880843556)
XLA Ops:
  6.5 0.0 all-gather.2.cloned.1.call-start
  6.5 0.7 compare_select_fusion
  7.2 0.7 compare_and_fusion
  7.9 0.8 mul.50
  8.7 1.8 fusion.12
  10.5 0.1 reshape.98
  10.6 1.9 fusion.14
  12.4 0.8 gather_fusion
  13.2 0.8 broadcast_select_fusion
  14.1 0.0 all-gather.2.cloned.1.call-update
  14.1 62.2 %all-gather.2.cloned.1.call-done = bf16[16,2,16,6144]{3,2,1,0:T(8,128)(2,1)} async-done(((bf16[1,2,16,6144]{3,2,1,0:T(8,128)(2,1)}), bf16[16,2,16,6144]{3,2,1,0:T(8,128)(2,1)}) %all-gather.2.cloned.1.call-update) | async-done | bytes 6291472 | tf_op jit(solution)/shard_map/all_gather | solution.py:46
  76.3 2.1 constant_dynamic-slice_fusion
  78.4 12.9 %fusion.4 = f32[256,2048]{1,0:T(8,128)} fusion(bf16[256,6144]{1,0:T(8,128)(2,1)S(1)} %bitcast.51, bf16[1,6144,2048]{2,1,0:T(8,128)(2,1)} %param.10), kind=kOutput, calls=%fused_computation.5 | convolution fusion | flops 6442450944 | bytes 30408704 | tf_op jit(solution)/shard_map/dot_general | solution.py:49
  91.3 22.7 %fusion.6 = bf16[256,6144]{1,0:T(8,128)(2,1)} fusion(bf16[1,2048,6144]{2,1,0:T(8,128)(2,1)} %param.12, bf16[256,6144]{1,0:T(8,128)(2,1)S(1)} %bitcast.52, bf16[1,6144,2048]{2,1,0:T(8,128)(2,1)} %param.11, f32[256,2048]{1,0:T(8,128)} %fusion.4), kind=kOutput, calls=%fused_computation.7 | convolution fusion | flops 12889620480 | bytes 58720256 | tf_op jit(solution)/shard_map/dot_general | solution.py:52
  114.0 0.0 copy-start.2
  114.0 0.0 copy-start.3
  114.0 5.8 %all-to-all-start = ((bf16[16,16,6144]{2,1,0:T(8,128)(2,1)}), bf16[16,16,6144]{2,1,0:T(8,128)(2,1)}, u32[]{:S(2)}, u32[]{:S(2)}) async-start(bf16[16,16,6144]{2,1,0:T(8,128)(2,1)} %bitcast.12), calls=%async_computation | async-start | bytes 6291456 | tf_op jit(solution)/shard_map/all_to_all | solution.py:56
  119.8 0.0 copy-start
  119.8 0.0 copy-start.1
  119.8 0.0 copy-done.2
  119.8 0.0 copy-done.3
  119.9 0.1 compare_select_fusion.2
  119.9 69.8 %all-to-all-done = bf16[16,16,6144]{2,1,0:T(8,128)(2,1)} async-done(((bf16[16,16,6144]{2,1,0:T(8,128)(2,1)}), bf16[16,16,6144]{2,1,0:T(8,128)(2,1)}, u32[]{:S(2)}, u32[]{:S(2)}) %all-to-all-start) | async-done | bytes 3145760 | tf_op jit(solution)/shard_map/all_to_all | solution.py:56
  189.7 2.4 %convert_reduce_fusion = f32[2,16,6144]{2,1,0:T(8,128)S(1)} fusion(bf16[16,16,6144]{2,1,0:T(8,128)(2,1)} %all-to-all-done), kind=kLoop, calls=%fused_computation.12 | loop fusion | flops 2949120 | bytes 3932160 | tf_op jit(solution)/shard_map/reduce_sum | solution.py:57
  192.1 0.0 copy-done
  192.1 0.0 copy-done.1
  192.1 2.8 %fusion.11 = bf16[1,128,6144]{2,1,0:T(8,128)(2,1)S(1)} fusion(f32[2,16,6144]{2,1,0:T(8,128)S(1)} %convert_reduce_fusion, bf16[1,128,6144]{2,1,0:T(8,128)(2,1)S(1)} %copy-done, f32[2,16]{1,0:T(2,128)S(1)} %compare_select_fusion.2, s32[2,16]{1,0:T(2,128)S(1)} %bitcast.55), kind=kOutput, calls=%fused_computation.11 | convolution fusion | flops 304357376 | bytes 3932416 | tf_op jit(solution)/shard_map/ect,ecd->td/dot_general | solution.py:63
  194.9 1.5 collective-permute-start
  196.5 35.1 %collective-permute-done = bf16[1,128,6144]{2,1,0:T(8,128)(2,1)S(1)} collective-permute-done((bf16[1,128,6144]{2,1,0:T(8,128)(2,1)S(1)}, bf16[1,128,6144]{2,1,0:T(8,128)(2,1)S(1)}, u32[]{:S(2)}, u32[]{:S(2)}) %collective-permute-start) | collective-permute-done | bytes 1572896 | tf_op jit(solution)/shard_map/ppermute | solution.py:10
  231.6 1.1 copy.10
  (2 shorter events, 0.0 us)
Async XLA Ops:
  6.5 69.8 %all-gather.2.cloned.1.call-start = ((), (), s32[]{:S(2)}) async-start(), calls=%async_computation.1 | async-start | bytes 6684672 | tf_op jit(solution)/shard_map/all_gather | solution.py:46
  114.0 5.9 %copy-start.2 = (f32[1,1,2,16]{3,2,1,0:T(2,128)S(1)}, f32[1,1,2,16]{3,2,1,0:T(2,128)}, u32[]{:S(2)}) copy-start(f32[1,1,2,16]{3,2,1,0:T(2,128)} %param.15) | copy-start | bytes 388
  114.0 5.9 %copy-start.3 = (s32[1,1,2]{2,1,0:T(1,128)S(1)}, s32[1,1,2]{2,1,0:T(1,128)}, u32[]{:S(2)}) copy-start(s32[1,1,2]{2,1,0:T(1,128)} %param.14) | copy-start | bytes 28
  114.0 75.7 %all-to-all-start = ((bf16[16,16,6144]{2,1,0:T(8,128)(2,1)}), bf16[16,16,6144]{2,1,0:T(8,128)(2,1)}, u32[]{:S(2)}, u32[]{:S(2)}) async-start(bf16[16,16,6144]{2,1,0:T(8,128)(2,1)} %bitcast.12), calls=%async_computation | async-start | bytes 6291456 | tf_op jit(solution)/shard_map/all_to_all | solution.py:56
  119.8 72.3 %copy-start = (bf16[1,128,6144]{2,1,0:T(8,128)(2,1)S(1)}, bf16[1,128,6144]{2,1,0:T(8,128)(2,1)}, u32[]{:S(2)}) copy-start(bf16[1,128,6144]{2,1,0:T(8,128)(2,1)} %param.8) | copy-start | bytes 4718596
  119.8 72.3 %copy-start.1 = (s32[1,1,2,16]{3,2,1,0:T(2,128)S(1)}, s32[1,1,2,16]{3,2,1,0:T(2,128)}, u32[]{:S(2)}) copy-start(s32[1,1,2,16]{3,2,1,0:T(2,128)} %param.13) | copy-start | bytes 388
  194.9 36.7 %collective-permute-start = (bf16[1,128,6144]{2,1,0:T(8,128)(2,1)S(1)}, bf16[1,128,6144]{2,1,0:T(8,128)(2,1)S(1)}, u32[]{:S(2)}, u32[]{:S(2)}) collective-permute-start(bf16[1,128,6144]{2,1,0:T(8,128)(2,1)S(1)} %fusion.11), channel_id=1, source_target_pairs={{16,0},{0,16},{17,1},{1,17},{18,2},{2,18},{19,3},{3,19},{20,4},{4,... | collective-permute-start | bytes 4718600 | tf_op jit(solution)/shard_map/ppermute | solution.py:10
Sparse Core Ops, SparseCore 0:
  14.2 62.0 all-gather.1
where the time goes:
time: 240 us
  waiting for transfers between devices  167 us (70%)
  matrix products  38.4 us (16%)
  between operations  13.5 us (6%)
  other arithmetic  9.15 us (4%)
  starting transfers between devices  7.38 us (3%)
  local copies, waits for them, and re-layouts  4.12 us (2%)
    all_to_all x1, waiting for transfers between devices, body(): lax.all_to_all(partials, 'dp', split_axis=0, concat_axis=0, tiled=True)  69.8 us
    all_gather x1, waiting for transfers between devices, body(): lax.all_gather(picked[None], 'dp', axis=0, tiled=True)  62.2 us
    ppermute x1, waiting for transfers between devices, passed_along(): return lax.ppermute(block, axis, route)  35.1 us
    dot_general x1, matrix products, body(): jnp.dot(activated, down_rows, preferred_element_type=jnp.float32)  22.7 us
    dot_general x1, matrix products, body(): jnp.dot(flat_rows, gate_cols, preferred_element_type=jnp.float32)  12.9 us
    all_to_all x1, starting transfers between devices, body(): lax.all_to_all(partials, 'dp', split_axis=0, concat_axis=0, tiled=True)  5.84 us
  transfers between devices with their start and end apart: 3, of which 3 were waited for; matrix products, arithmetic and copies ran while one was open for 0% of the time, Pallas kernels for 0%

commit v1 on v0

v1 whole, which is shorter than its diff:
```python
import jax
import jax.numpy as jnp
from jax import lax
from jax.sharding import Mesh, PartitionSpec as P


def shifted(block, axes, size, distance):
    route = [(i, (i + distance) % size) for i in range(size)]
    return lax.ppermute(block, axes, route)


def body(
    hidden_states,
    norm_gain,
    gate_weight,
    up_weight,
    down_weight,
    route_rows,
    route_count,
    route_gate,
):
    states = hidden_states[0]
    scale_gain = norm_gain[0]
    gate_cols = gate_weight[0]
    up_cols = up_weight[0]
    down_rows = down_weight[0]
    slot_rows = route_rows[0, 0]
    live_count = route_count[0, 0]
    slot_gates = route_gate[0, 0]
    tok_count, width = states.shape
    experts, capacity = slot_rows.shape
    sections = lax.axis_size("section")
    n_ex = lax.axis_size("ex")
    n_chip = lax.axis_size("chip")
    n_core = lax.axis_size("core")
    ex_me = lax.axis_index("ex")
    core_me = lax.axis_index("core")

    live_mask = jnp.arange(capacity)[None, :] < live_count[:, None]
    weighting = jnp.where(live_mask, slot_gates, 0.0)
    states_in = shifted(states, "section", sections, 1)
    rows_in = shifted(slot_rows, "section", sections, 1)
    weights_in = shifted(weighting, "section", sections, 1)

    chosen = jnp.take(states, slot_rows.reshape(-1), axis=0).astype(jnp.float32)
    normed = (
        chosen
        * lax.rsqrt(jnp.mean(chosen * chosen, axis=-1, keepdims=True) + 1e-05)
        * scale_gain.astype(jnp.float32)
    ).astype(jnp.bfloat16)
    picked = normed.reshape(experts, capacity, width)

    parts = [lax.dynamic_index_in_dim(picked, ex_me, 0, keepdims=False)]
    for k in range(1, n_ex):
        outgoing = lax.dynamic_index_in_dim(picked, (ex_me + k) % n_ex, 0, keepdims=False)
        parts.append(shifted(outgoing, "ex", n_ex, k))
    block = jnp.stack(parts)
    gathered = lax.all_gather(block, "chip", axis=0, tiled=False)
    gathered = lax.all_gather(gathered, "core", axis=0, tiled=False)
    flat_rows = gathered.reshape(-1, width)

    gate_part = jnp.dot(flat_rows, gate_cols, preferred_element_type=jnp.float32)
    up_part = jnp.dot(flat_rows, up_cols, preferred_element_type=jnp.float32)
    activated = (jax.nn.silu(gate_part) * up_part).astype(jnp.bfloat16)
    partial_out = jnp.dot(activated, down_rows, preferred_element_type=jnp.float32).astype(
        jnp.bfloat16
    )
    partials = partial_out.reshape(gathered.shape)

    summed = lax.dynamic_index_in_dim(partials, core_me, 0, keepdims=False).astype(jnp.float32)
    for k in range(1, n_core):
        outgoing = lax.dynamic_index_in_dim(partials, (core_me + k) % n_core, 0, keepdims=False)
        summed = summed + shifted(outgoing, "core", n_core, k).astype(jnp.float32)
    reduced = lax.psum_scatter(summed, "chip", scatter_dimension=0, tiled=False)

    got = []
    for k in range(n_ex):
        if k == 0:
            got.append(shifted(reduced[0], "section", sections, 1))
        else:
            route = []
            for s in range(sections):
                for e in range(n_ex):
                    route.append((s * n_ex + e, ((s + 1) % sections) * n_ex + (e - k) % n_ex))
            got.append(lax.ppermute(reduced[k], ("section", "ex"), route))
    stacked = jnp.stack(got)
    order = (ex_me + jnp.arange(n_ex)) % n_ex
    expert_out = jnp.zeros_like(stacked).at[order].set(stacked)

    one_hot = (rows_in[..., None] == jnp.arange(tok_count)[None, None, :]).astype(
        jnp.float32
    ) * weights_in[..., None]
    branch = jnp.einsum("ect,ecd->td", one_hot, expert_out, precision=lax.Precision.HIGHEST)
    layer_out = (states_in.astype(jnp.float32) + branch).astype(jnp.bfloat16)
    return layer_out[None]


def solution(mesh):
    def run(*args):
        experts = args[5].shape[2]
        sections, ranks = mesh.devices.shape
        owners = ranks // experts
        cores = 2 if owners % 2 == 0 else 1
        devices = mesh.devices.reshape(sections, experts, owners // cores, cores)
        fine = Mesh(devices, ("section", "ex", "chip", "core"))
        dp = ("ex", "chip", "core")
        placed = (
            P("section", dp, None),
            P("section", None),
            P("section", None, dp),
            P("section", None, dp),
            P("section", dp, None),
            P("section", dp, None, None),
            P("section", dp, None),
            P("section", dp, None, None),
        )
        return jax.shard_map(
            body, mesh=fine, in_specs=placed, out_specs=P("section", dp, None), check_vma=False
        )(*args)

    return run
```

time: 240 us -> 218 us (0.908)
  the two profiles are of different devices: /device:TPU:12 before, /device:TPU:0 now
where the time goes in v1:
time: 218 us
  waiting for transfers between devices  137 us (63%)
  matrix products  40.6 us (19%)
  between operations  13.2 us (6%)
  starting transfers between devices  12.1 us (6%)
  local copies, waits for them, and re-layouts  9.01 us (4%)
  other arithmetic  5.56 us (3%)
    reduce_scatter x1, waiting for transfers between devices, body(): reduced = lax.psum_scatter(summed, 'chip', scatter_dimension=0, tiled=False)  58 us
    all_gather x1, waiting for transfers between devices, body(): gathered = lax.all_gather(block, 'chip', axis=0, tiled=False)  36.9 us
    dot_general x1, matrix products, body(): jnp.dot(activated, down_rows, preferred_element_type=jnp.float32)  22.1 us
    ppermute x6, waiting for transfers between devices, shifted(): return lax.ppermute(block, axes, route)  18.8 us
    all_gather x1, waiting for transfers between devices, body(): gathered = lax.all_gather(gathered, 'core', axis=0, tiled=False)  13.5 us
    dot_general x1, matrix products, body(): jnp.dot(flat_rows, gate_cols, preferred_element_type=jnp.float32)  13.4 us
    ppermute x1, waiting for transfers between devices, body(): got.append(lax.ppermute(reduced[k], ('section', 'ex'), route))  10.2 us
    ppermute x6, starting transfers between devices, shifted(): return lax.ppermute(block, axes, route)  9.61 us
  transfers between devices with their start and end apart: 10, of which 7 were waited for; matrix products, arithmetic and copies ran while one was open for 1% of the time, Pallas kernels for 0%

profile of v1, /device:TPU:0, one launch (start us, length us, event | category | flops | bytes accessed | tf_op | source)
XLA Modules:
  0.0 217.9 jit_solution(14681833098117078266)
XLA Ops:
  6.5 0.0 copy-start.1
  6.5 0.0 all-gather.5.cloned.1.call-start
  6.5 0.8 reshape_squeeze.5
  7.3 0.8 reshape_squeeze.6
  8.1 0.7 compare_and_fusion.1
  8.8 2.8 %gather_fusion = bf16[32,6144]{1,0:T(8,128)(2,1)S(1)} fusion(bf16[128,6144]{1,0:T(8,128)(2,1)} %bitcast.55, s32[1024]{0:T(1024)S(1)} %pad_clamp_fusion), kind=kCustom, calls=%fused_computation | custom fusion | bytes 786560 | tf_op jit(solution)/shard_map/jit(_take)/gather | solution.py:45
  11.6 0.3 multiply_reduce_fusion
  11.9 0.1 rsqrt.12
  11.9 0.0 copy-done.1
  12.0 0.2 multiply_convert_fusion
  12.2 4.1 %collective-permute-start.3 = (bf16[16,6144]{1,0:T(8,128)(2,1)S(1)}, bf16[16,6144]{1,0:T(8,128)(2,1)S(1)}, u32[]{:S(2)}, u32[]{:S(2)}) collective-permute-start(bf16[16,6144]{1,0:T(8,128)(2,1)S(1)} %get-tuple-element.8), channel_id=1, source_target_pairs={{0,8},{8,0},{1,9},{9,1},{2,10},{10,2},{3,11},{11,3},{4,12},{12,4},... | collective-permute-start | bytes 589832 | tf_op jit(solution)/shard_map/ppermute | solution.py:9
  16.3 9.1 %collective-permute-done.3 = bf16[16,6144]{1,0:T(8,128)(2,1)S(1)} collective-permute-done((bf16[16,6144]{1,0:T(8,128)(2,1)S(1)}, bf16[16,6144]{1,0:T(8,128)(2,1)S(1)}, u32[]{:S(2)}, u32[]{:S(2)}) %collective-permute-start.3) | collective-permute-done | bytes 196640 | tf_op jit(solution)/shard_map/ppermute | solution.py:9
  25.4 0.8 pad_maximum_fusion.1
  26.2 0.0 all-gather.5.cloned.1.call-update
  26.2 0.0 all-gather.7.cloned.1.call-start
  26.3 36.9 %all-gather.5.cloned.1.call-done = bf16[8,16,6144]{2,1,0:T(8,128)(2,1)} async-done(((bf16[2,16,6144]{2,1,0:T(8,128)(2,1)}), bf16[8,16,6144]{2,1,0:T(8,128)(2,1)}) %all-gather.5.cloned.1.call-update) | async-done | bytes 1572880 | tf_op jit(solution)/shard_map/all_gather | solution.py:58
  63.2 0.0 all-gather.7.cloned.1.call-update
  63.2 0.0 reduce-scatter.2.cloned.1.call-start
  63.3 13.5 %all-gather.7.cloned.1.call-done = bf16[8,2,16,6144]{3,2,1,0:T(8,128)(2,1)} async-done(((bf16[4,2,16,6144]{3,2,1,0:T(8,128)(2,1)}), bf16[8,2,16,6144]{3,2,1,0:T(8,128)(2,1)}) %all-gather.7.cloned.1.call-update) | async-done | bytes 3145744 | tf_op jit(solution)/shard_map/all_gather | solution.py:59
  76.7 13.4 %fusion.4 = f32[256,2048]{1,0:T(8,128)} fusion(bf16[256,6144]{1,0:T(8,128)(2,1)} %bitcast.66, bf16[1,6144,2048]{2,1,0:T(8,128)(2,1)} %param.10), kind=kOutput, calls=%fused_computation.6 | convolution fusion | flops 6442450944 | bytes 30408704 | tf_op jit(solution)/shard_map/dot_general | solution.py:62
  90.2 22.1 %fusion.6 = bf16[256,6144]{1,0:T(8,128)(2,1)S(1)} fusion(bf16[1,2048,6144]{2,1,0:T(8,128)(2,1)} %param.12, bf16[256,6144]{1,0:T(8,128)(2,1)} %bitcast.67, bf16[1,6144,2048]{2,1,0:T(8,128)(2,1)} %param.11, f32[256,2048]{1,0:T(8,128)} %fusion.4), kind=kOutput, calls=%fused_computation.8 | convolution fusion | flops 12889620480 | bytes 58720256 | tf_op jit(solution)/shard_map/dot_general | solution.py:65
  112.3 1.3 dynamic-slice_bitcast_fusion
  113.5 0.2 collective-permute-start.4
  113.7 3.5 %collective-permute-done.4 = bf16[4,2,16,6144]{3,2,1,0:T(8,128)(2,1)} collective-permute-done((bf16[4,2,16,6144]{3,2,1,0:T(8,128)(2,1)}, bf16[4,2,16,6144]{3,2,1,0:T(8,128)(2,1)}, u32[]{:S(2)}, u32[]{:S(2)}) %collective-permute-start.4) | collective-permute-done | bytes 1572896 | tf_op jit(solution)/shard_map/ppermute | solution.py:9
  117.3 3.4 %convert_add_fusion = f32[4,2,16,6144]{3,2,1,0:T(8,128)} fusion(bf16[4,2,16,6144]{3,2,1,0:T(8,128)(2,1)} %collective-permute-done.4, bf16[2,4,2,16,6144]{4,3,2,1,0:T(8,128)(2,1)S(1)} %bitcast.59, s32[]{:T(128)S(6)} %select_n.89), kind=kLoop, calls=%fused_computation.10 | loop fusion | flops 2359296 | bytes 6291460 | tf_op jit(solution)/shard_map/add | solution.py:73
  120.7 0.0 copy-start
  120.7 0.0 copy-start.2
  120.7 0.0 copy-start.3
  120.7 0.0 copy-start.4
  120.7 0.0 reduce-scatter.2.cloned.1.call-update
  120.7 1.4 copy-done
  122.1 1.7 collective-permute-start
  123.8 58.0 %reduce-scatter.2.cloned.1.call-done = f32[1,2,16,6144]{3,2,1,0:T(8,128)} async-done(((f32[4,2,16,6144]{3,2,1,0:T(8,128)}), f32[1,2,16,6144]{3,2,1,0:T(8,128)}) %reduce-scatter.2.cloned.1.call-update) | async-done | bytes 786448 | tf_op jit(solution)/shard_map/reduce_scatter | solution.py:74
  181.8 1.2 slice_bitcast_fusion.1
  183.0 1.5 collective-permute-start.5
  184.5 2.4 %collective-permute-start.6 = (f32[16,6144]{1,0:T(8,128)S(1)}, f32[16,6144]{1,0:T(8,128)S(1)}, u32[]{:S(2)}, u32[]{:S(2)}) collective-permute-start(f32[16,6144]{1,0:T(8,128)S(1)} %get-tuple-element.6), channel_id=1, source_target_pairs={{0,24},{8,16},{16,8},{24,0},{1,25},{9,17},{17,9},{25,1},{2,26},{10... | collective-permute-start | bytes 1179656 | tf_op jit(solution)/shard_map/ppermute | solution.py:85
  186.9 0.0 copy-done.2
  186.9 0.0 copy-done.3
  186.9 0.1 compare_select_fusion.6
  187.0 1.5 collective-permute-start.2
  188.5 0.0 copy-done.4
  188.5 0.6 collective-permute-start.1
  189.1 6.2 %collective-permute-done.5 = f32[16,6144]{1,0:T(8,128)S(1)} collective-permute-done((f32[16,6144]{1,0:T(8,128)S(1)}, f32[16,6144]{1,0:T(8,128)S(1)}, u32[]{:S(2)}, u32[]{:S(2)}) %collective-permute-start.5) | collective-permute-done | bytes 393248 | tf_op jit(solution)/shard_map/ppermute | solution.py:9
  195.2 10.2 %collective-permute-done.6 = f32[16,6144]{1,0:T(8,128)S(1)} collective-permute-done((f32[16,6144]{1,0:T(8,128)S(1)}, f32[16,6144]{1,0:T(8,128)S(1)}, u32[]{:S(2)}, u32[]{:S(2)}) %collective-permute-start.6) | collective-permute-done | bytes 393248 | tf_op jit(solution)/shard_map/ppermute | solution.py:85
  205.4 0.1 pad_maximum_fusion
  205.4 0.1 broadcast_in_dim.32
  205.5 0.7 scatter_fusion
  206.2 0.0 collective-permute-done.2
  206.2 0.0 collective-permute-done.1
  206.3 0.0 collective-permute-done
  206.3 5.1 %fusion.22 = bf16[1,128,6144]{2,1,0:T(8,128)(2,1)} fusion(bf16[128,6144]{1,0:T(8,128)(2,1)} %collective-permute-done, f32[2,16,6144]{2,1,0:T(8,128)S(1)} %scatter_fusion, f32[2,16]{1,0:T(2,128)S(1)} %collective-permute-done.2, s32[2,16]{1,0:T(2,128)S(1)} %collective-permute-done.1), kind=kOutput, calls=%fused_computation.19 | convolution fusion | flops 304357376 | bytes 3932416 | tf_op jit(solution)/shard_map/ect,ecd->td/dot_general | solution.py:93
  (7 shorter events, 0.1 us)
Async XLA Ops:
  6.5 5.4 %copy-start.1 = (bf16[1,6144]{1,0:T(2,128)(2,1)S(1)}, bf16[1,6144]{1,0:T(2,128)(2,1)}, u32[]{:S(2)}) copy-start(bf16[1,6144]{1,0:T(2,128)(2,1)} %param.9) | copy-start | bytes 36868
  6.5 56.6 %all-gather.5.cloned.1.call-start = ((), (), s32[]{:S(2)}) async-start(), calls=%async_computation.2 | async-start | bytes 1966080 | tf_op jit(solution)/shard_map/all_gather | solution.py:58
  12.2 13.2 %collective-permute-start.3 = (bf16[16,6144]{1,0:T(8,128)(2,1)S(1)}, bf16[16,6144]{1,0:T(8,128)(2,1)S(1)}, u32[]{:S(2)}, u32[]{:S(2)}) collective-permute-start(bf16[16,6144]{1,0:T(8,128)(2,1)S(1)} %get-tuple-element.8), channel_id=1, source_target_pairs={{0,8},{8,0},{1,9},{9,1},{2,10},{10,2},{3,11},{11,3},{4,12},{12,4},... | collective-permute-start | bytes 589832 | tf_op jit(solution)/shard_map/ppermute | solution.py:9
  26.2 50.5 %all-gather.7.cloned.1.call-start = ((), (), s32[]{:S(2)}) async-start(), calls=%async_computation.3 | async-start | bytes 4718592 | tf_op jit(solution)/shard_map/all_gather | solution.py:59
  63.2 118.6 %reduce-scatter.2.cloned.1.call-start = ((), (), s32[]{:S(2)}) async-start(), calls=%async_computation.1 | async-start | bytes 3932160 | tf_op jit(solution)/shard_map/reduce_scatter | solution.py:74
  113.5 3.8 %collective-permute-start.4 = (bf16[4,2,16,6144]{3,2,1,0:T(8,128)(2,1)}, bf16[4,2,16,6144]{3,2,1,0:T(8,128)(2,1)}, u32[]{:S(2)}, u32[]{:S(2)}) collective-permute-start(bf16[4,2,16,6144]{3,2,1,0:T(8,128)(2,1)} %dynamic-slice_bitcast_fusion), channel_id=1, source_target_pairs={{0,1},{1,0},{2,3},{3,2},{4,5},{5,4},{6,7},{7,6},{8,9},{9,8},{10,11... | collective-permute-start | bytes 4718600 | tf_op jit(solution)/shard_map/ppermute | solution.py:9
  120.7 1.4 copy-start
  120.7 66.2 %copy-start.2 = (f32[1,1,2,16]{3,2,1,0:T(2,128)S(1)}, f32[1,1,2,16]{3,2,1,0:T(2,128)}, u32[]{:S(2)}) copy-start(f32[1,1,2,16]{3,2,1,0:T(2,128)} %param.15) | copy-start | bytes 388
  120.7 66.2 %copy-start.3 = (s32[1,1,2]{2,1,0:T(1,128)S(1)}, s32[1,1,2]{2,1,0:T(1,128)}, u32[]{:S(2)}) copy-start(s32[1,1,2]{2,1,0:T(1,128)} %param.14) | copy-start | bytes 28
  120.7 67.8 %copy-start.4 = (s32[1,1,2,16]{3,2,1,0:T(2,128)S(1)}, s32[1,1,2,16]{3,2,1,0:T(2,128)}, u32[]{:S(2)}) copy-start(s32[1,1,2,16]{3,2,1,0:T(2,128)} %param.13) | copy-start | bytes 388
  122.1 84.1 %collective-permute-start = (bf16[128,6144]{1,0:T(8,128)(2,1)S(1)}, bf16[128,6144]{1,0:T(8,128)(2,1)}, u32[]{:S(2)}, u32[]{:S(2)}) collective-permute-start(bf16[128,6144]{1,0:T(8,128)(2,1)S(1)} %bitcast.56), channel_id=1, source_target_pairs={{0,16},{16,0},{1,17},{17,1},{2,18},{18,2},{3,19},{19,3},{4,20},{20... | collective-permute-start | bytes 4718600 | tf_op jit(solution)/shard_map/ppermute | solution.py:9
  183.0 12.2 %collective-permute-start.5 = (f32[16,6144]{1,0:T(8,128)S(1)}, f32[16,6144]{1,0:T(8,128)S(1)}, u32[]{:S(2)}, u32[]{:S(2)}) collective-permute-start(f32[16,6144]{1,0:T(8,128)S(1)} %get-tuple-element.5), channel_id=1, source_target_pairs={{0,16},{16,0},{1,17},{17,1},{2,18},{18,2},{3,19},{19,3},{4,20},{20... | collective-permute-start | bytes 1179656 | tf_op jit(solution)/shard_map/ppermute | solution.py:9
  184.5 20.8 %collective-permute-start.6 = (f32[16,6144]{1,0:T(8,128)S(1)}, f32[16,6144]{1,0:T(8,128)S(1)}, u32[]{:S(2)}, u32[]{:S(2)}) collective-permute-start(f32[16,6144]{1,0:T(8,128)S(1)} %get-tuple-element.6), channel_id=1, source_target_pairs={{0,24},{8,16},{16,8},{24,0},{1,25},{9,17},{17,9},{25,1},{2,26},{10... | collective-permute-start | bytes 1179656 | tf_op jit(solution)/shard_map/ppermute | solution.py:85
  187.0 19.2 %collective-permute-start.2 = (f32[2,16]{1,0:T(2,128)S(1)}, f32[2,16]{1,0:T(2,128)S(1)}, u32[]{:S(2)}, u32[]{:S(2)}) collective-permute-start(f32[2,16]{1,0:T(2,128)S(1)} %compare_select_fusion.6), channel_id=1, source_target_pairs={{0,16},{16,0},{1,17},{17,1},{2,18},{18,2},{3,19},{19,3},{4,20},{20... | collective-permute-start | bytes 392 | tf_op jit(solution)/shard_map/ppermute | solution.py:9
  188.5 17.8 %collective-permute-start.1 = (s32[2,16]{1,0:T(2,128)S(1)}, s32[2,16]{1,0:T(2,128)S(1)}, u32[]{:S(2)}, u32[]{:S(2)}) collective-permute-start(s32[2,16]{1,0:T(2,128)S(1)} %bitcast.68), channel_id=1, source_target_pairs={{0,16},{16,0},{1,17},{17,1},{2,18},{18,2},{3,19},{19,3},{4,20},{20... | collective-permute-start | bytes 392 | tf_op jit(solution)/shard_map/ppermute | solution.py:9
Sparse Core Ops, SparseCore 0:
  26.4 36.7 all-gather.4
  64.7 11.9 all-gather.6
  120.9 60.9 reduce-scatter.1

commit v2 on v1

--- a/solution.py
+++ b/solution.py
@@ -3,9 +3,28 @@
 from jax import lax
 from jax.sharding import Mesh, PartitionSpec as P
 
+CHIP_SUM_DTYPE = jnp.float32
+HAND_DTYPE = jnp.float32
+
 
 def shifted(block, axes, size, distance):
     route = [(i, (i + distance) % size) for i in range(size)]
+    return lax.ppermute(block, axes, route)
+
+
+def partnered(block, axes, size, step):
+    if size & (size - 1) == 0:
+        route = [(i, i ^ step) for i in range(size)]
+    else:
+        route = [(i, (i + step) % size) for i in range(size)]
+    return lax.ppermute(block, axes, route)
+
+
+def back_partnered(block, axes, size, step):
+    if size & (size - 1) == 0:
+        route = [(i, i ^ step) for i in range(size)]
+    else:
+        route = [(i, (i - step) % size) for i in range(size)]
     return lax.ppermute(block, axes, route)
 
 
@@ -34,7 +53,6 @@
     n_chip = lax.axis_size("chip")
     n_core = lax.axis_size("core")
     ex_me = lax.axis_index("ex")
-    core_me = lax.axis_index("core")
 
     live_mask = jnp.arange(capacity)[None, :] < live_count[:, None]
     weighting = jnp.where(live_mask, slot_gates, 0.0)
@@ -55,8 +73,10 @@
         outgoing = lax.dynamic_index_in_dim(picked, (ex_me + k) % n_ex, 0, keepdims=False)
         parts.append(shifted(outgoing, "ex", n_ex, k))
     block = jnp.stack(parts)
-    gathered = lax.all_gather(block, "chip", axis=0, tiled=False)
-    gathered = lax.all_gather(gathered, "core", axis=0, tiled=False)
+    chip_rows = [block] + [partnered(block, "chip", n_chip, m) for m in range(1, n_chip)]
+    chip_rows = jnp.stack(chip_rows)
+    core_rows = [chip_rows] + [partnered(chip_rows, "core", n_core, q) for q in range(1, n_core)]
+    gathered = jnp.stack(core_rows)
     flat_rows = gathered.reshape(-1, width)
 
     gate_part = jnp.dot(flat_rows, gate_cols, preferred_element_type=jnp.float32)
@@ -67,23 +87,26 @@
     )
     partials = partial_out.reshape(gathered.shape)
 
-    summed = lax.dynamic_index_in_dim(partials, core_me, 0, keepdims=False).astype(jnp.float32)
-    for k in range(1, n_core):
-        outgoing = lax.dynamic_index_in_dim(partials, (core_me + k) % n_core, 0, keepdims=False)
-        summed = summed + shifted(outgoing, "core", n_core, k).astype(jnp.float32)
-    reduced = lax.psum_scatter(summed, "chip", scatter_dimension=0, tiled=False)
+    summed = partials[0].astype(jnp.float32)
+    for q in range(1, n_core):
+        summed = summed + back_partnered(partials[q], "core", n_core, q).astype(jnp.float32)
+    reduced = summed[0]
+    for m in range(1, n_chip):
+        sent = back_partnered(summed[m].astype(CHIP_SUM_DTYPE), "chip", n_chip, m)
+        reduced = reduced + sent.astype(jnp.float32)
 
     got = []
     for k in range(n_ex):
+        outgoing = reduced[k].astype(HAND_DTYPE)
         if k == 0:
-            got.append(shifted(reduced[0], "section", sections, 1))
+            got.append(shifted(outgoing, "section", sections, 1))
         else:
             route = []
             for s in range(sections):
                 for e in range(n_ex):
                     route.append((s * n_ex + e, ((s + 1) % sections) * n_ex + (e - k) % n_ex))
-            got.append(lax.ppermute(reduced[k], ("section", "ex"), route))
-    stacked = jnp.stack(got)
+            got.append(lax.ppermute(outgoing, ("section", "ex"), route))
+    stacked = jnp.stack(got).astype(jnp.float32)
     order = (ex_me + jnp.arange(n_ex)) % n_ex
     expert_out = jnp.zeros_like(stacked).at[order].set(stacked)
 

time: 218 us -> 151 us (0.69)
  waiting for transfers between devices: 137 us -> 80.3 us
  between operations: 13.2 us -> 0.2 us
  starting transfers between devices: 12.1 us -> 19.7 us
  other arithmetic: 5.56 us -> 2.55 us
    ppermute x1 -> x9, waiting for transfers between devices: 10.2 us -> 68.8 us  [the longest x4 37.2 us: back_partnered(): return lax.ppermute(block, axes, route)]
    reduce_scatter x1 -> x0, waiting for transfers between devices: 58 us -> none  [body(): reduced = lax.psum_scatter(summed, 'chip', scatter_dimension=0, tiled=False)]
    all_gather x2 -> x0, waiting for transfers between devices: 50.4 us -> none  [the longest x1 36.9 us: body(): gathered = lax.all_gather(block, 'chip', axis=0, tiled=False)]
    ppermute x1 -> x9, starting transfers between devices: 2.4 us -> 10.7 us  [the longest x4 3.76 us: back_partnered(): return lax.ppermute(block, axes, route)]
    ppermute x6 -> x5, waiting for transfers between devices: 18.8 us -> 11.5 us  [shifted(): return lax.ppermute(block, axes, route)]
    add x1 -> x2, other arithmetic: 3.42 us -> 0.6 us  [the longest x1 0.38 us: body(): summed + back_partnered(partials[q], 'core', n_core, q).astype(jnp.float32)]
    squeeze x2, local copies, waits for them, and re-layouts: 2.42 us -> 0.23 us  [the longest x1 0.17 us: body(): sent = back_partnered(summed[m].astype(CHIP_SUM_DTYPE), 'chip', n_chip, m)]
    ppermute x6 -> x5, starting transfers between devices: 9.61 us -> 8.93 us  [shifted(): return lax.ppermute(block, axes, route)]
  transfers between devices with their start and end apart: 10 -> 14, of which waited for: 7 -> 11; matrix products, arithmetic and copies ran while one was open for 1% -> 1% of each run, Pallas kernels for 0% -> 0%
where the time goes in v2:
time: 151 us; the launch traced here: 150 us
  waiting for transfers between devices  80.3 us (53%)
  matrix products  40.3 us (27%)
  starting transfers between devices  19.7 us (13%)
  local copies, waits for them, and re-layouts  7.29 us (5%)
  other arithmetic  2.55 us (2%)
    ppermute x4, waiting for transfers between devices, back_partnered(): return lax.ppermute(block, axes, route)  37.2 us
    dot_general x1, matrix products, body(): jnp.dot(activated, down_rows, preferred_element_type=jnp.float32)  22.2 us
    ppermute x4, waiting for transfers between devices, partnered(): return lax.ppermute(block, axes, route)  19.8 us
    dot_general x1, matrix products, body(): up_part = jnp.dot(flat_rows, up_cols, preferred_element_type=jnp.float32)  13 us
    ppermute x1, waiting for transfers between devices, body(): got.append(lax.ppermute(outgoing, ('section', 'ex'), route))  11.8 us
    ppermute x5, waiting for transfers between devices, shifted(): return lax.ppermute(block, axes, route)  11.5 us
    ppermute x5, starting transfers between devices, shifted(): return lax.ppermute(block, axes, route)  8.93 us
    dot_general x1, matrix products, body(): jnp.einsum('ect,ecd->td', one_hot, expert_out, precision=lax.Precision.HI...  5.09 us
  transfers between devices with their start and end apart: 14, of which 11 were waited for; matrix products, arithmetic and copies ran while one was open for 1% of the time, Pallas kernels for 0%

profile of v2, /device:TPU:0, one launch (start us, length us, event | category | flops | bytes accessed | tf_op | source)
XLA Modules:
  0.0 150.3 jit_solution(796086355019964224)
XLA Ops:
  0.0 0.0 copy-start.2
  0.0 0.8 reshape_squeeze.5
  0.8 0.8 reshape_squeeze.6
  1.5 0.7 compare_and_fusion.1
  2.2 2.8 %gather_fusion = bf16[32,6144]{1,0:T(8,128)(2,1)S(1)} fusion(bf16[128,6144]{1,0:T(8,128)(2,1)} %bitcast.71, s32[1024]{0:T(1024)S(1)} %pad_clamp_fusion), kind=kCustom, calls=%fused_computation | custom fusion | bytes 786560 | tf_op jit(solution)/shard_map/jit(_take)/gather | solution.py:63
  5.0 0.3 multiply_reduce_fusion
  5.3 0.1 rsqrt.12
  5.4 0.0 copy-done.2
  5.4 0.2 multiply_convert_fusion.2
  5.7 4.1 %collective-permute-start.3 = (bf16[16,6144]{1,0:T(8,128)(2,1)S(1)}, bf16[16,6144]{1,0:T(8,128)(2,1)S(1)}, u32[]{:S(2)}, u32[]{:S(2)}) collective-permute-start(bf16[16,6144]{1,0:T(8,128)(2,1)S(1)} %get-tuple-element.17), channel_id=1, source_target_pairs={{0,8},{8,0},{1,9},{9,1},{2,10},{10,2},{3,11},{11,3},{4,12},{12,4},... | collective-permute-start | bytes 589832 | tf_op jit(solution)/shard_map/ppermute | solution.py:12
  9.8 9.1 %collective-permute-done.3 = bf16[16,6144]{1,0:T(8,128)(2,1)S(1)} collective-permute-done((bf16[16,6144]{1,0:T(8,128)(2,1)S(1)}, bf16[16,6144]{1,0:T(8,128)(2,1)S(1)}, u32[]{:S(2)}, u32[]{:S(2)}) %collective-permute-start.3) | collective-permute-done | bytes 196640 | tf_op jit(solution)/shard_map/ppermute | solution.py:12
  18.9 0.1 fusion.29
  19.0 1.6 %collective-permute-start.4 = (bf16[2,16,6144]{2,1,0:T(8,128)(2,1)S(1)}, bf16[2,16,6144]{2,1,0:T(8,128)(2,1)S(1)}, u32[]{:S(2)}, u32[]{:S(2)}) collective-permute-start(bf16[2,16,6144]{2,1,0:T(8,128)(2,1)S(1)} %get-tuple-element.15), channel_id=1, source_target_pairs={{0,2},{2,0},{4,6},{6,4},{1,3},{3,1},{5,7},{7,5},{8,10},{10,8},{12,... | collective-permute-start | bytes 1179656 | tf_op jit(solution)/shard_map/ppermute | solution.py:20
  20.6 0.7 collective-permute-start.5
  21.3 1.2 collective-permute-start.6
  22.5 7.7 %collective-permute-done.4 = bf16[2,16,6144]{2,1,0:T(8,128)(2,1)S(1)} collective-permute-done((bf16[2,16,6144]{2,1,0:T(8,128)(2,1)S(1)}, bf16[2,16,6144]{2,1,0:T(8,128)(2,1)S(1)}, u32[]{:S(2)}, u32[]{:S(2)}) %collective-permute-start.4) | collective-permute-done | bytes 393248 | tf_op jit(solution)/shard_map/ppermute | solution.py:20
  30.2 2.5 %collective-permute-done.5 = bf16[2,16,6144]{2,1,0:T(8,128)(2,1)S(1)} collective-permute-done((bf16[2,16,6144]{2,1,0:T(8,128)(2,1)S(1)}, bf16[2,16,6144]{2,1,0:T(8,128)(2,1)S(1)}, u32[]{:S(2)}, u32[]{:S(2)}) %collective-permute-start.5) | collective-permute-done | bytes 393248 | tf_op jit(solution)/shard_map/ppermute | solution.py:20
  32.6 6.3 %collective-permute-done.6 = bf16[2,16,6144]{2,1,0:T(8,128)(2,1)S(1)} collective-permute-done((bf16[2,16,6144]{2,1,0:T(8,128)(2,1)S(1)}, bf16[2,16,6144]{2,1,0:T(8,128)(2,1)S(1)}, u32[]{:S(2)}, u32[]{:S(2)}) %collective-permute-start.6) | collective-permute-done | bytes 393248 | tf_op jit(solution)/shard_map/ppermute | solution.py:20
  38.9 0.3 fusion.30
  39.2 0.1 collective-permute-start.7
  39.3 3.4 %collective-permute-done.7 = bf16[4,2,16,6144]{3,2,1,0:T(8,128)(2,1)S(1)} collective-permute-done((bf16[4,2,16,6144]{3,2,1,0:T(8,128)(2,1)S(1)}, bf16[4,2,16,6144]{3,2,1,0:T(8,128)(2,1)S(1)}, u32[]{:S(2)}, u32[]{:S(2)}) %collective-permute-start.7) | collective-permute-done | bytes 1572896 | tf_op jit(solution)/shard_map/ppermute | solution.py:20
  42.7 0.3 pad_maximum_fusion
  43.0 0.0 copy-start.1
  43.0 1.6 %copy-done.1 = bf16[2,4,2,16,6144]{4,3,2,1,0:T(8,128)(2,1)} copy-done((bf16[2,4,2,16,6144]{4,3,2,1,0:T(8,128)(2,1)}, bf16[2,4,2,16,6144]{4,3,2,1,0:T(8,128)(2,1)S(1)}, u32[]{:S(2)}) %copy-start.1) | copy-done | bytes 3145752
  44.6 13.0 %fusion.2 = f32[256,2048]{1,0:T(8,128)} fusion(bf16[256,6144]{1,0:T(8,128)(2,1)S(1)} %bitcast.75, bf16[1,6144,2048]{2,1,0:T(8,128)(2,1)} %param.11), kind=kOutput, calls=%fused_computation.4 | convolution fusion | flops 6442450944 | bytes 30408704 | tf_op jit(solution)/shard_map/dot_general | solution.py:83
  57.6 22.2 %fusion.6 = bf16[256,6144]{1,0:T(8,128)(2,1)S(1)} fusion(bf16[1,2048,6144]{2,1,0:T(8,128)(2,1)} %param.12, f32[256,2048]{1,0:T(8,128)} %fusion.2, bf16[256,6144]{1,0:T(8,128)(2,1)} %bitcast.76, bf16[1,6144,2048]{2,1,0:T(8,128)(2,1)} %param.10), kind=kOutput, calls=%fused_computation.8 | convolution fusion | flops 12889620480 | bytes 58720256 | tf_op jit(solution)/shard_map/dot_general | solution.py:85
  79.8 0.2 fusion.31
  80.0 0.2 collective-permute-start.8
  80.2 3.3 %collective-permute-done.8 = bf16[4,2,16,6144]{3,2,1,0:T(8,128)(2,1)S(1)} collective-permute-done((bf16[4,2,16,6144]{3,2,1,0:T(8,128)(2,1)S(1)}, bf16[4,2,16,6144]{3,2,1,0:T(8,128)(2,1)S(1)}, u32[]{:S(2)}, u32[]{:S(2)}) %collective-permute-start.8) | collective-permute-done | bytes 1572896 | tf_op jit(solution)/shard_map/ppermute | solution.py:28
  83.5 0.4 convert_add_fusion
  83.9 0.0 copy-start
  83.9 0.2 slice_bitcast_fusion.2
  84.1 0.0 copy-start.3
  84.1 0.0 copy-start.4
  84.1 0.0 copy-start.5
  84.1 1.5 %collective-permute-start.10 = (f32[2,16,6144]{2,1,0:T(8,128)S(1)}, f32[2,16,6144]{2,1,0:T(8,128)S(1)}, u32[]{:S(2)}, u32[]{:S(2)}) collective-permute-start(f32[2,16,6144]{2,1,0:T(8,128)S(1)} %get-tuple-element.7), channel_id=1, source_target_pairs={{0,4},{2,6},{4,0},{6,2},{1,5},{3,7},{5,1},{7,3},{8,12},{10,14},{12... | collective-permute-start | bytes 2359304 | tf_op jit(solution)/shard_map/ppermute | solution.py:28
  85.7 1.3 collective-permute-start.11
  86.9 0.8 collective-permute-start.9
  87.7 0.0 copy-done
  87.7 1.2 collective-permute-start
  88.9 15.6 %collective-permute-done.10 = f32[2,16,6144]{2,1,0:T(8,128)S(1)} collective-permute-done((f32[2,16,6144]{2,1,0:T(8,128)S(1)}, f32[2,16,6144]{2,1,0:T(8,128)S(1)}, u32[]{:S(2)}, u32[]{:S(2)}) %collective-permute-start.10) | collective-permute-done | bytes 786464 | tf_op jit(solution)/shard_map/ppermute | solution.py:28
  104.6 16.9 %collective-permute-done.11 = f32[2,16,6144]{2,1,0:T(8,128)S(1)} collective-permute-done((f32[2,16,6144]{2,1,0:T(8,128)S(1)}, f32[2,16,6144]{2,1,0:T(8,128)S(1)}, u32[]{:S(2)}, u32[]{:S(2)}) %collective-permute-start.11) | collective-permute-done | bytes 786464 | tf_op jit(solution)/shard_map/ppermute | solution.py:28
  121.5 1.4 collective-permute-done.9
  122.8 0.2 fusion.17
  123.1 0.1 slice_bitcast_fusion.5
  123.1 1.6 %collective-permute-start.12 = (f32[16,6144]{1,0:T(8,128)S(1)}, f32[16,6144]{1,0:T(8,128)S(1)}, u32[]{:S(2)}, u32[]{:S(2)}) collective-permute-start(f32[16,6144]{1,0:T(8,128)S(1)} %get-tuple-element.12), channel_id=1, source_target_pairs={{0,16},{16,0},{1,17},{17,1},{2,18},{18,2},{3,19},{19,3},{4,20},{20... | collective-permute-start | bytes 1179656 | tf_op jit(solution)/shard_map/ppermute | solution.py:12
  124.7 3.4 %collective-permute-start.13 = (f32[16,6144]{1,0:T(8,128)S(1)}, f32[16,6144]{1,0:T(8,128)S(1)}, u32[]{:S(2)}, u32[]{:S(2)}) collective-permute-start(f32[16,6144]{1,0:T(8,128)S(1)} %get-tuple-element.13), channel_id=1, source_target_pairs={{0,24},{8,16},{16,8},{24,0},{1,25},{9,17},{17,9},{25,1},{2,26},{10... | collective-permute-start | bytes 1179656 | tf_op jit(solution)/shard_map/ppermute | solution.py:108
  128.0 0.0 copy-done.3
  128.0 0.0 copy-done.4
  128.0 0.1 compare_select_fusion.6
  128.1 1.5 collective-permute-start.2
  129.6 0.0 copy-done.5
  129.6 0.5 collective-permute-start.1
  130.2 2.4 %collective-permute-done.12 = f32[16,6144]{1,0:T(8,128)S(1)} collective-permute-done((f32[16,6144]{1,0:T(8,128)S(1)}, f32[16,6144]{1,0:T(8,128)S(1)}, u32[]{:S(2)}, u32[]{:S(2)}) %collective-permute-start.12) | collective-permute-done | bytes 393248 | tf_op jit(solution)/shard_map/ppermute | solution.py:12
  132.5 11.8 %collective-permute-done.13 = f32[16,6144]{1,0:T(8,128)S(1)} collective-permute-done((f32[16,6144]{1,0:T(8,128)S(1)}, f32[16,6144]{1,0:T(8,128)S(1)}, u32[]{:S(2)}, u32[]{:S(2)}) %collective-permute-start.13) | collective-permute-done | bytes 393248 | tf_op jit(solution)/shard_map/ppermute | solution.py:108
  144.3 0.1 pad_maximum_fusion.2
  144.4 0.1 broadcast_in_dim.32
  144.4 0.7 scatter_fusion
  145.2 0.0 collective-permute-done.2
  145.2 0.0 collective-permute-done.1
  145.2 0.0 collective-permute-done
  145.2 5.1 %fusion.9 = bf16[1,128,6144]{2,1,0:T(8,128)(2,1)} fusion(bf16[128,6144]{1,0:T(8,128)(2,1)} %collective-permute-done, f32[2,16,6144]{2,1,0:T(8,128)S(1)} %scatter_fusion, f32[2,16]{1,0:T(2,128)S(1)} %collective-permute-done.2, s32[2,16]{1,0:T(2,128)S(1)} %collective-permute-done.1), kind=kOutput, calls=%fused_computation.14 | convolution fusion | flops 304357376 | bytes 3932416 | tf_op jit(solution)/shard_map/ect,ecd->td/dot_general | solution.py:116
  (7 shorter events, 0.1 us)
Async XLA Ops:
  0.0 5.4 %copy-start.2 = (bf16[1,6144]{1,0:T(2,128)(2,1)S(1)}, bf16[1,6144]{1,0:T(2,128)(2,1)}, u32[]{:S(2)}) copy-start(bf16[1,6144]{1,0:T(2,128)(2,1)} %param.9) | copy-start | bytes 36868
  5.7 13.2 %collective-permute-start.3 = (bf16[16,6144]{1,0:T(8,128)(2,1)S(1)}, bf16[16,6144]{1,0:T(8,128)(2,1)S(1)}, u32[]{:S(2)}, u32[]{:S(2)}) collective-permute-start(bf16[16,6144]{1,0:T(8,128)(2,1)S(1)} %get-tuple-element.17), channel_id=1, source_target_pairs={{0,8},{8,0},{1,9},{9,1},{2,10},{10,2},{3,11},{11,3},{4,12},{12,4},... | collective-permute-start | bytes 589832 | tf_op jit(solution)/shard_map/ppermute | solution.py:12
  19.0 11.2 %collective-permute-start.4 = (bf16[2,16,6144]{2,1,0:T(8,128)(2,1)S(1)}, bf16[2,16,6144]{2,1,0:T(8,128)(2,1)S(1)}, u32[]{:S(2)}, u32[]{:S(2)}) collective-permute-start(bf16[2,16,6144]{2,1,0:T(8,128)(2,1)S(1)} %get-tuple-element.15), channel_id=1, source_target_pairs={{0,2},{2,0},{4,6},{6,4},{1,3},{3,1},{5,7},{7,5},{8,10},{10,8},{12,... | collective-permute-start | bytes 1179656 | tf_op jit(solution)/shard_map/ppermute | solution.py:20
  20.6 12.1 %collective-permute-start.5 = (bf16[2,16,6144]{2,1,0:T(8,128)(2,1)S(1)}, bf16[2,16,6144]{2,1,0:T(8,128)(2,1)S(1)}, u32[]{:S(2)}, u32[]{:S(2)}) collective-permute-start(bf16[2,16,6144]{2,1,0:T(8,128)(2,1)S(1)} %get-tuple-element.15), channel_id=1, source_target_pairs={{0,4},{2,6},{4,0},{6,2},{1,5},{3,7},{5,1},{7,3},{8,12},{10,14},{12... | collective-permute-start | bytes 1179656 | tf_op jit(solution)/shard_map/ppermute | solution.py:20
  21.3 17.7 %collective-permute-start.6 = (bf16[2,16,6144]{2,1,0:T(8,128)(2,1)S(1)}, bf16[2,16,6144]{2,1,0:T(8,128)(2,1)S(1)}, u32[]{:S(2)}, u32[]{:S(2)}) collective-permute-start(bf16[2,16,6144]{2,1,0:T(8,128)(2,1)S(1)} %get-tuple-element.15), channel_id=1, source_target_pairs={{0,6},{2,4},{4,2},{6,0},{1,7},{3,5},{5,3},{7,1},{8,14},{10,12},{12... | collective-permute-start | bytes 1179656 | tf_op jit(solution)/shard_map/ppermute | solution.py:20
  39.2 3.5 %collective-permute-start.7 = (bf16[4,2,16,6144]{3,2,1,0:T(8,128)(2,1)S(1)}, bf16[4,2,16,6144]{3,2,1,0:T(8,128)(2,1)S(1)}, u32[]{:S(2)}, u32[]{:S(2)}) collective-permute-start(bf16[4,2,16,6144]{3,2,1,0:T(8,128)(2,1)S(1)} %get-tuple-element.11), channel_id=1, source_target_pairs={{0,1},{1,0},{2,3},{3,2},{4,5},{5,4},{6,7},{7,6},{8,9},{9,8},{10,11... | collective-permute-start | bytes 4718600 | tf_op jit(solution)/shard_map/ppermute | solution.py:20
  43.0 1.7 %copy-start.1 = (bf16[2,4,2,16,6144]{4,3,2,1,0:T(8,128)(2,1)}, bf16[2,4,2,16,6144]{4,3,2,1,0:T(8,128)(2,1)S(1)}, u32[]{:S(2)}) copy-start(bf16[2,4,2,16,6144]{4,3,2,1,0:T(8,128)(2,1)S(1)} %pad_maximum_fusion) | copy-start | bytes 9437188
  80.0 3.5 %collective-permute-start.8 = (bf16[4,2,16,6144]{3,2,1,0:T(8,128)(2,1)S(1)}, bf16[4,2,16,6144]{3,2,1,0:T(8,128)(2,1)S(1)}, u32[]{:S(2)}, u32[]{:S(2)}) collective-permute-start(bf16[4,2,16,6144]{3,2,1,0:T(8,128)(2,1)S(1)} %bitcast.78), channel_id=1, source_target_pairs={{0,1},{1,0},{2,3},{3,2},{4,5},{5,4},{6,7},{7,6},{8,9},{9,8},{10,11... | collective-permute-start | bytes 4718600 | tf_op jit(solution)/shard_map/ppermute | solution.py:28
  83.9 3.8 %copy-start = (bf16[1,128,6144]{2,1,0:T(8,128)(2,1)S(1)}, bf16[1,128,6144]{2,1,0:T(8,128)(2,1)}, u32[]{:S(2)}) copy-start(bf16[1,128,6144]{2,1,0:T(8,128)(2,1)} %param.8) | copy-start | bytes 4718596
  84.1 43.9 %copy-start.3 = (f32[1,1,2,16]{3,2,1,0:T(2,128)S(1)}, f32[1,1,2,16]{3,2,1,0:T(2,128)}, u32[]{:S(2)}) copy-start(f32[1,1,2,16]{3,2,1,0:T(2,128)} %param.15) | copy-start | bytes 388
  84.1 43.9 %copy-start.4 = (s32[1,1,2]{2,1,0:T(1,128)S(1)}, s32[1,1,2]{2,1,0:T(1,128)}, u32[]{:S(2)}) copy-start(s32[1,1,2]{2,1,0:T(1,128)} %param.14) | copy-start | bytes 28
  84.1 45.5 %copy-start.5 = (s32[1,1,2,16]{3,2,1,0:T(2,128)S(1)}, s32[1,1,2,16]{3,2,1,0:T(2,128)}, u32[]{:S(2)}) copy-start(s32[1,1,2,16]{3,2,1,0:T(2,128)} %param.13) | copy-start | bytes 388
  84.1 20.5 %collective-permute-start.10 = (f32[2,16,6144]{2,1,0:T(8,128)S(1)}, f32[2,16,6144]{2,1,0:T(8,128)S(1)}, u32[]{:S(2)}, u32[]{:S(2)}) collective-permute-start(f32[2,16,6144]{2,1,0:T(8,128)S(1)} %get-tuple-element.7), channel_id=1, source_target_pairs={{0,4},{2,6},{4,0},{6,2},{1,5},{3,7},{5,1},{7,3},{8,12},{10,14},{12... | collective-permute-start | bytes 2359304 | tf_op jit(solution)/shard_map/ppermute | solution.py:28
  85.7 35.8 %collective-permute-start.11 = (f32[2,16,6144]{2,1,0:T(8,128)S(1)}, f32[2,16,6144]{2,1,0:T(8,128)S(1)}, u32[]{:S(2)}, u32[]{:S(2)}) collective-permute-start(f32[2,16,6144]{2,1,0:T(8,128)S(1)} %get-tuple-element.6), channel_id=1, source_target_pairs={{0,6},{2,4},{4,2},{6,0},{1,7},{3,5},{5,3},{7,1},{8,14},{10,12},{12... | collective-permute-start | bytes 2359304 | tf_op jit(solution)/shard_map/ppermute | solution.py:28
  86.9 35.9 %collective-permute-start.9 = (f32[2,16,6144]{2,1,0:T(8,128)S(1)}, f32[2,16,6144]{2,1,0:T(8,128)S(1)}, u32[]{:S(2)}, u32[]{:S(2)}) collective-permute-start(f32[2,16,6144]{2,1,0:T(8,128)S(1)} %get-tuple-element.5), channel_id=1, source_target_pairs={{0,2},{2,0},{4,6},{6,4},{1,3},{3,1},{5,7},{7,5},{8,10},{10,8},{12,... | collective-permute-start | bytes 2359304 | tf_op jit(solution)/shard_map/ppermute | solution.py:28
  87.7 57.5 %collective-permute-start = (bf16[128,6144]{1,0:T(8,128)(2,1)S(1)}, bf16[128,6144]{1,0:T(8,128)(2,1)}, u32[]{:S(2)}, u32[]{:S(2)}) collective-permute-start(bf16[128,6144]{1,0:T(8,128)(2,1)S(1)} %bitcast.72), channel_id=1, source_target_pairs={{0,16},{16,0},{1,17},{17,1},{2,18},{18,2},{3,19},{19,3},{4,20},{20... | collective-permute-start | bytes 4718600 | tf_op jit(solution)/shard_map/ppermute | solution.py:12
  123.1 9.4 %collective-permute-start.12 = (f32[16,6144]{1,0:T(8,128)S(1)}, f32[16,6144]{1,0:T(8,128)S(1)}, u32[]{:S(2)}, u32[]{:S(2)}) collective-permute-start(f32[16,6144]{1,0:T(8,128)S(1)} %get-tuple-element.12), channel_id=1, source_target_pairs={{0,16},{16,0},{1,17},{17,1},{2,18},{18,2},{3,19},{19,3},{4,20},{20... | collective-permute-start | bytes 1179656 | tf_op jit(solution)/shard_map/ppermute | solution.py:12
  124.7 19.6 %collective-permute-start.13 = (f32[16,6144]{1,0:T(8,128)S(1)}, f32[16,6144]{1,0:T(8,128)S(1)}, u32[]{:S(2)}, u32[]{:S(2)}) collective-permute-start(f32[16,6144]{1,0:T(8,128)S(1)} %get-tuple-element.13), channel_id=1, source_target_pairs={{0,24},{8,16},{16,8},{24,0},{1,25},{9,17},{17,9},{25,1},{2,26},{10... | collective-permute-start | bytes 1179656 | tf_op jit(solution)/shard_map/ppermute | solution.py:108
  128.1 17.1 %collective-permute-start.2 = (f32[2,16]{1,0:T(2,128)S(1)}, f32[2,16]{1,0:T(2,128)S(1)}, u32[]{:S(2)}, u32[]{:S(2)}) collective-permute-start(f32[2,16]{1,0:T(2,128)S(1)} %compare_select_fusion.6), channel_id=1, source_target_pairs={{0,16},{16,0},{1,17},{17,1},{2,18},{18,2},{3,19},{19,3},{4,20},{20... | collective-permute-start | bytes 392 | tf_op jit(solution)/shard_map/ppermute | solution.py:12
  129.6 15.6 %collective-permute-start.1 = (s32[2,16]{1,0:T(2,128)S(1)}, s32[2,16]{1,0:T(2,128)S(1)}, u32[]{:S(2)}, u32[]{:S(2)}) collective-permute-start(s32[2,16]{1,0:T(2,128)S(1)} %bitcast.87), channel_id=1, source_target_pairs={{0,16},{16,0},{1,17},{17,1},{2,18},{18,2},{3,19},{19,3},{4,20},{20... | collective-permute-start | bytes 392 | tf_op jit(solution)/shard_map/ppermute | solution.py:12

commit v3 on v2

--- a/solution.py
+++ b/solution.py
@@ -3,8 +3,8 @@
 from jax import lax
 from jax.sharding import Mesh, PartitionSpec as P
 
-CHIP_SUM_DTYPE = jnp.float32
-HAND_DTYPE = jnp.float32
+CHIP_SUM_DTYPE = jnp.bfloat16
+HAND_DTYPE = jnp.bfloat16
 
 
 def shifted(block, axes, size, distance):
@@ -60,7 +60,8 @@
     rows_in = shifted(slot_rows, "section", sections, 1)
     weights_in = shifted(weighting, "section", sections, 1)
 
-    chosen = jnp.take(states, slot_rows.reshape(-1), axis=0).astype(jnp.float32)
+    selector = (slot_rows.reshape(-1)[:, None] == jnp.arange(tok_count)[None, :]).astype(states.dtype)
+    chosen = jnp.dot(selector, states, preferred_element_type=jnp.float32)
     normed = (
         chosen
         * lax.rsqrt(jnp.mean(chosen * chosen, axis=-1, keepdims=True) + 1e-05)
@@ -72,11 +73,14 @@
     for k in range(1, n_ex):
         outgoing = lax.dynamic_index_in_dim(picked, (ex_me + k) % n_ex, 0, keepdims=False)
         parts.append(shifted(outgoing, "ex", n_ex, k))
-    block = jnp.stack(parts)
-    chip_rows = [block] + [partnered(block, "chip", n_chip, m) for m in range(1, n_chip)]
-    chip_rows = jnp.stack(chip_rows)
-    core_rows = [chip_rows] + [partnered(chip_rows, "core", n_core, q) for q in range(1, n_core)]
-    gathered = jnp.stack(core_rows)
+    chip_rows = [parts] + [
+        [partnered(part, "chip", n_chip, m) for part in parts] for m in range(1, n_chip)
+    ]
+    chip_rows = [jnp.stack([chip_rows[m][k] for m in range(n_chip)]) for k in range(n_ex)]
+    core_rows = [chip_rows] + [
+        [partnered(rows, "core", n_core, q) for rows in chip_rows] for q in range(1, n_core)
+    ]
+    gathered = jnp.stack([jnp.stack(core_rows[q], axis=1) for q in range(n_core)])
     flat_rows = gathered.reshape(-1, width)
 
     gate_part = jnp.dot(flat_rows, gate_cols, preferred_element_type=jnp.float32)

time: 151 us -> 128 us (0.85)
  waiting for transfers between devices: 80.3 us -> 58.9 us
  local copies, waits for them, and re-layouts: 7.29 us -> 3.91 us
  starting transfers between devices: 19.7 us -> 21.3 us
    ppermute x4, waiting for transfers between devices: 37.2 us -> 19.1 us  [back_partnered(): return lax.ppermute(block, axes, route)]
    ppermute x5, waiting for transfers between devices: 11.5 us -> 27.4 us  [shifted(): return lax.ppermute(block, axes, route)]
    ppermute x1, waiting for transfers between devices: 11.8 us -> 0.01 us  [body(): got.append(lax.ppermute(outgoing, ('section', 'ex'), route))]
    ppermute x4 -> x8, waiting for transfers between devices: 19.8 us -> 12.5 us  [partnered(): return lax.ppermute(block, axes, route)]
    ppermute x4 -> x8, starting transfers between devices: 3.62 us -> 6.98 us  [partnered(): return lax.ppermute(block, axes, route)]
    gather x1 -> x0, local copies, waits for them, and re-layouts: 2.77 us -> none  [body(): chosen = jnp.take(states, slot_rows.reshape(-1), axis=0).astype(jnp.float32)]
    slice x1, local copies, waits for them, and re-layouts: 0.2 us -> 2.2 us  [body(): partials[q]]
    ppermute x1, starting transfers between devices: 3.35 us -> 1.4 us  [body(): got.append(lax.ppermute(outgoing, ('section', 'ex'), route))]
  transfers between devices with their start and end apart: 14 -> 18, of which waited for: 11 -> 11; matrix products, arithmetic and copies ran while one was open for 1% -> 1% of each run, Pallas kernels for 0% -> 0%
where the time goes in v3:
time: 128 us; the launch traced here: 127 us
  waiting for transfers between devices  58.9 us (46%)
  matrix products  41.5 us (32%)
  starting transfers between devices  21.3 us (17%)
  local copies, waits for them, and re-layouts  3.91 us (3%)
  other arithmetic  1.58 us (1%)
    ppermute x5, waiting for transfers between devices, shifted(): return lax.ppermute(block, axes, route)  27.4 us
    dot_general x1, matrix products, body(): jnp.dot(activated, down_rows, preferred_element_type=jnp.float32)  22.6 us
    ppermute x4, waiting for transfers between devices, back_partnered(): return lax.ppermute(block, axes, route)  19.1 us
    dot_general x1, matrix products, body(): jnp.dot(flat_rows, gate_cols, preferred_element_type=jnp.float32)  13 us
    ppermute x8, waiting for transfers between devices, partnered(): return lax.ppermute(block, axes, route)  12.5 us
    ppermute x5, starting transfers between devices, shifted(): return lax.ppermute(block, axes, route)  9.17 us
    ppermute x8, starting transfers between devices, partnered(): return lax.ppermute(block, axes, route)  6.98 us
    dot_general x1, matrix products, body(): jnp.einsum('ect,ecd->td', one_hot, expert_out, precision=lax.Precision.HI...  3.97 us
  transfers between devices with their start and end apart: 18, of which 11 were waited for; matrix products, arithmetic and copies ran while one was open for 1% of the time, Pallas kernels for 0%

profile of v3, /device:TPU:0, one launch (start us, length us, event | category | flops | bytes accessed | tf_op | source)
XLA Modules:
  0.0 127.4 jit_solution(9322592924418177624)
XLA Ops:
  0.0 0.0 copy-start
  0.0 0.8 eq.35
  0.8 1.9 %multiply_reduce_fusion = (f32[32]{0:T(128)S(1)}, f32[32,6144]{1,0:T(8,128)S(1)}) fusion(bf16[1,128,6144]{2,1,0:T(8,128)(2,1)} %param.8, s32[32]{0:T(128)S(1)} %eq.35), kind=kOutput, calls=%fused_computation.31 | convolution fusion | flops 50728928 | bytes 2359552 | tf_op jit(solution)/shard_map/dot_general | solution.py:64
  2.7 0.0 copy-done
  2.7 0.1 multiply_convert_fusion
  2.9 4.1 %collective-permute-start.6 = (bf16[16,6144]{1,0:T(8,128)(2,1)S(1)}, bf16[16,6144]{1,0:T(8,128)(2,1)S(1)}, u32[]{:S(2)}, u32[]{:S(2)}) collective-permute-start(bf16[16,6144]{1,0:T(8,128)(2,1)S(1)} %get-tuple-element.19), channel_id=1, source_target_pairs={{0,8},{8,0},{1,9},{9,1},{2,10},{10,2},{3,11},{11,3},{4,12},{12,4},... | collective-permute-start | bytes 589832 | tf_op jit(solution)/shard_map/ppermute | solution.py:12
  7.0 2.5 %collective-permute-start.5 = (bf16[16,6144]{1,0:T(8,128)(2,1)S(1)}, bf16[16,6144]{1,0:T(8,128)(2,1)S(1)}, u32[]{:S(2)}, u32[]{:S(2)}) collective-permute-start(bf16[16,6144]{1,0:T(8,128)(2,1)S(1)} %bitcast.94), channel_id=1, source_target_pairs={{0,6},{2,4},{4,2},{6,0},{1,7},{3,5},{5,3},{7,1},{8,14},{10,12},{12... | collective-permute-start | bytes 589832 | tf_op jit(solution)/shard_map/ppermute | solution.py:20
  9.6 0.5 collective-permute-start.3
  10.1 0.4 collective-permute-start.4
  10.5 5.7 %collective-permute-done.6 = bf16[16,6144]{1,0:T(8,128)(2,1)S(1)} collective-permute-done((bf16[16,6144]{1,0:T(8,128)(2,1)S(1)}, bf16[16,6144]{1,0:T(8,128)(2,1)S(1)}, u32[]{:S(2)}, u32[]{:S(2)}) %collective-permute-start.6) | collective-permute-done | bytes 196640 | tf_op jit(solution)/shard_map/ppermute | solution.py:12
  16.2 1.6 %collective-permute-start.7 = (bf16[16,6144]{1,0:T(8,128)(2,1)S(1)}, bf16[16,6144]{1,0:T(8,128)(2,1)S(1)}, u32[]{:S(2)}, u32[]{:S(2)}) collective-permute-start(bf16[16,6144]{1,0:T(8,128)(2,1)S(1)} %collective-permute-done.6), channel_id=1, source_target_pairs={{0,2},{2,0},{4,6},{6,4},{1,3},{3,1},{5,7},{7,5},{8,10},{10,8},{12,... | collective-permute-start | bytes 589832 | tf_op jit(solution)/shard_map/ppermute | solution.py:20
  17.8 0.6 collective-permute-start.8
  18.4 0.4 collective-permute-done.5
  18.9 1.2 collective-permute-start.9
  20.0 0.0 collective-permute-done.3
  20.0 3.1 %collective-permute-done.4 = bf16[16,6144]{1,0:T(8,128)(2,1)S(1)} collective-permute-done((bf16[16,6144]{1,0:T(8,128)(2,1)S(1)}, bf16[16,6144]{1,0:T(8,128)(2,1)S(1)}, u32[]{:S(2)}, u32[]{:S(2)}) %collective-permute-start.4) | collective-permute-done | bytes 196640 | tf_op jit(solution)/shard_map/ppermute | solution.py:20
  23.1 0.1 fusion.43
  23.2 0.1 collective-permute-start.10
  23.3 0.0 collective-permute-done.7
  23.3 4.0 %collective-permute-done.8 = bf16[16,6144]{1,0:T(8,128)(2,1)S(1)} collective-permute-done((bf16[16,6144]{1,0:T(8,128)(2,1)S(1)}, bf16[16,6144]{1,0:T(8,128)(2,1)S(1)}, u32[]{:S(2)}, u32[]{:S(2)}) %collective-permute-start.8) | collective-permute-done | bytes 196640 | tf_op jit(solution)/shard_map/ppermute | solution.py:20
  27.3 2.7 %collective-permute-done.9 = bf16[16,6144]{1,0:T(8,128)(2,1)S(1)} collective-permute-done((bf16[16,6144]{1,0:T(8,128)(2,1)S(1)}, bf16[16,6144]{1,0:T(8,128)(2,1)S(1)}, u32[]{:S(2)}, u32[]{:S(2)}) %collective-permute-start.9) | collective-permute-done | bytes 196640 | tf_op jit(solution)/shard_map/ppermute | solution.py:20
  30.0 0.1 fusion.42
  30.2 0.1 collective-permute-start.11
  30.2 0.0 collective-permute-done.10
  30.3 2.3 %collective-permute-done.11 = bf16[4,16,6144]{2,1,0:T(8,128)(2,1)S(1)} collective-permute-done((bf16[4,16,6144]{2,1,0:T(8,128)(2,1)S(1)}, bf16[4,16,6144]{2,1,0:T(8,128)(2,1)S(1)}, u32[]{:S(2)}, u32[]{:S(2)}) %collective-permute-start.11) | collective-permute-done | bytes 786464 | tf_op jit(solution)/shard_map/ppermute | solution.py:20
  32.5 0.1 maximum_bitcast_fusion.1
  32.7 0.2 pad_maximum_fusion
  32.9 13.0 %fusion.4 = f32[256,2048]{1,0:T(8,128)} fusion(bf16[256,6144]{1,0:T(8,128)(2,1)S(1)} %bitcast.90, bf16[1,6144,2048]{2,1,0:T(8,128)(2,1)} %param.10), kind=kOutput, calls=%fused_computation.5 | convolution fusion | flops 6442450944 | bytes 30408704 | tf_op jit(solution)/shard_map/dot_general | solution.py:86
  45.9 22.6 %fusion.6 = bf16[256,6144]{1,0:T(8,128)(2,1)} fusion(bf16[1,2048,6144]{2,1,0:T(8,128)(2,1)} %param.12, bf16[256,6144]{1,0:T(8,128)(2,1)S(1)} %bitcast.91, bf16[1,6144,2048]{2,1,0:T(8,128)(2,1)} %param.11, f32[256,2048]{1,0:T(8,128)} %fusion.4), kind=kOutput, calls=%fused_computation.7 | convolution fusion | flops 12889620480 | bytes 58720256 | tf_op jit(solution)/shard_map/dot_general | solution.py:89
  68.5 2.2 %fusion.44 = (bf16[128,6144]{1,0:T(8,128)(2,1)S(1)}, bf16[128,6144]{1,0:T(8,128)(2,1)S(1)}) fusion(bf16[256,6144]{1,0:T(8,128)(2,1)} %fusion.6), kind=kLoop, calls=%fused_computation.62 | loop fusion | bytes 6291456 | tf_op jit(solution)/shard_map/slice | solution.py:96
  70.7 0.2 collective-permute-start.12
  70.9 3.3 %collective-permute-done.12 = bf16[4,2,16,6144]{3,2,1,0:T(8,128)(2,1)S(1)} collective-permute-done((bf16[4,2,16,6144]{3,2,1,0:T(8,128)(2,1)S(1)}, bf16[4,2,16,6144]{3,2,1,0:T(8,128)(2,1)S(1)}, u32[]{:S(2)}, u32[]{:S(2)}) %collective-permute-start.12) | collective-permute-done | bytes 1572896 | tf_op jit(solution)/shard_map/ppermute | solution.py:28
  74.2 0.5 fusion.41
  74.6 0.1 slice_bitcast_fusion.3
  74.7 0.0 copy-start.1
  74.7 0.0 copy-start.2
  74.8 0.0 copy-start.3
  74.8 1.5 %collective-permute-start.13 = (bf16[2,16,6144]{2,1,0:T(8,128)(2,1)S(1)}, bf16[2,16,6144]{2,1,0:T(8,128)(2,1)S(1)}, u32[]{:S(2)}, u32[]{:S(2)}) collective-permute-start(bf16[2,16,6144]{2,1,0:T(8,128)(2,1)S(1)} %get-tuple-element.9), channel_id=1, source_target_pairs={{0,2},{2,0},{4,6},{6,4},{1,3},{3,1},{5,7},{7,5},{8,10},{10,8},{12,... | collective-permute-start | bytes 1179656 | tf_op jit(solution)/shard_map/ppermute | solution.py:28
  76.3 0.6 collective-permute-start.14
  76.9 1.4 %collective-permute-start.15 = (bf16[2,16,6144]{2,1,0:T(8,128)(2,1)S(1)}, bf16[2,16,6144]{2,1,0:T(8,128)(2,1)S(1)}, u32[]{:S(2)}, u32[]{:S(2)}) collective-permute-start(bf16[2,16,6144]{2,1,0:T(8,128)(2,1)S(1)} %get-tuple-element.10), channel_id=1, source_target_pairs={{0,6},{2,4},{4,2},{6,0},{1,7},{3,5},{5,3},{7,1},{8,14},{10,12},{12... | collective-permute-start | bytes 1179656 | tf_op jit(solution)/shard_map/ppermute | solution.py:28
  78.3 1.5 %collective-permute-start = (bf16[128,6144]{1,0:T(8,128)(2,1)}, bf16[128,6144]{1,0:T(8,128)(2,1)S(1)}, u32[]{:S(2)}, u32[]{:S(2)}) collective-permute-start(bf16[128,6144]{1,0:T(8,128)(2,1)} %bitcast), channel_id=1, source_target_pairs={{0,16},{16,0},{1,17},{17,1},{2,18},{18,2},{3,19},{19,3},{4,20},{20... | collective-permute-start | bytes 4718600 | tf_op jit(solution)/shard_map/ppermute | solution.py:12
  79.8 6.2 %collective-permute-done.13 = bf16[2,16,6144]{2,1,0:T(8,128)(2,1)S(1)} collective-permute-done((bf16[2,16,6144]{2,1,0:T(8,128)(2,1)S(1)}, bf16[2,16,6144]{2,1,0:T(8,128)(2,1)S(1)}, u32[]{:S(2)}, u32[]{:S(2)}) %collective-permute-start.13) | collective-permute-done | bytes 393248 | tf_op jit(solution)/shard_map/ppermute | solution.py:28
  86.0 2.3 %collective-permute-done.14 = bf16[2,16,6144]{2,1,0:T(8,128)(2,1)S(1)} collective-permute-done((bf16[2,16,6144]{2,1,0:T(8,128)(2,1)S(1)}, bf16[2,16,6144]{2,1,0:T(8,128)(2,1)S(1)}, u32[]{:S(2)}, u32[]{:S(2)}) %collective-permute-start.14) | collective-permute-done | bytes 393248 | tf_op jit(solution)/shard_map/ppermute | solution.py:28
  88.3 7.3 %collective-permute-done.15 = bf16[2,16,6144]{2,1,0:T(8,128)(2,1)S(1)} collective-permute-done((bf16[2,16,6144]{2,1,0:T(8,128)(2,1)S(1)}, bf16[2,16,6144]{2,1,0:T(8,128)(2,1)S(1)}, u32[]{:S(2)}, u32[]{:S(2)}) %collective-permute-start.15) | collective-permute-done | bytes 393248 | tf_op jit(solution)/shard_map/ppermute | solution.py:28
  95.6 0.2 fusion.27
  95.8 1.6 %collective-permute-start.16 = (bf16[16,6144]{1,0:T(8,128)(2,1)S(1)}, bf16[16,6144]{1,0:T(8,128)(2,1)S(1)}, u32[]{:S(2)}, u32[]{:S(2)}) collective-permute-start(bf16[16,6144]{1,0:T(8,128)(2,1)S(1)} %get-tuple-element.16), channel_id=1, source_target_pairs={{0,16},{16,0},{1,17},{17,1},{2,18},{18,2},{3,19},{19,3},{4,20},{20... | collective-permute-start | bytes 589832 | tf_op jit(solution)/shard_map/ppermute | solution.py:12
  97.4 1.4 %collective-permute-start.17 = (bf16[16,6144]{1,0:T(8,128)(2,1)S(1)}, bf16[16,6144]{1,0:T(8,128)(2,1)S(1)}, u32[]{:S(2)}, u32[]{:S(2)}) collective-permute-start(bf16[16,6144]{1,0:T(8,128)(2,1)S(1)} %get-tuple-element.17), channel_id=1, source_target_pairs={{0,24},{8,16},{16,8},{24,0},{1,25},{9,17},{17,9},{25,1},{2,26},{10... | collective-permute-start | bytes 589832 | tf_op jit(solution)/shard_map/ppermute | solution.py:112
  98.8 0.0 copy-done.1
  98.8 0.0 copy-done.2
  98.8 0.1 compare_select_fusion.3
  98.9 1.5 %collective-permute-start.2 = (f32[2,16]{1,0:T(2,128)S(1)}, f32[2,16]{1,0:T(2,128)S(1)}, u32[]{:S(2)}, u32[]{:S(2)}) collective-permute-start(f32[2,16]{1,0:T(2,128)S(1)} %compare_select_fusion.3), channel_id=1, source_target_pairs={{0,16},{16,0},{1,17},{17,1},{2,18},{18,2},{3,19},{19,3},{4,20},{20... | collective-permute-start | bytes 392 | tf_op jit(solution)/shard_map/ppermute | solution.py:12
  100.4 0.0 copy-done.3
  100.4 0.5 collective-permute-start.1
  100.9 21.7 %collective-permute-done.16 = bf16[16,6144]{1,0:T(8,128)(2,1)S(1)} collective-permute-done((bf16[16,6144]{1,0:T(8,128)(2,1)S(1)}, bf16[16,6144]{1,0:T(8,128)(2,1)S(1)}, u32[]{:S(2)}, u32[]{:S(2)}) %collective-permute-start.16) | collective-permute-done | bytes 196640 | tf_op jit(solution)/shard_map/ppermute | solution.py:12
  122.6 0.0 collective-permute-done.17
  122.6 0.1 maximum_convert_fusion
  122.6 0.1 broadcast_in_dim.9
  122.7 0.7 scatter_fusion
  123.4 0.0 collective-permute-done.2
  123.4 0.0 collective-permute-done.1
  123.5 0.0 collective-permute-done
  123.5 4.0 %fusion.22 = bf16[1,128,6144]{2,1,0:T(8,128)(2,1)} fusion(bf16[128,6144]{1,0:T(8,128)(2,1)S(1)} %collective-permute-done, f32[2,16,6144]{2,1,0:T(8,128)S(1)} %scatter_fusion, f32[2,16]{1,0:T(2,128)S(1)} %collective-permute-done.2, s32[2,16]{1,0:T(2,128)S(1)} %collective-permute-done.1), kind=kOutput, calls=%fused_computation.19 | convolution fusion | flops 304357376 | bytes 3932416 | tf_op jit(solution)/shard_map/ect,ecd->td/dot_general | solution.py:120
  (5 shorter events, 0.1 us)
Async XLA Ops:
  0.0 2.7 %copy-start = (bf16[1,6144]{1,0:T(2,128)(2,1)S(1)}, bf16[1,6144]{1,0:T(2,128)(2,1)}, u32[]{:S(2)}) copy-start(bf16[1,6144]{1,0:T(2,128)(2,1)} %param.9) | copy-start | bytes 36868
  2.9 13.3 %collective-permute-start.6 = (bf16[16,6144]{1,0:T(8,128)(2,1)S(1)}, bf16[16,6144]{1,0:T(8,128)(2,1)S(1)}, u32[]{:S(2)}, u32[]{:S(2)}) collective-permute-start(bf16[16,6144]{1,0:T(8,128)(2,1)S(1)} %get-tuple-element.19), channel_id=1, source_target_pairs={{0,8},{8,0},{1,9},{9,1},{2,10},{10,2},{3,11},{11,3},{4,12},{12,4},... | collective-permute-start | bytes 589832 | tf_op jit(solution)/shard_map/ppermute | solution.py:12
  7.0 11.8 %collective-permute-start.5 = (bf16[16,6144]{1,0:T(8,128)(2,1)S(1)}, bf16[16,6144]{1,0:T(8,128)(2,1)S(1)}, u32[]{:S(2)}, u32[]{:S(2)}) collective-permute-start(bf16[16,6144]{1,0:T(8,128)(2,1)S(1)} %bitcast.94), channel_id=1, source_target_pairs={{0,6},{2,4},{4,2},{6,0},{1,7},{3,5},{5,3},{7,1},{8,14},{10,12},{12... | collective-permute-start | bytes 589832 | tf_op jit(solution)/shard_map/ppermute | solution.py:20
  9.6 10.5 %collective-permute-start.3 = (bf16[16,6144]{1,0:T(8,128)(2,1)S(1)}, bf16[16,6144]{1,0:T(8,128)(2,1)S(1)}, u32[]{:S(2)}, u32[]{:S(2)}) collective-permute-start(bf16[16,6144]{1,0:T(8,128)(2,1)S(1)} %bitcast.95), channel_id=1, source_target_pairs={{0,2},{2,0},{4,6},{6,4},{1,3},{3,1},{5,7},{7,5},{8,10},{10,8},{12,... | collective-permute-start | bytes 589832 | tf_op jit(solution)/shard_map/ppermute | solution.py:20
  10.1 13.0 %collective-permute-start.4 = (bf16[16,6144]{1,0:T(8,128)(2,1)S(1)}, bf16[16,6144]{1,0:T(8,128)(2,1)S(1)}, u32[]{:S(2)}, u32[]{:S(2)}) collective-permute-start(bf16[16,6144]{1,0:T(8,128)(2,1)S(1)} %bitcast.96), channel_id=1, source_target_pairs={{0,4},{2,6},{4,0},{6,2},{1,5},{3,7},{5,1},{7,3},{8,12},{10,14},{12... | collective-permute-start | bytes 589832 | tf_op jit(solution)/shard_map/ppermute | solution.py:20
  16.2 7.1 %collective-permute-start.7 = (bf16[16,6144]{1,0:T(8,128)(2,1)S(1)}, bf16[16,6144]{1,0:T(8,128)(2,1)S(1)}, u32[]{:S(2)}, u32[]{:S(2)}) collective-permute-start(bf16[16,6144]{1,0:T(8,128)(2,1)S(1)} %collective-permute-done.6), channel_id=1, source_target_pairs={{0,2},{2,0},{4,6},{6,4},{1,3},{3,1},{5,7},{7,5},{8,10},{10,8},{12,... | collective-permute-start | bytes 589832 | tf_op jit(solution)/shard_map/ppermute | solution.py:20
  17.8 9.5 %collective-permute-start.8 = (bf16[16,6144]{1,0:T(8,128)(2,1)S(1)}, bf16[16,6144]{1,0:T(8,128)(2,1)S(1)}, u32[]{:S(2)}, u32[]{:S(2)}) collective-permute-start(bf16[16,6144]{1,0:T(8,128)(2,1)S(1)} %collective-permute-done.6), channel_id=1, source_target_pairs={{0,4},{2,6},{4,0},{6,2},{1,5},{3,7},{5,1},{7,3},{8,12},{10,14},{12... | collective-permute-start | bytes 589832 | tf_op jit(solution)/shard_map/ppermute | solution.py:20
  18.9 11.2 %collective-permute-start.9 = (bf16[16,6144]{1,0:T(8,128)(2,1)S(1)}, bf16[16,6144]{1,0:T(8,128)(2,1)S(1)}, u32[]{:S(2)}, u32[]{:S(2)}) collective-permute-start(bf16[16,6144]{1,0:T(8,128)(2,1)S(1)} %collective-permute-done.6), channel_id=1, source_target_pairs={{0,6},{2,4},{4,2},{6,0},{1,7},{3,5},{5,3},{7,1},{8,14},{10,12},{12... | collective-permute-start | bytes 589832 | tf_op jit(solution)/shard_map/ppermute | solution.py:20
  23.2 7.0 %collective-permute-start.10 = (bf16[4,16,6144]{2,1,0:T(8,128)(2,1)S(1)}, bf16[4,16,6144]{2,1,0:T(8,128)(2,1)S(1)}, u32[]{:S(2)}, u32[]{:S(2)}) collective-permute-start(bf16[4,16,6144]{2,1,0:T(8,128)(2,1)S(1)} %get-tuple-element.13), channel_id=1, source_target_pairs={{0,1},{1,0},{2,3},{3,2},{4,5},{5,4},{6,7},{7,6},{8,9},{9,8},{10,11... | collective-permute-start | bytes 2359304 | tf_op jit(solution)/shard_map/ppermute | solution.py:20
  30.2 2.4 %collective-permute-start.11 = (bf16[4,16,6144]{2,1,0:T(8,128)(2,1)S(1)}, bf16[4,16,6144]{2,1,0:T(8,128)(2,1)S(1)}, u32[]{:S(2)}, u32[]{:S(2)}) collective-permute-start(bf16[4,16,6144]{2,1,0:T(8,128)(2,1)S(1)} %get-tuple-element.15), channel_id=1, source_target_pairs={{0,1},{1,0},{2,3},{3,2},{4,5},{5,4},{6,7},{7,6},{8,9},{9,8},{10,11... | collective-permute-start | bytes 2359304 | tf_op jit(solution)/shard_map/ppermute | solution.py:20
  70.7 3.5 %collective-permute-start.12 = (bf16[4,2,16,6144]{3,2,1,0:T(8,128)(2,1)S(1)}, bf16[4,2,16,6144]{3,2,1,0:T(8,128)(2,1)S(1)}, u32[]{:S(2)}, u32[]{:S(2)}) collective-permute-start(bf16[4,2,16,6144]{3,2,1,0:T(8,128)(2,1)S(1)} %bitcast.93), channel_id=1, source_target_pairs={{0,1},{1,0},{2,3},{3,2},{4,5},{5,4},{6,7},{7,6},{8,9},{9,8},{10,11... | collective-permute-start | bytes 4718600 | tf_op jit(solution)/shard_map/ppermute | solution.py:28
  74.7 24.1 %copy-start.1 = (f32[1,1,2,16]{3,2,1,0:T(2,128)S(1)}, f32[1,1,2,16]{3,2,1,0:T(2,128)}, u32[]{:S(2)}) copy-start(f32[1,1,2,16]{3,2,1,0:T(2,128)} %param.15) | copy-start | bytes 388
  74.7 24.0 %copy-start.2 = (s32[1,1,2]{2,1,0:T(1,128)S(1)}, s32[1,1,2]{2,1,0:T(1,128)}, u32[]{:S(2)}) copy-start(s32[1,1,2]{2,1,0:T(1,128)} %param.14) | copy-start | bytes 28
  74.8 25.6 %copy-start.3 = (s32[1,1,2,16]{3,2,1,0:T(2,128)S(1)}, s32[1,1,2,16]{3,2,1,0:T(2,128)}, u32[]{:S(2)}) copy-start(s32[1,1,2,16]{3,2,1,0:T(2,128)} %param.13) | copy-start | bytes 388
  74.8 11.2 %collective-permute-start.13 = (bf16[2,16,6144]{2,1,0:T(8,128)(2,1)S(1)}, bf16[2,16,6144]{2,1,0:T(8,128)(2,1)S(1)}, u32[]{:S(2)}, u32[]{:S(2)}) collective-permute-start(bf16[2,16,6144]{2,1,0:T(8,128)(2,1)S(1)} %get-tuple-element.9), channel_id=1, source_target_pairs={{0,2},{2,0},{4,6},{6,4},{1,3},{3,1},{5,7},{7,5},{8,10},{10,8},{12,... | collective-permute-start | bytes 1179656 | tf_op jit(solution)/shard_map/ppermute | solution.py:28
  76.3 12.0 %collective-permute-start.14 = (bf16[2,16,6144]{2,1,0:T(8,128)(2,1)S(1)}, bf16[2,16,6144]{2,1,0:T(8,128)(2,1)S(1)}, u32[]{:S(2)}, u32[]{:S(2)}) collective-permute-start(bf16[2,16,6144]{2,1,0:T(8,128)(2,1)S(1)} %get-tuple-element.11), channel_id=1, source_target_pairs={{0,4},{2,6},{4,0},{6,2},{1,5},{3,7},{5,1},{7,3},{8,12},{10,14},{12... | collective-permute-start | bytes 1179656 | tf_op jit(solution)/shard_map/ppermute | solution.py:28
  76.9 18.7 %collective-permute-start.15 = (bf16[2,16,6144]{2,1,0:T(8,128)(2,1)S(1)}, bf16[2,16,6144]{2,1,0:T(8,128)(2,1)S(1)}, u32[]{:S(2)}, u32[]{:S(2)}) collective-permute-start(bf16[2,16,6144]{2,1,0:T(8,128)(2,1)S(1)} %get-tuple-element.10), channel_id=1, source_target_pairs={{0,6},{2,4},{4,2},{6,0},{1,7},{3,5},{5,3},{7,1},{8,14},{10,12},{12... | collective-permute-start | bytes 1179656 | tf_op jit(solution)/shard_map/ppermute | solution.py:28
  78.3 45.1 %collective-permute-start = (bf16[128,6144]{1,0:T(8,128)(2,1)}, bf16[128,6144]{1,0:T(8,128)(2,1)S(1)}, u32[]{:S(2)}, u32[]{:S(2)}) collective-permute-start(bf16[128,6144]{1,0:T(8,128)(2,1)} %bitcast), channel_id=1, source_target_pairs={{0,16},{16,0},{1,17},{17,1},{2,18},{18,2},{3,19},{19,3},{4,20},{20... | collective-permute-start | bytes 4718600 | tf_op jit(solution)/shard_map/ppermute | solution.py:12
  95.8 26.7 %collective-permute-start.16 = (bf16[16,6144]{1,0:T(8,128)(2,1)S(1)}, bf16[16,6144]{1,0:T(8,128)(2,1)S(1)}, u32[]{:S(2)}, u32[]{:S(2)}) collective-permute-start(bf16[16,6144]{1,0:T(8,128)(2,1)S(1)} %get-tuple-element.16), channel_id=1, source_target_pairs={{0,16},{16,0},{1,17},{17,1},{2,18},{18,2},{3,19},{19,3},{4,20},{20... | collective-permute-start | bytes 589832 | tf_op jit(solution)/shard_map/ppermute | solution.py:12
  97.4 25.2 %collective-permute-start.17 = (bf16[16,6144]{1,0:T(8,128)(2,1)S(1)}, bf16[16,6144]{1,0:T(8,128)(2,1)S(1)}, u32[]{:S(2)}, u32[]{:S(2)}) collective-permute-start(bf16[16,6144]{1,0:T(8,128)(2,1)S(1)} %get-tuple-element.17), channel_id=1, source_target_pairs={{0,24},{8,16},{16,8},{24,0},{1,25},{9,17},{17,9},{25,1},{2,26},{10... | collective-permute-start | bytes 589832 | tf_op jit(solution)/shard_map/ppermute | solution.py:112
  98.9 24.6 %collective-permute-start.2 = (f32[2,16]{1,0:T(2,128)S(1)}, f32[2,16]{1,0:T(2,128)S(1)}, u32[]{:S(2)}, u32[]{:S(2)}) collective-permute-start(f32[2,16]{1,0:T(2,128)S(1)} %compare_select_fusion.3), channel_id=1, source_target_pairs={{0,16},{16,0},{1,17},{17,1},{2,18},{18,2},{3,19},{19,3},{4,20},{20... | collective-permute-start | bytes 392 | tf_op jit(solution)/shard_map/ppermute | solution.py:12
  100.4 23.1 %collective-permute-start.1 = (s32[2,16]{1,0:T(2,128)S(1)}, s32[2,16]{1,0:T(2,128)S(1)}, u32[]{:S(2)}, u32[]{:S(2)}) collective-permute-start(s32[2,16]{1,0:T(2,128)S(1)} %bitcast.110), channel_id=1, source_target_pairs={{0,16},{16,0},{1,17},{17,1},{2,18},{18,2},{3,19},{19,3},{4,20},{20... | collective-permute-start | bytes 392 | tf_op jit(solution)/shard_map/ppermute | solution.py:12

commit v4 on v3

--- a/solution.py
+++ b/solution.py
@@ -89,6 +89,9 @@
     partial_out = jnp.dot(activated, down_rows, preferred_element_type=jnp.float32).astype(
         jnp.bfloat16
     )
+    states_in, rows_in, weights_in, partial_out = lax.optimization_barrier(
+        (states_in, rows_in, weights_in, partial_out)
+    )
     partials = partial_out.reshape(gathered.shape)
 
     summed = partials[0].astype(jnp.float32)

time: 128 us -> 115 us (0.90)
  waiting for transfers between devices: 58.9 us -> 46 us
    ppermute x5, waiting for transfers between devices: 27.4 us -> 9.55 us  [shifted(): return lax.ppermute(block, axes, route)]
    ppermute x1, waiting for transfers between devices: 0.01 us -> 5.46 us  [body(): got.append(lax.ppermute(outgoing, ('section', 'ex'), route))]
    ppermute x8, waiting for transfers between devices: 12.5 us -> 10.4 us  [partnered(): return lax.ppermute(block, axes, route)]
    slice x1, local copies, waits for them, and re-layouts: 2.2 us -> 0.21 us  [body(): partials[q]]
    unnamed x8 -> x10, local copies, waits for them, and re-layouts: 0.02 us -> 1.63 us
    ppermute x4, waiting for transfers between devices: 19.1 us -> 20.7 us  [back_partnered(): return lax.ppermute(block, axes, route)]
  transfers between devices with their start and end apart: 18 -> 18, of which waited for: 11 -> 11; matrix products, arithmetic and copies ran while one was open for 1% -> 31% of each run, Pallas kernels for 0% -> 0%
where the time goes in v4:
time: 115 us
  waiting for transfers between devices  46 us (40%)
  matrix products  42.1 us (37%)
  starting transfers between devices  21.3 us (19%)
  local copies, waits for them, and re-layouts  3.53 us (3%)
  other arithmetic  1.59 us (1%)
    dot_general x1, matrix products, body(): jnp.dot(activated, down_rows, preferred_element_type=jnp.float32)  22.1 us
    ppermute x4, waiting for transfers between devices, back_partnered(): return lax.ppermute(block, axes, route)  20.7 us
    dot_general x1, matrix products, body(): jnp.dot(flat_rows, gate_cols, preferred_element_type=jnp.float32)  13 us
    ppermute x8, waiting for transfers between devices, partnered(): return lax.ppermute(block, axes, route)  10.4 us
    ppermute x5, waiting for transfers between devices, shifted(): return lax.ppermute(block, axes, route)  9.55 us
    ppermute x5, starting transfers between devices, shifted(): return lax.ppermute(block, axes, route)  8.28 us
    ppermute x8, starting transfers between devices, partnered(): return lax.ppermute(block, axes, route)  7.12 us
    ppermute x1, waiting for transfers between devices, body(): got.append(lax.ppermute(outgoing, ('section', 'ex'), route))  5.46 us
  transfers between devices with their start and end apart: 18, of which 11 were waited for; matrix products, arithmetic and copies ran while one was open for 31% of the time, Pallas kernels for 0%

profile of v4, /device:TPU:0, one launch (start us, length us, event | category | flops | bytes accessed | tf_op | source)
XLA Modules:
  0.0 114.7 jit_solution(16237943971188602508)
XLA Ops:
  0.0 0.0 copy-start.1
  0.0 0.8 eq.32
  0.8 1.9 %multiply_reduce_fusion = (f32[32]{0:T(128)S(1)}, f32[32,6144]{1,0:T(8,128)S(1)}) fusion(bf16[1,128,6144]{2,1,0:T(8,128)(2,1)} %param.8, s32[32]{0:T(128)S(1)} %eq.32), kind=kOutput, calls=%fused_computation.31 | convolution fusion | flops 50728928 | bytes 2359552 | tf_op jit(solution)/shard_map/dot_general | solution.py:64
  2.7 0.0 copy-done.1
  2.7 0.1 multiply_convert_fusion
  2.9 4.1 %collective-permute-start.6 = (bf16[16,6144]{1,0:T(8,128)(2,1)S(1)}, bf16[16,6144]{1,0:T(8,128)(2,1)S(1)}, u32[]{:S(2)}, u32[]{:S(2)}) collective-permute-start(bf16[16,6144]{1,0:T(8,128)(2,1)S(1)} %get-tuple-element.27), channel_id=1, source_target_pairs={{0,8},{8,0},{1,9},{9,1},{2,10},{10,2},{3,11},{11,3},{4,12},{12,4},... | collective-permute-start | bytes 589832 | tf_op jit(solution)/shard_map/ppermute | solution.py:12
  7.0 1.5 %collective-permute-start.3 = (bf16[16,6144]{1,0:T(8,128)(2,1)S(1)}, bf16[16,6144]{1,0:T(8,128)(2,1)S(1)}, u32[]{:S(2)}, u32[]{:S(2)}) collective-permute-start(bf16[16,6144]{1,0:T(8,128)(2,1)S(1)} %bitcast.94), channel_id=1, source_target_pairs={{0,2},{2,0},{4,6},{6,4},{1,3},{3,1},{5,7},{7,5},{8,10},{10,8},{12,... | collective-permute-start | bytes 589832 | tf_op jit(solution)/shard_map/ppermute | solution.py:20
  8.6 1.6 %collective-permute-start.4 = (bf16[16,6144]{1,0:T(8,128)(2,1)S(1)}, bf16[16,6144]{1,0:T(8,128)(2,1)S(1)}, u32[]{:S(2)}, u32[]{:S(2)}) collective-permute-start(bf16[16,6144]{1,0:T(8,128)(2,1)S(1)} %bitcast.95), channel_id=1, source_target_pairs={{0,4},{2,6},{4,0},{6,2},{1,5},{3,7},{5,1},{7,3},{8,12},{10,14},{12... | collective-permute-start | bytes 589832 | tf_op jit(solution)/shard_map/ppermute | solution.py:20
  10.1 0.4 collective-permute-start.5
  10.5 5.7 %collective-permute-done.6 = bf16[16,6144]{1,0:T(8,128)(2,1)S(1)} collective-permute-done((bf16[16,6144]{1,0:T(8,128)(2,1)S(1)}, bf16[16,6144]{1,0:T(8,128)(2,1)S(1)}, u32[]{:S(2)}, u32[]{:S(2)}) %collective-permute-start.6) | collective-permute-done | bytes 196640 | tf_op jit(solution)/shard_map/ppermute | solution.py:12
  16.2 1.6 %collective-permute-start.7 = (bf16[16,6144]{1,0:T(8,128)(2,1)S(1)}, bf16[16,6144]{1,0:T(8,128)(2,1)S(1)}, u32[]{:S(2)}, u32[]{:S(2)}) collective-permute-start(bf16[16,6144]{1,0:T(8,128)(2,1)S(1)} %collective-permute-done.6), channel_id=1, source_target_pairs={{0,2},{2,0},{4,6},{6,4},{1,3},{3,1},{5,7},{7,5},{8,10},{10,8},{12,... | collective-permute-start | bytes 589832 | tf_op jit(solution)/shard_map/ppermute | solution.py:20
  17.8 0.6 collective-permute-start.8
  18.4 0.0 collective-permute-done.3
  18.4 1.3 %collective-permute-start.9 = (bf16[16,6144]{1,0:T(8,128)(2,1)S(1)}, bf16[16,6144]{1,0:T(8,128)(2,1)S(1)}, u32[]{:S(2)}, u32[]{:S(2)}) collective-permute-start(bf16[16,6144]{1,0:T(8,128)(2,1)S(1)} %collective-permute-done.6), channel_id=1, source_target_pairs={{0,6},{2,4},{4,2},{6,0},{1,7},{3,5},{5,3},{7,1},{8,14},{10,12},{12... | collective-permute-start | bytes 589832 | tf_op jit(solution)/shard_map/ppermute | solution.py:20
  19.7 0.0 collective-permute-done.4
  19.7 3.9 %collective-permute-done.5 = bf16[16,6144]{1,0:T(8,128)(2,1)S(1)} collective-permute-done((bf16[16,6144]{1,0:T(8,128)(2,1)S(1)}, bf16[16,6144]{1,0:T(8,128)(2,1)S(1)}, u32[]{:S(2)}, u32[]{:S(2)}) %collective-permute-start.5) | collective-permute-done | bytes 196640 | tf_op jit(solution)/shard_map/ppermute | solution.py:20
  23.6 0.0 copy-start.2
  23.6 0.0 copy-start.3
  23.7 0.0 copy-start.4
  23.7 0.1 fusion.43
  23.8 0.1 collective-permute-start.10
  23.9 2.6 %collective-permute-done.7 = bf16[16,6144]{1,0:T(8,128)(2,1)S(1)} collective-permute-done((bf16[16,6144]{1,0:T(8,128)(2,1)S(1)}, bf16[16,6144]{1,0:T(8,128)(2,1)S(1)}, u32[]{:S(2)}, u32[]{:S(2)}) %collective-permute-start.7) | collective-permute-done | bytes 196640 | tf_op jit(solution)/shard_map/ppermute | solution.py:20
  26.5 1.3 %collective-permute-done.8 = bf16[16,6144]{1,0:T(8,128)(2,1)S(1)} collective-permute-done((bf16[16,6144]{1,0:T(8,128)(2,1)S(1)}, bf16[16,6144]{1,0:T(8,128)(2,1)S(1)}, u32[]{:S(2)}, u32[]{:S(2)}) %collective-permute-start.8) | collective-permute-done | bytes 196640 | tf_op jit(solution)/shard_map/ppermute | solution.py:20
  27.8 2.5 %collective-permute-done.9 = bf16[16,6144]{1,0:T(8,128)(2,1)S(1)} collective-permute-done((bf16[16,6144]{1,0:T(8,128)(2,1)S(1)}, bf16[16,6144]{1,0:T(8,128)(2,1)S(1)}, u32[]{:S(2)}, u32[]{:S(2)}) %collective-permute-start.9) | collective-permute-done | bytes 196640 | tf_op jit(solution)/shard_map/ppermute | solution.py:20
  30.3 0.1 fusion.42
  30.5 0.1 collective-permute-start.11
  30.5 1.6 %collective-permute-start = (bf16[128,6144]{1,0:T(8,128)(2,1)}, bf16[128,6144]{1,0:T(8,128)(2,1)}, u32[]{:S(2)}, u32[]{:S(2)}) collective-permute-start(bf16[128,6144]{1,0:T(8,128)(2,1)} %bitcast), channel_id=1, source_target_pairs={{0,16},{16,0},{1,17},{17,1},{2,18},{18,2},{3,19},{19,3},{4,20},{20... | collective-permute-start | bytes 4718600 | tf_op jit(solution)/shard_map/ppermute | solution.py:12
  32.1 0.0 copy-done.2
  32.1 0.0 copy-done.3
  32.1 0.1 compare_select_fusion.3
  32.2 0.5 collective-permute-start.2
  32.7 0.0 copy-done.4
  32.7 1.5 %collective-permute-start.1 = (s32[2,16]{1,0:T(2,128)S(1)}, s32[2,16]{1,0:T(2,128)S(1)}, u32[]{:S(2)}, u32[]{:S(2)}) collective-permute-start(s32[2,16]{1,0:T(2,128)S(1)} %bitcast.110), channel_id=1, source_target_pairs={{0,16},{16,0},{1,17},{17,1},{2,18},{18,2},{3,19},{19,3},{4,20},{20... | collective-permute-start | bytes 392 | tf_op jit(solution)/shard_map/ppermute | solution.py:12
  34.2 0.0 collective-permute-done.10
  34.2 0.0 collective-permute-done.11
  34.2 0.1 maximum_bitcast_fusion.1
  34.4 0.2 pad_maximum_fusion
  34.6 0.0 copy-start
  34.6 1.6 %copy-done = bf16[2,4,2,16,6144]{4,3,2,1,0:T(8,128)(2,1)} copy-done((bf16[2,4,2,16,6144]{4,3,2,1,0:T(8,128)(2,1)}, bf16[2,4,2,16,6144]{4,3,2,1,0:T(8,128)(2,1)S(1)}, u32[]{:S(2)}) %copy-start) | copy-done | bytes 3145752
  36.2 13.0 %fusion.4 = f32[256,2048]{1,0:T(8,128)} fusion(bf16[256,6144]{1,0:T(8,128)(2,1)S(1)} %bitcast.90, bf16[1,6144,2048]{2,1,0:T(8,128)(2,1)} %param.10), kind=kOutput, calls=%fused_computation.5 | convolution fusion | flops 6442450944 | bytes 30408704 | tf_op jit(solution)/shard_map/dot_general | solution.py:86
  49.2 22.1 %fusion.6 = bf16[256,6144]{1,0:T(8,128)(2,1)S(1)} fusion(bf16[1,2048,6144]{2,1,0:T(8,128)(2,1)} %param.12, bf16[256,6144]{1,0:T(8,128)(2,1)} %bitcast.91, bf16[1,6144,2048]{2,1,0:T(8,128)(2,1)} %param.11, f32[256,2048]{1,0:T(8,128)} %fusion.4), kind=kOutput, calls=%fused_computation.7 | convolution fusion | flops 12889620480 | bytes 58720256 | tf_op jit(solution)/shard_map/dot_general | solution.py:89
  71.3 0.0 collective-permute-done.2
  71.3 0.0 collective-permute-done.1
  71.3 0.0 collective-permute-done
  71.3 0.2 fusion.44
  71.5 0.1 collective-permute-start.12
  71.6 3.4 %collective-permute-done.12 = bf16[4,2,16,6144]{3,2,1,0:T(8,128)(2,1)S(1)} collective-permute-done((bf16[4,2,16,6144]{3,2,1,0:T(8,128)(2,1)S(1)}, bf16[4,2,16,6144]{3,2,1,0:T(8,128)(2,1)S(1)}, u32[]{:S(2)}, u32[]{:S(2)}) %collective-permute-start.12) | collective-permute-done | bytes 1572896 | tf_op jit(solution)/shard_map/ppermute | solution.py:28
  75.0 0.5 fusion.41
  75.5 0.1 slice_bitcast_fusion.3
  75.6 1.6 %collective-permute-start.13 = (bf16[2,16,6144]{2,1,0:T(8,128)(2,1)S(1)}, bf16[2,16,6144]{2,1,0:T(8,128)(2,1)S(1)}, u32[]{:S(2)}, u32[]{:S(2)}) collective-permute-start(bf16[2,16,6144]{2,1,0:T(8,128)(2,1)S(1)} %get-tuple-element.17), channel_id=1, source_target_pairs={{0,2},{2,0},{4,6},{6,4},{1,3},{3,1},{5,7},{7,5},{8,10},{10,8},{12,... | collective-permute-start | bytes 1179656 | tf_op jit(solution)/shard_map/ppermute | solution.py:28
  77.2 0.2 collective-permute-start.14
  77.4 1.8 %collective-permute-start.15 = (bf16[2,16,6144]{2,1,0:T(8,128)(2,1)S(1)}, bf16[2,16,6144]{2,1,0:T(8,128)(2,1)S(1)}, u32[]{:S(2)}, u32[]{:S(2)}) collective-permute-start(bf16[2,16,6144]{2,1,0:T(8,128)(2,1)S(1)} %get-tuple-element.18), channel_id=1, source_target_pairs={{0,6},{2,4},{4,2},{6,0},{1,7},{3,5},{5,3},{7,1},{8,14},{10,12},{12... | collective-permute-start | bytes 1179656 | tf_op jit(solution)/shard_map/ppermute | solution.py:28
  79.1 7.7 %collective-permute-done.13 = bf16[2,16,6144]{2,1,0:T(8,128)(2,1)S(1)} collective-permute-done((bf16[2,16,6144]{2,1,0:T(8,128)(2,1)S(1)}, bf16[2,16,6144]{2,1,0:T(8,128)(2,1)S(1)}, u32[]{:S(2)}, u32[]{:S(2)}) %collective-permute-start.13) | collective-permute-done | bytes 393248 | tf_op jit(solution)/shard_map/ppermute | solution.py:28
  86.8 2.4 %collective-permute-done.14 = bf16[2,16,6144]{2,1,0:T(8,128)(2,1)S(1)} collective-permute-done((bf16[2,16,6144]{2,1,0:T(8,128)(2,1)S(1)}, bf16[2,16,6144]{2,1,0:T(8,128)(2,1)S(1)}, u32[]{:S(2)}, u32[]{:S(2)}) %collective-permute-start.14) | collective-permute-done | bytes 393248 | tf_op jit(solution)/shard_map/ppermute | solution.py:28
  89.2 7.2 %collective-permute-done.15 = bf16[2,16,6144]{2,1,0:T(8,128)(2,1)S(1)} collective-permute-done((bf16[2,16,6144]{2,1,0:T(8,128)(2,1)S(1)}, bf16[2,16,6144]{2,1,0:T(8,128)(2,1)S(1)}, u32[]{:S(2)}, u32[]{:S(2)}) %collective-permute-start.15) | collective-permute-done | bytes 393248 | tf_op jit(solution)/shard_map/ppermute | solution.py:28
  96.4 0.2 fusion.27
  96.6 0.6 collective-permute-start.16
  97.2 2.2 %collective-permute-start.17 = (bf16[16,6144]{1,0:T(8,128)(2,1)S(1)}, bf16[16,6144]{1,0:T(8,128)(2,1)S(1)}, u32[]{:S(2)}, u32[]{:S(2)}) collective-permute-start(bf16[16,6144]{1,0:T(8,128)(2,1)S(1)} %get-tuple-element.25), channel_id=1, source_target_pairs={{0,24},{8,16},{16,8},{24,0},{1,25},{9,17},{17,9},{25,1},{2,26},{10... | collective-permute-start | bytes 589832 | tf_op jit(solution)/shard_map/ppermute | solution.py:115
  99.5 3.8 %collective-permute-done.16 = bf16[16,6144]{1,0:T(8,128)(2,1)S(1)} collective-permute-done((bf16[16,6144]{1,0:T(8,128)(2,1)S(1)}, bf16[16,6144]{1,0:T(8,128)(2,1)S(1)}, u32[]{:S(2)}, u32[]{:S(2)}) %collective-permute-start.16) | collective-permute-done | bytes 196640 | tf_op jit(solution)/shard_map/ppermute | solution.py:12
  103.3 5.5 %collective-permute-done.17 = bf16[16,6144]{1,0:T(8,128)(2,1)S(1)} collective-permute-done((bf16[16,6144]{1,0:T(8,128)(2,1)S(1)}, bf16[16,6144]{1,0:T(8,128)(2,1)S(1)}, u32[]{:S(2)}, u32[]{:S(2)}) %collective-permute-start.17) | collective-permute-done | bytes 196640 | tf_op jit(solution)/shard_map/ppermute | solution.py:115
  108.8 0.1 maximum_convert_fusion
  108.8 0.1 broadcast_in_dim.9
  108.9 0.7 scatter_fusion
  109.6 5.1 %fusion.22 = bf16[1,128,6144]{2,1,0:T(8,128)(2,1)} fusion(bf16[128,6144]{1,0:T(8,128)(2,1)} %collective-permute-done, f32[2,16,6144]{2,1,0:T(8,128)S(1)} %scatter_fusion, f32[2,16]{1,0:T(2,128)S(1)} %collective-permute-done.2, s32[2,16]{1,0:T(2,128)S(1)} %collective-permute-done.1), kind=kOutput, calls=%fused_computation.19 | convolution fusion | flops 304357376 | bytes 3932416 | tf_op jit(solution)/shard_map/ect,ecd->td/dot_general | solution.py:123
  (5 shorter events, 0.1 us)
Async XLA Ops:
  0.0 2.7 %copy-start.1 = (bf16[1,6144]{1,0:T(2,128)(2,1)S(1)}, bf16[1,6144]{1,0:T(2,128)(2,1)}, u32[]{:S(2)}) copy-start(bf16[1,6144]{1,0:T(2,128)(2,1)} %param.9) | copy-start | bytes 36868
  2.9 13.3 %collective-permute-start.6 = (bf16[16,6144]{1,0:T(8,128)(2,1)S(1)}, bf16[16,6144]{1,0:T(8,128)(2,1)S(1)}, u32[]{:S(2)}, u32[]{:S(2)}) collective-permute-start(bf16[16,6144]{1,0:T(8,128)(2,1)S(1)} %get-tuple-element.27), channel_id=1, source_target_pairs={{0,8},{8,0},{1,9},{9,1},{2,10},{10,2},{3,11},{11,3},{4,12},{12,4},... | collective-permute-start | bytes 589832 | tf_op jit(solution)/shard_map/ppermute | solution.py:12
  7.0 11.4 %collective-permute-start.3 = (bf16[16,6144]{1,0:T(8,128)(2,1)S(1)}, bf16[16,6144]{1,0:T(8,128)(2,1)S(1)}, u32[]{:S(2)}, u32[]{:S(2)}) collective-permute-start(bf16[16,6144]{1,0:T(8,128)(2,1)S(1)} %bitcast.94), channel_id=1, source_target_pairs={{0,2},{2,0},{4,6},{6,4},{1,3},{3,1},{5,7},{7,5},{8,10},{10,8},{12,... | collective-permute-start | bytes 589832 | tf_op jit(solution)/shard_map/ppermute | solution.py:20
  8.6 11.2 %collective-permute-start.4 = (bf16[16,6144]{1,0:T(8,128)(2,1)S(1)}, bf16[16,6144]{1,0:T(8,128)(2,1)S(1)}, u32[]{:S(2)}, u32[]{:S(2)}) collective-permute-start(bf16[16,6144]{1,0:T(8,128)(2,1)S(1)} %bitcast.95), channel_id=1, source_target_pairs={{0,4},{2,6},{4,0},{6,2},{1,5},{3,7},{5,1},{7,3},{8,12},{10,14},{12... | collective-permute-start | bytes 589832 | tf_op jit(solution)/shard_map/ppermute | solution.py:20
  10.1 13.5 %collective-permute-start.5 = (bf16[16,6144]{1,0:T(8,128)(2,1)S(1)}, bf16[16,6144]{1,0:T(8,128)(2,1)S(1)}, u32[]{:S(2)}, u32[]{:S(2)}) collective-permute-start(bf16[16,6144]{1,0:T(8,128)(2,1)S(1)} %bitcast.96), channel_id=1, source_target_pairs={{0,6},{2,4},{4,2},{6,0},{1,7},{3,5},{5,3},{7,1},{8,14},{10,12},{12... | collective-permute-start | bytes 589832 | tf_op jit(solution)/shard_map/ppermute | solution.py:20
  16.2 10.2 %collective-permute-start.7 = (bf16[16,6144]{1,0:T(8,128)(2,1)S(1)}, bf16[16,6144]{1,0:T(8,128)(2,1)S(1)}, u32[]{:S(2)}, u32[]{:S(2)}) collective-permute-start(bf16[16,6144]{1,0:T(8,128)(2,1)S(1)} %collective-permute-done.6), channel_id=1, source_target_pairs={{0,2},{2,0},{4,6},{6,4},{1,3},{3,1},{5,7},{7,5},{8,10},{10,8},{12,... | collective-permute-start | bytes 589832 | tf_op jit(solution)/shard_map/ppermute | solution.py:20
  17.8 10.0 %collective-permute-start.8 = (bf16[16,6144]{1,0:T(8,128)(2,1)S(1)}, bf16[16,6144]{1,0:T(8,128)(2,1)S(1)}, u32[]{:S(2)}, u32[]{:S(2)}) collective-permute-start(bf16[16,6144]{1,0:T(8,128)(2,1)S(1)} %collective-permute-done.6), channel_id=1, source_target_pairs={{0,4},{2,6},{4,0},{6,2},{1,5},{3,7},{5,1},{7,3},{8,12},{10,14},{12... | collective-permute-start | bytes 589832 | tf_op jit(solution)/shard_map/ppermute | solution.py:20
  18.4 11.9 %collective-permute-start.9 = (bf16[16,6144]{1,0:T(8,128)(2,1)S(1)}, bf16[16,6144]{1,0:T(8,128)(2,1)S(1)}, u32[]{:S(2)}, u32[]{:S(2)}) collective-permute-start(bf16[16,6144]{1,0:T(8,128)(2,1)S(1)} %collective-permute-done.6), channel_id=1, source_target_pairs={{0,6},{2,4},{4,2},{6,0},{1,7},{3,5},{5,3},{7,1},{8,14},{10,12},{12... | collective-permute-start | bytes 589832 | tf_op jit(solution)/shard_map/ppermute | solution.py:20
  23.6 8.4 %copy-start.2 = (f32[1,1,2,16]{3,2,1,0:T(2,128)S(1)}, f32[1,1,2,16]{3,2,1,0:T(2,128)}, u32[]{:S(2)}) copy-start(f32[1,1,2,16]{3,2,1,0:T(2,128)} %param.15) | copy-start | bytes 388
  23.6 8.4 %copy-start.3 = (s32[1,1,2]{2,1,0:T(1,128)S(1)}, s32[1,1,2]{2,1,0:T(1,128)}, u32[]{:S(2)}) copy-start(s32[1,1,2]{2,1,0:T(1,128)} %param.14) | copy-start | bytes 28
  23.7 9.1 %copy-start.4 = (s32[1,1,2,16]{3,2,1,0:T(2,128)S(1)}, s32[1,1,2,16]{3,2,1,0:T(2,128)}, u32[]{:S(2)}) copy-start(s32[1,1,2,16]{3,2,1,0:T(2,128)} %param.13) | copy-start | bytes 388
  23.8 10.4 %collective-permute-start.10 = (bf16[4,16,6144]{2,1,0:T(8,128)(2,1)S(1)}, bf16[4,16,6144]{2,1,0:T(8,128)(2,1)S(1)}, u32[]{:S(2)}, u32[]{:S(2)}) collective-permute-start(bf16[4,16,6144]{2,1,0:T(8,128)(2,1)S(1)} %get-tuple-element.21), channel_id=1, source_target_pairs={{0,1},{1,0},{2,3},{3,2},{4,5},{5,4},{6,7},{7,6},{8,9},{9,8},{10,11... | collective-permute-start | bytes 2359304 | tf_op jit(solution)/shard_map/ppermute | solution.py:20
  30.5 3.7 %collective-permute-start.11 = (bf16[4,16,6144]{2,1,0:T(8,128)(2,1)S(1)}, bf16[4,16,6144]{2,1,0:T(8,128)(2,1)S(1)}, u32[]{:S(2)}, u32[]{:S(2)}) collective-permute-start(bf16[4,16,6144]{2,1,0:T(8,128)(2,1)S(1)} %get-tuple-element.23), channel_id=1, source_target_pairs={{0,1},{1,0},{2,3},{3,2},{4,5},{5,4},{6,7},{7,6},{8,9},{9,8},{10,11... | collective-permute-start | bytes 2359304 | tf_op jit(solution)/shard_map/ppermute | solution.py:20
  30.5 40.8 %collective-permute-start = (bf16[128,6144]{1,0:T(8,128)(2,1)}, bf16[128,6144]{1,0:T(8,128)(2,1)}, u32[]{:S(2)}, u32[]{:S(2)}) collective-permute-start(bf16[128,6144]{1,0:T(8,128)(2,1)} %bitcast), channel_id=1, source_target_pairs={{0,16},{16,0},{1,17},{17,1},{2,18},{18,2},{3,19},{19,3},{4,20},{20... | collective-permute-start | bytes 4718600 | tf_op jit(solution)/shard_map/ppermute | solution.py:12
  32.2 39.1 %collective-permute-start.2 = (f32[2,16]{1,0:T(2,128)S(1)}, f32[2,16]{1,0:T(2,128)S(1)}, u32[]{:S(2)}, u32[]{:S(2)}) collective-permute-start(f32[2,16]{1,0:T(2,128)S(1)} %compare_select_fusion.3), channel_id=1, source_target_pairs={{0,16},{16,0},{1,17},{17,1},{2,18},{18,2},{3,19},{19,3},{4,20},{20... | collective-permute-start | bytes 392 | tf_op jit(solution)/shard_map/ppermute | solution.py:12
  32.7 38.6 %collective-permute-start.1 = (s32[2,16]{1,0:T(2,128)S(1)}, s32[2,16]{1,0:T(2,128)S(1)}, u32[]{:S(2)}, u32[]{:S(2)}) collective-permute-start(s32[2,16]{1,0:T(2,128)S(1)} %bitcast.110), channel_id=1, source_target_pairs={{0,16},{16,0},{1,17},{17,1},{2,18},{18,2},{3,19},{19,3},{4,20},{20... | collective-permute-start | bytes 392 | tf_op jit(solution)/shard_map/ppermute | solution.py:12
  34.6 1.6 %copy-start = (bf16[2,4,2,16,6144]{4,3,2,1,0:T(8,128)(2,1)}, bf16[2,4,2,16,6144]{4,3,2,1,0:T(8,128)(2,1)S(1)}, u32[]{:S(2)}) copy-start(bf16[2,4,2,16,6144]{4,3,2,1,0:T(8,128)(2,1)S(1)} %pad_maximum_fusion) | copy-start | bytes 9437188
  71.5 3.5 %collective-permute-start.12 = (bf16[4,2,16,6144]{3,2,1,0:T(8,128)(2,1)S(1)}, bf16[4,2,16,6144]{3,2,1,0:T(8,128)(2,1)S(1)}, u32[]{:S(2)}, u32[]{:S(2)}) collective-permute-start(bf16[4,2,16,6144]{3,2,1,0:T(8,128)(2,1)S(1)} %bitcast.93), channel_id=1, source_target_pairs={{0,1},{1,0},{2,3},{3,2},{4,5},{5,4},{6,7},{7,6},{8,9},{9,8},{10,11... | collective-permute-start | bytes 4718600 | tf_op jit(solution)/shard_map/ppermute | solution.py:28
  75.6 11.2 %collective-permute-start.13 = (bf16[2,16,6144]{2,1,0:T(8,128)(2,1)S(1)}, bf16[2,16,6144]{2,1,0:T(8,128)(2,1)S(1)}, u32[]{:S(2)}, u32[]{:S(2)}) collective-permute-start(bf16[2,16,6144]{2,1,0:T(8,128)(2,1)S(1)} %get-tuple-element.17), channel_id=1, source_target_pairs={{0,2},{2,0},{4,6},{6,4},{1,3},{3,1},{5,7},{7,5},{8,10},{10,8},{12,... | collective-permute-start | bytes 1179656 | tf_op jit(solution)/shard_map/ppermute | solution.py:28
  77.2 12.0 %collective-permute-start.14 = (bf16[2,16,6144]{2,1,0:T(8,128)(2,1)S(1)}, bf16[2,16,6144]{2,1,0:T(8,128)(2,1)S(1)}, u32[]{:S(2)}, u32[]{:S(2)}) collective-permute-start(bf16[2,16,6144]{2,1,0:T(8,128)(2,1)S(1)} %get-tuple-element.19), channel_id=1, source_target_pairs={{0,4},{2,6},{4,0},{6,2},{1,5},{3,7},{5,1},{7,3},{8,12},{10,14},{12... | collective-permute-start | bytes 1179656 | tf_op jit(solution)/shard_map/ppermute | solution.py:28
  77.4 19.0 %collective-permute-start.15 = (bf16[2,16,6144]{2,1,0:T(8,128)(2,1)S(1)}, bf16[2,16,6144]{2,1,0:T(8,128)(2,1)S(1)}, u32[]{:S(2)}, u32[]{:S(2)}) collective-permute-start(bf16[2,16,6144]{2,1,0:T(8,128)(2,1)S(1)} %get-tuple-element.18), channel_id=1, source_target_pairs={{0,6},{2,4},{4,2},{6,0},{1,7},{3,5},{5,3},{7,1},{8,14},{10,12},{12... | collective-permute-start | bytes 1179656 | tf_op jit(solution)/shard_map/ppermute | solution.py:28
  96.6 6.7 %collective-permute-start.16 = (bf16[16,6144]{1,0:T(8,128)(2,1)S(1)}, bf16[16,6144]{1,0:T(8,128)(2,1)S(1)}, u32[]{:S(2)}, u32[]{:S(2)}) collective-permute-start(bf16[16,6144]{1,0:T(8,128)(2,1)S(1)} %get-tuple-element.24), channel_id=1, source_target_pairs={{0,16},{16,0},{1,17},{17,1},{2,18},{18,2},{3,19},{19,3},{4,20},{20... | collective-permute-start | bytes 589832 | tf_op jit(solution)/shard_map/ppermute | solution.py:12
  97.2 11.5 %collective-permute-start.17 = (bf16[16,6144]{1,0:T(8,128)(2,1)S(1)}, bf16[16,6144]{1,0:T(8,128)(2,1)S(1)}, u32[]{:S(2)}, u32[]{:S(2)}) collective-permute-start(bf16[16,6144]{1,0:T(8,128)(2,1)S(1)} %get-tuple-element.25), channel_id=1, source_target_pairs={{0,24},{8,16},{16,8},{24,0},{1,25},{9,17},{17,9},{25,1},{2,26},{10... | collective-permute-start | bytes 589832 | tf_op jit(solution)/shard_map/ppermute | solution.py:115

commit v5 on v3

--- a/solution.py
+++ b/solution.py
@@ -3,8 +3,7 @@
 from jax import lax
 from jax.sharding import Mesh, PartitionSpec as P
 
-CHIP_SUM_DTYPE = jnp.bfloat16
-HAND_DTYPE = jnp.bfloat16
+SUM_DTYPE = jnp.bfloat16
 
 
 def shifted(block, axes, size, distance):
@@ -12,20 +11,13 @@
     return lax.ppermute(block, axes, route)
 
 
-def partnered(block, axes, size, step):
-    if size & (size - 1) == 0:
-        route = [(i, i ^ step) for i in range(size)]
-    else:
-        route = [(i, (i + step) % size) for i in range(size)]
-    return lax.ppermute(block, axes, route)
-
-
-def back_partnered(block, axes, size, step):
-    if size & (size - 1) == 0:
-        route = [(i, i ^ step) for i in range(size)]
-    else:
-        route = [(i, (i - step) % size) for i in range(size)]
-    return lax.ppermute(block, axes, route)
+def chip_route(n_chip, n_core, stage, levels):
+    route = []
+    for k in range(n_chip):
+        for c in range(n_core):
+            bit = (stage + c) % levels
+            route.append((k * n_core + c, (k ^ (1 << bit)) * n_core + c))
+    return route
 
 
 def body(
@@ -52,13 +44,16 @@
     n_ex = lax.axis_size("ex")
     n_chip = lax.axis_size("chip")
     n_core = lax.axis_size("core")
+    levels = n_chip.bit_length() - 1
     ex_me = lax.axis_index("ex")
 
     live_mask = jnp.arange(capacity)[None, :] < live_count[:, None]
     weighting = jnp.where(live_mask, slot_gates, 0.0)
+    selector_out = (slot_rows[..., None] == jnp.arange(tok_count)[None, None, :]).astype(
+        jnp.float32
+    ) * weighting[..., None]
     states_in = shifted(states, "section", sections, 1)
-    rows_in = shifted(slot_rows, "section", sections, 1)
-    weights_in = shifted(weighting, "section", sections, 1)
+    selector_in = shifted(selector_out, "section", sections, 1)
 
     selector = (slot_rows.reshape(-1)[:, None] == jnp.arange(tok_count)[None, :]).astype(states.dtype)
     chosen = jnp.dot(selector, states, preferred_element_type=jnp.float32)
@@ -73,12 +68,15 @@
     for k in range(1, n_ex):
         outgoing = lax.dynamic_index_in_dim(picked, (ex_me + k) % n_ex, 0, keepdims=False)
         parts.append(shifted(outgoing, "ex", n_ex, k))
-    chip_rows = [parts] + [
-        [partnered(part, "chip", n_chip, m) for part in parts] for m in range(1, n_chip)
-    ]
-    chip_rows = [jnp.stack([chip_rows[m][k] for m in range(n_chip)]) for k in range(n_ex)]
+    chip_rows = []
+    for part in parts:
+        held = part[None]
+        for stage in range(levels):
+            arrived = lax.ppermute(held, ("chip", "core"), chip_route(n_chip, n_core, stage, levels))
+            held = jnp.concatenate([held, arrived])
+        chip_rows.append(held)
     core_rows = [chip_rows] + [
-        [partnered(rows, "core", n_core, q) for rows in chip_rows] for q in range(1, n_core)
+        [shifted(rows, "core", n_core, q) for rows in chip_rows] for q in range(1, n_core)
     ]
     gathered = jnp.stack([jnp.stack(core_rows[q], axis=1) for q in range(n_core)])
     flat_rows = gathered.reshape(-1, width)
@@ -89,19 +87,24 @@
     partial_out = jnp.dot(activated, down_rows, preferred_element_type=jnp.float32).astype(
         jnp.bfloat16
     )
+    states_in, selector_in, partial_out = lax.optimization_barrier(
+        (states_in, selector_in, partial_out)
+    )
     partials = partial_out.reshape(gathered.shape)
 
     summed = partials[0].astype(jnp.float32)
     for q in range(1, n_core):
-        summed = summed + back_partnered(partials[q], "core", n_core, q).astype(jnp.float32)
+        summed = summed + shifted(partials[q], "core", n_core, -q).astype(jnp.float32)
+    for stage in reversed(range(levels)):
+        half = summed.shape[0] // 2
+        sent = summed[half:].astype(SUM_DTYPE)
+        arrived = lax.ppermute(sent, ("chip", "core"), chip_route(n_chip, n_core, stage, levels))
+        summed = summed[:half] + arrived.astype(jnp.float32)
     reduced = summed[0]
-    for m in range(1, n_chip):
-        sent = back_partnered(summed[m].astype(CHIP_SUM_DTYPE), "chip", n_chip, m)
-        reduced = reduced + sent.astype(jnp.float32)
 
     got = []
     for k in range(n_ex):
-        outgoing = reduced[k].astype(HAND_DTYPE)
+        outgoing = reduced[k].astype(SUM_DTYPE)
         if k == 0:
             got.append(shifted(outgoing, "section", sections, 1))
         else:
@@ -114,10 +117,7 @@
     order = (ex_me + jnp.arange(n_ex)) % n_ex
     expert_out = jnp.zeros_like(stacked).at[order].set(stacked)
 
-    one_hot = (rows_in[..., None] == jnp.arange(tok_count)[None, None, :]).astype(
-        jnp.float32
-    ) * weights_in[..., None]
-    branch = jnp.einsum("ect,ecd->td", one_hot, expert_out, precision=lax.Precision.HIGHEST)
+    branch = jnp.einsum("ect,ecd->td", selector_in, expert_out, precision=lax.Precision.HIGHEST)
     layer_out = (states_in.astype(jnp.float32) + branch).astype(jnp.bfloat16)
     return layer_out[None]
 

time: 128 us -> 114 us (0.89)
  waiting for transfers between devices: 58.9 us -> 49.3 us
  starting transfers between devices: 21.3 us -> 17.4 us
    ppermute x5 -> x7, waiting for transfers between devices: 27.4 us -> 13.2 us  [shifted(): return lax.ppermute(block, axes, route)]
    ppermute x1, waiting for transfers between devices: 0.01 us -> 6.6 us  [body(): got.append(lax.ppermute(outgoing, ('section', 'ex'), route))]
    ppermute x12 -> x6, starting transfers between devices: 10.7 us -> 7.1 us  [the longest x4 4.64 us: body(): lax.ppermute(held, ('chip', 'core'), chip_route(n_chip, n_core, stage, le...]
    ppermute x12 -> x6, waiting for transfers between devices: 31.5 us -> 29.5 us  [the longest x2 17.4 us: body(): lax.ppermute(sent, ('chip', 'core'), chip_route(n_chip, n_core, stage, le...]
    slice x1, local copies, waits for them, and re-layouts: 2.2 us -> 0.2 us  [body(): partials[q]]
    unnamed x8 -> x10, local copies, waits for them, and re-layouts: 0.02 us -> 1.67 us
    ppermute x5 -> x7, starting transfers between devices: 9.17 us -> 8.27 us  [shifted(): return lax.ppermute(block, axes, route)]
  transfers between devices with their start and end apart: 18 -> 14, of which waited for: 11 -> 9; matrix products, arithmetic and copies ran while one was open for 1% -> 31% of each run, Pallas kernels for 0% -> 0%
where the time goes in v5:
time: 114 us
  waiting for transfers between devices  49.3 us (43%)
  matrix products  41.9 us (37%)
  starting transfers between devices  17.4 us (15%)
  local copies, waits for them, and re-layouts  3.61 us (3%)
  other arithmetic  1.68 us (1%)
    dot_general x1, matrix products, body(): jnp.dot(activated, down_rows, preferred_element_type=jnp.float32)  22.1 us
    ppermute x2, waiting for transfers between devices, body(): lax.ppermute(sent, ('chip', 'core'), chip_route(n_chip, n_core, stage, le...  17.4 us
    ppermute x7, waiting for transfers between devices, shifted(): return lax.ppermute(block, axes, route)  13.2 us
    dot_general x1, matrix products, body(): jnp.dot(flat_rows, gate_cols, preferred_element_type=jnp.float32)  13 us
    ppermute x4, waiting for transfers between devices, body(): lax.ppermute(held, ('chip', 'core'), chip_route(n_chip, n_core, stage, le...  12.1 us
    ppermute x7, starting transfers between devices, shifted(): return lax.ppermute(block, axes, route)  8.27 us
    ppermute x1, waiting for transfers between devices, body(): got.append(lax.ppermute(outgoing, ('section', 'ex'), route))  6.6 us
    dot_general x1, matrix products, body(): jnp.einsum('ect,ecd->td', selector_in, expert_out, precision=lax.Precisio...  4.96 us
  transfers between devices with their start and end apart: 14, of which 9 were waited for; matrix products, arithmetic and copies ran while one was open for 31% of the time, Pallas kernels for 0%

profile of v5, /device:TPU:0, one launch (start us, length us, event | category | flops | bytes accessed | tf_op | source)
XLA Modules:
  0.0 114.2 jit_solution(17268112327459558556)
XLA Ops:
  0.0 0.0 copy-start.1
  0.0 0.8 eq.38
  0.8 1.9 %multiply_reduce_fusion = (f32[32]{0:T(128)S(1)}, f32[32,6144]{1,0:T(8,128)S(1)}) fusion(bf16[1,128,6144]{2,1,0:T(8,128)(2,1)} %param.8, s32[32]{0:T(128)S(1)} %eq.38), kind=kOutput, calls=%fused_computation.31 | convolution fusion | flops 50728928 | bytes 2359552 | tf_op jit(solution)/shard_map/dot_general | solution.py:59
  2.7 0.0 copy-done.1
  2.7 0.1 multiply_convert_fusion
  2.9 4.1 %collective-permute-start.4 = (bf16[16,6144]{1,0:T(8,128)(2,1)S(1)}, bf16[16,6144]{1,0:T(8,128)(2,1)S(1)}, u32[]{:S(2)}, u32[]{:S(2)}) collective-permute-start(bf16[16,6144]{1,0:T(8,128)(2,1)S(1)} %get-tuple-element.20), channel_id=1, source_target_pairs={{0,8},{8,0},{1,9},{9,1},{2,10},{10,2},{3,11},{11,3},{4,12},{12,4},... | collective-permute-start | bytes 589832 | tf_op jit(solution)/shard_map/ppermute | solution.py:11
  7.0 1.5 %collective-permute-start.2 = (bf16[1,16,6144]{2,1,0:T(8,128)(2,1)S(1)}, bf16[1,16,6144]{2,1,0:T(8,128)(2,1)S(1)}, u32[]{:S(2)}, u32[]{:S(2)}) collective-permute-start(bf16[1,16,6144]{2,1,0:T(8,128)(2,1)S(1)} %get-tuple-element.19), channel_id=1, source_target_pairs={{0,2},{1,5},{2,0},{3,7},{4,6},{5,1},{6,4},{7,3},{8,10},{9,13},{10,... | collective-permute-start | bytes 589832 | tf_op jit(solution)/shard_map/ppermute | solution.py:75
  8.6 7.6 %collective-permute-done.4 = bf16[16,6144]{1,0:T(8,128)(2,1)S(1)} collective-permute-done((bf16[16,6144]{1,0:T(8,128)(2,1)S(1)}, bf16[16,6144]{1,0:T(8,128)(2,1)S(1)}, u32[]{:S(2)}, u32[]{:S(2)}) %collective-permute-start.4) | collective-permute-done | bytes 196640 | tf_op jit(solution)/shard_map/ppermute | solution.py:11
  16.1 1.6 %collective-permute-start.5 = (bf16[1,16,6144]{2,1,0:T(8,128)(2,1)S(1)}, bf16[1,16,6144]{2,1,0:T(8,128)(2,1)S(1)}, u32[]{:S(2)}, u32[]{:S(2)}) collective-permute-start(bf16[1,16,6144]{2,1,0:T(8,128)(2,1)S(1)} %bitcast.72), channel_id=1, source_target_pairs={{0,2},{1,5},{2,0},{3,7},{4,6},{5,1},{6,4},{7,3},{8,10},{9,13},{10,... | collective-permute-start | bytes 589832 | tf_op jit(solution)/shard_map/ppermute | solution.py:75
  17.7 0.0 collective-permute-done.2
  17.8 0.7 collective-permute-start.3
  18.5 5.3 %collective-permute-done.5 = bf16[1,16,6144]{2,1,0:T(8,128)(2,1)S(1)} collective-permute-done((bf16[1,16,6144]{2,1,0:T(8,128)(2,1)S(1)}, bf16[1,16,6144]{2,1,0:T(8,128)(2,1)S(1)}, u32[]{:S(2)}, u32[]{:S(2)}) %collective-permute-start.5) | collective-permute-done | bytes 196640 | tf_op jit(solution)/shard_map/ppermute | solution.py:75
  23.9 0.0 copy-start.3
  23.9 0.0 copy-start.4
  23.9 0.0 copy-start.2
  23.9 0.8 collective-permute-start.6
  24.7 0.9 collective-permute-done.3
  25.6 0.1 fusion.33
  25.7 0.2 collective-permute-start.7
  25.9 5.8 %collective-permute-done.6 = bf16[2,16,6144]{2,1,0:T(8,128)(2,1)S(1)} collective-permute-done((bf16[2,16,6144]{2,1,0:T(8,128)(2,1)S(1)}, bf16[2,16,6144]{2,1,0:T(8,128)(2,1)S(1)}, u32[]{:S(2)}, u32[]{:S(2)}) %collective-permute-start.6) | collective-permute-done | bytes 393248 | tf_op jit(solution)/shard_map/ppermute | solution.py:75
  31.8 0.1 fusion.32
  31.9 0.1 collective-permute-start.8
  31.9 1.6 %collective-permute-start = (bf16[128,6144]{1,0:T(8,128)(2,1)}, bf16[128,6144]{1,0:T(8,128)(2,1)}, u32[]{:S(2)}, u32[]{:S(2)}) collective-permute-start(bf16[128,6144]{1,0:T(8,128)(2,1)} %bitcast), channel_id=1, source_target_pairs={{0,16},{16,0},{1,17},{17,1},{2,18},{18,2},{3,19},{19,3},{4,20},{20... | collective-permute-start | bytes 4718600 | tf_op jit(solution)/shard_map/ppermute | solution.py:11
  33.6 0.0 copy-done.3
  33.6 0.0 copy-done.4
  33.6 0.1 compare_select_fusion.3
  33.6 0.0 copy-done.2
  33.7 0.1 fusion.25
  33.7 0.5 collective-permute-start.1
  34.2 0.0 collective-permute-done.7
  34.2 0.0 collective-permute-done.8
  34.2 0.1 maximum_bitcast_fusion.1
  34.4 0.2 pad_maximum_fusion
  34.6 0.0 copy-start
  34.6 1.6 %copy-done = bf16[2,4,2,16,6144]{4,3,2,1,0:T(8,128)(2,1)} copy-done((bf16[2,4,2,16,6144]{4,3,2,1,0:T(8,128)(2,1)}, bf16[2,4,2,16,6144]{4,3,2,1,0:T(8,128)(2,1)S(1)}, u32[]{:S(2)}) %copy-start) | copy-done | bytes 3145752
  36.2 13.0 %fusion.4 = f32[256,2048]{1,0:T(8,128)} fusion(bf16[256,6144]{1,0:T(8,128)(2,1)S(1)} %bitcast.68, bf16[1,6144,2048]{2,1,0:T(8,128)(2,1)} %param.10), kind=kOutput, calls=%fused_computation.5 | convolution fusion | flops 6442450944 | bytes 30408704 | tf_op jit(solution)/shard_map/dot_general | solution.py:84
  49.2 22.1 %fusion.6 = bf16[256,6144]{1,0:T(8,128)(2,1)S(1)} fusion(bf16[1,2048,6144]{2,1,0:T(8,128)(2,1)} %param.12, bf16[256,6144]{1,0:T(8,128)(2,1)} %bitcast.69, bf16[1,6144,2048]{2,1,0:T(8,128)(2,1)} %param.11, f32[256,2048]{1,0:T(8,128)} %fusion.4), kind=kOutput, calls=%fused_computation.7 | convolution fusion | flops 12889620480 | bytes 58720256 | tf_op jit(solution)/shard_map/dot_general | solution.py:87
  71.3 0.0 collective-permute-done.1
  71.3 0.0 collective-permute-done
  71.3 0.2 fusion.34
  71.6 0.2 collective-permute-start.9
  71.8 3.3 %collective-permute-done.9 = bf16[4,2,16,6144]{3,2,1,0:T(8,128)(2,1)S(1)} collective-permute-done((bf16[4,2,16,6144]{3,2,1,0:T(8,128)(2,1)S(1)}, bf16[4,2,16,6144]{3,2,1,0:T(8,128)(2,1)S(1)}, u32[]{:S(2)}, u32[]{:S(2)}) %collective-permute-start.9) | collective-permute-done | bytes 1572896 | tf_op jit(solution)/shard_map/ppermute | solution.py:11
  75.0 0.4 convert_add_fusion
  75.4 0.1 slice.54
  75.5 0.8 collective-permute-start.10
  76.3 11.2 %collective-permute-done.10 = bf16[2,2,16,6144]{3,2,1,0:T(8,128)(2,1)S(1)} collective-permute-done((bf16[2,2,16,6144]{3,2,1,0:T(8,128)(2,1)S(1)}, bf16[2,2,16,6144]{3,2,1,0:T(8,128)(2,1)S(1)}, u32[]{:S(2)}, u32[]{:S(2)}) %collective-permute-start.10) | collective-permute-done | bytes 786464 | tf_op jit(solution)/shard_map/ppermute | solution.py:101
  87.6 0.2 slice_add_fusion
  87.8 1.6 %collective-permute-start.11 = (bf16[1,2,16,6144]{3,2,1,0:T(8,128)(2,1)S(1)}, bf16[1,2,16,6144]{3,2,1,0:T(8,128)(2,1)S(1)}, u32[]{:S(2)}, u32[]{:S(2)}) collective-permute-start(bf16[1,2,16,6144]{3,2,1,0:T(8,128)(2,1)S(1)} %slice.55), channel_id=1, source_target_pairs={{0,2},{1,5},{2,0},{3,7},{4,6},{5,1},{6,4},{7,3},{8,10},{9,13},{10,... | collective-permute-start | bytes 1179656 | tf_op jit(solution)/shard_map/ppermute | solution.py:101
  89.4 6.2 %collective-permute-done.11 = bf16[1,2,16,6144]{3,2,1,0:T(8,128)(2,1)S(1)} collective-permute-done((bf16[1,2,16,6144]{3,2,1,0:T(8,128)(2,1)S(1)}, bf16[1,2,16,6144]{3,2,1,0:T(8,128)(2,1)S(1)}, u32[]{:S(2)}, u32[]{:S(2)}) %collective-permute-start.11) | collective-permute-done | bytes 393248 | tf_op jit(solution)/shard_map/ppermute | solution.py:101
  95.6 0.1 fusion.24
  95.8 1.6 %collective-permute-start.12 = (bf16[16,6144]{1,0:T(8,128)(2,1)S(1)}, bf16[16,6144]{1,0:T(8,128)(2,1)S(1)}, u32[]{:S(2)}, u32[]{:S(2)}) collective-permute-start(bf16[16,6144]{1,0:T(8,128)(2,1)S(1)} %get-tuple-element.17), channel_id=1, source_target_pairs={{0,16},{16,0},{1,17},{17,1},{2,18},{18,2},{3,19},{19,3},{4,20},{20... | collective-permute-start | bytes 589832 | tf_op jit(solution)/shard_map/ppermute | solution.py:11
  97.4 2.1 %collective-permute-start.13 = (bf16[16,6144]{1,0:T(8,128)(2,1)S(1)}, bf16[16,6144]{1,0:T(8,128)(2,1)S(1)}, u32[]{:S(2)}, u32[]{:S(2)}) collective-permute-start(bf16[16,6144]{1,0:T(8,128)(2,1)S(1)} %get-tuple-element.18), channel_id=1, source_target_pairs={{0,24},{8,16},{16,8},{24,0},{1,25},{9,17},{17,9},{25,1},{2,26},{10... | collective-permute-start | bytes 589832 | tf_op jit(solution)/shard_map/ppermute | solution.py:115
  99.4 2.3 %collective-permute-done.12 = bf16[16,6144]{1,0:T(8,128)(2,1)S(1)} collective-permute-done((bf16[16,6144]{1,0:T(8,128)(2,1)S(1)}, bf16[16,6144]{1,0:T(8,128)(2,1)S(1)}, u32[]{:S(2)}, u32[]{:S(2)}) %collective-permute-start.12) | collective-permute-done | bytes 196640 | tf_op jit(solution)/shard_map/ppermute | solution.py:11
  101.8 6.6 %collective-permute-done.13 = bf16[16,6144]{1,0:T(8,128)(2,1)S(1)} collective-permute-done((bf16[16,6144]{1,0:T(8,128)(2,1)S(1)}, bf16[16,6144]{1,0:T(8,128)(2,1)S(1)}, u32[]{:S(2)}, u32[]{:S(2)}) %collective-permute-start.13) | collective-permute-done | bytes 196640 | tf_op jit(solution)/shard_map/ppermute | solution.py:115
  108.4 0.1 maximum_convert_fusion
  108.4 0.1 broadcast_in_dim.12
  108.5 0.7 scatter_fusion
  109.2 5.0 %fusion.22 = bf16[1,128,6144]{2,1,0:T(8,128)(2,1)} fusion(bf16[128,6144]{1,0:T(8,128)(2,1)} %collective-permute-done, f32[2,16,128]{2,1,0:T(8,128)S(1)} %collective-permute-done.1, f32[2,16,6144]{2,1,0:T(8,128)S(1)} %scatter_fusion), kind=kOutput, calls=%fused_computation.19 | convolution fusion | flops 304349184 | bytes 3948544 | tf_op jit(solution)/shard_map/ect,ecd->td/dot_general | solution.py:120
  (8 shorter events, 0.2 us)
Async XLA Ops:
  0.0 2.7 %copy-start.1 = (bf16[1,6144]{1,0:T(2,128)(2,1)S(1)}, bf16[1,6144]{1,0:T(2,128)(2,1)}, u32[]{:S(2)}) copy-start(bf16[1,6144]{1,0:T(2,128)(2,1)} %param.9) | copy-start | bytes 36868
  2.9 13.2 %collective-permute-start.4 = (bf16[16,6144]{1,0:T(8,128)(2,1)S(1)}, bf16[16,6144]{1,0:T(8,128)(2,1)S(1)}, u32[]{:S(2)}, u32[]{:S(2)}) collective-permute-start(bf16[16,6144]{1,0:T(8,128)(2,1)S(1)} %get-tuple-element.20), channel_id=1, source_target_pairs={{0,8},{8,0},{1,9},{9,1},{2,10},{10,2},{3,11},{11,3},{4,12},{12,4},... | collective-permute-start | bytes 589832 | tf_op jit(solution)/shard_map/ppermute | solution.py:11
  7.0 10.7 %collective-permute-start.2 = (bf16[1,16,6144]{2,1,0:T(8,128)(2,1)S(1)}, bf16[1,16,6144]{2,1,0:T(8,128)(2,1)S(1)}, u32[]{:S(2)}, u32[]{:S(2)}) collective-permute-start(bf16[1,16,6144]{2,1,0:T(8,128)(2,1)S(1)} %get-tuple-element.19), channel_id=1, source_target_pairs={{0,2},{1,5},{2,0},{3,7},{4,6},{5,1},{6,4},{7,3},{8,10},{9,13},{10,... | collective-permute-start | bytes 589832 | tf_op jit(solution)/shard_map/ppermute | solution.py:75
  16.1 7.7 %collective-permute-start.5 = (bf16[1,16,6144]{2,1,0:T(8,128)(2,1)S(1)}, bf16[1,16,6144]{2,1,0:T(8,128)(2,1)S(1)}, u32[]{:S(2)}, u32[]{:S(2)}) collective-permute-start(bf16[1,16,6144]{2,1,0:T(8,128)(2,1)S(1)} %bitcast.72), channel_id=1, source_target_pairs={{0,2},{1,5},{2,0},{3,7},{4,6},{5,1},{6,4},{7,3},{8,10},{9,13},{10,... | collective-permute-start | bytes 589832 | tf_op jit(solution)/shard_map/ppermute | solution.py:75
  17.8 7.8 %collective-permute-start.3 = (bf16[2,16,6144]{2,1,0:T(8,128)(2,1)S(1)}, bf16[2,16,6144]{2,1,0:T(8,128)(2,1)S(1)}, u32[]{:S(2)}, u32[]{:S(2)}) collective-permute-start(bf16[2,16,6144]{2,1,0:T(8,128)(2,1)S(1)} %pad_maximum_fusion.3), channel_id=1, source_target_pairs={{0,4},{1,3},{2,6},{3,1},{4,0},{5,7},{6,2},{7,5},{8,12},{9,11},{10,... | collective-permute-start | bytes 1179656 | tf_op jit(solution)/shard_map/ppermute | solution.py:75
  23.9 9.7 %copy-start.3 = (f32[1,1,2,16]{3,2,1,0:T(2,128)S(1)}, f32[1,1,2,16]{3,2,1,0:T(2,128)}, u32[]{:S(2)}) copy-start(f32[1,1,2,16]{3,2,1,0:T(2,128)} %param.15) | copy-start | bytes 388
  23.9 9.7 %copy-start.4 = (s32[1,1,2]{2,1,0:T(1,128)S(1)}, s32[1,1,2]{2,1,0:T(1,128)}, u32[]{:S(2)}) copy-start(s32[1,1,2]{2,1,0:T(1,128)} %param.14) | copy-start | bytes 28
  23.9 9.8 %copy-start.2 = (s32[1,1,2,16]{3,2,1,0:T(2,128)S(1)}, s32[1,1,2,16]{3,2,1,0:T(2,128)}, u32[]{:S(2)}) copy-start(s32[1,1,2,16]{3,2,1,0:T(2,128)} %param.13) | copy-start | bytes 388
  23.9 7.8 %collective-permute-start.6 = (bf16[2,16,6144]{2,1,0:T(8,128)(2,1)S(1)}, bf16[2,16,6144]{2,1,0:T(8,128)(2,1)S(1)}, u32[]{:S(2)}, u32[]{:S(2)}) collective-permute-start(bf16[2,16,6144]{2,1,0:T(8,128)(2,1)S(1)} %pad_maximum_fusion.4), channel_id=1, source_target_pairs={{0,4},{1,3},{2,6},{3,1},{4,0},{5,7},{6,2},{7,5},{8,12},{9,11},{10,... | collective-permute-start | bytes 1179656 | tf_op jit(solution)/shard_map/ppermute | solution.py:75
  25.7 8.5 %collective-permute-start.7 = (bf16[4,16,6144]{2,1,0:T(8,128)(2,1)S(1)}, bf16[4,16,6144]{2,1,0:T(8,128)(2,1)S(1)}, u32[]{:S(2)}, u32[]{:S(2)}) collective-permute-start(bf16[4,16,6144]{2,1,0:T(8,128)(2,1)S(1)} %get-tuple-element.14), channel_id=1, source_target_pairs={{0,1},{1,0},{2,3},{3,2},{4,5},{5,4},{6,7},{7,6},{8,9},{9,8},{10,11... | collective-permute-start | bytes 2359304 | tf_op jit(solution)/shard_map/ppermute | solution.py:11
  31.9 2.4 %collective-permute-start.8 = (bf16[4,16,6144]{2,1,0:T(8,128)(2,1)S(1)}, bf16[4,16,6144]{2,1,0:T(8,128)(2,1)S(1)}, u32[]{:S(2)}, u32[]{:S(2)}) collective-permute-start(bf16[4,16,6144]{2,1,0:T(8,128)(2,1)S(1)} %get-tuple-element.16), channel_id=1, source_target_pairs={{0,1},{1,0},{2,3},{3,2},{4,5},{5,4},{6,7},{7,6},{8,9},{9,8},{10,11... | collective-permute-start | bytes 2359304 | tf_op jit(solution)/shard_map/ppermute | solution.py:11
  31.9 39.4 %collective-permute-start = (bf16[128,6144]{1,0:T(8,128)(2,1)}, bf16[128,6144]{1,0:T(8,128)(2,1)}, u32[]{:S(2)}, u32[]{:S(2)}) collective-permute-start(bf16[128,6144]{1,0:T(8,128)(2,1)} %bitcast), channel_id=1, source_target_pairs={{0,16},{16,0},{1,17},{17,1},{2,18},{18,2},{3,19},{19,3},{4,20},{20... | collective-permute-start | bytes 4718600 | tf_op jit(solution)/shard_map/ppermute | solution.py:11
  33.7 37.6 %collective-permute-start.1 = (f32[2,16,128]{2,1,0:T(8,128)S(1)}, f32[2,16,128]{2,1,0:T(8,128)S(1)}, u32[]{:S(2)}, u32[]{:S(2)}) collective-permute-start(f32[2,16,128]{2,1,0:T(8,128)S(1)} %fusion.25), channel_id=1, source_target_pairs={{0,16},{16,0},{1,17},{17,1},{2,18},{18,2},{3,19},{19,3},{4,20},{20... | collective-permute-start | bytes 49160 | tf_op jit(solution)/shard_map/ppermute | solution.py:11
  34.6 1.7 %copy-start = (bf16[2,4,2,16,6144]{4,3,2,1,0:T(8,128)(2,1)}, bf16[2,4,2,16,6144]{4,3,2,1,0:T(8,128)(2,1)S(1)}, u32[]{:S(2)}) copy-start(bf16[2,4,2,16,6144]{4,3,2,1,0:T(8,128)(2,1)S(1)} %pad_maximum_fusion) | copy-start | bytes 9437188
  71.6 3.5 %collective-permute-start.9 = (bf16[4,2,16,6144]{3,2,1,0:T(8,128)(2,1)S(1)}, bf16[4,2,16,6144]{3,2,1,0:T(8,128)(2,1)S(1)}, u32[]{:S(2)}, u32[]{:S(2)}) collective-permute-start(bf16[4,2,16,6144]{3,2,1,0:T(8,128)(2,1)S(1)} %bitcast.71), channel_id=1, source_target_pairs={{0,1},{1,0},{2,3},{3,2},{4,5},{5,4},{6,7},{7,6},{8,9},{9,8},{10,11... | collective-permute-start | bytes 4718600 | tf_op jit(solution)/shard_map/ppermute | solution.py:11
  75.5 12.1 %collective-permute-start.10 = (bf16[2,2,16,6144]{3,2,1,0:T(8,128)(2,1)S(1)}, bf16[2,2,16,6144]{3,2,1,0:T(8,128)(2,1)S(1)}, u32[]{:S(2)}, u32[]{:S(2)}) collective-permute-start(bf16[2,2,16,6144]{3,2,1,0:T(8,128)(2,1)S(1)} %slice.54), channel_id=1, source_target_pairs={{0,4},{1,3},{2,6},{3,1},{4,0},{5,7},{6,2},{7,5},{8,12},{9,11},{10,... | collective-permute-start | bytes 2359304 | tf_op jit(solution)/shard_map/ppermute | solution.py:101
  87.8 7.8 %collective-permute-start.11 = (bf16[1,2,16,6144]{3,2,1,0:T(8,128)(2,1)S(1)}, bf16[1,2,16,6144]{3,2,1,0:T(8,128)(2,1)S(1)}, u32[]{:S(2)}, u32[]{:S(2)}) collective-permute-start(bf16[1,2,16,6144]{3,2,1,0:T(8,128)(2,1)S(1)} %slice.55), channel_id=1, source_target_pairs={{0,2},{1,5},{2,0},{3,7},{4,6},{5,1},{6,4},{7,3},{8,10},{9,13},{10,... | collective-permute-start | bytes 1179656 | tf_op jit(solution)/shard_map/ppermute | solution.py:101
  95.8 6.0 %collective-permute-start.12 = (bf16[16,6144]{1,0:T(8,128)(2,1)S(1)}, bf16[16,6144]{1,0:T(8,128)(2,1)S(1)}, u32[]{:S(2)}, u32[]{:S(2)}) collective-permute-start(bf16[16,6144]{1,0:T(8,128)(2,1)S(1)} %get-tuple-element.17), channel_id=1, source_target_pairs={{0,16},{16,0},{1,17},{17,1},{2,18},{18,2},{3,19},{19,3},{4,20},{20... | collective-permute-start | bytes 589832 | tf_op jit(solution)/shard_map/ppermute | solution.py:11
  97.4 11.0 %collective-permute-start.13 = (bf16[16,6144]{1,0:T(8,128)(2,1)S(1)}, bf16[16,6144]{1,0:T(8,128)(2,1)S(1)}, u32[]{:S(2)}, u32[]{:S(2)}) collective-permute-start(bf16[16,6144]{1,0:T(8,128)(2,1)S(1)} %get-tuple-element.18), channel_id=1, source_target_pairs={{0,24},{8,16},{16,8},{24,0},{1,25},{9,17},{17,9},{25,1},{2,26},{10... | collective-permute-start | bytes 589832 | tf_op jit(solution)/shard_map/ppermute | solution.py:115

commit v6 on v5

--- a/solution.py
+++ b/solution.py
@@ -4,6 +4,7 @@
 from jax.sharding import Mesh, PartitionSpec as P
 
 SUM_DTYPE = jnp.bfloat16
+PIECES = 2
 
 
 def shifted(block, axes, size, distance):
@@ -52,7 +53,10 @@
     selector_out = (slot_rows[..., None] == jnp.arange(tok_count)[None, None, :]).astype(
         jnp.float32
     ) * weighting[..., None]
-    states_in = shifted(states, "section", sections, 1)
+    order = (ex_me + jnp.arange(n_ex)) % n_ex
+    selector_out = jnp.take(selector_out, order, axis=0)
+    early_in = shifted(states[: tok_count // 2], "section", sections, 1)
+    late_in = shifted(states[tok_count // 2 :], "section", sections, 1)
     selector_in = shifted(selector_out, "section", sections, 1)
 
     selector = (slot_rows.reshape(-1)[:, None] == jnp.arange(tok_count)[None, :]).astype(states.dtype)
@@ -79,45 +83,53 @@
         [shifted(rows, "core", n_core, q) for rows in chip_rows] for q in range(1, n_core)
     ]
     gathered = jnp.stack([jnp.stack(core_rows[q], axis=1) for q in range(n_core)])
+    early_in, gathered = lax.optimization_barrier((early_in, gathered))
     flat_rows = gathered.reshape(-1, width)
 
     gate_part = jnp.dot(flat_rows, gate_cols, preferred_element_type=jnp.float32)
     up_part = jnp.dot(flat_rows, up_cols, preferred_element_type=jnp.float32)
     activated = (jax.nn.silu(gate_part) * up_part).astype(jnp.bfloat16)
-    partial_out = jnp.dot(activated, down_rows, preferred_element_type=jnp.float32).astype(
-        jnp.bfloat16
+
+    pieces = PIECES if width % (PIECES * 128) == 0 else 1
+    span = width // pieces
+    got = [[] for _ in range(n_ex)]
+    for piece in range(pieces):
+        cols = down_rows[:, piece * span:(piece + 1) * span]
+        partial_out = jnp.dot(activated, cols, preferred_element_type=jnp.float32).astype(
+            jnp.bfloat16
+        )
+        if piece == 0:
+            late_in, selector_in, partial_out = lax.optimization_barrier(
+                (late_in, selector_in, partial_out)
+            )
+        partials = partial_out.reshape(gathered.shape[:-1] + (span,))
+
+        summed = partials[0].astype(jnp.float32)
+        for q in range(1, n_core):
+            summed = summed + shifted(partials[q], "core", n_core, -q).astype(jnp.float32)
+        for stage in reversed(range(levels)):
+            half = summed.shape[0] // 2
+            sent = summed[half:].astype(SUM_DTYPE)
+            arrived = lax.ppermute(sent, ("chip", "core"), chip_route(n_chip, n_core, stage, levels))
+            summed = summed[:half] + arrived.astype(jnp.float32)
+        reduced = summed[0]
+
+        for k in range(n_ex):
+            outgoing = reduced[k].astype(SUM_DTYPE)
+            if k == 0:
+                got[k].append(shifted(outgoing, "section", sections, 1))
+            else:
+                route = []
+                for s in range(sections):
+                    for e in range(n_ex):
+                        route.append((s * n_ex + e, ((s + 1) % sections) * n_ex + (e - k) % n_ex))
+                got[k].append(lax.ppermute(outgoing, ("section", "ex"), route))
+    expert_out = jnp.stack([jnp.concatenate(pieces_k, axis=-1) for pieces_k in got])
+    states_in = jnp.concatenate([early_in, late_in])
+
+    branch = jnp.einsum(
+        "ect,ecd->td", selector_in, expert_out.astype(jnp.float32), precision=lax.Precision.HIGHEST
     )
-    states_in, selector_in, partial_out = lax.optimization_barrier(
-        (states_in, selector_in, partial_out)
-    )
-    partials = partial_out.reshape(gathered.shape)
-
-    summed = partials[0].astype(jnp.float32)
-    for q in range(1, n_core):
-        summed = summed + shifted(partials[q], "core", n_core, -q).astype(jnp.float32)
-    for stage in reversed(range(levels)):
-        half = summed.shape[0] // 2
-        sent = summed[half:].astype(SUM_DTYPE)
-        arrived = lax.ppermute(sent, ("chip", "core"), chip_route(n_chip, n_core, stage, levels))
-        summed = summed[:half] + arrived.astype(jnp.float32)
-    reduced = summed[0]
-
-    got = []
-    for k in range(n_ex):
-        outgoing = reduced[k].astype(SUM_DTYPE)
-        if k == 0:
-            got.append(shifted(outgoing, "section", sections, 1))
-        else:
-            route = []
-            for s in range(sections):
-                for e in range(n_ex):
-                    route.append((s * n_ex + e, ((s + 1) % sections) * n_ex + (e - k) % n_ex))
-            got.append(lax.ppermute(outgoing, ("section", "ex"), route))
-    stacked = jnp.stack(got).astype(jnp.float32)
-    order = (ex_me + jnp.arange(n_ex)) % n_ex
-    expert_out = jnp.zeros_like(stacked).at[order].set(stacked)
-
-    branch = jnp.einsum("ect,ecd->td", selector_in, expert_out, precision=lax.Precision.HIGHEST)
     layer_out = (states_in.astype(jnp.float32) + branch).astype(jnp.bfloat16)
     return layer_out[None]
 

time: 114 us -> 113 us (level)
  waiting for transfers between devices: 49.3 us -> 37.5 us
  starting transfers between devices: 17.4 us -> 22.1 us
  other arithmetic: 1.68 us -> 4.94 us
  matrix products: 41.9 us -> 44.7 us
    ppermute x7 -> x10, waiting for transfers between devices: 13.2 us -> 8.04 us  [shifted(): return lax.ppermute(block, axes, route)]
    ppermute x2 -> x4, waiting for transfers between devices: 17.4 us -> 12.7 us  [body(): lax.ppermute(sent, ('chip', 'core'), chip_route(n_chip, n_core, stage, le...]
    dot_general x2 -> x4, matrix products: 27 us -> 31.1 us  [the longest x2 16 us: body(): jnp.dot(activated, cols, preferred_element_type=jnp.float32)]
    ppermute x1 -> x2, waiting for transfers between devices: 6.6 us -> 3.83 us  [body(): got[k].append(lax.ppermute(outgoing, ('section', 'ex'), route))]
    another operation x2, other arithmetic: 0.23 us -> 2.01 us  [body(): jnp.stack(core_rows[q], axis=1)]
    ppermute x1 -> x2, starting transfers between devices: 2.05 us -> 3.82 us  [body(): got[k].append(lax.ppermute(outgoing, ('section', 'ex'), route))]
    ppermute x7 -> x10, starting transfers between devices: 8.27 us -> 9.95 us  [shifted(): return lax.ppermute(block, axes, route)]
    unnamed x10, local copies, waits for them, and re-layouts: 1.67 us -> 0.03 us
  transfers between devices with their start and end apart: 14 -> 20, of which waited for: 9 -> 10; matrix products, arithmetic and copies ran while one was open for 31% -> 41% of each run, Pallas kernels for 0% -> 0%
where the time goes in v6:
time: 113 us; the launch traced here: 112 us
  matrix products  44.7 us (40%)
  waiting for transfers between devices  37.5 us (33%)
  starting transfers between devices  22.1 us (20%)
  other arithmetic  4.94 us (4%)
  local copies, waits for them, and re-layouts  2.75 us (2%)
    dot_general x2, matrix products, body(): jnp.dot(activated, cols, preferred_element_type=jnp.float32)  16 us
    ppermute x4, waiting for transfers between devices, body(): lax.ppermute(held, ('chip', 'core'), chip_route(n_chip, n_core, stage, le...  12.9 us
    ppermute x4, waiting for transfers between devices, body(): lax.ppermute(sent, ('chip', 'core'), chip_route(n_chip, n_core, stage, le...  12.7 us
    dot_general x1, matrix products, body(): up_part = jnp.dot(flat_rows, up_cols, preferred_element_type=jnp.float32)  12.4 us
    dot_general x1, matrix products, body(): jnp.dot(flat_rows, gate_cols, preferred_element_type=jnp.float32)  11.7 us
    ppermute x10, starting transfers between devices, shifted(): return lax.ppermute(block, axes, route)  9.95 us
    ppermute x10, waiting for transfers between devices, shifted(): return lax.ppermute(block, axes, route)  8.04 us
    ppermute x4, starting transfers between devices, body(): lax.ppermute(held, ('chip', 'core'), chip_route(n_chip, n_core, stage, le...  4.69 us
  transfers between devices with their start and end apart: 20, of which 10 were waited for; matrix products, arithmetic and copies ran while one was open for 41% of the time, Pallas kernels for 0%

profile of v6, /device:TPU:0, one launch (start us, length us, event | category | flops | bytes accessed | tf_op | source)
XLA Modules:
  0.0 112.4 jit_solution(4990845933337712346)
XLA Ops:
  0.0 0.8 eq.34
  0.8 2.0 %multiply_reduce_fusion = (f32[32]{0:T(128)S(1)}, f32[32,6144]{1,0:T(8,128)S(1)}) fusion(bf16[1,128,6144]{2,1,0:T(8,128)(2,1)} %param.8, s32[32]{0:T(128)S(1)} %eq.34), kind=kOutput, calls=%fused_computation.32 | convolution fusion | flops 50728928 | bytes 2359552 | tf_op jit(solution)/shard_map/dot_general | solution.py:63
  2.9 0.1 multiply_convert_fusion
  3.1 3.0 %collective-permute-start.1 = (bf16[1,16,6144]{2,1,0:T(8,128)(2,1)S(1)}, bf16[1,16,6144]{2,1,0:T(8,128)(2,1)S(1)}, u32[]{:S(2)}, u32[]{:S(2)}) collective-permute-start(bf16[1,16,6144]{2,1,0:T(8,128)(2,1)S(1)} %get-tuple-element.25), channel_id=1, source_target_pairs={{0,2},{1,5},{2,0},{3,7},{4,6},{5,1},{6,4},{7,3},{8,10},{9,13},{10,... | collective-permute-start | bytes 589832 | tf_op jit(solution)/shard_map/ppermute | solution.py:79
  6.1 2.6 %collective-permute-start.3 = (bf16[16,6144]{1,0:T(8,128)(2,1)S(1)}, bf16[16,6144]{1,0:T(8,128)(2,1)S(1)}, u32[]{:S(2)}, u32[]{:S(2)}) collective-permute-start(bf16[16,6144]{1,0:T(8,128)(2,1)S(1)} %get-tuple-element.26), channel_id=1, source_target_pairs={{0,8},{8,0},{1,9},{9,1},{2,10},{10,2},{3,11},{11,3},{4,12},{12,4},... | collective-permute-start | bytes 589832 | tf_op jit(solution)/shard_map/ppermute | solution.py:12
  8.7 1.0 slice_bitcast_fusion.1
  9.7 1.5 %collective-permute-start = (bf16[64,6144]{1,0:T(8,128)(2,1)}, bf16[64,6144]{1,0:T(8,128)(2,1)S(1)}, u32[]{:S(2)}, u32[]{:S(2)}) collective-permute-start(bf16[64,6144]{1,0:T(8,128)(2,1)} %get-tuple-element.19), channel_id=1, source_target_pairs={{0,16},{16,0},{1,17},{17,1},{2,18},{18,2},{3,19},{19,3},{4,20},{20... | collective-permute-start | bytes 2359304 | tf_op jit(solution)/shard_map/ppermute | solution.py:12
  11.2 6.4 %collective-permute-done.3 = bf16[16,6144]{1,0:T(8,128)(2,1)S(1)} collective-permute-done((bf16[16,6144]{1,0:T(8,128)(2,1)S(1)}, bf16[16,6144]{1,0:T(8,128)(2,1)S(1)}, u32[]{:S(2)}, u32[]{:S(2)}) %collective-permute-start.3) | collective-permute-done | bytes 196640 | tf_op jit(solution)/shard_map/ppermute | solution.py:12
  17.6 1.5 %collective-permute-start.4 = (bf16[1,16,6144]{2,1,0:T(8,128)(2,1)S(1)}, bf16[1,16,6144]{2,1,0:T(8,128)(2,1)S(1)}, u32[]{:S(2)}, u32[]{:S(2)}) collective-permute-start(bf16[1,16,6144]{2,1,0:T(8,128)(2,1)S(1)} %bitcast.84), channel_id=1, source_target_pairs={{0,2},{1,5},{2,0},{3,7},{4,6},{5,1},{6,4},{7,3},{8,10},{9,13},{10,... | collective-permute-start | bytes 589832 | tf_op jit(solution)/shard_map/ppermute | solution.py:79
  19.1 0.0 collective-permute-done.1
  19.2 0.1 collective-permute-start.2
  19.3 6.1 %collective-permute-done.4 = bf16[1,16,6144]{2,1,0:T(8,128)(2,1)S(1)} collective-permute-done((bf16[1,16,6144]{2,1,0:T(8,128)(2,1)S(1)}, bf16[1,16,6144]{2,1,0:T(8,128)(2,1)S(1)}, u32[]{:S(2)}, u32[]{:S(2)}) %collective-permute-start.4) | collective-permute-done | bytes 196640 | tf_op jit(solution)/shard_map/ppermute | solution.py:79
  25.4 0.0 copy-start.3
  25.4 0.0 copy-start.4
  25.5 0.0 copy-start.2
  25.5 0.1 collective-permute-start.5
  25.5 1.5 %collective-permute-done.2 = bf16[2,16,6144]{2,1,0:T(8,128)(2,1)S(1)} collective-permute-done((bf16[2,16,6144]{2,1,0:T(8,128)(2,1)S(1)}, bf16[2,16,6144]{2,1,0:T(8,128)(2,1)S(1)}, u32[]{:S(2)}, u32[]{:S(2)}) %collective-permute-start.2) | collective-permute-done | bytes 393248 | tf_op jit(solution)/shard_map/ppermute | solution.py:79
  27.0 1.0 fusion.37
  28.0 0.0 collective-permute-start.6
  28.1 5.3 %collective-permute-done.5 = bf16[2,16,6144]{2,1,0:T(8,128)(2,1)S(1)} collective-permute-done((bf16[2,16,6144]{2,1,0:T(8,128)(2,1)S(1)}, bf16[2,16,6144]{2,1,0:T(8,128)(2,1)S(1)}, u32[]{:S(2)}, u32[]{:S(2)}) %collective-permute-start.5) | collective-permute-done | bytes 393248 | tf_op jit(solution)/shard_map/ppermute | solution.py:79
  33.3 1.0 fusion.36
  34.3 0.0 collective-permute-start.7
  34.3 0.1 compare_select_fusion.6
  34.4 0.1 fusion.30
  34.5 0.6 gather_fusion
  35.1 0.1 broadcast_select_fusion
  35.1 1.5 %collective-permute-start.9 = (f32[2,16,128]{2,1,0:T(8,128)S(1)}, f32[2,16,128]{2,1,0:T(8,128)S(1)}, u32[]{:S(2)}, u32[]{:S(2)}) collective-permute-start(f32[2,16,128]{2,1,0:T(8,128)S(1)} %broadcast_select_fusion), channel_id=1, source_target_pairs={{0,16},{16,0},{1,17},{17,1},{2,18},{18,2},{3,19},{19,3},{4,20},{20... | collective-permute-start | bytes 49160 | tf_op jit(solution)/shard_map/ppermute | solution.py:12
  36.7 0.5 collective-permute-start.8
  37.2 1.5 %maximum_bitcast_fusion.1 = bf16[1,4,2,16,6144]{4,3,2,1,0:T(8,128)(2,1)S(1)} fusion(bf16[4,1,16,6144]{3,2,1,0:T(8,128)(2,1)} %bitcast.11, bf16[4,1,16,6144]{3,2,1,0:T(8,128)(2,1)} %bitcast.10), kind=kLoop, calls=%fused_computation.19 | loop fusion | flops 786432 | bytes 3145728 | tf_op jit(solution)/shard_map/stack | solution.py:85
  38.7 0.3 pad_maximum_fusion
  39.0 0.0 collective-permute-done
  39.0 11.7 %fusion.2 = f32[256,2048]{1,0:T(8,128)S(1)} fusion(bf16[256,6144]{1,0:T(8,128)(2,1)S(1)} %bitcast.79, bf16[1,6144,2048]{2,1,0:T(8,128)(2,1)} %param.10), kind=kOutput, calls=%fused_computation.3 | convolution fusion | flops 6442450944 | bytes 30408704 | tf_op jit(solution)/shard_map/dot_general | solution.py:89
  50.6 12.4 %fusion.20 = bf16[256,2048]{1,0:T(8,128)(2,1)S(1)} fusion(bf16[256,6144]{1,0:T(8,128)(2,1)S(1)} %bitcast.80, bf16[1,6144,2048]{2,1,0:T(8,128)(2,1)} %param.11, f32[256,2048]{1,0:T(8,128)S(1)} %fusion.2), kind=kOutput, calls=%fused_computation.17 | convolution fusion | flops 6445596672 | bytes 31457280 | tf_op jit(solution)/shard_map/dot_general | solution.py:90
  63.0 8.0 %fusion.11 = bf16[256,3072]{1,0:T(8,128)(2,1)S(1)} fusion(bf16[256,2048]{1,0:T(8,128)(2,1)S(1)} %fusion.20, bf16[2048,6144]{1,0:T(8,128)(2,1)} %bitcast.92), kind=kOutput, calls=%fused_computation.13 | convolution fusion | flops 3222011904 | bytes 15204352 | tf_op jit(solution)/shard_map/dot_general | solution.py:98
  71.0 0.0 collective-permute-done.9
  71.1 0.1 fusion.38
  71.2 0.1 collective-permute-start.10
  71.3 8.0 %fusion.14 = bf16[256,3072]{1,0:T(8,128)(2,1)S(1)} fusion(bf16[256,2048]{1,0:T(8,128)(2,1)S(1)} %fusion.20, bf16[2048,6144]{1,0:T(8,128)(2,1)} %bitcast.93), kind=kOutput, calls=%fused_computation.14 | convolution fusion | flops 3222011904 | bytes 15204352 | tf_op jit(solution)/shard_map/dot_general | solution.py:98
  79.3 0.1 fusion.39
  79.4 0.6 collective-permute-start.14
  79.9 0.0 collective-permute-done.10
  79.9 0.2 convert_add_fusion.1
  80.2 0.1 collective-permute-start.11
  80.3 1.6 %collective-permute-done.14 = bf16[4,2,16,3072]{3,2,1,0:T(8,128)(2,1)S(1)} collective-permute-done((bf16[4,2,16,3072]{3,2,1,0:T(8,128)(2,1)S(1)}, bf16[4,2,16,3072]{3,2,1,0:T(8,128)(2,1)S(1)}, u32[]{:S(2)}, u32[]{:S(2)}) %collective-permute-start.14) | collective-permute-done | bytes 786464 | tf_op jit(solution)/shard_map/ppermute | solution.py:12
  81.9 0.2 convert_add_fusion
  82.1 0.5 collective-permute-start.15
  82.6 5.4 %collective-permute-done.11 = bf16[2,2,16,3072]{3,2,1,0:T(8,128)(2,1)S(1)} collective-permute-done((bf16[2,2,16,3072]{3,2,1,0:T(8,128)(2,1)S(1)}, bf16[2,2,16,3072]{3,2,1,0:T(8,128)(2,1)S(1)}, u32[]{:S(2)}, u32[]{:S(2)}) %collective-permute-start.11) | collective-permute-done | bytes 393248 | tf_op jit(solution)/shard_map/ppermute | solution.py:113
  88.0 0.1 slice_add_fusion.1
  88.1 1.5 %collective-permute-start.12 = (bf16[1,2,16,3072]{3,2,1,0:T(8,128)(2,1)S(1)}, bf16[1,2,16,3072]{3,2,1,0:T(8,128)(2,1)S(1)}, u32[]{:S(2)}, u32[]{:S(2)}) collective-permute-start(bf16[1,2,16,3072]{3,2,1,0:T(8,128)(2,1)S(1)} %slice.151), channel_id=1, source_target_pairs={{0,2},{1,5},{2,0},{3,7},{4,6},{5,1},{6,4},{7,3},{8,10},{9,13},{10,... | collective-permute-start | bytes 589832 | tf_op jit(solution)/shard_map/ppermute | solution.py:113
  89.7 4.8 %collective-permute-done.15 = bf16[2,2,16,3072]{3,2,1,0:T(8,128)(2,1)S(1)} collective-permute-done((bf16[2,2,16,3072]{3,2,1,0:T(8,128)(2,1)S(1)}, bf16[2,2,16,3072]{3,2,1,0:T(8,128)(2,1)S(1)}, u32[]{:S(2)}, u32[]{:S(2)}) %collective-permute-start.15) | collective-permute-done | bytes 393248 | tf_op jit(solution)/shard_map/ppermute | solution.py:113
  94.5 0.1 slice_add_fusion
  94.6 1.5 %collective-permute-start.16 = (bf16[1,2,16,3072]{3,2,1,0:T(8,128)(2,1)S(1)}, bf16[1,2,16,3072]{3,2,1,0:T(8,128)(2,1)S(1)}, u32[]{:S(2)}, u32[]{:S(2)}) collective-permute-start(bf16[1,2,16,3072]{3,2,1,0:T(8,128)(2,1)S(1)} %slice.150), channel_id=1, source_target_pairs={{0,2},{1,5},{2,0},{3,7},{4,6},{5,1},{6,4},{7,3},{8,10},{9,13},{10,... | collective-permute-start | bytes 589832 | tf_op jit(solution)/shard_map/ppermute | solution.py:113
  96.1 0.0 collective-permute-done.12
  96.2 1.6 %collective-permute-start.13 = (bf16[16,3072]{1,0:T(8,128)(2,1)S(1)}, bf16[16,3072]{1,0:T(8,128)(2,1)S(1)}, u32[]{:S(2)}, u32[]{:S(2)}) collective-permute-start(bf16[16,3072]{1,0:T(8,128)(2,1)S(1)} %get-tuple-element.27), channel_id=1, source_target_pairs={{0,16},{16,0},{1,17},{17,1},{2,18},{18,2},{3,19},{19,3},{4,20},{20... | collective-permute-start | bytes 294920 | tf_op jit(solution)/shard_map/ppermute | solution.py:12
  97.8 2.5 %collective-permute-done.16 = bf16[1,2,16,3072]{3,2,1,0:T(8,128)(2,1)S(1)} collective-permute-done((bf16[1,2,16,3072]{3,2,1,0:T(8,128)(2,1)S(1)}, bf16[1,2,16,3072]{3,2,1,0:T(8,128)(2,1)S(1)}, u32[]{:S(2)}, u32[]{:S(2)}) %collective-permute-start.16) | collective-permute-done | bytes 196640 | tf_op jit(solution)/shard_map/ppermute | solution.py:113
  100.3 0.1 fusion.25
  100.4 1.6 %collective-permute-start.17 = (bf16[16,3072]{1,0:T(8,128)(2,1)S(1)}, bf16[16,3072]{1,0:T(8,128)(2,1)S(1)}, u32[]{:S(2)}, u32[]{:S(2)}) collective-permute-start(bf16[16,3072]{1,0:T(8,128)(2,1)S(1)} %get-tuple-element.29), channel_id=1, source_target_pairs={{0,16},{16,0},{1,17},{17,1},{2,18},{18,2},{3,19},{19,3},{4,20},{20... | collective-permute-start | bytes 294920 | tf_op jit(solution)/shard_map/ppermute | solution.py:12
  102.0 0.8 collective-permute-start.18
  102.8 3.0 %collective-permute-start.19 = (bf16[16,3072]{1,0:T(8,128)(2,1)S(1)}, bf16[16,3072]{1,0:T(8,128)(2,1)S(1)}, u32[]{:S(2)}, u32[]{:S(2)}) collective-permute-start(bf16[16,3072]{1,0:T(8,128)(2,1)S(1)} %get-tuple-element.30), channel_id=1, source_target_pairs={{0,24},{8,16},{16,8},{24,0},{1,25},{9,17},{17,9},{25,1},{2,26},{10... | collective-permute-start | bytes 294920 | tf_op jit(solution)/shard_map/ppermute | solution.py:126
  105.8 0.0 collective-permute-done.13
  105.8 0.0 collective-permute-done.17
  105.8 2.8 %collective-permute-done.18 = bf16[16,3072]{1,0:T(8,128)(2,1)S(1)} collective-permute-done((bf16[16,3072]{1,0:T(8,128)(2,1)S(1)}, bf16[16,3072]{1,0:T(8,128)(2,1)S(1)}, u32[]{:S(2)}, u32[]{:S(2)}) %collective-permute-start.18) | collective-permute-done | bytes 98336 | tf_op jit(solution)/shard_map/ppermute | solution.py:126
  108.6 1.1 collective-permute-done.19
  109.7 2.7 %fusion.10 = bf16[1,128,6144]{2,1,0:T(8,128)(2,1)} fusion(f32[2,16,128]{2,1,0:T(8,128)S(1)} %collective-permute-done.9, bf16[64,6144]{1,0:T(8,128)(2,1)S(1)} %collective-permute-done.8, bf16[64,6144]{1,0:T(8,128)(2,1)S(1)} %collective-permute-done, bf16[1,16,6144]{2,1,0:T(8,128)(2,1)S(1)} %maximum_bitcast_fusion.3, ...), kind=kOutput, calls=%fused_computation.12 | convolution fusion | flops 306905088 | bytes 3555328 | tf_op jit(solution)/shard_map/ect,ecd->td/dot_general | solution.py:130
  (27 shorter events, 0.4 us)
Async XLA Ops:
  0.0 2.8 %copy-start.1 = (bf16[1,6144]{1,0:T(2,128)(2,1)S(1)}, bf16[1,6144]{1,0:T(2,128)(2,1)}, u32[]{:S(2)}) copy-start(bf16[1,6144]{1,0:T(2,128)(2,1)} %param.9) | copy-start | bytes 36868
  0.8 7.9 %copy-start = (bf16[1,128,6144]{2,1,0:T(8,128)(2,1)S(1)}, bf16[1,128,6144]{2,1,0:T(8,128)(2,1)}, u32[]{:S(2)}) copy-start(bf16[1,128,6144]{2,1,0:T(8,128)(2,1)} %param.8) | copy-start | bytes 4718596
  3.1 16.1 %collective-permute-start.1 = (bf16[1,16,6144]{2,1,0:T(8,128)(2,1)S(1)}, bf16[1,16,6144]{2,1,0:T(8,128)(2,1)S(1)}, u32[]{:S(2)}, u32[]{:S(2)}) collective-permute-start(bf16[1,16,6144]{2,1,0:T(8,128)(2,1)S(1)} %get-tuple-element.25), channel_id=1, source_target_pairs={{0,2},{1,5},{2,0},{3,7},{4,6},{5,1},{6,4},{7,3},{8,10},{9,13},{10,... | collective-permute-start | bytes 589832 | tf_op jit(solution)/shard_map/ppermute | solution.py:79
  6.1 11.5 %collective-permute-start.3 = (bf16[16,6144]{1,0:T(8,128)(2,1)S(1)}, bf16[16,6144]{1,0:T(8,128)(2,1)S(1)}, u32[]{:S(2)}, u32[]{:S(2)}) collective-permute-start(bf16[16,6144]{1,0:T(8,128)(2,1)S(1)} %get-tuple-element.26), channel_id=1, source_target_pairs={{0,8},{8,0},{1,9},{9,1},{2,10},{10,2},{3,11},{11,3},{4,12},{12,4},... | collective-permute-start | bytes 589832 | tf_op jit(solution)/shard_map/ppermute | solution.py:12
  9.7 29.3 %collective-permute-start = (bf16[64,6144]{1,0:T(8,128)(2,1)}, bf16[64,6144]{1,0:T(8,128)(2,1)S(1)}, u32[]{:S(2)}, u32[]{:S(2)}) collective-permute-start(bf16[64,6144]{1,0:T(8,128)(2,1)} %get-tuple-element.19), channel_id=1, source_target_pairs={{0,16},{16,0},{1,17},{17,1},{2,18},{18,2},{3,19},{19,3},{4,20},{20... | collective-permute-start | bytes 2359304 | tf_op jit(solution)/shard_map/ppermute | solution.py:12
  17.6 7.8 %collective-permute-start.4 = (bf16[1,16,6144]{2,1,0:T(8,128)(2,1)S(1)}, bf16[1,16,6144]{2,1,0:T(8,128)(2,1)S(1)}, u32[]{:S(2)}, u32[]{:S(2)}) collective-permute-start(bf16[1,16,6144]{2,1,0:T(8,128)(2,1)S(1)} %bitcast.84), channel_id=1, source_target_pairs={{0,2},{1,5},{2,0},{3,7},{4,6},{5,1},{6,4},{7,3},{8,10},{9,13},{10,... | collective-permute-start | bytes 589832 | tf_op jit(solution)/shard_map/ppermute | solution.py:79
  19.2 7.8 %collective-permute-start.2 = (bf16[2,16,6144]{2,1,0:T(8,128)(2,1)S(1)}, bf16[2,16,6144]{2,1,0:T(8,128)(2,1)S(1)}, u32[]{:S(2)}, u32[]{:S(2)}) collective-permute-start(bf16[2,16,6144]{2,1,0:T(8,128)(2,1)S(1)} %pad_maximum_fusion.3), channel_id=1, source_target_pairs={{0,4},{1,3},{2,6},{3,1},{4,0},{5,7},{6,2},{7,5},{8,12},{9,11},{10,... | collective-permute-start | bytes 1179656 | tf_op jit(solution)/shard_map/ppermute | solution.py:79
  25.4 8.9 %copy-start.3 = (f32[1,1,2,16]{3,2,1,0:T(2,128)S(1)}, f32[1,1,2,16]{3,2,1,0:T(2,128)}, u32[]{:S(2)}) copy-start(f32[1,1,2,16]{3,2,1,0:T(2,128)} %param.15) | copy-start | bytes 388
  25.4 8.9 %copy-start.4 = (s32[1,1,2]{2,1,0:T(1,128)S(1)}, s32[1,1,2]{2,1,0:T(1,128)}, u32[]{:S(2)}) copy-start(s32[1,1,2]{2,1,0:T(1,128)} %param.14) | copy-start | bytes 28
  25.5 8.9 %copy-start.2 = (s32[1,1,2,16]{3,2,1,0:T(2,128)S(1)}, s32[1,1,2,16]{3,2,1,0:T(2,128)}, u32[]{:S(2)}) copy-start(s32[1,1,2,16]{3,2,1,0:T(2,128)} %param.13) | copy-start | bytes 388
  25.5 7.8 %collective-permute-start.5 = (bf16[2,16,6144]{2,1,0:T(8,128)(2,1)S(1)}, bf16[2,16,6144]{2,1,0:T(8,128)(2,1)S(1)}, u32[]{:S(2)}, u32[]{:S(2)}) collective-permute-start(bf16[2,16,6144]{2,1,0:T(8,128)(2,1)S(1)} %pad_maximum_fusion.4), channel_id=1, source_target_pairs={{0,4},{1,3},{2,6},{3,1},{4,0},{5,7},{6,2},{7,5},{8,12},{9,11},{10,... | collective-permute-start | bytes 1179656 | tf_op jit(solution)/shard_map/ppermute | solution.py:79
  28.0 9.1 %collective-permute-start.6 = (bf16[4,16,6144]{2,1,0:T(8,128)(2,1)}, bf16[4,16,6144]{2,1,0:T(8,128)(2,1)}, u32[]{:S(2)}, u32[]{:S(2)}) collective-permute-start(bf16[4,16,6144]{2,1,0:T(8,128)(2,1)} %get-tuple-element.22), channel_id=1, source_target_pairs={{0,1},{1,0},{2,3},{3,2},{4,5},{5,4},{6,7},{7,6},{8,9},{9,8},{10,11... | collective-permute-start | bytes 2359304 | tf_op jit(solution)/shard_map/ppermute | solution.py:12
  34.3 2.9 %collective-permute-start.7 = (bf16[4,16,6144]{2,1,0:T(8,128)(2,1)}, bf16[4,16,6144]{2,1,0:T(8,128)(2,1)}, u32[]{:S(2)}, u32[]{:S(2)}) collective-permute-start(bf16[4,16,6144]{2,1,0:T(8,128)(2,1)} %get-tuple-element.24), channel_id=1, source_target_pairs={{0,1},{1,0},{2,3},{3,2},{4,5},{5,4},{6,7},{7,6},{8,9},{9,8},{10,11... | collective-permute-start | bytes 2359304 | tf_op jit(solution)/shard_map/ppermute | solution.py:12
  35.1 35.9 %collective-permute-start.9 = (f32[2,16,128]{2,1,0:T(8,128)S(1)}, f32[2,16,128]{2,1,0:T(8,128)S(1)}, u32[]{:S(2)}, u32[]{:S(2)}) collective-permute-start(f32[2,16,128]{2,1,0:T(8,128)S(1)} %broadcast_select_fusion), channel_id=1, source_target_pairs={{0,16},{16,0},{1,17},{17,1},{2,18},{18,2},{3,19},{19,3},{4,20},{20... | collective-permute-start | bytes 49160 | tf_op jit(solution)/shard_map/ppermute | solution.py:12
  36.7 34.4 %collective-permute-start.8 = (bf16[64,6144]{1,0:T(8,128)(2,1)S(1)}, bf16[64,6144]{1,0:T(8,128)(2,1)S(1)}, u32[]{:S(2)}, u32[]{:S(2)}) collective-permute-start(bf16[64,6144]{1,0:T(8,128)(2,1)S(1)} %get-tuple-element.20), channel_id=1, source_target_pairs={{0,16},{16,0},{1,17},{17,1},{2,18},{18,2},{3,19},{19,3},{4,20},{20... | collective-permute-start | bytes 2359304 | tf_op jit(solution)/shard_map/ppermute | solution.py:12
  71.2 8.8 %collective-permute-start.10 = (bf16[4,2,16,3072]{3,2,1,0:T(8,128)(2,1)S(1)}, bf16[4,2,16,3072]{3,2,1,0:T(8,128)(2,1)S(1)}, u32[]{:S(2)}, u32[]{:S(2)}) collective-permute-start(bf16[4,2,16,3072]{3,2,1,0:T(8,128)(2,1)S(1)} %bitcast.88), channel_id=1, source_target_pairs={{0,1},{1,0},{2,3},{3,2},{4,5},{5,4},{6,7},{7,6},{8,9},{9,8},{10,11... | collective-permute-start | bytes 2359304 | tf_op jit(solution)/shard_map/ppermute | solution.py:12
  79.4 2.5 %collective-permute-start.14 = (bf16[4,2,16,3072]{3,2,1,0:T(8,128)(2,1)S(1)}, bf16[4,2,16,3072]{3,2,1,0:T(8,128)(2,1)S(1)}, u32[]{:S(2)}, u32[]{:S(2)}) collective-permute-start(bf16[4,2,16,3072]{3,2,1,0:T(8,128)(2,1)S(1)} %bitcast.87), channel_id=1, source_target_pairs={{0,1},{1,0},{2,3},{3,2},{4,5},{5,4},{6,7},{7,6},{8,9},{9,8},{10,11... | collective-permute-start | bytes 2359304 | tf_op jit(solution)/shard_map/ppermute | solution.py:12
  80.2 7.8 %collective-permute-start.11 = (bf16[2,2,16,3072]{3,2,1,0:T(8,128)(2,1)S(1)}, bf16[2,2,16,3072]{3,2,1,0:T(8,128)(2,1)S(1)}, u32[]{:S(2)}, u32[]{:S(2)}) collective-permute-start(bf16[2,2,16,3072]{3,2,1,0:T(8,128)(2,1)S(1)} %slice.149), channel_id=1, source_target_pairs={{0,4},{1,3},{2,6},{3,1},{4,0},{5,7},{6,2},{7,5},{8,12},{9,11},{10,... | collective-permute-start | bytes 1179656 | tf_op jit(solution)/shard_map/ppermute | solution.py:113
  82.1 12.4 %collective-permute-start.15 = (bf16[2,2,16,3072]{3,2,1,0:T(8,128)(2,1)S(1)}, bf16[2,2,16,3072]{3,2,1,0:T(8,128)(2,1)S(1)}, u32[]{:S(2)}, u32[]{:S(2)}) collective-permute-start(bf16[2,2,16,3072]{3,2,1,0:T(8,128)(2,1)S(1)} %slice.148), channel_id=1, source_target_pairs={{0,4},{1,3},{2,6},{3,1},{4,0},{5,7},{6,2},{7,5},{8,12},{9,11},{10,... | collective-permute-start | bytes 1179656 | tf_op jit(solution)/shard_map/ppermute | solution.py:113
  88.1 8.0 %collective-permute-start.12 = (bf16[1,2,16,3072]{3,2,1,0:T(8,128)(2,1)S(1)}, bf16[1,2,16,3072]{3,2,1,0:T(8,128)(2,1)S(1)}, u32[]{:S(2)}, u32[]{:S(2)}) collective-permute-start(bf16[1,2,16,3072]{3,2,1,0:T(8,128)(2,1)S(1)} %slice.151), channel_id=1, source_target_pairs={{0,2},{1,5},{2,0},{3,7},{4,6},{5,1},{6,4},{7,3},{8,10},{9,13},{10,... | collective-permute-start | bytes 589832 | tf_op jit(solution)/shard_map/ppermute | solution.py:113
  94.6 5.7 %collective-permute-start.16 = (bf16[1,2,16,3072]{3,2,1,0:T(8,128)(2,1)S(1)}, bf16[1,2,16,3072]{3,2,1,0:T(8,128)(2,1)S(1)}, u32[]{:S(2)}, u32[]{:S(2)}) collective-permute-start(bf16[1,2,16,3072]{3,2,1,0:T(8,128)(2,1)S(1)} %slice.150), channel_id=1, source_target_pairs={{0,2},{1,5},{2,0},{3,7},{4,6},{5,1},{6,4},{7,3},{8,10},{9,13},{10,... | collective-permute-start | bytes 589832 | tf_op jit(solution)/shard_map/ppermute | solution.py:113
  96.2 9.6 %collective-permute-start.13 = (bf16[16,3072]{1,0:T(8,128)(2,1)S(1)}, bf16[16,3072]{1,0:T(8,128)(2,1)S(1)}, u32[]{:S(2)}, u32[]{:S(2)}) collective-permute-start(bf16[16,3072]{1,0:T(8,128)(2,1)S(1)} %get-tuple-element.27), channel_id=1, source_target_pairs={{0,16},{16,0},{1,17},{17,1},{2,18},{18,2},{3,19},{19,3},{4,20},{20... | collective-permute-start | bytes 294920 | tf_op jit(solution)/shard_map/ppermute | solution.py:12
  100.4 5.4 %collective-permute-start.17 = (bf16[16,3072]{1,0:T(8,128)(2,1)S(1)}, bf16[16,3072]{1,0:T(8,128)(2,1)S(1)}, u32[]{:S(2)}, u32[]{:S(2)}) collective-permute-start(bf16[16,3072]{1,0:T(8,128)(2,1)S(1)} %get-tuple-element.29), channel_id=1, source_target_pairs={{0,16},{16,0},{1,17},{17,1},{2,18},{18,2},{3,19},{19,3},{4,20},{20... | collective-permute-start | bytes 294920 | tf_op jit(solution)/shard_map/ppermute | solution.py:12
  102.0 6.6 %collective-permute-start.18 = (bf16[16,3072]{1,0:T(8,128)(2,1)S(1)}, bf16[16,3072]{1,0:T(8,128)(2,1)S(1)}, u32[]{:S(2)}, u32[]{:S(2)}) collective-permute-start(bf16[16,3072]{1,0:T(8,128)(2,1)S(1)} %get-tuple-element.28), channel_id=1, source_target_pairs={{0,24},{8,16},{16,8},{24,0},{1,25},{9,17},{17,9},{25,1},{2,26},{10... | collective-permute-start | bytes 294920 | tf_op jit(solution)/shard_map/ppermute | solution.py:126
  102.8 6.9 %collective-permute-start.19 = (bf16[16,3072]{1,0:T(8,128)(2,1)S(1)}, bf16[16,3072]{1,0:T(8,128)(2,1)S(1)}, u32[]{:S(2)}, u32[]{:S(2)}) collective-permute-start(bf16[16,3072]{1,0:T(8,128)(2,1)S(1)} %get-tuple-element.30), channel_id=1, source_target_pairs={{0,24},{8,16},{16,8},{24,0},{1,25},{9,17},{17,9},{25,1},{2,26},{10... | collective-permute-start | bytes 294920 | tf_op jit(solution)/shard_map/ppermute | solution.py:126

commit v7 on v6

--- a/solution.py
+++ b/solution.py
@@ -60,25 +60,33 @@
     selector_in = shifted(selector_out, "section", sections, 1)
 
     selector = (slot_rows.reshape(-1)[:, None] == jnp.arange(tok_count)[None, :]).astype(states.dtype)
-    chosen = jnp.dot(selector, states, preferred_element_type=jnp.float32)
-    normed = (
-        chosen
-        * lax.rsqrt(jnp.mean(chosen * chosen, axis=-1, keepdims=True) + 1e-05)
-        * scale_gain.astype(jnp.float32)
-    ).astype(jnp.bfloat16)
-    picked = normed.reshape(experts, capacity, width)
+    raw = jnp.dot(selector, states, preferred_element_type=jnp.float32).astype(states.dtype)
+    raw = raw.reshape(experts, capacity, width)
+    gain = scale_gain.astype(jnp.float32)
 
-    parts = [lax.dynamic_index_in_dim(picked, ex_me, 0, keepdims=False)]
-    for k in range(1, n_ex):
-        outgoing = lax.dynamic_index_in_dim(picked, (ex_me + k) % n_ex, 0, keepdims=False)
-        parts.append(shifted(outgoing, "ex", n_ex, k))
-    chip_rows = []
-    for part in parts:
-        held = part[None]
+    def normalized(rows):
+        rows = rows.astype(jnp.float32)
+        return (
+            rows * lax.rsqrt(jnp.mean(rows * rows, axis=-1, keepdims=True) + 1e-05) * gain
+        ).astype(jnp.bfloat16)
+
+    def doubled(held):
+        held = held[None]
         for stage in range(levels):
             arrived = lax.ppermute(held, ("chip", "core"), chip_route(n_chip, n_core, stage, levels))
             held = jnp.concatenate([held, arrived])
-        chip_rows.append(held)
+        return held
+
+    splits = 2 if capacity % 2 == 0 else 1
+    chip_rows = [doubled(normalized(lax.dynamic_index_in_dim(raw, ex_me, 0, keepdims=False)))]
+    for k in range(1, n_ex):
+        outgoing = lax.dynamic_index_in_dim(raw, (ex_me + k) % n_ex, 0, keepdims=False)
+        step = capacity // splits
+        halves = []
+        for h in range(splits):
+            landed = shifted(outgoing[h * step:(h + 1) * step], "ex", n_ex, k)
+            halves.append(doubled(normalized(landed)))
+        chip_rows.append(jnp.concatenate(halves, axis=1))
     core_rows = [chip_rows] + [
         [shifted(rows, "core", n_core, q) for rows in chip_rows] for q in range(1, n_core)
     ]

time: 113 us -> 111 us (0.982)
  starting transfers between devices: 22.1 us -> 26.7 us
  waiting for transfers between devices: 37.5 us -> 33.5 us
  other arithmetic: 4.94 us -> 2.35 us
    ppermute x10 -> x11, waiting for transfers between devices: 8.04 us -> 5.19 us  [shifted(): return lax.ppermute(block, axes, route)]
    ppermute x4 -> x6, starting transfers between devices: 4.69 us -> 6.99 us  [doubled(): lax.ppermute(held, ('chip', 'core'), chip_route(n_chip, n_core, stage, le...]
    another operation x2, other arithmetic: 2.01 us -> 0.18 us  [body(): jnp.stack(core_rows[q], axis=1)]
    ppermute x10 -> x11, starting transfers between devices: 9.95 us -> 11.6 us  [shifted(): return lax.ppermute(block, axes, route)]
    another operation x2, other arithmetic: 1.78 us -> 0.35 us  [body(): jnp.stack([jnp.stack(core_rows[q], axis=1) for q in range(n_core)])]
    ppermute x4 -> x6, waiting for transfers between devices: 12.9 us -> 11.6 us  [doubled(): lax.ppermute(held, ('chip', 'core'), chip_route(n_chip, n_core, stage, le...]
  transfers between devices with their start and end apart: 20 -> 23, of which waited for: 10 -> 15; matrix products, arithmetic and copies ran while one was open for 41% -> 40% of each run, Pallas kernels for 0% -> 0%
where the time goes in v7:
time: 111 us
  matrix products  44.5 us (40%)
  waiting for transfers between devices  33.5 us (30%)
  starting transfers between devices  26.7 us (24%)
  local copies, waits for them, and re-layouts  3.49 us (3%)
  other arithmetic  2.35 us (2%)
    dot_general x2, matrix products, body(): jnp.dot(activated, cols, preferred_element_type=jnp.float32)  16 us
    ppermute x4, waiting for transfers between devices, body(): lax.ppermute(sent, ('chip', 'core'), chip_route(n_chip, n_core, stage, le...  12.7 us
    dot_general x1, matrix products, body(): up_part = jnp.dot(flat_rows, up_cols, preferred_element_type=jnp.float32)  12.4 us
    dot_general x1, matrix products, body(): jnp.dot(flat_rows, gate_cols, preferred_element_type=jnp.float32)  11.7 us
    ppermute x11, starting transfers between devices, shifted(): return lax.ppermute(block, axes, route)  11.6 us
    ppermute x6, waiting for transfers between devices, doubled(): lax.ppermute(held, ('chip', 'core'), chip_route(n_chip, n_core, stage, le...  11.6 us
    ppermute x6, starting transfers between devices, doubled(): lax.ppermute(held, ('chip', 'core'), chip_route(n_chip, n_core, stage, le...  6.99 us
    ppermute x11, waiting for transfers between devices, shifted(): return lax.ppermute(block, axes, route)  5.19 us
  transfers between devices with their start and end apart: 23, of which 15 were waited for; matrix products, arithmetic and copies ran while one was open for 40% of the time, Pallas kernels for 0%

profile of v7, /device:TPU:0, one launch (start us, length us, event | category | flops | bytes accessed | tf_op | source)
XLA Modules:
  0.0 110.8 jit_solution(3384898813356952588)
XLA Ops:
  0.0 0.9 eq.34
  0.9 1.8 %convolution_convert_fusion = bf16[32,6144]{1,0:T(8,128)(2,1)S(1)} fusion(bf16[1,128,6144]{2,1,0:T(8,128)(2,1)} %param.8, s32[32]{0:T(128)S(1)} %eq.34), kind=kOutput, calls=%fused_computation.13 | convolution fusion | flops 50532352 | bytes 1966208 | tf_op jit(solution)/shard_map/dot_general | solution.py:63
  2.7 0.7 dynamic-slice_bitcast_fusion.1
  3.3 4.0 %collective-permute-start.6 = (bf16[8,6144]{1,0:T(8,128)(2,1)}, bf16[8,6144]{1,0:T(8,128)(2,1)S(1)}, u32[]{:S(2)}, u32[]{:S(2)}) collective-permute-start(bf16[8,6144]{1,0:T(8,128)(2,1)} %get-tuple-element.24), channel_id=1, source_target_pairs={{0,8},{8,0},{1,9},{9,1},{2,10},{10,2},{3,11},{11,3},{4,12},{12,4},... | collective-permute-start | bytes 294920 | tf_op jit(solution)/shard_map/ppermute | solution.py:12
  7.4 0.2 fusion.24
  7.6 0.1 fusion.26
  7.8 1.9 %collective-permute-start.1 = (bf16[1,16,6144]{2,1,0:T(8,128)(2,1)S(1)}, bf16[1,16,6144]{2,1,0:T(8,128)(2,1)S(1)}, u32[]{:S(2)}, u32[]{:S(2)}) collective-permute-start(bf16[1,16,6144]{2,1,0:T(8,128)(2,1)S(1)} %fusion.26), channel_id=1, source_target_pairs={{0,2},{1,5},{2,0},{3,7},{4,6},{5,1},{6,4},{7,3},{8,10},{9,13},{10,... | collective-permute-start | bytes 589832 | tf_op jit(solution)/shard_map/ppermute | solution.py:76
  9.7 1.0 slice_bitcast_fusion.1
  10.7 1.5 %collective-permute-start = (bf16[64,6144]{1,0:T(8,128)(2,1)}, bf16[64,6144]{1,0:T(8,128)(2,1)S(1)}, u32[]{:S(2)}, u32[]{:S(2)}) collective-permute-start(bf16[64,6144]{1,0:T(8,128)(2,1)} %get-tuple-element.19), channel_id=1, source_target_pairs={{0,16},{16,0},{1,17},{17,1},{2,18},{18,2},{3,19},{19,3},{4,20},{20... | collective-permute-start | bytes 2359304 | tf_op jit(solution)/shard_map/ppermute | solution.py:12
  12.2 0.1 compare_select_fusion.6
  12.3 0.1 fusion.40
  12.4 0.5 gather_fusion
  12.9 2.5 %collective-permute-done.6 = bf16[8,6144]{1,0:T(8,128)(2,1)S(1)} collective-permute-done((bf16[8,6144]{1,0:T(8,128)(2,1)}, bf16[8,6144]{1,0:T(8,128)(2,1)S(1)}, u32[]{:S(2)}, u32[]{:S(2)}) %collective-permute-start.6) | collective-permute-done | bytes 98336 | tf_op jit(solution)/shard_map/ppermute | solution.py:12
  15.4 0.2 fusion.35
  15.6 1.1 collective-permute-done.3
  16.7 0.2 fusion.32
  16.9 0.1 fusion.39
  17.0 1.6 %collective-permute-start.4 = (bf16[1,8,6144]{2,1,0:T(8,128)(2,1)S(1)}, bf16[1,8,6144]{2,1,0:T(8,128)(2,1)S(1)}, u32[]{:S(2)}, u32[]{:S(2)}) collective-permute-start(bf16[1,8,6144]{2,1,0:T(8,128)(2,1)S(1)} %get-tuple-element.29), channel_id=1, source_target_pairs={{0,2},{1,5},{2,0},{3,7},{4,6},{5,1},{6,4},{7,3},{8,10},{9,13},{10,... | collective-permute-start | bytes 294920 | tf_op jit(solution)/shard_map/ppermute | solution.py:76
  18.6 0.5 collective-permute-start.7
  19.2 2.5 %collective-permute-done.4 = bf16[1,8,6144]{2,1,0:T(8,128)(2,1)S(1)} collective-permute-done((bf16[1,8,6144]{2,1,0:T(8,128)(2,1)S(1)}, bf16[1,8,6144]{2,1,0:T(8,128)(2,1)S(1)}, u32[]{:S(2)}, u32[]{:S(2)}) %collective-permute-start.4) | collective-permute-done | bytes 98336 | tf_op jit(solution)/shard_map/ppermute | solution.py:76
  21.7 0.8 collective-permute-start.5
  22.5 1.4 %collective-permute-done.7 = bf16[1,8,6144]{2,1,0:T(8,128)(2,1)S(1)} collective-permute-done((bf16[1,8,6144]{2,1,0:T(8,128)(2,1)S(1)}, bf16[1,8,6144]{2,1,0:T(8,128)(2,1)S(1)}, u32[]{:S(2)}, u32[]{:S(2)}) %collective-permute-start.7) | collective-permute-done | bytes 98336 | tf_op jit(solution)/shard_map/ppermute | solution.py:76
  24.0 0.1 collective-permute-start.8
  24.1 2.0 %collective-permute-start.2 = (bf16[2,16,6144]{2,1,0:T(8,128)(2,1)S(1)}, bf16[2,16,6144]{2,1,0:T(8,128)(2,1)S(1)}, u32[]{:S(2)}, u32[]{:S(2)}) collective-permute-start(bf16[2,16,6144]{2,1,0:T(8,128)(2,1)S(1)} %pad_maximum_fusion.2), channel_id=1, source_target_pairs={{0,4},{1,3},{2,6},{3,1},{4,0},{5,7},{6,2},{7,5},{8,12},{9,11},{10,... | collective-permute-start | bytes 1179656 | tf_op jit(solution)/shard_map/ppermute | solution.py:76
  26.2 1.3 %collective-permute-done.5 = bf16[2,8,6144]{2,1,0:T(8,128)(2,1)S(1)} collective-permute-done((bf16[2,8,6144]{2,1,0:T(8,128)(2,1)S(1)}, bf16[2,8,6144]{2,1,0:T(8,128)(2,1)S(1)}, u32[]{:S(2)}, u32[]{:S(2)}) %collective-permute-start.5) | collective-permute-done | bytes 196640 | tf_op jit(solution)/shard_map/ppermute | solution.py:76
  27.4 2.3 %collective-permute-done.8 = bf16[2,8,6144]{2,1,0:T(8,128)(2,1)S(1)} collective-permute-done((bf16[2,8,6144]{2,1,0:T(8,128)(2,1)S(1)}, bf16[2,8,6144]{2,1,0:T(8,128)(2,1)S(1)}, u32[]{:S(2)}, u32[]{:S(2)}) %collective-permute-start.8) | collective-permute-done | bytes 196640 | tf_op jit(solution)/shard_map/ppermute | solution.py:76
  29.7 0.1 maximum_maximum_fusion
  29.8 0.1 collective-permute-start.10
  29.8 4.1 %collective-permute-done.2 = bf16[2,16,6144]{2,1,0:T(8,128)(2,1)S(1)} collective-permute-done((bf16[2,16,6144]{2,1,0:T(8,128)(2,1)S(1)}, bf16[2,16,6144]{2,1,0:T(8,128)(2,1)S(1)}, u32[]{:S(2)}, u32[]{:S(2)}) %collective-permute-start.2) | collective-permute-done | bytes 393248 | tf_op jit(solution)/shard_map/ppermute | solution.py:76
  33.9 0.1 fusion.46
  34.0 0.1 collective-permute-start.9
  34.1 0.1 broadcast_select_fusion
  34.2 1.6 %collective-permute-start.12 = (f32[2,16,128]{2,1,0:T(8,128)S(1)}, f32[2,16,128]{2,1,0:T(8,128)S(1)}, u32[]{:S(2)}, u32[]{:S(2)}) collective-permute-start(f32[2,16,128]{2,1,0:T(8,128)S(1)} %broadcast_select_fusion), channel_id=1, source_target_pairs={{0,16},{16,0},{1,17},{17,1},{2,18},{18,2},{3,19},{19,3},{4,20},{20... | collective-permute-start | bytes 49160 | tf_op jit(solution)/shard_map/ppermute | solution.py:12
  35.8 0.4 collective-permute-start.11
  36.2 0.1 fusion.54
  36.3 0.1 collective-permute-done.9
  36.4 0.1 maximum_bitcast_fusion.1
  36.5 0.2 pad_maximum_fusion
  36.8 11.7 %fusion.2 = f32[256,2048]{1,0:T(8,128)S(1)} fusion(bf16[256,6144]{1,0:T(8,128)(2,1)S(1)} %bitcast.82, bf16[1,6144,2048]{2,1,0:T(8,128)(2,1)} %param.10), kind=kOutput, calls=%fused_computation.3 | convolution fusion | flops 6442450944 | bytes 30408704 | tf_op jit(solution)/shard_map/dot_general | solution.py:97
  48.4 12.4 %fusion.20 = bf16[256,2048]{1,0:T(8,128)(2,1)S(1)} fusion(bf16[256,6144]{1,0:T(8,128)(2,1)S(1)} %bitcast.83, bf16[1,6144,2048]{2,1,0:T(8,128)(2,1)} %param.11, f32[256,2048]{1,0:T(8,128)S(1)} %fusion.2), kind=kOutput, calls=%fused_computation.18 | convolution fusion | flops 6445596672 | bytes 31457280 | tf_op jit(solution)/shard_map/dot_general | solution.py:98
  60.8 8.0 %fusion.11 = bf16[256,3072]{1,0:T(8,128)(2,1)S(1)} fusion(bf16[256,2048]{1,0:T(8,128)(2,1)S(1)} %fusion.20, bf16[2048,6144]{1,0:T(8,128)(2,1)} %bitcast.97), kind=kOutput, calls=%fused_computation.14 | convolution fusion | flops 3222011904 | bytes 15204352 | tf_op jit(solution)/shard_map/dot_general | solution.py:106
  68.8 0.1 fusion.47
  68.9 0.2 collective-permute-start.13
  69.1 8.0 %fusion.14 = bf16[256,3072]{1,0:T(8,128)(2,1)S(1)} fusion(bf16[256,2048]{1,0:T(8,128)(2,1)S(1)} %fusion.20, bf16[2048,6144]{1,0:T(8,128)(2,1)} %bitcast.98), kind=kOutput, calls=%fused_computation.15 | convolution fusion | flops 3222011904 | bytes 15204352 | tf_op jit(solution)/shard_map/dot_general | solution.py:106
  77.1 0.1 fusion.48
  77.2 0.4 collective-permute-start.17
  77.7 0.2 convert_add_fusion.1
  77.9 0.6 collective-permute-start.14
  78.6 1.0 collective-permute-done.17
  79.6 0.2 convert_add_fusion
  79.8 0.6 collective-permute-start.18
  80.5 5.3 %collective-permute-done.14 = bf16[2,2,16,3072]{3,2,1,0:T(8,128)(2,1)S(1)} collective-permute-done((bf16[2,2,16,3072]{3,2,1,0:T(8,128)(2,1)S(1)}, bf16[2,2,16,3072]{3,2,1,0:T(8,128)(2,1)S(1)}, u32[]{:S(2)}, u32[]{:S(2)}) %collective-permute-start.14) | collective-permute-done | bytes 393248 | tf_op jit(solution)/shard_map/ppermute | solution.py:121
  85.9 1.5 %collective-permute-start.15 = (bf16[1,2,16,3072]{3,2,1,0:T(8,128)(2,1)S(1)}, bf16[1,2,16,3072]{3,2,1,0:T(8,128)(2,1)S(1)}, u32[]{:S(2)}, u32[]{:S(2)}) collective-permute-start(bf16[1,2,16,3072]{3,2,1,0:T(8,128)(2,1)S(1)} %slice.167), channel_id=1, source_target_pairs={{0,2},{1,5},{2,0},{3,7},{4,6},{5,1},{6,4},{7,3},{8,10},{9,13},{10,... | collective-permute-start | bytes 589832 | tf_op jit(solution)/shard_map/ppermute | solution.py:121
  87.4 4.7 %collective-permute-done.18 = bf16[2,2,16,3072]{3,2,1,0:T(8,128)(2,1)S(1)} collective-permute-done((bf16[2,2,16,3072]{3,2,1,0:T(8,128)(2,1)S(1)}, bf16[2,2,16,3072]{3,2,1,0:T(8,128)(2,1)S(1)}, u32[]{:S(2)}, u32[]{:S(2)}) %collective-permute-start.18) | collective-permute-done | bytes 393248 | tf_op jit(solution)/shard_map/ppermute | solution.py:121
  92.2 1.5 %collective-permute-start.19 = (bf16[1,2,16,3072]{3,2,1,0:T(8,128)(2,1)S(1)}, bf16[1,2,16,3072]{3,2,1,0:T(8,128)(2,1)S(1)}, u32[]{:S(2)}, u32[]{:S(2)}) collective-permute-start(bf16[1,2,16,3072]{3,2,1,0:T(8,128)(2,1)S(1)} %slice.166), channel_id=1, source_target_pairs={{0,2},{1,5},{2,0},{3,7},{4,6},{5,1},{6,4},{7,3},{8,10},{9,13},{10,... | collective-permute-start | bytes 589832 | tf_op jit(solution)/shard_map/ppermute | solution.py:121
  93.7 1.6 %collective-permute-start.16 = (bf16[16,3072]{1,0:T(8,128)(2,1)S(1)}, bf16[16,3072]{1,0:T(8,128)(2,1)S(1)}, u32[]{:S(2)}, u32[]{:S(2)}) collective-permute-start(bf16[16,3072]{1,0:T(8,128)(2,1)S(1)} %get-tuple-element.25), channel_id=1, source_target_pairs={{0,16},{16,0},{1,17},{17,1},{2,18},{18,2},{3,19},{19,3},{4,20},{20... | collective-permute-start | bytes 294920 | tf_op jit(solution)/shard_map/ppermute | solution.py:12
  95.3 2.6 %collective-permute-done.19 = bf16[1,2,16,3072]{3,2,1,0:T(8,128)(2,1)S(1)} collective-permute-done((bf16[1,2,16,3072]{3,2,1,0:T(8,128)(2,1)S(1)}, bf16[1,2,16,3072]{3,2,1,0:T(8,128)(2,1)S(1)}, u32[]{:S(2)}, u32[]{:S(2)}) %collective-permute-start.19) | collective-permute-done | bytes 196640 | tf_op jit(solution)/shard_map/ppermute | solution.py:121
  98.0 1.7 %collective-permute-start.20 = (bf16[16,3072]{1,0:T(8,128)(2,1)S(1)}, bf16[16,3072]{1,0:T(8,128)(2,1)S(1)}, u32[]{:S(2)}, u32[]{:S(2)}) collective-permute-start(bf16[16,3072]{1,0:T(8,128)(2,1)S(1)} %get-tuple-element.27), channel_id=1, source_target_pairs={{0,16},{16,0},{1,17},{17,1},{2,18},{18,2},{3,19},{19,3},{4,20},{20... | collective-permute-start | bytes 294920 | tf_op jit(solution)/shard_map/ppermute | solution.py:12
  99.7 1.5 %collective-permute-start.21 = (bf16[16,3072]{1,0:T(8,128)(2,1)S(1)}, bf16[16,3072]{1,0:T(8,128)(2,1)S(1)}, u32[]{:S(2)}, u32[]{:S(2)}) collective-permute-start(bf16[16,3072]{1,0:T(8,128)(2,1)S(1)} %get-tuple-element.26), channel_id=1, source_target_pairs={{0,24},{8,16},{16,8},{24,0},{1,25},{9,17},{17,9},{25,1},{2,26},{10... | collective-permute-start | bytes 294920 | tf_op jit(solution)/shard_map/ppermute | solution.py:134
  101.2 2.3 %collective-permute-start.22 = (bf16[16,3072]{1,0:T(8,128)(2,1)S(1)}, bf16[16,3072]{1,0:T(8,128)(2,1)S(1)}, u32[]{:S(2)}, u32[]{:S(2)}) collective-permute-start(bf16[16,3072]{1,0:T(8,128)(2,1)S(1)} %get-tuple-element.28), channel_id=1, source_target_pairs={{0,24},{8,16},{16,8},{24,0},{1,25},{9,17},{17,9},{25,1},{2,26},{10... | collective-permute-start | bytes 294920 | tf_op jit(solution)/shard_map/ppermute | solution.py:134
  103.5 0.5 collective-permute-done.20
  104.0 3.0 %collective-permute-done.21 = bf16[16,3072]{1,0:T(8,128)(2,1)S(1)} collective-permute-done((bf16[16,3072]{1,0:T(8,128)(2,1)S(1)}, bf16[16,3072]{1,0:T(8,128)(2,1)S(1)}, u32[]{:S(2)}, u32[]{:S(2)}) %collective-permute-start.21) | collective-permute-done | bytes 98336 | tf_op jit(solution)/shard_map/ppermute | solution.py:134
  107.0 1.1 collective-permute-done.22
  108.1 2.7 %fusion.10 = bf16[1,128,6144]{2,1,0:T(8,128)(2,1)} fusion(f32[2,16,128]{2,1,0:T(8,128)S(1)} %collective-permute-done.12, bf16[64,6144]{1,0:T(8,128)(2,1)S(1)} %collective-permute-done.11, bf16[64,6144]{1,0:T(8,128)(2,1)S(1)} %collective-permute-done, bf16[1,16,6144]{2,1,0:T(8,128)(2,1)S(1)} %maximum_bitcast_fusion.3, ...), kind=kOutput, calls=%fused_computation.12 | convolution fusion | flops 306905088 | bytes 3555328 | tf_op jit(solution)/shard_map/ect,ecd->td/dot_general | solution.py:138
  (41 shorter events, 0.6 us)
Async XLA Ops:
  0.0 9.7 %copy-start = (bf16[1,128,6144]{2,1,0:T(8,128)(2,1)S(1)}, bf16[1,128,6144]{2,1,0:T(8,128)(2,1)}, u32[]{:S(2)}) copy-start(bf16[1,128,6144]{2,1,0:T(8,128)(2,1)} %param.8) | copy-start | bytes 4718596
  0.0 7.4 %copy-start.1 = (bf16[1,6144]{1,0:T(2,128)(2,1)S(1)}, bf16[1,6144]{1,0:T(2,128)(2,1)}, u32[]{:S(2)}) copy-start(bf16[1,6144]{1,0:T(2,128)(2,1)} %param.9) | copy-start | bytes 36868
  3.3 12.1 %collective-permute-start.6 = (bf16[8,6144]{1,0:T(8,128)(2,1)}, bf16[8,6144]{1,0:T(8,128)(2,1)S(1)}, u32[]{:S(2)}, u32[]{:S(2)}) collective-permute-start(bf16[8,6144]{1,0:T(8,128)(2,1)} %get-tuple-element.24), channel_id=1, source_target_pairs={{0,8},{8,0},{1,9},{9,1},{2,10},{10,2},{3,11},{11,3},{4,12},{12,4},... | collective-permute-start | bytes 294920 | tf_op jit(solution)/shard_map/ppermute | solution.py:12
  7.4 9.3 %collective-permute-start.3 = (bf16[8,6144]{1,0:T(8,128)(2,1)S(1)}, bf16[8,6144]{1,0:T(8,128)(2,1)S(1)}, u32[]{:S(2)}, u32[]{:S(2)}) collective-permute-start(bf16[8,6144]{1,0:T(8,128)(2,1)S(1)} %get-tuple-element.23), channel_id=1, source_target_pairs={{0,8},{8,0},{1,9},{9,1},{2,10},{10,2},{3,11},{11,3},{4,12},{12,4},... | collective-permute-start | bytes 294920 | tf_op jit(solution)/shard_map/ppermute | solution.py:12
  7.8 4.4 %copy-start.3 = (f32[1,1,2,16]{3,2,1,0:T(2,128)S(1)}, f32[1,1,2,16]{3,2,1,0:T(2,128)}, u32[]{:S(2)}) copy-start(f32[1,1,2,16]{3,2,1,0:T(2,128)} %param.15) | copy-start | bytes 388
  7.8 4.4 %copy-start.4 = (s32[1,1,2]{2,1,0:T(1,128)S(1)}, s32[1,1,2]{2,1,0:T(1,128)}, u32[]{:S(2)}) copy-start(s32[1,1,2]{2,1,0:T(1,128)} %param.14) | copy-start | bytes 28
  7.8 4.5 %copy-start.2 = (s32[1,1,2,16]{3,2,1,0:T(2,128)S(1)}, s32[1,1,2,16]{3,2,1,0:T(2,128)}, u32[]{:S(2)}) copy-start(s32[1,1,2,16]{3,2,1,0:T(2,128)} %param.13) | copy-start | bytes 388
  7.8 16.3 %collective-permute-start.1 = (bf16[1,16,6144]{2,1,0:T(8,128)(2,1)S(1)}, bf16[1,16,6144]{2,1,0:T(8,128)(2,1)S(1)}, u32[]{:S(2)}, u32[]{:S(2)}) collective-permute-start(bf16[1,16,6144]{2,1,0:T(8,128)(2,1)S(1)} %fusion.26), channel_id=1, source_target_pairs={{0,2},{1,5},{2,0},{3,7},{4,6},{5,1},{6,4},{7,3},{8,10},{9,13},{10,... | collective-permute-start | bytes 589832 | tf_op jit(solution)/shard_map/ppermute | solution.py:76
  10.7 26.1 %collective-permute-start = (bf16[64,6144]{1,0:T(8,128)(2,1)}, bf16[64,6144]{1,0:T(8,128)(2,1)S(1)}, u32[]{:S(2)}, u32[]{:S(2)}) collective-permute-start(bf16[64,6144]{1,0:T(8,128)(2,1)} %get-tuple-element.19), channel_id=1, source_target_pairs={{0,16},{16,0},{1,17},{17,1},{2,18},{18,2},{3,19},{19,3},{4,20},{20... | collective-permute-start | bytes 2359304 | tf_op jit(solution)/shard_map/ppermute | solution.py:12
  17.0 4.7 %collective-permute-start.4 = (bf16[1,8,6144]{2,1,0:T(8,128)(2,1)S(1)}, bf16[1,8,6144]{2,1,0:T(8,128)(2,1)S(1)}, u32[]{:S(2)}, u32[]{:S(2)}) collective-permute-start(bf16[1,8,6144]{2,1,0:T(8,128)(2,1)S(1)} %get-tuple-element.29), channel_id=1, source_target_pairs={{0,2},{1,5},{2,0},{3,7},{4,6},{5,1},{6,4},{7,3},{8,10},{9,13},{10,... | collective-permute-start | bytes 294920 | tf_op jit(solution)/shard_map/ppermute | solution.py:76
  18.6 5.3 %collective-permute-start.7 = (bf16[1,8,6144]{2,1,0:T(8,128)(2,1)S(1)}, bf16[1,8,6144]{2,1,0:T(8,128)(2,1)S(1)}, u32[]{:S(2)}, u32[]{:S(2)}) collective-permute-start(bf16[1,8,6144]{2,1,0:T(8,128)(2,1)S(1)} %get-tuple-element.30), channel_id=1, source_target_pairs={{0,2},{1,5},{2,0},{3,7},{4,6},{5,1},{6,4},{7,3},{8,10},{9,13},{10,... | collective-permute-start | bytes 294920 | tf_op jit(solution)/shard_map/ppermute | solution.py:76
  21.7 5.7 %collective-permute-start.5 = (bf16[2,8,6144]{2,1,0:T(8,128)(2,1)S(1)}, bf16[2,8,6144]{2,1,0:T(8,128)(2,1)S(1)}, u32[]{:S(2)}, u32[]{:S(2)}) collective-permute-start(bf16[2,8,6144]{2,1,0:T(8,128)(2,1)S(1)} %pad_maximum_fusion.3), channel_id=1, source_target_pairs={{0,4},{1,3},{2,6},{3,1},{4,0},{5,7},{6,2},{7,5},{8,12},{9,11},{10,... | collective-permute-start | bytes 589832 | tf_op jit(solution)/shard_map/ppermute | solution.py:76
  24.0 5.7 %collective-permute-start.8 = (bf16[2,8,6144]{2,1,0:T(8,128)(2,1)S(1)}, bf16[2,8,6144]{2,1,0:T(8,128)(2,1)S(1)}, u32[]{:S(2)}, u32[]{:S(2)}) collective-permute-start(bf16[2,8,6144]{2,1,0:T(8,128)(2,1)S(1)} %pad_maximum_fusion.4), channel_id=1, source_target_pairs={{0,4},{1,3},{2,6},{3,1},{4,0},{5,7},{6,2},{7,5},{8,12},{9,11},{10,... | collective-permute-start | bytes 589832 | tf_op jit(solution)/shard_map/ppermute | solution.py:76
  24.1 9.8 %collective-permute-start.2 = (bf16[2,16,6144]{2,1,0:T(8,128)(2,1)S(1)}, bf16[2,16,6144]{2,1,0:T(8,128)(2,1)S(1)}, u32[]{:S(2)}, u32[]{:S(2)}) collective-permute-start(bf16[2,16,6144]{2,1,0:T(8,128)(2,1)S(1)} %pad_maximum_fusion.2), channel_id=1, source_target_pairs={{0,4},{1,3},{2,6},{3,1},{4,0},{5,7},{6,2},{7,5},{8,12},{9,11},{10,... | collective-permute-start | bytes 1179656 | tf_op jit(solution)/shard_map/ppermute | solution.py:76
  29.8 6.5 %collective-permute-start.10 = (bf16[4,16,6144]{2,1,0:T(8,128)(2,1)S(1)}, bf16[4,16,6144]{2,1,0:T(8,128)(2,1)S(1)}, u32[]{:S(2)}, u32[]{:S(2)}) collective-permute-start(bf16[4,16,6144]{2,1,0:T(8,128)(2,1)S(1)} %maximum_maximum_fusion), channel_id=1, source_target_pairs={{0,1},{1,0},{2,3},{3,2},{4,5},{5,4},{6,7},{7,6},{8,9},{9,8},{10,11... | collective-permute-start | bytes 2359304 | tf_op jit(solution)/shard_map/ppermute | solution.py:12
  34.0 2.4 %collective-permute-start.9 = (bf16[4,16,6144]{2,1,0:T(8,128)(2,1)S(1)}, bf16[4,16,6144]{2,1,0:T(8,128)(2,1)S(1)}, u32[]{:S(2)}, u32[]{:S(2)}) collective-permute-start(bf16[4,16,6144]{2,1,0:T(8,128)(2,1)S(1)} %get-tuple-element.22), channel_id=1, source_target_pairs={{0,1},{1,0},{2,3},{3,2},{4,5},{5,4},{6,7},{7,6},{8,9},{9,8},{10,11... | collective-permute-start | bytes 2359304 | tf_op jit(solution)/shard_map/ppermute | solution.py:12
  34.2 34.6 %collective-permute-start.12 = (f32[2,16,128]{2,1,0:T(8,128)S(1)}, f32[2,16,128]{2,1,0:T(8,128)S(1)}, u32[]{:S(2)}, u32[]{:S(2)}) collective-permute-start(f32[2,16,128]{2,1,0:T(8,128)S(1)} %broadcast_select_fusion), channel_id=1, source_target_pairs={{0,16},{16,0},{1,17},{17,1},{2,18},{18,2},{3,19},{19,3},{4,20},{20... | collective-permute-start | bytes 49160 | tf_op jit(solution)/shard_map/ppermute | solution.py:12
  35.8 33.0 %collective-permute-start.11 = (bf16[64,6144]{1,0:T(8,128)(2,1)S(1)}, bf16[64,6144]{1,0:T(8,128)(2,1)S(1)}, u32[]{:S(2)}, u32[]{:S(2)}) collective-permute-start(bf16[64,6144]{1,0:T(8,128)(2,1)S(1)} %get-tuple-element.20), channel_id=1, source_target_pairs={{0,16},{16,0},{1,17},{17,1},{2,18},{18,2},{3,19},{19,3},{4,20},{20... | collective-permute-start | bytes 2359304 | tf_op jit(solution)/shard_map/ppermute | solution.py:12
  68.9 8.7 %collective-permute-start.13 = (bf16[4,2,16,3072]{3,2,1,0:T(8,128)(2,1)S(1)}, bf16[4,2,16,3072]{3,2,1,0:T(8,128)(2,1)S(1)}, u32[]{:S(2)}, u32[]{:S(2)}) collective-permute-start(bf16[4,2,16,3072]{3,2,1,0:T(8,128)(2,1)S(1)} %bitcast.92), channel_id=1, source_target_pairs={{0,1},{1,0},{2,3},{3,2},{4,5},{5,4},{6,7},{7,6},{8,9},{9,8},{10,11... | collective-permute-start | bytes 2359304 | tf_op jit(solution)/shard_map/ppermute | solution.py:12
  77.2 2.4 %collective-permute-start.17 = (bf16[4,2,16,3072]{3,2,1,0:T(8,128)(2,1)S(1)}, bf16[4,2,16,3072]{3,2,1,0:T(8,128)(2,1)S(1)}, u32[]{:S(2)}, u32[]{:S(2)}) collective-permute-start(bf16[4,2,16,3072]{3,2,1,0:T(8,128)(2,1)S(1)} %bitcast.91), channel_id=1, source_target_pairs={{0,1},{1,0},{2,3},{3,2},{4,5},{5,4},{6,7},{7,6},{8,9},{9,8},{10,11... | collective-permute-start | bytes 2359304 | tf_op jit(solution)/shard_map/ppermute | solution.py:12
  77.9 7.8 %collective-permute-start.14 = (bf16[2,2,16,3072]{3,2,1,0:T(8,128)(2,1)S(1)}, bf16[2,2,16,3072]{3,2,1,0:T(8,128)(2,1)S(1)}, u32[]{:S(2)}, u32[]{:S(2)}) collective-permute-start(bf16[2,2,16,3072]{3,2,1,0:T(8,128)(2,1)S(1)} %slice.165), channel_id=1, source_target_pairs={{0,4},{1,3},{2,6},{3,1},{4,0},{5,7},{6,2},{7,5},{8,12},{9,11},{10,... | collective-permute-start | bytes 1179656 | tf_op jit(solution)/shard_map/ppermute | solution.py:121
  79.8 12.2 %collective-permute-start.18 = (bf16[2,2,16,3072]{3,2,1,0:T(8,128)(2,1)S(1)}, bf16[2,2,16,3072]{3,2,1,0:T(8,128)(2,1)S(1)}, u32[]{:S(2)}, u32[]{:S(2)}) collective-permute-start(bf16[2,2,16,3072]{3,2,1,0:T(8,128)(2,1)S(1)} %slice.164), channel_id=1, source_target_pairs={{0,4},{1,3},{2,6},{3,1},{4,0},{5,7},{6,2},{7,5},{8,12},{9,11},{10,... | collective-permute-start | bytes 1179656 | tf_op jit(solution)/shard_map/ppermute | solution.py:121
  85.9 7.8 %collective-permute-start.15 = (bf16[1,2,16,3072]{3,2,1,0:T(8,128)(2,1)S(1)}, bf16[1,2,16,3072]{3,2,1,0:T(8,128)(2,1)S(1)}, u32[]{:S(2)}, u32[]{:S(2)}) collective-permute-start(bf16[1,2,16,3072]{3,2,1,0:T(8,128)(2,1)S(1)} %slice.167), channel_id=1, source_target_pairs={{0,2},{1,5},{2,0},{3,7},{4,6},{5,1},{6,4},{7,3},{8,10},{9,13},{10,... | collective-permute-start | bytes 589832 | tf_op jit(solution)/shard_map/ppermute | solution.py:121
  92.2 5.7 %collective-permute-start.19 = (bf16[1,2,16,3072]{3,2,1,0:T(8,128)(2,1)S(1)}, bf16[1,2,16,3072]{3,2,1,0:T(8,128)(2,1)S(1)}, u32[]{:S(2)}, u32[]{:S(2)}) collective-permute-start(bf16[1,2,16,3072]{3,2,1,0:T(8,128)(2,1)S(1)} %slice.166), channel_id=1, source_target_pairs={{0,2},{1,5},{2,0},{3,7},{4,6},{5,1},{6,4},{7,3},{8,10},{9,13},{10,... | collective-permute-start | bytes 589832 | tf_op jit(solution)/shard_map/ppermute | solution.py:121
  93.7 9.8 %collective-permute-start.16 = (bf16[16,3072]{1,0:T(8,128)(2,1)S(1)}, bf16[16,3072]{1,0:T(8,128)(2,1)S(1)}, u32[]{:S(2)}, u32[]{:S(2)}) collective-permute-start(bf16[16,3072]{1,0:T(8,128)(2,1)S(1)} %get-tuple-element.25), channel_id=1, source_target_pairs={{0,16},{16,0},{1,17},{17,1},{2,18},{18,2},{3,19},{19,3},{4,20},{20... | collective-permute-start | bytes 294920 | tf_op jit(solution)/shard_map/ppermute | solution.py:12
  98.0 6.0 %collective-permute-start.20 = (bf16[16,3072]{1,0:T(8,128)(2,1)S(1)}, bf16[16,3072]{1,0:T(8,128)(2,1)S(1)}, u32[]{:S(2)}, u32[]{:S(2)}) collective-permute-start(bf16[16,3072]{1,0:T(8,128)(2,1)S(1)} %get-tuple-element.27), channel_id=1, source_target_pairs={{0,16},{16,0},{1,17},{17,1},{2,18},{18,2},{3,19},{19,3},{4,20},{20... | collective-permute-start | bytes 294920 | tf_op jit(solution)/shard_map/ppermute | solution.py:12
  99.7 7.3 %collective-permute-start.21 = (bf16[16,3072]{1,0:T(8,128)(2,1)S(1)}, bf16[16,3072]{1,0:T(8,128)(2,1)S(1)}, u32[]{:S(2)}, u32[]{:S(2)}) collective-permute-start(bf16[16,3072]{1,0:T(8,128)(2,1)S(1)} %get-tuple-element.26), channel_id=1, source_target_pairs={{0,24},{8,16},{16,8},{24,0},{1,25},{9,17},{17,9},{25,1},{2,26},{10... | collective-permute-start | bytes 294920 | tf_op jit(solution)/shard_map/ppermute | solution.py:134
  101.2 6.9 %collective-permute-start.22 = (bf16[16,3072]{1,0:T(8,128)(2,1)S(1)}, bf16[16,3072]{1,0:T(8,128)(2,1)S(1)}, u32[]{:S(2)}, u32[]{:S(2)}) collective-permute-start(bf16[16,3072]{1,0:T(8,128)(2,1)S(1)} %get-tuple-element.28), channel_id=1, source_target_pairs={{0,24},{8,16},{16,8},{24,0},{1,25},{9,17},{17,9},{25,1},{2,26},{10... | collective-permute-start | bytes 294920 | tf_op jit(solution)/shard_map/ppermute | solution.py:134

commit v8 on v7

--- a/solution.py
+++ b/solution.py
@@ -4,7 +4,7 @@
 from jax.sharding import Mesh, PartitionSpec as P
 
 SUM_DTYPE = jnp.bfloat16
-PIECES = 2
+PIECES = 1
 
 
 def shifted(block, axes, size, distance):

time: 111 us -> 114 us (1.027)
  waiting for transfers between devices: 33.5 us -> 45.2 us
  starting transfers between devices: 26.7 us -> 20.6 us
  matrix products: 44.5 us -> 40.7 us
  local copies, waits for them, and re-layouts: 3.49 us -> 4.7 us
    dot_general x1 -> x0, matrix products: 12.4 us -> none  [body(): up_part = jnp.dot(flat_rows, up_cols, preferred_element_type=jnp.float32)]
    dot_general x2 -> x1, matrix products: 16 us -> 22.1 us  [body(): jnp.dot(activated, cols, preferred_element_type=jnp.float32)]
    ppermute x4 -> x2, waiting for transfers between devices: 12.7 us -> 17.8 us  [body(): lax.ppermute(sent, ('chip', 'core'), chip_route(n_chip, n_core, stage, le...]
    ppermute x11 -> x9, waiting for transfers between devices: 5.19 us -> 9.17 us  [shifted(): return lax.ppermute(block, axes, route)]
    ppermute x2 -> x1, waiting for transfers between devices: 4.08 us -> 6.69 us  [body(): got[k].append(lax.ppermute(outgoing, ('section', 'ex'), route))]
    ppermute x4 -> x2, starting transfers between devices: 4.24 us -> 2.11 us  [body(): lax.ppermute(sent, ('chip', 'core'), chip_route(n_chip, n_core, stage, le...]
    ppermute x2 -> x1, starting transfers between devices: 3.82 us -> 1.78 us  [body(): got[k].append(lax.ppermute(outgoing, ('section', 'ex'), route))]
    ppermute x11 -> x9, starting transfers between devices: 11.6 us -> 9.73 us  [shifted(): return lax.ppermute(block, axes, route)]
  transfers between devices with their start and end apart: 23 -> 18, of which waited for: 15 -> 13; matrix products, arithmetic and copies ran while one was open for 40% -> 34% of each run, Pallas kernels for 0% -> 0%
where the time goes in v8:
time: 114 us
  waiting for transfers between devices  45.2 us (40%)
  matrix products  40.7 us (36%)
  starting transfers between devices  20.6 us (18%)
  local copies, waits for them, and re-layouts  4.7 us (4%)
  other arithmetic  2.33 us (2%)
    dot_general x1, matrix products, body(): jnp.dot(activated, cols, preferred_element_type=jnp.float32)  22.1 us
    ppermute x2, waiting for transfers between devices, body(): lax.ppermute(sent, ('chip', 'core'), chip_route(n_chip, n_core, stage, le...  17.8 us
    dot_general x1, matrix products, body(): jnp.dot(flat_rows, gate_cols, preferred_element_type=jnp.float32)  13 us
    ppermute x6, waiting for transfers between devices, doubled(): lax.ppermute(held, ('chip', 'core'), chip_route(n_chip, n_core, stage, le...  11.6 us
    ppermute x9, starting transfers between devices, shifted(): return lax.ppermute(block, axes, route)  9.73 us
    ppermute x9, waiting for transfers between devices, shifted(): return lax.ppermute(block, axes, route)  9.17 us
    ppermute x6, starting transfers between devices, doubled(): lax.ppermute(held, ('chip', 'core'), chip_route(n_chip, n_core, stage, le...  6.94 us
    ppermute x1, waiting for transfers between devices, body(): got[k].append(lax.ppermute(outgoing, ('section', 'ex'), route))  6.69 us
  transfers between devices with their start and end apart: 18, of which 13 were waited for; matrix products, arithmetic and copies ran while one was open for 34% of the time, Pallas kernels for 0%

profile of v8, /device:TPU:0, one launch (start us, length us, event | category | flops | bytes accessed | tf_op | source)
XLA Modules:
  0.0 113.7 jit_solution(6909663201563210852)
XLA Ops:
  0.0 0.9 eq.34
  0.9 1.8 %convolution_convert_fusion = bf16[32,6144]{1,0:T(8,128)(2,1)S(1)} fusion(bf16[1,128,6144]{2,1,0:T(8,128)(2,1)} %param.8, s32[32]{0:T(128)S(1)} %eq.34), kind=kOutput, calls=%fused_computation.12 | convolution fusion | flops 50532352 | bytes 1966208 | tf_op jit(solution)/shard_map/dot_general | solution.py:63
  2.7 0.0 copy-start.6
  2.7 0.0 copy-start.7
  2.7 0.0 copy-start.5
  2.8 4.1 %collective-permute-start.6 = (bf16[8,6144]{1,0:T(8,128)(2,1)S(1)}, bf16[8,6144]{1,0:T(8,128)(2,1)S(1)}, u32[]{:S(2)}, u32[]{:S(2)}) collective-permute-start(bf16[8,6144]{1,0:T(8,128)(2,1)S(1)} %get-tuple-element.24), channel_id=1, source_target_pairs={{0,8},{8,0},{1,9},{9,1},{2,10},{10,2},{3,11},{11,3},{4,12},{12,4},... | collective-permute-start | bytes 294920 | tf_op jit(solution)/shard_map/ppermute | solution.py:12
  6.9 0.1 collective-permute-start.3
  7.0 0.2 fusion.28
  7.1 0.1 fusion.30
  7.3 1.8 %collective-permute-start.1 = (bf16[1,16,6144]{2,1,0:T(8,128)(2,1)S(1)}, bf16[1,16,6144]{2,1,0:T(8,128)(2,1)S(1)}, u32[]{:S(2)}, u32[]{:S(2)}) collective-permute-start(bf16[1,16,6144]{2,1,0:T(8,128)(2,1)S(1)} %fusion.30), channel_id=1, source_target_pairs={{0,2},{1,5},{2,0},{3,7},{4,6},{5,1},{6,4},{7,3},{8,10},{9,13},{10,... | collective-permute-start | bytes 589832 | tf_op jit(solution)/shard_map/ppermute | solution.py:76
  9.1 1.0 slice_bitcast_fusion.1
  10.1 1.5 %collective-permute-start = (bf16[64,6144]{1,0:T(8,128)(2,1)S(1)}, bf16[64,6144]{1,0:T(8,128)(2,1)S(1)}, u32[]{:S(2)}, u32[]{:S(2)}) collective-permute-start(bf16[64,6144]{1,0:T(8,128)(2,1)S(1)} %get-tuple-element.17), channel_id=1, source_target_pairs={{0,16},{16,0},{1,17},{17,1},{2,18},{18,2},{3,19},{19,3},{4,20},{20... | collective-permute-start | bytes 2359304 | tf_op jit(solution)/shard_map/ppermute | solution.py:12
  11.7 0.1 compare_select_fusion.6
  11.7 0.1 fusion.42
  11.8 0.5 gather_fusion
  12.4 2.3 %collective-permute-done.6 = bf16[8,6144]{1,0:T(8,128)(2,1)S(1)} collective-permute-done((bf16[8,6144]{1,0:T(8,128)(2,1)S(1)}, bf16[8,6144]{1,0:T(8,128)(2,1)S(1)}, u32[]{:S(2)}, u32[]{:S(2)}) %collective-permute-start.6) | collective-permute-done | bytes 98336 | tf_op jit(solution)/shard_map/ppermute | solution.py:12
  14.7 0.2 fusion.37
  14.9 1.1 collective-permute-done.3
  16.0 0.2 fusion.34
  16.1 0.1 fusion.41
  16.3 1.6 %collective-permute-start.4 = (bf16[1,8,6144]{2,1,0:T(8,128)(2,1)S(1)}, bf16[1,8,6144]{2,1,0:T(8,128)(2,1)S(1)}, u32[]{:S(2)}, u32[]{:S(2)}) collective-permute-start(bf16[1,8,6144]{2,1,0:T(8,128)(2,1)S(1)} %get-tuple-element.25), channel_id=1, source_target_pairs={{0,2},{1,5},{2,0},{3,7},{4,6},{5,1},{6,4},{7,3},{8,10},{9,13},{10,... | collective-permute-start | bytes 294920 | tf_op jit(solution)/shard_map/ppermute | solution.py:76
  17.9 0.5 collective-permute-start.7
  18.4 2.5 %collective-permute-done.4 = bf16[1,8,6144]{2,1,0:T(8,128)(2,1)S(1)} collective-permute-done((bf16[1,8,6144]{2,1,0:T(8,128)(2,1)S(1)}, bf16[1,8,6144]{2,1,0:T(8,128)(2,1)S(1)}, u32[]{:S(2)}, u32[]{:S(2)}) %collective-permute-start.4) | collective-permute-done | bytes 98336 | tf_op jit(solution)/shard_map/ppermute | solution.py:76
  21.0 0.8 collective-permute-start.5
  21.8 1.4 %collective-permute-done.7 = bf16[1,8,6144]{2,1,0:T(8,128)(2,1)S(1)} collective-permute-done((bf16[1,8,6144]{2,1,0:T(8,128)(2,1)S(1)}, bf16[1,8,6144]{2,1,0:T(8,128)(2,1)S(1)}, u32[]{:S(2)}, u32[]{:S(2)}) %collective-permute-start.7) | collective-permute-done | bytes 98336 | tf_op jit(solution)/shard_map/ppermute | solution.py:76
  23.2 0.1 collective-permute-start.8
  23.4 0.0 collective-permute-done.1
  23.4 2.0 %collective-permute-start.2 = (bf16[2,16,6144]{2,1,0:T(8,128)(2,1)S(1)}, bf16[2,16,6144]{2,1,0:T(8,128)(2,1)S(1)}, u32[]{:S(2)}, u32[]{:S(2)}) collective-permute-start(bf16[2,16,6144]{2,1,0:T(8,128)(2,1)S(1)} %pad_maximum_fusion.2), channel_id=1, source_target_pairs={{0,4},{1,3},{2,6},{3,1},{4,0},{5,7},{6,2},{7,5},{8,12},{9,11},{10,... | collective-permute-start | bytes 1179656 | tf_op jit(solution)/shard_map/ppermute | solution.py:76
  25.4 1.3 %collective-permute-done.5 = bf16[2,8,6144]{2,1,0:T(8,128)(2,1)S(1)} collective-permute-done((bf16[2,8,6144]{2,1,0:T(8,128)(2,1)S(1)}, bf16[2,8,6144]{2,1,0:T(8,128)(2,1)S(1)}, u32[]{:S(2)}, u32[]{:S(2)}) %collective-permute-start.5) | collective-permute-done | bytes 196640 | tf_op jit(solution)/shard_map/ppermute | solution.py:76
  26.7 2.3 %collective-permute-done.8 = bf16[2,8,6144]{2,1,0:T(8,128)(2,1)S(1)} collective-permute-done((bf16[2,8,6144]{2,1,0:T(8,128)(2,1)S(1)}, bf16[2,8,6144]{2,1,0:T(8,128)(2,1)S(1)}, u32[]{:S(2)}, u32[]{:S(2)}) %collective-permute-start.8) | collective-permute-done | bytes 196640 | tf_op jit(solution)/shard_map/ppermute | solution.py:76
  29.0 0.1 maximum_maximum_fusion
  29.0 0.1 collective-permute-start.10
  29.1 4.1 %collective-permute-done.2 = bf16[2,16,6144]{2,1,0:T(8,128)(2,1)S(1)} collective-permute-done((bf16[2,16,6144]{2,1,0:T(8,128)(2,1)S(1)}, bf16[2,16,6144]{2,1,0:T(8,128)(2,1)S(1)}, u32[]{:S(2)}, u32[]{:S(2)}) %collective-permute-start.2) | collective-permute-done | bytes 393248 | tf_op jit(solution)/shard_map/ppermute | solution.py:76
  33.2 0.1 fusion.49
  33.3 0.1 collective-permute-start.9
  33.4 0.1 broadcast_select_fusion
  33.5 1.6 %collective-permute-start.12 = (f32[2,16,128]{2,1,0:T(8,128)S(1)}, f32[2,16,128]{2,1,0:T(8,128)S(1)}, u32[]{:S(2)}, u32[]{:S(2)}) collective-permute-start(f32[2,16,128]{2,1,0:T(8,128)S(1)} %broadcast_select_fusion), channel_id=1, source_target_pairs={{0,16},{16,0},{1,17},{17,1},{2,18},{18,2},{3,19},{19,3},{4,20},{20... | collective-permute-start | bytes 49160 | tf_op jit(solution)/shard_map/ppermute | solution.py:12
  35.1 0.4 collective-permute-start.11
  35.5 0.1 fusion.54
  35.5 0.0 collective-permute-done.10
  35.5 0.1 collective-permute-done.9
  35.6 0.1 maximum_bitcast_fusion.1
  35.8 0.2 pad_maximum_fusion
  36.0 1.6 %copy-done.1 = bf16[2,4,2,16,6144]{4,3,2,1,0:T(8,128)(2,1)} copy-done((bf16[2,4,2,16,6144]{4,3,2,1,0:T(8,128)(2,1)}, bf16[2,4,2,16,6144]{4,3,2,1,0:T(8,128)(2,1)S(1)}, u32[]{:S(2)}) %copy-start.1) | copy-done | bytes 3145752
  37.7 0.2 copy-done.2
  37.9 13.0 %fusion.4 = f32[256,2048]{1,0:T(8,128)} fusion(bf16[256,6144]{1,0:T(8,128)(2,1)S(1)} %bitcast.78, bf16[1,6144,2048]{2,1,0:T(8,128)(2,1)} %param.10), kind=kOutput, calls=%fused_computation.5 | convolution fusion | flops 6442450944 | bytes 30408704 | tf_op jit(solution)/shard_map/dot_general | solution.py:97
  50.9 22.1 %fusion.6 = bf16[256,6144]{1,0:T(8,128)(2,1)S(1)} fusion(bf16[1,2048,6144]{2,1,0:T(8,128)(2,1)} %param.12, bf16[256,6144]{1,0:T(8,128)(2,1)} %bitcast.79, bf16[1,6144,2048]{2,1,0:T(8,128)(2,1)} %param.11, f32[256,2048]{1,0:T(8,128)} %fusion.4), kind=kOutput, calls=%fused_computation.7 | convolution fusion | flops 12889620480 | bytes 58720256 | tf_op jit(solution)/shard_map/dot_general | solution.py:106
  73.0 0.0 collective-permute-done.12
  73.0 0.2 fusion.50
  73.2 0.2 collective-permute-start.13
  73.4 3.3 %collective-permute-done.13 = bf16[4,2,16,6144]{3,2,1,0:T(8,128)(2,1)S(1)} collective-permute-done((bf16[4,2,16,6144]{3,2,1,0:T(8,128)(2,1)S(1)}, bf16[4,2,16,6144]{3,2,1,0:T(8,128)(2,1)S(1)}, u32[]{:S(2)}, u32[]{:S(2)}) %collective-permute-start.13) | collective-permute-done | bytes 1572896 | tf_op jit(solution)/shard_map/ppermute | solution.py:12
  76.7 0.4 convert_add_fusion
  77.1 0.1 slice.90
  77.2 0.6 collective-permute-start.14
  77.8 11.4 %collective-permute-done.14 = bf16[2,2,16,6144]{3,2,1,0:T(8,128)(2,1)S(1)} collective-permute-done((bf16[2,2,16,6144]{3,2,1,0:T(8,128)(2,1)S(1)}, bf16[2,2,16,6144]{3,2,1,0:T(8,128)(2,1)S(1)}, u32[]{:S(2)}, u32[]{:S(2)}) %collective-permute-start.14) | collective-permute-done | bytes 786464 | tf_op jit(solution)/shard_map/ppermute | solution.py:121
  89.2 0.2 slice_add_fusion
  89.5 1.5 %collective-permute-start.15 = (bf16[1,2,16,6144]{3,2,1,0:T(8,128)(2,1)S(1)}, bf16[1,2,16,6144]{3,2,1,0:T(8,128)(2,1)S(1)}, u32[]{:S(2)}, u32[]{:S(2)}) collective-permute-start(bf16[1,2,16,6144]{3,2,1,0:T(8,128)(2,1)S(1)} %slice.91), channel_id=1, source_target_pairs={{0,2},{1,5},{2,0},{3,7},{4,6},{5,1},{6,4},{7,3},{8,10},{9,13},{10,... | collective-permute-start | bytes 1179656 | tf_op jit(solution)/shard_map/ppermute | solution.py:121
  90.9 6.4 %collective-permute-done.15 = bf16[1,2,16,6144]{3,2,1,0:T(8,128)(2,1)S(1)} collective-permute-done((bf16[1,2,16,6144]{3,2,1,0:T(8,128)(2,1)S(1)}, bf16[1,2,16,6144]{3,2,1,0:T(8,128)(2,1)S(1)}, u32[]{:S(2)}, u32[]{:S(2)}) %collective-permute-start.15) | collective-permute-done | bytes 393248 | tf_op jit(solution)/shard_map/ppermute | solution.py:121
  97.3 0.1 fusion.27
  97.4 1.7 %collective-permute-start.16 = (bf16[16,6144]{1,0:T(8,128)(2,1)S(1)}, bf16[16,6144]{1,0:T(8,128)(2,1)S(1)}, u32[]{:S(2)}, u32[]{:S(2)}) collective-permute-start(bf16[16,6144]{1,0:T(8,128)(2,1)S(1)} %get-tuple-element.21), channel_id=1, source_target_pairs={{0,16},{16,0},{1,17},{17,1},{2,18},{18,2},{3,19},{19,3},{4,20},{20... | collective-permute-start | bytes 589832 | tf_op jit(solution)/shard_map/ppermute | solution.py:12
  99.1 1.8 %collective-permute-start.17 = (bf16[16,6144]{1,0:T(8,128)(2,1)S(1)}, bf16[16,6144]{1,0:T(8,128)(2,1)S(1)}, u32[]{:S(2)}, u32[]{:S(2)}) collective-permute-start(bf16[16,6144]{1,0:T(8,128)(2,1)S(1)} %get-tuple-element.22), channel_id=1, source_target_pairs={{0,24},{8,16},{16,8},{24,0},{1,25},{9,17},{17,9},{25,1},{2,26},{10... | collective-permute-start | bytes 589832 | tf_op jit(solution)/shard_map/ppermute | solution.py:134
  100.9 2.4 %collective-permute-done.16 = bf16[16,6144]{1,0:T(8,128)(2,1)S(1)} collective-permute-done((bf16[16,6144]{1,0:T(8,128)(2,1)S(1)}, bf16[16,6144]{1,0:T(8,128)(2,1)S(1)}, u32[]{:S(2)}, u32[]{:S(2)}) %collective-permute-start.16) | collective-permute-done | bytes 196640 | tf_op jit(solution)/shard_map/ppermute | solution.py:12
  103.3 6.7 %collective-permute-done.17 = bf16[16,6144]{1,0:T(8,128)(2,1)S(1)} collective-permute-done((bf16[16,6144]{1,0:T(8,128)(2,1)S(1)}, bf16[16,6144]{1,0:T(8,128)(2,1)S(1)}, u32[]{:S(2)}, u32[]{:S(2)}) %collective-permute-start.17) | collective-permute-done | bytes 196640 | tf_op jit(solution)/shard_map/ppermute | solution.py:134
  109.9 3.8 %fusion.11 = bf16[1,128,6144]{2,1,0:T(8,128)(2,1)} fusion(f32[2,16,128]{2,1,0:T(8,128)S(1)} %collective-permute-done.12, bf16[64,6144]{1,0:T(8,128)(2,1)} %collective-permute-done.11, bf16[64,6144]{1,0:T(8,128)(2,1)S(1)} %copy-done.3, bf16[1,16,6144]{2,1,0:T(8,128)(2,1)S(1)} %bitcast.89, bf16[1,16,6144]{2,1,0:T(8,128)(2,1)S(1)} %bitcast.88), kind=kOutput, calls=%fused_computation.11 | convolution fusion | flops 306905088 | bytes 3555328 | tf_op jit(solution)/shard_map/ect,ecd->td/dot_general | solution.py:138
  (26 shorter events, 0.3 us)
Async XLA Ops:
  0.0 9.1 %copy-start = (bf16[1,128,6144]{2,1,0:T(8,128)(2,1)S(1)}, bf16[1,128,6144]{2,1,0:T(8,128)(2,1)}, u32[]{:S(2)}) copy-start(bf16[1,128,6144]{2,1,0:T(8,128)(2,1)} %param.8) | copy-start | bytes 4718596
  0.0 6.9 %copy-start.4 = (bf16[1,6144]{1,0:T(2,128)(2,1)S(1)}, bf16[1,6144]{1,0:T(2,128)(2,1)}, u32[]{:S(2)}) copy-start(bf16[1,6144]{1,0:T(2,128)(2,1)} %param.9) | copy-start | bytes 36868
  2.7 9.0 %copy-start.6 = (f32[1,1,2,16]{3,2,1,0:T(2,128)S(1)}, f32[1,1,2,16]{3,2,1,0:T(2,128)}, u32[]{:S(2)}) copy-start(f32[1,1,2,16]{3,2,1,0:T(2,128)} %param.15) | copy-start | bytes 388
  2.7 9.0 %copy-start.7 = (s32[1,1,2]{2,1,0:T(1,128)S(1)}, s32[1,1,2]{2,1,0:T(1,128)}, u32[]{:S(2)}) copy-start(s32[1,1,2]{2,1,0:T(1,128)} %param.14) | copy-start | bytes 28
  2.7 9.0 %copy-start.5 = (s32[1,1,2,16]{3,2,1,0:T(2,128)S(1)}, s32[1,1,2,16]{3,2,1,0:T(2,128)}, u32[]{:S(2)}) copy-start(s32[1,1,2,16]{3,2,1,0:T(2,128)} %param.13) | copy-start | bytes 388
  2.8 11.9 %collective-permute-start.6 = (bf16[8,6144]{1,0:T(8,128)(2,1)S(1)}, bf16[8,6144]{1,0:T(8,128)(2,1)S(1)}, u32[]{:S(2)}, u32[]{:S(2)}) collective-permute-start(bf16[8,6144]{1,0:T(8,128)(2,1)S(1)} %get-tuple-element.24), channel_id=1, source_target_pairs={{0,8},{8,0},{1,9},{9,1},{2,10},{10,2},{3,11},{11,3},{4,12},{12,4},... | collective-permute-start | bytes 294920 | tf_op jit(solution)/shard_map/ppermute | solution.py:12
  6.9 9.1 %collective-permute-start.3 = (bf16[8,6144]{1,0:T(8,128)(2,1)S(1)}, bf16[8,6144]{1,0:T(8,128)(2,1)S(1)}, u32[]{:S(2)}, u32[]{:S(2)}) collective-permute-start(bf16[8,6144]{1,0:T(8,128)(2,1)S(1)} %get-tuple-element.23), channel_id=1, source_target_pairs={{0,8},{8,0},{1,9},{9,1},{2,10},{10,2},{3,11},{11,3},{4,12},{12,4},... | collective-permute-start | bytes 294920 | tf_op jit(solution)/shard_map/ppermute | solution.py:12
  7.3 16.1 %collective-permute-start.1 = (bf16[1,16,6144]{2,1,0:T(8,128)(2,1)S(1)}, bf16[1,16,6144]{2,1,0:T(8,128)(2,1)S(1)}, u32[]{:S(2)}, u32[]{:S(2)}) collective-permute-start(bf16[1,16,6144]{2,1,0:T(8,128)(2,1)S(1)} %fusion.30), channel_id=1, source_target_pairs={{0,2},{1,5},{2,0},{3,7},{4,6},{5,1},{6,4},{7,3},{8,10},{9,13},{10,... | collective-permute-start | bytes 589832 | tf_op jit(solution)/shard_map/ppermute | solution.py:76
  10.1 25.9 %collective-permute-start = (bf16[64,6144]{1,0:T(8,128)(2,1)S(1)}, bf16[64,6144]{1,0:T(8,128)(2,1)S(1)}, u32[]{:S(2)}, u32[]{:S(2)}) collective-permute-start(bf16[64,6144]{1,0:T(8,128)(2,1)S(1)} %get-tuple-element.17), channel_id=1, source_target_pairs={{0,16},{16,0},{1,17},{17,1},{2,18},{18,2},{3,19},{19,3},{4,20},{20... | collective-permute-start | bytes 2359304 | tf_op jit(solution)/shard_map/ppermute | solution.py:12
  16.3 4.7 %collective-permute-start.4 = (bf16[1,8,6144]{2,1,0:T(8,128)(2,1)S(1)}, bf16[1,8,6144]{2,1,0:T(8,128)(2,1)S(1)}, u32[]{:S(2)}, u32[]{:S(2)}) collective-permute-start(bf16[1,8,6144]{2,1,0:T(8,128)(2,1)S(1)} %get-tuple-element.25), channel_id=1, source_target_pairs={{0,2},{1,5},{2,0},{3,7},{4,6},{5,1},{6,4},{7,3},{8,10},{9,13},{10,... | collective-permute-start | bytes 294920 | tf_op jit(solution)/shard_map/ppermute | solution.py:76
  17.9 5.3 %collective-permute-start.7 = (bf16[1,8,6144]{2,1,0:T(8,128)(2,1)S(1)}, bf16[1,8,6144]{2,1,0:T(8,128)(2,1)S(1)}, u32[]{:S(2)}, u32[]{:S(2)}) collective-permute-start(bf16[1,8,6144]{2,1,0:T(8,128)(2,1)S(1)} %get-tuple-element.26), channel_id=1, source_target_pairs={{0,2},{1,5},{2,0},{3,7},{4,6},{5,1},{6,4},{7,3},{8,10},{9,13},{10,... | collective-permute-start | bytes 294920 | tf_op jit(solution)/shard_map/ppermute | solution.py:76
  21.0 5.7 %collective-permute-start.5 = (bf16[2,8,6144]{2,1,0:T(8,128)(2,1)S(1)}, bf16[2,8,6144]{2,1,0:T(8,128)(2,1)S(1)}, u32[]{:S(2)}, u32[]{:S(2)}) collective-permute-start(bf16[2,8,6144]{2,1,0:T(8,128)(2,1)S(1)} %pad_maximum_fusion.3), channel_id=1, source_target_pairs={{0,4},{1,3},{2,6},{3,1},{4,0},{5,7},{6,2},{7,5},{8,12},{9,11},{10,... | collective-permute-start | bytes 589832 | tf_op jit(solution)/shard_map/ppermute | solution.py:76
  23.2 5.7 %collective-permute-start.8 = (bf16[2,8,6144]{2,1,0:T(8,128)(2,1)S(1)}, bf16[2,8,6144]{2,1,0:T(8,128)(2,1)S(1)}, u32[]{:S(2)}, u32[]{:S(2)}) collective-permute-start(bf16[2,8,6144]{2,1,0:T(8,128)(2,1)S(1)} %pad_maximum_fusion.4), channel_id=1, source_target_pairs={{0,4},{1,3},{2,6},{3,1},{4,0},{5,7},{6,2},{7,5},{8,12},{9,11},{10,... | collective-permute-start | bytes 589832 | tf_op jit(solution)/shard_map/ppermute | solution.py:76
  23.4 9.8 %collective-permute-start.2 = (bf16[2,16,6144]{2,1,0:T(8,128)(2,1)S(1)}, bf16[2,16,6144]{2,1,0:T(8,128)(2,1)S(1)}, u32[]{:S(2)}, u32[]{:S(2)}) collective-permute-start(bf16[2,16,6144]{2,1,0:T(8,128)(2,1)S(1)} %pad_maximum_fusion.2), channel_id=1, source_target_pairs={{0,4},{1,3},{2,6},{3,1},{4,0},{5,7},{6,2},{7,5},{8,12},{9,11},{10,... | collective-permute-start | bytes 1179656 | tf_op jit(solution)/shard_map/ppermute | solution.py:76
  29.0 6.5 %collective-permute-start.10 = (bf16[4,16,6144]{2,1,0:T(8,128)(2,1)S(1)}, bf16[4,16,6144]{2,1,0:T(8,128)(2,1)S(1)}, u32[]{:S(2)}, u32[]{:S(2)}) collective-permute-start(bf16[4,16,6144]{2,1,0:T(8,128)(2,1)S(1)} %maximum_maximum_fusion), channel_id=1, source_target_pairs={{0,1},{1,0},{2,3},{3,2},{4,5},{5,4},{6,7},{7,6},{8,9},{9,8},{10,11... | collective-permute-start | bytes 2359304 | tf_op jit(solution)/shard_map/ppermute | solution.py:12
  33.3 2.4 %collective-permute-start.9 = (bf16[4,16,6144]{2,1,0:T(8,128)(2,1)S(1)}, bf16[4,16,6144]{2,1,0:T(8,128)(2,1)S(1)}, u32[]{:S(2)}, u32[]{:S(2)}) collective-permute-start(bf16[4,16,6144]{2,1,0:T(8,128)(2,1)S(1)} %get-tuple-element.20), channel_id=1, source_target_pairs={{0,1},{1,0},{2,3},{3,2},{4,5},{5,4},{6,7},{7,6},{8,9},{9,8},{10,11... | collective-permute-start | bytes 2359304 | tf_op jit(solution)/shard_map/ppermute | solution.py:12
  33.5 39.5 %collective-permute-start.12 = (f32[2,16,128]{2,1,0:T(8,128)S(1)}, f32[2,16,128]{2,1,0:T(8,128)S(1)}, u32[]{:S(2)}, u32[]{:S(2)}) collective-permute-start(f32[2,16,128]{2,1,0:T(8,128)S(1)} %broadcast_select_fusion), channel_id=1, source_target_pairs={{0,16},{16,0},{1,17},{17,1},{2,18},{18,2},{3,19},{19,3},{4,20},{20... | collective-permute-start | bytes 49160 | tf_op jit(solution)/shard_map/ppermute | solution.py:12
  35.1 37.9 %collective-permute-start.11 = (bf16[64,6144]{1,0:T(8,128)(2,1)}, bf16[64,6144]{1,0:T(8,128)(2,1)}, u32[]{:S(2)}, u32[]{:S(2)}) collective-permute-start(bf16[64,6144]{1,0:T(8,128)(2,1)} %get-tuple-element.18), channel_id=1, source_target_pairs={{0,16},{16,0},{1,17},{17,1},{2,18},{18,2},{3,19},{19,3},{4,20},{20... | collective-permute-start | bytes 2359304 | tf_op jit(solution)/shard_map/ppermute | solution.py:12
  36.0 1.6 %copy-start.1 = (bf16[2,4,2,16,6144]{4,3,2,1,0:T(8,128)(2,1)}, bf16[2,4,2,16,6144]{4,3,2,1,0:T(8,128)(2,1)S(1)}, u32[]{:S(2)}) copy-start(bf16[2,4,2,16,6144]{4,3,2,1,0:T(8,128)(2,1)S(1)} %pad_maximum_fusion) | copy-start | bytes 9437188
  36.0 1.8 %copy-start.2 = (bf16[64,6144]{1,0:T(8,128)(2,1)}, bf16[64,6144]{1,0:T(8,128)(2,1)S(1)}, u32[]{:S(2)}) copy-start(bf16[64,6144]{1,0:T(8,128)(2,1)S(1)} %collective-permute-done) | copy-start | bytes 2359300
  73.2 3.5 %collective-permute-start.13 = (bf16[4,2,16,6144]{3,2,1,0:T(8,128)(2,1)S(1)}, bf16[4,2,16,6144]{3,2,1,0:T(8,128)(2,1)S(1)}, u32[]{:S(2)}, u32[]{:S(2)}) collective-permute-start(bf16[4,2,16,6144]{3,2,1,0:T(8,128)(2,1)S(1)} %bitcast.83), channel_id=1, source_target_pairs={{0,1},{1,0},{2,3},{3,2},{4,5},{5,4},{6,7},{7,6},{8,9},{9,8},{10,11... | collective-permute-start | bytes 4718600 | tf_op jit(solution)/shard_map/ppermute | solution.py:12
  77.2 12.1 %collective-permute-start.14 = (bf16[2,2,16,6144]{3,2,1,0:T(8,128)(2,1)S(1)}, bf16[2,2,16,6144]{3,2,1,0:T(8,128)(2,1)S(1)}, u32[]{:S(2)}, u32[]{:S(2)}) collective-permute-start(bf16[2,2,16,6144]{3,2,1,0:T(8,128)(2,1)S(1)} %slice.90), channel_id=1, source_target_pairs={{0,4},{1,3},{2,6},{3,1},{4,0},{5,7},{6,2},{7,5},{8,12},{9,11},{10,... | collective-permute-start | bytes 2359304 | tf_op jit(solution)/shard_map/ppermute | solution.py:121
  89.4 20.6 %copy-start.3 = (bf16[64,6144]{1,0:T(8,128)(2,1)S(1)}, bf16[64,6144]{1,0:T(8,128)(2,1)}, u32[]{:S(2)}) copy-start(bf16[64,6144]{1,0:T(8,128)(2,1)} %copy-done.2) | copy-start | bytes 2359300
  89.5 7.8 %collective-permute-start.15 = (bf16[1,2,16,6144]{3,2,1,0:T(8,128)(2,1)S(1)}, bf16[1,2,16,6144]{3,2,1,0:T(8,128)(2,1)S(1)}, u32[]{:S(2)}, u32[]{:S(2)}) collective-permute-start(bf16[1,2,16,6144]{3,2,1,0:T(8,128)(2,1)S(1)} %slice.91), channel_id=1, source_target_pairs={{0,2},{1,5},{2,0},{3,7},{4,6},{5,1},{6,4},{7,3},{8,10},{9,13},{10,... | collective-permute-start | bytes 1179656 | tf_op jit(solution)/shard_map/ppermute | solution.py:121
  97.4 5.8 %collective-permute-start.16 = (bf16[16,6144]{1,0:T(8,128)(2,1)S(1)}, bf16[16,6144]{1,0:T(8,128)(2,1)S(1)}, u32[]{:S(2)}, u32[]{:S(2)}) collective-permute-start(bf16[16,6144]{1,0:T(8,128)(2,1)S(1)} %get-tuple-element.21), channel_id=1, source_target_pairs={{0,16},{16,0},{1,17},{17,1},{2,18},{18,2},{3,19},{19,3},{4,20},{20... | collective-permute-start | bytes 589832 | tf_op jit(solution)/shard_map/ppermute | solution.py:12
  99.1 10.8 %collective-permute-start.17 = (bf16[16,6144]{1,0:T(8,128)(2,1)S(1)}, bf16[16,6144]{1,0:T(8,128)(2,1)S(1)}, u32[]{:S(2)}, u32[]{:S(2)}) collective-permute-start(bf16[16,6144]{1,0:T(8,128)(2,1)S(1)} %get-tuple-element.22), channel_id=1, source_target_pairs={{0,24},{8,16},{16,8},{24,0},{1,25},{9,17},{17,9},{25,1},{2,26},{10... | collective-permute-start | bytes 589832 | tf_op jit(solution)/shard_map/ppermute | solution.py:134

commit v9 on v7

--- a/solution.py
+++ b/solution.py
@@ -78,15 +78,18 @@
         return held
 
     splits = 2 if capacity % 2 == 0 else 1
-    chip_rows = [doubled(normalized(lax.dynamic_index_in_dim(raw, ex_me, 0, keepdims=False)))]
+    own_rows = doubled(normalized(lax.dynamic_index_in_dim(raw, ex_me, 0, keepdims=False)))
+    step = capacity // splits
+    landed = []
     for k in range(1, n_ex):
         outgoing = lax.dynamic_index_in_dim(raw, (ex_me + k) % n_ex, 0, keepdims=False)
-        step = capacity // splits
-        halves = []
-        for h in range(splits):
-            landed = shifted(outgoing[h * step:(h + 1) * step], "ex", n_ex, k)
-            halves.append(doubled(normalized(landed)))
-        chip_rows.append(jnp.concatenate(halves, axis=1))
+        landed.append(
+            [shifted(outgoing[h * step:(h + 1) * step], "ex", n_ex, k) for h in range(splits)]
+        )
+    own_rows, landed = lax.optimization_barrier((own_rows, landed))
+    chip_rows = [own_rows]
+    for halves in landed:
+        chip_rows.append(jnp.concatenate([doubled(normalized(h)) for h in halves], axis=1))
     core_rows = [chip_rows] + [
         [shifted(rows, "core", n_core, q) for rows in chip_rows] for q in range(1, n_core)
     ]

time: 111 us -> 112 us (level)
  starting transfers between devices: 26.7 us -> 32.5 us
  waiting for transfers between devices: 33.5 us -> 28 us
    ppermute x11, waiting for transfers between devices: 5.19 us -> 0.11 us  [shifted(): return lax.ppermute(block, axes, route)]
    ppermute x4, starting transfers between devices: 4.24 us -> 7.32 us  [body(): lax.ppermute(sent, ('chip', 'core'), chip_route(n_chip, n_core, stage, le...]
    ppermute x6, starting transfers between devices: 6.99 us -> 9.36 us  [doubled(): lax.ppermute(held, ('chip', 'core'), chip_route(n_chip, n_core, stage, le...]
    ppermute x4, waiting for transfers between devices: 12.7 us -> 10.5 us  [body(): lax.ppermute(sent, ('chip', 'core'), chip_route(n_chip, n_core, stage, le...]
    ppermute x2, waiting for transfers between devices: 4.08 us -> 5.32 us  [body(): got[k].append(lax.ppermute(outgoing, ('section', 'ex'), route))]
  transfers between devices with their start and end apart: 23 -> 23, of which waited for: 15 -> 11; matrix products, arithmetic and copies ran while one was open for 40% -> 41% of each run, Pallas kernels for 0% -> 0%
where the time goes in v9:
time: 112 us
  matrix products  44.5 us (40%)
  starting transfers between devices  32.5 us (29%)
  waiting for transfers between devices  28 us (25%)
  local copies, waits for them, and re-layouts  3.58 us (3%)
  other arithmetic  2.83 us (3%)
    dot_general x2, matrix products, body(): jnp.dot(activated, cols, preferred_element_type=jnp.float32)  16 us
    dot_general x1, matrix products, body(): up_part = jnp.dot(flat_rows, up_cols, preferred_element_type=jnp.float32)  12.4 us
    ppermute x6, waiting for transfers between devices, doubled(): lax.ppermute(held, ('chip', 'core'), chip_route(n_chip, n_core, stage, le...  12.1 us
    ppermute x11, starting transfers between devices, shifted(): return lax.ppermute(block, axes, route)  12 us
    dot_general x1, matrix products, body(): jnp.dot(flat_rows, gate_cols, preferred_element_type=jnp.float32)  11.7 us
    ppermute x4, waiting for transfers between devices, body(): lax.ppermute(sent, ('chip', 'core'), chip_route(n_chip, n_core, stage, le...  10.5 us
    ppermute x6, starting transfers between devices, doubled(): lax.ppermute(held, ('chip', 'core'), chip_route(n_chip, n_core, stage, le...  9.36 us
    ppermute x4, starting transfers between devices, body(): lax.ppermute(sent, ('chip', 'core'), chip_route(n_chip, n_core, stage, le...  7.32 us
  transfers between devices with their start and end apart: 23, of which 11 were waited for; matrix products, arithmetic and copies ran while one was open for 41% of the time, Pallas kernels for 0%

profile of v9, /device:TPU:0, one launch (start us, length us, event | category | flops | bytes accessed | tf_op | source)
XLA Modules:
  0.0 111.7 jit_solution(4067798624639895282)
XLA Ops:
  0.0 0.9 eq.34
  0.9 1.8 %convolution_convert_fusion = bf16[32,6144]{1,0:T(8,128)(2,1)S(1)} fusion(bf16[1,128,6144]{2,1,0:T(8,128)(2,1)} %param.8, s32[32]{0:T(128)S(1)} %eq.34), kind=kOutput, calls=%fused_computation.13 | convolution fusion | flops 50532352 | bytes 1966208 | tf_op jit(solution)/shard_map/dot_general | solution.py:63
  2.7 4.1 %collective-permute-start.3 = (bf16[8,6144]{1,0:T(8,128)(2,1)S(1)}, bf16[8,6144]{1,0:T(8,128)(2,1)S(1)}, u32[]{:S(2)}, u32[]{:S(2)}) collective-permute-start(bf16[8,6144]{1,0:T(8,128)(2,1)S(1)} %get-tuple-element.28), channel_id=1, source_target_pairs={{0,8},{8,0},{1,9},{9,1},{2,10},{10,2},{3,11},{11,3},{4,12},{12,4},... | collective-permute-start | bytes 294920 | tf_op jit(solution)/shard_map/ppermute | solution.py:12
  6.8 0.1 collective-permute-start.4
  6.9 0.2 fusion.24
  7.1 0.1 fusion.26
  7.2 0.0 copy-start.4
  7.3 0.0 copy-start.3
  7.3 1.8 %collective-permute-start.1 = (bf16[1,16,6144]{2,1,0:T(8,128)(2,1)S(1)}, bf16[1,16,6144]{2,1,0:T(8,128)(2,1)S(1)}, u32[]{:S(2)}, u32[]{:S(2)}) collective-permute-start(bf16[1,16,6144]{2,1,0:T(8,128)(2,1)S(1)} %fusion.26), channel_id=1, source_target_pairs={{0,2},{1,5},{2,0},{3,7},{4,6},{5,1},{6,4},{7,3},{8,10},{9,13},{10,... | collective-permute-start | bytes 589832 | tf_op jit(solution)/shard_map/ppermute | solution.py:76
  9.1 1.0 slice_bitcast_fusion.1
  10.1 1.5 %collective-permute-start = (bf16[64,6144]{1,0:T(8,128)(2,1)}, bf16[64,6144]{1,0:T(8,128)(2,1)S(1)}, u32[]{:S(2)}, u32[]{:S(2)}) collective-permute-start(bf16[64,6144]{1,0:T(8,128)(2,1)} %get-tuple-element.25), channel_id=1, source_target_pairs={{0,16},{16,0},{1,17},{17,1},{2,18},{18,2},{3,19},{19,3},{4,20},{20... | collective-permute-start | bytes 2359304 | tf_op jit(solution)/shard_map/ppermute | solution.py:12
  11.6 1.4 %collective-permute-done.1 = bf16[1,16,6144]{2,1,0:T(8,128)(2,1)S(1)} collective-permute-done((bf16[1,16,6144]{2,1,0:T(8,128)(2,1)S(1)}, bf16[1,16,6144]{2,1,0:T(8,128)(2,1)S(1)}, u32[]{:S(2)}, u32[]{:S(2)}) %collective-permute-start.1) | collective-permute-done | bytes 196640 | tf_op jit(solution)/shard_map/ppermute | solution.py:76
  13.0 1.9 %collective-permute-start.2 = (bf16[2,16,6144]{2,1,0:T(8,128)(2,1)S(1)}, bf16[2,16,6144]{2,1,0:T(8,128)(2,1)S(1)}, u32[]{:S(2)}, u32[]{:S(2)}) collective-permute-start(bf16[2,16,6144]{2,1,0:T(8,128)(2,1)S(1)} %pad_maximum_fusion.2), channel_id=1, source_target_pairs={{0,4},{1,3},{2,6},{3,1},{4,0},{5,7},{6,2},{7,5},{8,12},{9,11},{10,... | collective-permute-start | bytes 1179656 | tf_op jit(solution)/shard_map/ppermute | solution.py:76
  15.0 0.1 compare_select_fusion.6
  15.0 0.1 fusion.40
  15.1 5.8 %collective-permute-done.2 = bf16[2,16,6144]{2,1,0:T(8,128)(2,1)S(1)} collective-permute-done((bf16[2,16,6144]{2,1,0:T(8,128)(2,1)S(1)}, bf16[2,16,6144]{2,1,0:T(8,128)(2,1)S(1)}, u32[]{:S(2)}, u32[]{:S(2)}) %collective-permute-start.2) | collective-permute-done | bytes 393248 | tf_op jit(solution)/shard_map/ppermute | solution.py:76
  20.9 0.1 pad_maximum_fusion.1
  21.0 0.2 fusion.32
  21.2 0.1 fusion.39
  21.3 1.8 %collective-permute-start.5 = (bf16[1,8,6144]{2,1,0:T(8,128)(2,1)S(1)}, bf16[1,8,6144]{2,1,0:T(8,128)(2,1)S(1)}, u32[]{:S(2)}, u32[]{:S(2)}) collective-permute-start(bf16[1,8,6144]{2,1,0:T(8,128)(2,1)S(1)} %get-tuple-element.33), channel_id=1, source_target_pairs={{0,2},{1,5},{2,0},{3,7},{4,6},{5,1},{6,4},{7,3},{8,10},{9,13},{10,... | collective-permute-start | bytes 294920 | tf_op jit(solution)/shard_map/ppermute | solution.py:76
  23.2 0.3 collective-permute-start.7
  23.5 2.5 %collective-permute-done.5 = bf16[1,8,6144]{2,1,0:T(8,128)(2,1)S(1)} collective-permute-done((bf16[1,8,6144]{2,1,0:T(8,128)(2,1)S(1)}, bf16[1,8,6144]{2,1,0:T(8,128)(2,1)S(1)}, u32[]{:S(2)}, u32[]{:S(2)}) %collective-permute-start.5) | collective-permute-done | bytes 98336 | tf_op jit(solution)/shard_map/ppermute | solution.py:76
  26.0 1.9 %collective-permute-start.6 = (bf16[2,8,6144]{2,1,0:T(8,128)(2,1)S(1)}, bf16[2,8,6144]{2,1,0:T(8,128)(2,1)S(1)}, u32[]{:S(2)}, u32[]{:S(2)}) collective-permute-start(bf16[2,8,6144]{2,1,0:T(8,128)(2,1)S(1)} %pad_maximum_fusion.3), channel_id=1, source_target_pairs={{0,4},{1,3},{2,6},{3,1},{4,0},{5,7},{6,2},{7,5},{8,12},{9,11},{10,... | collective-permute-start | bytes 589832 | tf_op jit(solution)/shard_map/ppermute | solution.py:76
  28.0 1.6 %collective-permute-start.8 = (bf16[2,8,6144]{2,1,0:T(8,128)(2,1)S(1)}, bf16[2,8,6144]{2,1,0:T(8,128)(2,1)S(1)}, u32[]{:S(2)}, u32[]{:S(2)}) collective-permute-start(bf16[2,8,6144]{2,1,0:T(8,128)(2,1)S(1)} %pad_maximum_fusion.4), channel_id=1, source_target_pairs={{0,4},{1,3},{2,6},{3,1},{4,0},{5,7},{6,2},{7,5},{8,12},{9,11},{10,... | collective-permute-start | bytes 589832 | tf_op jit(solution)/shard_map/ppermute | solution.py:76
  29.5 0.6 pad_clamp_fusion
  30.1 1.3 %gather_fusion = f32[2,16,128]{2,1,0:T(8,128)} fusion(f32[2,16,128]{2,1,0:T(8,128)S(1)} %fusion.40, s32[1024]{0:T(1024)} %pad_clamp_fusion), kind=kCustom, calls=%fused_computation | custom fusion | bytes 32776 | tf_op jit(solution)/shard_map/jit(_take)/gather | solution.py:57
  31.4 0.1 collective-permute-start.9
  31.5 0.3 collective-permute-done.6
  31.8 2.1 %collective-permute-done.8 = bf16[2,8,6144]{2,1,0:T(8,128)(2,1)S(1)} collective-permute-done((bf16[2,8,6144]{2,1,0:T(8,128)(2,1)S(1)}, bf16[2,8,6144]{2,1,0:T(8,128)(2,1)S(1)}, u32[]{:S(2)}, u32[]{:S(2)}) %collective-permute-start.8) | collective-permute-done | bytes 196640 | tf_op jit(solution)/shard_map/ppermute | solution.py:76
  33.9 0.1 maximum_maximum_fusion
  33.9 0.1 collective-permute-start.10
  34.0 0.1 broadcast_select_fusion
  34.1 1.8 %collective-permute-start.12 = (f32[2,16,128]{2,1,0:T(8,128)S(1)}, f32[2,16,128]{2,1,0:T(8,128)S(1)}, u32[]{:S(2)}, u32[]{:S(2)}) collective-permute-start(f32[2,16,128]{2,1,0:T(8,128)S(1)} %broadcast_select_fusion), channel_id=1, source_target_pairs={{0,16},{16,0},{1,17},{17,1},{2,18},{18,2},{3,19},{19,3},{4,20},{20... | collective-permute-start | bytes 49160 | tf_op jit(solution)/shard_map/ppermute | solution.py:12
  35.9 0.3 collective-permute-start.11
  36.1 0.1 fusion.53
  36.2 0.1 collective-permute-done.10
  36.3 0.1 maximum_bitcast_fusion.1
  36.4 0.3 pad_maximum_fusion
  36.8 11.7 %fusion.2 = f32[256,2048]{1,0:T(8,128)S(1)} fusion(bf16[256,6144]{1,0:T(8,128)(2,1)S(1)} %bitcast.82, bf16[1,6144,2048]{2,1,0:T(8,128)(2,1)} %param.10), kind=kOutput, calls=%fused_computation.3 | convolution fusion | flops 6442450944 | bytes 30408704 | tf_op jit(solution)/shard_map/dot_general | solution.py:100
  48.4 12.4 %fusion.20 = bf16[256,2048]{1,0:T(8,128)(2,1)S(1)} fusion(bf16[256,6144]{1,0:T(8,128)(2,1)S(1)} %bitcast.83, bf16[1,6144,2048]{2,1,0:T(8,128)(2,1)} %param.11, f32[256,2048]{1,0:T(8,128)S(1)} %fusion.2), kind=kOutput, calls=%fused_computation.18 | convolution fusion | flops 6445596672 | bytes 31457280 | tf_op jit(solution)/shard_map/dot_general | solution.py:101
  60.8 8.0 %fusion.11 = bf16[256,3072]{1,0:T(8,128)(2,1)S(1)} fusion(bf16[256,2048]{1,0:T(8,128)(2,1)S(1)} %fusion.20, bf16[2048,6144]{1,0:T(8,128)(2,1)} %bitcast.97), kind=kOutput, calls=%fused_computation.14 | convolution fusion | flops 3222011904 | bytes 15204352 | tf_op jit(solution)/shard_map/dot_general | solution.py:109
  68.9 0.1 fusion.46
  69.0 0.2 collective-permute-start.13
  69.2 8.0 %fusion.14 = bf16[256,3072]{1,0:T(8,128)(2,1)S(1)} fusion(bf16[256,2048]{1,0:T(8,128)(2,1)S(1)} %fusion.20, bf16[2048,6144]{1,0:T(8,128)(2,1)} %bitcast.98), kind=kOutput, calls=%fused_computation.15 | convolution fusion | flops 3222011904 | bytes 15204352 | tf_op jit(solution)/shard_map/dot_general | solution.py:109
  77.2 0.1 fusion.47
  77.3 0.4 collective-permute-start.17
  77.7 0.2 convert_add_fusion.1
  78.0 1.9 %collective-permute-start.14 = (bf16[2,2,16,3072]{3,2,1,0:T(8,128)(2,1)S(1)}, bf16[2,2,16,3072]{3,2,1,0:T(8,128)(2,1)S(1)}, u32[]{:S(2)}, u32[]{:S(2)}) collective-permute-start(bf16[2,2,16,3072]{3,2,1,0:T(8,128)(2,1)S(1)} %slice.165), channel_id=1, source_target_pairs={{0,4},{1,3},{2,6},{3,1},{4,0},{5,7},{6,2},{7,5},{8,12},{9,11},{10,... | collective-permute-start | bytes 1179656 | tf_op jit(solution)/shard_map/ppermute | solution.py:124
  79.9 0.2 convert_add_fusion
  80.1 1.7 %collective-permute-start.18 = (bf16[2,2,16,3072]{3,2,1,0:T(8,128)(2,1)S(1)}, bf16[2,2,16,3072]{3,2,1,0:T(8,128)(2,1)S(1)}, u32[]{:S(2)}, u32[]{:S(2)}) collective-permute-start(bf16[2,2,16,3072]{3,2,1,0:T(8,128)(2,1)S(1)} %slice.164), channel_id=1, source_target_pairs={{0,4},{1,3},{2,6},{3,1},{4,0},{5,7},{6,2},{7,5},{8,12},{9,11},{10,... | collective-permute-start | bytes 1179656 | tf_op jit(solution)/shard_map/ppermute | solution.py:124
  81.8 4.0 %collective-permute-done.14 = bf16[2,2,16,3072]{3,2,1,0:T(8,128)(2,1)S(1)} collective-permute-done((bf16[2,2,16,3072]{3,2,1,0:T(8,128)(2,1)S(1)}, bf16[2,2,16,3072]{3,2,1,0:T(8,128)(2,1)S(1)}, u32[]{:S(2)}, u32[]{:S(2)}) %collective-permute-start.14) | collective-permute-done | bytes 393248 | tf_op jit(solution)/shard_map/ppermute | solution.py:124
  85.8 0.1 slice_add_fusion.1
  85.9 1.8 %collective-permute-start.15 = (bf16[1,2,16,3072]{3,2,1,0:T(8,128)(2,1)S(1)}, bf16[1,2,16,3072]{3,2,1,0:T(8,128)(2,1)S(1)}, u32[]{:S(2)}, u32[]{:S(2)}) collective-permute-start(bf16[1,2,16,3072]{3,2,1,0:T(8,128)(2,1)S(1)} %slice.167), channel_id=1, source_target_pairs={{0,2},{1,5},{2,0},{3,7},{4,6},{5,1},{6,4},{7,3},{8,10},{9,13},{10,... | collective-permute-start | bytes 589832 | tf_op jit(solution)/shard_map/ppermute | solution.py:124
  87.8 4.3 %collective-permute-done.18 = bf16[2,2,16,3072]{3,2,1,0:T(8,128)(2,1)S(1)} collective-permute-done((bf16[2,2,16,3072]{3,2,1,0:T(8,128)(2,1)S(1)}, bf16[2,2,16,3072]{3,2,1,0:T(8,128)(2,1)S(1)}, u32[]{:S(2)}, u32[]{:S(2)}) %collective-permute-start.18) | collective-permute-done | bytes 393248 | tf_op jit(solution)/shard_map/ppermute | solution.py:124
  92.1 0.1 slice_add_fusion
  92.2 1.9 %collective-permute-start.19 = (bf16[1,2,16,3072]{3,2,1,0:T(8,128)(2,1)S(1)}, bf16[1,2,16,3072]{3,2,1,0:T(8,128)(2,1)S(1)}, u32[]{:S(2)}, u32[]{:S(2)}) collective-permute-start(bf16[1,2,16,3072]{3,2,1,0:T(8,128)(2,1)S(1)} %slice.166), channel_id=1, source_target_pairs={{0,2},{1,5},{2,0},{3,7},{4,6},{5,1},{6,4},{7,3},{8,10},{9,13},{10,... | collective-permute-start | bytes 589832 | tf_op jit(solution)/shard_map/ppermute | solution.py:124
  94.2 1.6 %collective-permute-start.16 = (bf16[16,3072]{1,0:T(8,128)(2,1)S(1)}, bf16[16,3072]{1,0:T(8,128)(2,1)S(1)}, u32[]{:S(2)}, u32[]{:S(2)}) collective-permute-start(bf16[16,3072]{1,0:T(8,128)(2,1)S(1)} %get-tuple-element.29), channel_id=1, source_target_pairs={{0,16},{16,0},{1,17},{17,1},{2,18},{18,2},{3,19},{19,3},{4,20},{20... | collective-permute-start | bytes 294920 | tf_op jit(solution)/shard_map/ppermute | solution.py:12
  95.7 2.2 %collective-permute-done.19 = bf16[1,2,16,3072]{3,2,1,0:T(8,128)(2,1)S(1)} collective-permute-done((bf16[1,2,16,3072]{3,2,1,0:T(8,128)(2,1)S(1)}, bf16[1,2,16,3072]{3,2,1,0:T(8,128)(2,1)S(1)}, u32[]{:S(2)}, u32[]{:S(2)}) %collective-permute-start.19) | collective-permute-done | bytes 196640 | tf_op jit(solution)/shard_map/ppermute | solution.py:124
  98.0 1.9 %collective-permute-start.20 = (bf16[16,3072]{1,0:T(8,128)(2,1)S(1)}, bf16[16,3072]{1,0:T(8,128)(2,1)S(1)}, u32[]{:S(2)}, u32[]{:S(2)}) collective-permute-start(bf16[16,3072]{1,0:T(8,128)(2,1)S(1)} %get-tuple-element.31), channel_id=1, source_target_pairs={{0,16},{16,0},{1,17},{17,1},{2,18},{18,2},{3,19},{19,3},{4,20},{20... | collective-permute-start | bytes 294920 | tf_op jit(solution)/shard_map/ppermute | solution.py:12
  99.9 2.8 %collective-permute-start.21 = (bf16[16,3072]{1,0:T(8,128)(2,1)S(1)}, bf16[16,3072]{1,0:T(8,128)(2,1)S(1)}, u32[]{:S(2)}, u32[]{:S(2)}) collective-permute-start(bf16[16,3072]{1,0:T(8,128)(2,1)S(1)} %get-tuple-element.30), channel_id=1, source_target_pairs={{0,24},{8,16},{16,8},{24,0},{1,25},{9,17},{17,9},{25,1},{2,26},{10... | collective-permute-start | bytes 294920 | tf_op jit(solution)/shard_map/ppermute | solution.py:137
  102.6 1.1 collective-permute-start.22
  103.7 2.6 %collective-permute-done.21 = bf16[16,3072]{1,0:T(8,128)(2,1)S(1)} collective-permute-done((bf16[16,3072]{1,0:T(8,128)(2,1)S(1)}, bf16[16,3072]{1,0:T(8,128)(2,1)S(1)}, u32[]{:S(2)}, u32[]{:S(2)}) %collective-permute-start.21) | collective-permute-done | bytes 98336 | tf_op jit(solution)/shard_map/ppermute | solution.py:137
  106.3 2.7 %collective-permute-done.22 = bf16[16,3072]{1,0:T(8,128)(2,1)S(1)} collective-permute-done((bf16[16,3072]{1,0:T(8,128)(2,1)S(1)}, bf16[16,3072]{1,0:T(8,128)(2,1)S(1)}, u32[]{:S(2)}, u32[]{:S(2)}) %collective-permute-start.22) | collective-permute-done | bytes 98336 | tf_op jit(solution)/shard_map/ppermute | solution.py:137
  109.1 2.7 %fusion.10 = bf16[1,128,6144]{2,1,0:T(8,128)(2,1)} fusion(f32[2,16,128]{2,1,0:T(8,128)S(1)} %collective-permute-done.12, bf16[64,6144]{1,0:T(8,128)(2,1)S(1)} %collective-permute-done.11, bf16[64,6144]{1,0:T(8,128)(2,1)S(1)} %collective-permute-done, bf16[1,16,6144]{2,1,0:T(8,128)(2,1)S(1)} %maximum_bitcast_fusion.3, ...), kind=kOutput, calls=%fused_computation.12 | convolution fusion | flops 306905088 | bytes 3555328 | tf_op jit(solution)/shard_map/ect,ecd->td/dot_general | solution.py:141
  (42 shorter events, 0.5 us)
Async XLA Ops:
  0.0 9.1 %copy-start = (bf16[1,128,6144]{2,1,0:T(8,128)(2,1)S(1)}, bf16[1,128,6144]{2,1,0:T(8,128)(2,1)}, u32[]{:S(2)}) copy-start(bf16[1,128,6144]{2,1,0:T(8,128)(2,1)} %param.8) | copy-start | bytes 4718596
  0.0 7.1 %copy-start.2 = (bf16[1,6144]{1,0:T(2,128)(2,1)S(1)}, bf16[1,6144]{1,0:T(2,128)(2,1)}, u32[]{:S(2)}) copy-start(bf16[1,6144]{1,0:T(2,128)(2,1)} %param.9) | copy-start | bytes 36868
  2.7 18.3 %collective-permute-start.3 = (bf16[8,6144]{1,0:T(8,128)(2,1)S(1)}, bf16[8,6144]{1,0:T(8,128)(2,1)S(1)}, u32[]{:S(2)}, u32[]{:S(2)}) collective-permute-start(bf16[8,6144]{1,0:T(8,128)(2,1)S(1)} %get-tuple-element.28), channel_id=1, source_target_pairs={{0,8},{8,0},{1,9},{9,1},{2,10},{10,2},{3,11},{11,3},{4,12},{12,4},... | collective-permute-start | bytes 294920 | tf_op jit(solution)/shard_map/ppermute | solution.py:12
  6.8 14.2 %collective-permute-start.4 = (bf16[8,6144]{1,0:T(8,128)(2,1)S(1)}, bf16[8,6144]{1,0:T(8,128)(2,1)S(1)}, u32[]{:S(2)}, u32[]{:S(2)}) collective-permute-start(bf16[8,6144]{1,0:T(8,128)(2,1)S(1)} %get-tuple-element.27), channel_id=1, source_target_pairs={{0,8},{8,0},{1,9},{9,1},{2,10},{10,2},{3,11},{11,3},{4,12},{12,4},... | collective-permute-start | bytes 294920 | tf_op jit(solution)/shard_map/ppermute | solution.py:12
  7.2 7.7 %copy-start.4 = (f32[1,1,2,16]{3,2,1,0:T(2,128)S(1)}, f32[1,1,2,16]{3,2,1,0:T(2,128)}, u32[]{:S(2)}) copy-start(f32[1,1,2,16]{3,2,1,0:T(2,128)} %param.15) | copy-start | bytes 388
  7.2 7.7 %copy-start.5 = (s32[1,1,2]{2,1,0:T(1,128)S(1)}, s32[1,1,2]{2,1,0:T(1,128)}, u32[]{:S(2)}) copy-start(s32[1,1,2]{2,1,0:T(1,128)} %param.14) | copy-start | bytes 28
  7.3 7.8 %copy-start.3 = (s32[1,1,2,16]{3,2,1,0:T(2,128)S(1)}, s32[1,1,2,16]{3,2,1,0:T(2,128)}, u32[]{:S(2)}) copy-start(s32[1,1,2,16]{3,2,1,0:T(2,128)} %param.13) | copy-start | bytes 388
  7.3 5.7 %collective-permute-start.1 = (bf16[1,16,6144]{2,1,0:T(8,128)(2,1)S(1)}, bf16[1,16,6144]{2,1,0:T(8,128)(2,1)S(1)}, u32[]{:S(2)}, u32[]{:S(2)}) collective-permute-start(bf16[1,16,6144]{2,1,0:T(8,128)(2,1)S(1)} %fusion.26), channel_id=1, source_target_pairs={{0,2},{1,5},{2,0},{3,7},{4,6},{5,1},{6,4},{7,3},{8,10},{9,13},{10,... | collective-permute-start | bytes 589832 | tf_op jit(solution)/shard_map/ppermute | solution.py:76
  10.1 26.6 %collective-permute-start = (bf16[64,6144]{1,0:T(8,128)(2,1)}, bf16[64,6144]{1,0:T(8,128)(2,1)S(1)}, u32[]{:S(2)}, u32[]{:S(2)}) collective-permute-start(bf16[64,6144]{1,0:T(8,128)(2,1)} %get-tuple-element.25), channel_id=1, source_target_pairs={{0,16},{16,0},{1,17},{17,1},{2,18},{18,2},{3,19},{19,3},{4,20},{20... | collective-permute-start | bytes 2359304 | tf_op jit(solution)/shard_map/ppermute | solution.py:12
  13.0 7.8 %collective-permute-start.2 = (bf16[2,16,6144]{2,1,0:T(8,128)(2,1)S(1)}, bf16[2,16,6144]{2,1,0:T(8,128)(2,1)S(1)}, u32[]{:S(2)}, u32[]{:S(2)}) collective-permute-start(bf16[2,16,6144]{2,1,0:T(8,128)(2,1)S(1)} %pad_maximum_fusion.2), channel_id=1, source_target_pairs={{0,4},{1,3},{2,6},{3,1},{4,0},{5,7},{6,2},{7,5},{8,12},{9,11},{10,... | collective-permute-start | bytes 1179656 | tf_op jit(solution)/shard_map/ppermute | solution.py:76
  21.3 4.7 %collective-permute-start.5 = (bf16[1,8,6144]{2,1,0:T(8,128)(2,1)S(1)}, bf16[1,8,6144]{2,1,0:T(8,128)(2,1)S(1)}, u32[]{:S(2)}, u32[]{:S(2)}) collective-permute-start(bf16[1,8,6144]{2,1,0:T(8,128)(2,1)S(1)} %get-tuple-element.33), channel_id=1, source_target_pairs={{0,2},{1,5},{2,0},{3,7},{4,6},{5,1},{6,4},{7,3},{8,10},{9,13},{10,... | collective-permute-start | bytes 294920 | tf_op jit(solution)/shard_map/ppermute | solution.py:76
  23.2 4.8 %collective-permute-start.7 = (bf16[1,8,6144]{2,1,0:T(8,128)(2,1)S(1)}, bf16[1,8,6144]{2,1,0:T(8,128)(2,1)S(1)}, u32[]{:S(2)}, u32[]{:S(2)}) collective-permute-start(bf16[1,8,6144]{2,1,0:T(8,128)(2,1)S(1)} %get-tuple-element.34), channel_id=1, source_target_pairs={{0,2},{1,5},{2,0},{3,7},{4,6},{5,1},{6,4},{7,3},{8,10},{9,13},{10,... | collective-permute-start | bytes 294920 | tf_op jit(solution)/shard_map/ppermute | solution.py:76
  26.0 5.7 %collective-permute-start.6 = (bf16[2,8,6144]{2,1,0:T(8,128)(2,1)S(1)}, bf16[2,8,6144]{2,1,0:T(8,128)(2,1)S(1)}, u32[]{:S(2)}, u32[]{:S(2)}) collective-permute-start(bf16[2,8,6144]{2,1,0:T(8,128)(2,1)S(1)} %pad_maximum_fusion.3), channel_id=1, source_target_pairs={{0,4},{1,3},{2,6},{3,1},{4,0},{5,7},{6,2},{7,5},{8,12},{9,11},{10,... | collective-permute-start | bytes 589832 | tf_op jit(solution)/shard_map/ppermute | solution.py:76
  28.0 5.9 %collective-permute-start.8 = (bf16[2,8,6144]{2,1,0:T(8,128)(2,1)S(1)}, bf16[2,8,6144]{2,1,0:T(8,128)(2,1)S(1)}, u32[]{:S(2)}, u32[]{:S(2)}) collective-permute-start(bf16[2,8,6144]{2,1,0:T(8,128)(2,1)S(1)} %pad_maximum_fusion.4), channel_id=1, source_target_pairs={{0,4},{1,3},{2,6},{3,1},{4,0},{5,7},{6,2},{7,5},{8,12},{9,11},{10,... | collective-permute-start | bytes 589832 | tf_op jit(solution)/shard_map/ppermute | solution.py:76
  31.4 2.6 %copy-start.1 = (f32[2,16,128]{2,1,0:T(8,128)S(1)}, f32[2,16,128]{2,1,0:T(8,128)}, u32[]{:S(2)}) copy-start(f32[2,16,128]{2,1,0:T(8,128)} %gather_fusion) | copy-start | bytes 49156
  31.4 4.8 %collective-permute-start.9 = (bf16[4,16,6144]{2,1,0:T(8,128)(2,1)S(1)}, bf16[4,16,6144]{2,1,0:T(8,128)(2,1)S(1)}, u32[]{:S(2)}, u32[]{:S(2)}) collective-permute-start(bf16[4,16,6144]{2,1,0:T(8,128)(2,1)S(1)} %pad_maximum_fusion.1), channel_id=1, source_target_pairs={{0,1},{1,0},{2,3},{3,2},{4,5},{5,4},{6,7},{7,6},{8,9},{9,8},{10,11... | collective-permute-start | bytes 2359304 | tf_op jit(solution)/shard_map/ppermute | solution.py:12
  33.9 2.4 %collective-permute-start.10 = (bf16[4,16,6144]{2,1,0:T(8,128)(2,1)S(1)}, bf16[4,16,6144]{2,1,0:T(8,128)(2,1)S(1)}, u32[]{:S(2)}, u32[]{:S(2)}) collective-permute-start(bf16[4,16,6144]{2,1,0:T(8,128)(2,1)S(1)} %maximum_maximum_fusion), channel_id=1, source_target_pairs={{0,1},{1,0},{2,3},{3,2},{4,5},{5,4},{6,7},{7,6},{8,9},{9,8},{10,11... | collective-permute-start | bytes 2359304 | tf_op jit(solution)/shard_map/ppermute | solution.py:12
  34.1 34.7 %collective-permute-start.12 = (f32[2,16,128]{2,1,0:T(8,128)S(1)}, f32[2,16,128]{2,1,0:T(8,128)S(1)}, u32[]{:S(2)}, u32[]{:S(2)}) collective-permute-start(f32[2,16,128]{2,1,0:T(8,128)S(1)} %broadcast_select_fusion), channel_id=1, source_target_pairs={{0,16},{16,0},{1,17},{17,1},{2,18},{18,2},{3,19},{19,3},{4,20},{20... | collective-permute-start | bytes 49160 | tf_op jit(solution)/shard_map/ppermute | solution.py:12
  35.9 33.0 %collective-permute-start.11 = (bf16[64,6144]{1,0:T(8,128)(2,1)S(1)}, bf16[64,6144]{1,0:T(8,128)(2,1)S(1)}, u32[]{:S(2)}, u32[]{:S(2)}) collective-permute-start(bf16[64,6144]{1,0:T(8,128)(2,1)S(1)} %get-tuple-element.26), channel_id=1, source_target_pairs={{0,16},{16,0},{1,17},{17,1},{2,18},{18,2},{3,19},{19,3},{4,20},{20... | collective-permute-start | bytes 2359304 | tf_op jit(solution)/shard_map/ppermute | solution.py:12
  69.0 8.8 %collective-permute-start.13 = (bf16[4,2,16,3072]{3,2,1,0:T(8,128)(2,1)S(1)}, bf16[4,2,16,3072]{3,2,1,0:T(8,128)(2,1)S(1)}, u32[]{:S(2)}, u32[]{:S(2)}) collective-permute-start(bf16[4,2,16,3072]{3,2,1,0:T(8,128)(2,1)S(1)} %bitcast.92), channel_id=1, source_target_pairs={{0,1},{1,0},{2,3},{3,2},{4,5},{5,4},{6,7},{7,6},{8,9},{9,8},{10,11... | collective-permute-start | bytes 2359304 | tf_op jit(solution)/shard_map/ppermute | solution.py:12
  77.3 2.6 %collective-permute-start.17 = (bf16[4,2,16,3072]{3,2,1,0:T(8,128)(2,1)S(1)}, bf16[4,2,16,3072]{3,2,1,0:T(8,128)(2,1)S(1)}, u32[]{:S(2)}, u32[]{:S(2)}) collective-permute-start(bf16[4,2,16,3072]{3,2,1,0:T(8,128)(2,1)S(1)} %bitcast.91), channel_id=1, source_target_pairs={{0,1},{1,0},{2,3},{3,2},{4,5},{5,4},{6,7},{7,6},{8,9},{9,8},{10,11... | collective-permute-start | bytes 2359304 | tf_op jit(solution)/shard_map/ppermute | solution.py:12
  78.0 7.8 %collective-permute-start.14 = (bf16[2,2,16,3072]{3,2,1,0:T(8,128)(2,1)S(1)}, bf16[2,2,16,3072]{3,2,1,0:T(8,128)(2,1)S(1)}, u32[]{:S(2)}, u32[]{:S(2)}) collective-permute-start(bf16[2,2,16,3072]{3,2,1,0:T(8,128)(2,1)S(1)} %slice.165), channel_id=1, source_target_pairs={{0,4},{1,3},{2,6},{3,1},{4,0},{5,7},{6,2},{7,5},{8,12},{9,11},{10,... | collective-permute-start | bytes 1179656 | tf_op jit(solution)/shard_map/ppermute | solution.py:124
  80.1 11.9 %collective-permute-start.18 = (bf16[2,2,16,3072]{3,2,1,0:T(8,128)(2,1)S(1)}, bf16[2,2,16,3072]{3,2,1,0:T(8,128)(2,1)S(1)}, u32[]{:S(2)}, u32[]{:S(2)}) collective-permute-start(bf16[2,2,16,3072]{3,2,1,0:T(8,128)(2,1)S(1)} %slice.164), channel_id=1, source_target_pairs={{0,4},{1,3},{2,6},{3,1},{4,0},{5,7},{6,2},{7,5},{8,12},{9,11},{10,... | collective-permute-start | bytes 1179656 | tf_op jit(solution)/shard_map/ppermute | solution.py:124
  85.9 8.2 %collective-permute-start.15 = (bf16[1,2,16,3072]{3,2,1,0:T(8,128)(2,1)S(1)}, bf16[1,2,16,3072]{3,2,1,0:T(8,128)(2,1)S(1)}, u32[]{:S(2)}, u32[]{:S(2)}) collective-permute-start(bf16[1,2,16,3072]{3,2,1,0:T(8,128)(2,1)S(1)} %slice.167), channel_id=1, source_target_pairs={{0,2},{1,5},{2,0},{3,7},{4,6},{5,1},{6,4},{7,3},{8,10},{9,13},{10,... | collective-permute-start | bytes 589832 | tf_op jit(solution)/shard_map/ppermute | solution.py:124
  92.2 5.7 %collective-permute-start.19 = (bf16[1,2,16,3072]{3,2,1,0:T(8,128)(2,1)S(1)}, bf16[1,2,16,3072]{3,2,1,0:T(8,128)(2,1)S(1)}, u32[]{:S(2)}, u32[]{:S(2)}) collective-permute-start(bf16[1,2,16,3072]{3,2,1,0:T(8,128)(2,1)S(1)} %slice.166), channel_id=1, source_target_pairs={{0,2},{1,5},{2,0},{3,7},{4,6},{5,1},{6,4},{7,3},{8,10},{9,13},{10,... | collective-permute-start | bytes 589832 | tf_op jit(solution)/shard_map/ppermute | solution.py:124
  94.2 9.5 %collective-permute-start.16 = (bf16[16,3072]{1,0:T(8,128)(2,1)S(1)}, bf16[16,3072]{1,0:T(8,128)(2,1)S(1)}, u32[]{:S(2)}, u32[]{:S(2)}) collective-permute-start(bf16[16,3072]{1,0:T(8,128)(2,1)S(1)} %get-tuple-element.29), channel_id=1, source_target_pairs={{0,16},{16,0},{1,17},{17,1},{2,18},{18,2},{3,19},{19,3},{4,20},{20... | collective-permute-start | bytes 294920 | tf_op jit(solution)/shard_map/ppermute | solution.py:12
  98.0 5.7 %collective-permute-start.20 = (bf16[16,3072]{1,0:T(8,128)(2,1)S(1)}, bf16[16,3072]{1,0:T(8,128)(2,1)S(1)}, u32[]{:S(2)}, u32[]{:S(2)}) collective-permute-start(bf16[16,3072]{1,0:T(8,128)(2,1)S(1)} %get-tuple-element.31), channel_id=1, source_target_pairs={{0,16},{16,0},{1,17},{17,1},{2,18},{18,2},{3,19},{19,3},{4,20},{20... | collective-permute-start | bytes 294920 | tf_op jit(solution)/shard_map/ppermute | solution.py:12
  99.9 6.4 %collective-permute-start.21 = (bf16[16,3072]{1,0:T(8,128)(2,1)S(1)}, bf16[16,3072]{1,0:T(8,128)(2,1)S(1)}, u32[]{:S(2)}, u32[]{:S(2)}) collective-permute-start(bf16[16,3072]{1,0:T(8,128)(2,1)S(1)} %get-tuple-element.30), channel_id=1, source_target_pairs={{0,24},{8,16},{16,8},{24,0},{1,25},{9,17},{17,9},{25,1},{2,26},{10... | collective-permute-start | bytes 294920 | tf_op jit(solution)/shard_map/ppermute | solution.py:137
  102.6 6.4 %collective-permute-start.22 = (bf16[16,3072]{1,0:T(8,128)(2,1)S(1)}, bf16[16,3072]{1,0:T(8,128)(2,1)S(1)}, u32[]{:S(2)}, u32[]{:S(2)}) collective-permute-start(bf16[16,3072]{1,0:T(8,128)(2,1)S(1)} %get-tuple-element.32), channel_id=1, source_target_pairs={{0,24},{8,16},{16,8},{24,0},{1,25},{9,17},{17,9},{25,1},{2,26},{10... | collective-permute-start | bytes 294920 | tf_op jit(solution)/shard_map/ppermute | solution.py:137

commit v10 on v7

--- a/solution.py
+++ b/solution.py
@@ -115,6 +115,8 @@
         summed = partials[0].astype(jnp.float32)
         for q in range(1, n_core):
             summed = summed + shifted(partials[q], "core", n_core, -q).astype(jnp.float32)
+        if piece + 1 < pieces:
+            summed, activated = lax.optimization_barrier((summed, activated))
         for stage in reversed(range(levels)):
             half = summed.shape[0] // 2
             sent = summed[half:].astype(SUM_DTYPE)

time: 111 us -> 113 us (1.018)
  waiting for transfers between devices: 33.5 us -> 35.8 us
    ppermute x2, waiting for transfers between devices: 4.08 us -> 7.95 us  [body(): got[k].append(lax.ppermute(outgoing, ('section', 'ex'), route))]
    ppermute x4, waiting for transfers between devices: 12.7 us -> 9.52 us  [body(): lax.ppermute(sent, ('chip', 'core'), chip_route(n_chip, n_core, stage, le...]
    ppermute x11, waiting for transfers between devices: 5.19 us -> 6.74 us  [shifted(): return lax.ppermute(block, axes, route)]
  transfers between devices with their start and end apart: 23 -> 23, of which waited for: 15 -> 15; matrix products, arithmetic and copies ran while one was open for 40% -> 39% of each run, Pallas kernels for 0% -> 0%
where the time goes in v10:
time: 113 us
  matrix products  44.5 us (39%)
  waiting for transfers between devices  35.8 us (32%)
  starting transfers between devices  26.6 us (24%)
  local copies, waits for them, and re-layouts  3.49 us (3%)
  other arithmetic  2.36 us (2%)
    dot_general x2, matrix products, body(): jnp.dot(activated, cols, preferred_element_type=jnp.float32)  16 us
    dot_general x1, matrix products, body(): up_part = jnp.dot(flat_rows, up_cols, preferred_element_type=jnp.float32)  12.4 us
    ppermute x11, starting transfers between devices, shifted(): return lax.ppermute(block, axes, route)  11.8 us
    dot_general x1, matrix products, body(): jnp.dot(flat_rows, gate_cols, preferred_element_type=jnp.float32)  11.7 us
    ppermute x6, waiting for transfers between devices, doubled(): lax.ppermute(held, ('chip', 'core'), chip_route(n_chip, n_core, stage, le...  11.6 us
    ppermute x4, waiting for transfers between devices, body(): lax.ppermute(sent, ('chip', 'core'), chip_route(n_chip, n_core, stage, le...  9.52 us
    ppermute x2, waiting for transfers between devices, body(): got[k].append(lax.ppermute(outgoing, ('section', 'ex'), route))  7.95 us
    ppermute x6, starting transfers between devices, doubled(): lax.ppermute(held, ('chip', 'core'), chip_route(n_chip, n_core, stage, le...  6.99 us
  transfers between devices with their start and end apart: 23, of which 15 were waited for; matrix products, arithmetic and copies ran while one was open for 39% of the time, Pallas kernels for 0%

profile of v10, /device:TPU:0, one launch (start us, length us, event | category | flops | bytes accessed | tf_op | source)
XLA Modules:
  0.0 113.0 jit_solution(6348811889291842802)
XLA Ops:
  0.0 0.9 eq.34
  0.9 1.8 %convolution_convert_fusion = bf16[32,6144]{1,0:T(8,128)(2,1)S(1)} fusion(bf16[1,128,6144]{2,1,0:T(8,128)(2,1)} %param.8, s32[32]{0:T(128)S(1)} %eq.34), kind=kOutput, calls=%fused_computation.13 | convolution fusion | flops 50532352 | bytes 1966208 | tf_op jit(solution)/shard_map/dot_general | solution.py:63
  2.7 0.7 dynamic-slice_bitcast_fusion.1
  3.3 4.0 %collective-permute-start.6 = (bf16[8,6144]{1,0:T(8,128)(2,1)}, bf16[8,6144]{1,0:T(8,128)(2,1)S(1)}, u32[]{:S(2)}, u32[]{:S(2)}) collective-permute-start(bf16[8,6144]{1,0:T(8,128)(2,1)} %get-tuple-element.28), channel_id=1, source_target_pairs={{0,8},{8,0},{1,9},{9,1},{2,10},{10,2},{3,11},{11,3},{4,12},{12,4},... | collective-permute-start | bytes 294920 | tf_op jit(solution)/shard_map/ppermute | solution.py:12
  7.4 0.2 fusion.24
  7.6 0.1 fusion.26
  7.8 1.9 %collective-permute-start.1 = (bf16[1,16,6144]{2,1,0:T(8,128)(2,1)S(1)}, bf16[1,16,6144]{2,1,0:T(8,128)(2,1)S(1)}, u32[]{:S(2)}, u32[]{:S(2)}) collective-permute-start(bf16[1,16,6144]{2,1,0:T(8,128)(2,1)S(1)} %fusion.26), channel_id=1, source_target_pairs={{0,2},{1,5},{2,0},{3,7},{4,6},{5,1},{6,4},{7,3},{8,10},{9,13},{10,... | collective-permute-start | bytes 589832 | tf_op jit(solution)/shard_map/ppermute | solution.py:76
  9.7 1.0 slice_bitcast_fusion.1
  10.7 1.5 %collective-permute-start = (bf16[64,6144]{1,0:T(8,128)(2,1)}, bf16[64,6144]{1,0:T(8,128)(2,1)S(1)}, u32[]{:S(2)}, u32[]{:S(2)}) collective-permute-start(bf16[64,6144]{1,0:T(8,128)(2,1)} %get-tuple-element.23), channel_id=1, source_target_pairs={{0,16},{16,0},{1,17},{17,1},{2,18},{18,2},{3,19},{19,3},{4,20},{20... | collective-permute-start | bytes 2359304 | tf_op jit(solution)/shard_map/ppermute | solution.py:12
  12.2 0.1 compare_select_fusion.6
  12.3 0.1 fusion.40
  12.4 0.5 gather_fusion
  12.9 2.5 %collective-permute-done.6 = bf16[8,6144]{1,0:T(8,128)(2,1)S(1)} collective-permute-done((bf16[8,6144]{1,0:T(8,128)(2,1)}, bf16[8,6144]{1,0:T(8,128)(2,1)S(1)}, u32[]{:S(2)}, u32[]{:S(2)}) %collective-permute-start.6) | collective-permute-done | bytes 98336 | tf_op jit(solution)/shard_map/ppermute | solution.py:12
  15.4 0.2 fusion.35
  15.6 1.1 collective-permute-done.3
  16.7 0.2 fusion.32
  16.9 0.1 fusion.39
  17.0 1.6 %collective-permute-start.4 = (bf16[1,8,6144]{2,1,0:T(8,128)(2,1)S(1)}, bf16[1,8,6144]{2,1,0:T(8,128)(2,1)S(1)}, u32[]{:S(2)}, u32[]{:S(2)}) collective-permute-start(bf16[1,8,6144]{2,1,0:T(8,128)(2,1)S(1)} %get-tuple-element.33), channel_id=1, source_target_pairs={{0,2},{1,5},{2,0},{3,7},{4,6},{5,1},{6,4},{7,3},{8,10},{9,13},{10,... | collective-permute-start | bytes 294920 | tf_op jit(solution)/shard_map/ppermute | solution.py:76
  18.6 0.5 collective-permute-start.7
  19.2 2.5 %collective-permute-done.4 = bf16[1,8,6144]{2,1,0:T(8,128)(2,1)S(1)} collective-permute-done((bf16[1,8,6144]{2,1,0:T(8,128)(2,1)S(1)}, bf16[1,8,6144]{2,1,0:T(8,128)(2,1)S(1)}, u32[]{:S(2)}, u32[]{:S(2)}) %collective-permute-start.4) | collective-permute-done | bytes 98336 | tf_op jit(solution)/shard_map/ppermute | solution.py:76
  21.7 0.8 collective-permute-start.5
  22.5 1.4 %collective-permute-done.7 = bf16[1,8,6144]{2,1,0:T(8,128)(2,1)S(1)} collective-permute-done((bf16[1,8,6144]{2,1,0:T(8,128)(2,1)S(1)}, bf16[1,8,6144]{2,1,0:T(8,128)(2,1)S(1)}, u32[]{:S(2)}, u32[]{:S(2)}) %collective-permute-start.7) | collective-permute-done | bytes 98336 | tf_op jit(solution)/shard_map/ppermute | solution.py:76
  24.0 0.1 collective-permute-start.8
  24.1 2.0 %collective-permute-start.2 = (bf16[2,16,6144]{2,1,0:T(8,128)(2,1)S(1)}, bf16[2,16,6144]{2,1,0:T(8,128)(2,1)S(1)}, u32[]{:S(2)}, u32[]{:S(2)}) collective-permute-start(bf16[2,16,6144]{2,1,0:T(8,128)(2,1)S(1)} %pad_maximum_fusion.2), channel_id=1, source_target_pairs={{0,4},{1,3},{2,6},{3,1},{4,0},{5,7},{6,2},{7,5},{8,12},{9,11},{10,... | collective-permute-start | bytes 1179656 | tf_op jit(solution)/shard_map/ppermute | solution.py:76
  26.2 1.3 %collective-permute-done.5 = bf16[2,8,6144]{2,1,0:T(8,128)(2,1)S(1)} collective-permute-done((bf16[2,8,6144]{2,1,0:T(8,128)(2,1)S(1)}, bf16[2,8,6144]{2,1,0:T(8,128)(2,1)S(1)}, u32[]{:S(2)}, u32[]{:S(2)}) %collective-permute-start.5) | collective-permute-done | bytes 196640 | tf_op jit(solution)/shard_map/ppermute | solution.py:76
  27.4 2.3 %collective-permute-done.8 = bf16[2,8,6144]{2,1,0:T(8,128)(2,1)S(1)} collective-permute-done((bf16[2,8,6144]{2,1,0:T(8,128)(2,1)S(1)}, bf16[2,8,6144]{2,1,0:T(8,128)(2,1)S(1)}, u32[]{:S(2)}, u32[]{:S(2)}) %collective-permute-start.8) | collective-permute-done | bytes 196640 | tf_op jit(solution)/shard_map/ppermute | solution.py:76
  29.7 0.1 maximum_maximum_fusion
  29.8 0.1 collective-permute-start.10
  29.8 4.1 %collective-permute-done.2 = bf16[2,16,6144]{2,1,0:T(8,128)(2,1)S(1)} collective-permute-done((bf16[2,16,6144]{2,1,0:T(8,128)(2,1)S(1)}, bf16[2,16,6144]{2,1,0:T(8,128)(2,1)S(1)}, u32[]{:S(2)}, u32[]{:S(2)}) %collective-permute-start.2) | collective-permute-done | bytes 393248 | tf_op jit(solution)/shard_map/ppermute | solution.py:76
  33.9 0.1 fusion.46
  34.0 0.1 collective-permute-start.9
  34.1 0.1 broadcast_select_fusion
  34.2 1.6 %collective-permute-start.12 = (f32[2,16,128]{2,1,0:T(8,128)S(1)}, f32[2,16,128]{2,1,0:T(8,128)S(1)}, u32[]{:S(2)}, u32[]{:S(2)}) collective-permute-start(f32[2,16,128]{2,1,0:T(8,128)S(1)} %broadcast_select_fusion), channel_id=1, source_target_pairs={{0,16},{16,0},{1,17},{17,1},{2,18},{18,2},{3,19},{19,3},{4,20},{20... | collective-permute-start | bytes 49160 | tf_op jit(solution)/shard_map/ppermute | solution.py:12
  35.8 0.4 collective-permute-start.11
  36.2 0.1 fusion.54
  36.3 0.1 collective-permute-done.9
  36.4 0.1 maximum_bitcast_fusion.1
  36.5 0.2 pad_maximum_fusion
  36.8 11.7 %fusion.2 = f32[256,2048]{1,0:T(8,128)S(1)} fusion(bf16[256,6144]{1,0:T(8,128)(2,1)S(1)} %bitcast.82, bf16[1,6144,2048]{2,1,0:T(8,128)(2,1)} %param.10), kind=kOutput, calls=%fused_computation.3 | convolution fusion | flops 6442450944 | bytes 30408704 | tf_op jit(solution)/shard_map/dot_general | solution.py:97
  48.4 12.4 %fusion.20 = bf16[256,2048]{1,0:T(8,128)(2,1)S(1)} fusion(bf16[256,6144]{1,0:T(8,128)(2,1)S(1)} %bitcast.83, bf16[1,6144,2048]{2,1,0:T(8,128)(2,1)} %param.11, f32[256,2048]{1,0:T(8,128)S(1)} %fusion.2), kind=kOutput, calls=%fused_computation.18 | convolution fusion | flops 6445596672 | bytes 31457280 | tf_op jit(solution)/shard_map/dot_general | solution.py:98
  60.8 8.0 %fusion.11 = bf16[256,3072]{1,0:T(8,128)(2,1)S(1)} fusion(bf16[256,2048]{1,0:T(8,128)(2,1)S(1)} %fusion.20, bf16[2048,6144]{1,0:T(8,128)(2,1)} %bitcast.97), kind=kOutput, calls=%fused_computation.14 | convolution fusion | flops 3222011904 | bytes 15204352 | tf_op jit(solution)/shard_map/dot_general | solution.py:106
  68.8 0.1 fusion.48
  68.9 0.2 collective-permute-start.13
  69.1 2.1 %collective-permute-done.13 = bf16[4,2,16,3072]{3,2,1,0:T(8,128)(2,1)S(1)} collective-permute-done((bf16[4,2,16,3072]{3,2,1,0:T(8,128)(2,1)S(1)}, bf16[4,2,16,3072]{3,2,1,0:T(8,128)(2,1)S(1)}, u32[]{:S(2)}, u32[]{:S(2)}) %collective-permute-start.13) | collective-permute-done | bytes 786464 | tf_op jit(solution)/shard_map/ppermute | solution.py:12
  71.3 0.2 convert_add_fusion.1
  71.5 0.6 collective-permute-start.14
  72.2 8.0 %fusion.14 = bf16[256,3072]{1,0:T(8,128)(2,1)S(1)} fusion(bf16[256,2048]{1,0:T(8,128)(2,1)S(1)} %fusion.20, bf16[2048,6144]{1,0:T(8,128)(2,1)} %bitcast.98), kind=kOutput, calls=%fused_computation.15 | convolution fusion | flops 3222011904 | bytes 15204352 | tf_op jit(solution)/shard_map/dot_general | solution.py:106
  80.2 0.1 fusion.47
  80.3 0.8 collective-permute-start.17
  81.2 0.9 collective-permute-start.15
  82.1 0.9 collective-permute-done.17
  83.0 0.2 convert_add_fusion
  83.2 1.2 %collective-permute-start.18 = (bf16[2,2,16,3072]{3,2,1,0:T(8,128)(2,1)S(1)}, bf16[2,2,16,3072]{3,2,1,0:T(8,128)(2,1)S(1)}, u32[]{:S(2)}, u32[]{:S(2)}) collective-permute-start(bf16[2,2,16,3072]{3,2,1,0:T(8,128)(2,1)S(1)} %slice.163), channel_id=1, source_target_pairs={{0,4},{1,3},{2,6},{3,1},{4,0},{5,7},{6,2},{7,5},{8,12},{9,11},{10,... | collective-permute-start | bytes 1179656 | tf_op jit(solution)/shard_map/ppermute | solution.py:123
  84.4 3.1 %collective-permute-done.15 = bf16[1,2,16,3072]{3,2,1,0:T(8,128)(2,1)S(1)} collective-permute-done((bf16[1,2,16,3072]{3,2,1,0:T(8,128)(2,1)S(1)}, bf16[1,2,16,3072]{3,2,1,0:T(8,128)(2,1)S(1)}, u32[]{:S(2)}, u32[]{:S(2)}) %collective-permute-start.15) | collective-permute-done | bytes 196640 | tf_op jit(solution)/shard_map/ppermute | solution.py:123
  87.5 3.5 %collective-permute-done.18 = bf16[2,2,16,3072]{3,2,1,0:T(8,128)(2,1)S(1)} collective-permute-done((bf16[2,2,16,3072]{3,2,1,0:T(8,128)(2,1)S(1)}, bf16[2,2,16,3072]{3,2,1,0:T(8,128)(2,1)S(1)}, u32[]{:S(2)}, u32[]{:S(2)}) %collective-permute-start.18) | collective-permute-done | bytes 393248 | tf_op jit(solution)/shard_map/ppermute | solution.py:123
  91.2 1.3 %collective-permute-start.19 = (bf16[1,2,16,3072]{3,2,1,0:T(8,128)(2,1)S(1)}, bf16[1,2,16,3072]{3,2,1,0:T(8,128)(2,1)S(1)}, u32[]{:S(2)}, u32[]{:S(2)}) collective-permute-start(bf16[1,2,16,3072]{3,2,1,0:T(8,128)(2,1)S(1)} %slice.165), channel_id=1, source_target_pairs={{0,2},{1,5},{2,0},{3,7},{4,6},{5,1},{6,4},{7,3},{8,10},{9,13},{10,... | collective-permute-start | bytes 589832 | tf_op jit(solution)/shard_map/ppermute | solution.py:123
  92.4 1.6 %collective-permute-start.16 = (bf16[16,3072]{1,0:T(8,128)(2,1)S(1)}, bf16[16,3072]{1,0:T(8,128)(2,1)S(1)}, u32[]{:S(2)}, u32[]{:S(2)}) collective-permute-start(bf16[16,3072]{1,0:T(8,128)(2,1)S(1)} %get-tuple-element.29), channel_id=1, source_target_pairs={{0,16},{16,0},{1,17},{17,1},{2,18},{18,2},{3,19},{19,3},{4,20},{20... | collective-permute-start | bytes 294920 | tf_op jit(solution)/shard_map/ppermute | solution.py:12
  94.0 2.9 %collective-permute-done.19 = bf16[1,2,16,3072]{3,2,1,0:T(8,128)(2,1)S(1)} collective-permute-done((bf16[1,2,16,3072]{3,2,1,0:T(8,128)(2,1)S(1)}, bf16[1,2,16,3072]{3,2,1,0:T(8,128)(2,1)S(1)}, u32[]{:S(2)}, u32[]{:S(2)}) %collective-permute-start.19) | collective-permute-done | bytes 196640 | tf_op jit(solution)/shard_map/ppermute | solution.py:123
  97.0 1.6 %collective-permute-start.20 = (bf16[16,3072]{1,0:T(8,128)(2,1)S(1)}, bf16[16,3072]{1,0:T(8,128)(2,1)S(1)}, u32[]{:S(2)}, u32[]{:S(2)}) collective-permute-start(bf16[16,3072]{1,0:T(8,128)(2,1)S(1)} %get-tuple-element.31), channel_id=1, source_target_pairs={{0,16},{16,0},{1,17},{17,1},{2,18},{18,2},{3,19},{19,3},{4,20},{20... | collective-permute-start | bytes 294920 | tf_op jit(solution)/shard_map/ppermute | solution.py:12
  98.5 3.0 %collective-permute-start.21 = (bf16[16,3072]{1,0:T(8,128)(2,1)S(1)}, bf16[16,3072]{1,0:T(8,128)(2,1)S(1)}, u32[]{:S(2)}, u32[]{:S(2)}) collective-permute-start(bf16[16,3072]{1,0:T(8,128)(2,1)S(1)} %get-tuple-element.30), channel_id=1, source_target_pairs={{0,24},{8,16},{16,8},{24,0},{1,25},{9,17},{17,9},{25,1},{2,26},{10... | collective-permute-start | bytes 294920 | tf_op jit(solution)/shard_map/ppermute | solution.py:136
  101.5 0.8 collective-permute-start.22
  102.4 6.6 %collective-permute-done.21 = bf16[16,3072]{1,0:T(8,128)(2,1)S(1)} collective-permute-done((bf16[16,3072]{1,0:T(8,128)(2,1)S(1)}, bf16[16,3072]{1,0:T(8,128)(2,1)S(1)}, u32[]{:S(2)}, u32[]{:S(2)}) %collective-permute-start.21) | collective-permute-done | bytes 98336 | tf_op jit(solution)/shard_map/ppermute | solution.py:136
  108.9 1.4 %collective-permute-done.22 = bf16[16,3072]{1,0:T(8,128)(2,1)S(1)} collective-permute-done((bf16[16,3072]{1,0:T(8,128)(2,1)S(1)}, bf16[16,3072]{1,0:T(8,128)(2,1)S(1)}, u32[]{:S(2)}, u32[]{:S(2)}) %collective-permute-start.22) | collective-permute-done | bytes 98336 | tf_op jit(solution)/shard_map/ppermute | solution.py:136
  110.3 2.7 %fusion.10 = bf16[1,128,6144]{2,1,0:T(8,128)(2,1)} fusion(f32[2,16,128]{2,1,0:T(8,128)S(1)} %collective-permute-done.12, bf16[64,6144]{1,0:T(8,128)(2,1)S(1)} %collective-permute-done.11, bf16[64,6144]{1,0:T(8,128)(2,1)S(1)} %collective-permute-done, bf16[1,16,6144]{2,1,0:T(8,128)(2,1)S(1)} %maximum_bitcast_fusion.3, ...), kind=kOutput, calls=%fused_computation.12 | convolution fusion | flops 306905088 | bytes 3555328 | tf_op jit(solution)/shard_map/ect,ecd->td/dot_general | solution.py:140
  (41 shorter events, 0.7 us)
Async XLA Ops:
  0.0 9.7 %copy-start = (bf16[1,128,6144]{2,1,0:T(8,128)(2,1)S(1)}, bf16[1,128,6144]{2,1,0:T(8,128)(2,1)}, u32[]{:S(2)}) copy-start(bf16[1,128,6144]{2,1,0:T(8,128)(2,1)} %param.8) | copy-start | bytes 4718596
  0.0 7.4 %copy-start.1 = (bf16[1,6144]{1,0:T(2,128)(2,1)S(1)}, bf16[1,6144]{1,0:T(2,128)(2,1)}, u32[]{:S(2)}) copy-start(bf16[1,6144]{1,0:T(2,128)(2,1)} %param.9) | copy-start | bytes 36868
  3.3 12.1 %collective-permute-start.6 = (bf16[8,6144]{1,0:T(8,128)(2,1)}, bf16[8,6144]{1,0:T(8,128)(2,1)S(1)}, u32[]{:S(2)}, u32[]{:S(2)}) collective-permute-start(bf16[8,6144]{1,0:T(8,128)(2,1)} %get-tuple-element.28), channel_id=1, source_target_pairs={{0,8},{8,0},{1,9},{9,1},{2,10},{10,2},{3,11},{11,3},{4,12},{12,4},... | collective-permute-start | bytes 294920 | tf_op jit(solution)/shard_map/ppermute | solution.py:12
  7.4 9.3 %collective-permute-start.3 = (bf16[8,6144]{1,0:T(8,128)(2,1)S(1)}, bf16[8,6144]{1,0:T(8,128)(2,1)S(1)}, u32[]{:S(2)}, u32[]{:S(2)}) collective-permute-start(bf16[8,6144]{1,0:T(8,128)(2,1)S(1)} %get-tuple-element.27), channel_id=1, source_target_pairs={{0,8},{8,0},{1,9},{9,1},{2,10},{10,2},{3,11},{11,3},{4,12},{12,4},... | collective-permute-start | bytes 294920 | tf_op jit(solution)/shard_map/ppermute | solution.py:12
  7.8 4.4 %copy-start.3 = (f32[1,1,2,16]{3,2,1,0:T(2,128)S(1)}, f32[1,1,2,16]{3,2,1,0:T(2,128)}, u32[]{:S(2)}) copy-start(f32[1,1,2,16]{3,2,1,0:T(2,128)} %param.15) | copy-start | bytes 388
  7.8 4.4 %copy-start.4 = (s32[1,1,2]{2,1,0:T(1,128)S(1)}, s32[1,1,2]{2,1,0:T(1,128)}, u32[]{:S(2)}) copy-start(s32[1,1,2]{2,1,0:T(1,128)} %param.14) | copy-start | bytes 28
  7.8 4.5 %copy-start.2 = (s32[1,1,2,16]{3,2,1,0:T(2,128)S(1)}, s32[1,1,2,16]{3,2,1,0:T(2,128)}, u32[]{:S(2)}) copy-start(s32[1,1,2,16]{3,2,1,0:T(2,128)} %param.13) | copy-start | bytes 388
  7.8 16.3 %collective-permute-start.1 = (bf16[1,16,6144]{2,1,0:T(8,128)(2,1)S(1)}, bf16[1,16,6144]{2,1,0:T(8,128)(2,1)S(1)}, u32[]{:S(2)}, u32[]{:S(2)}) collective-permute-start(bf16[1,16,6144]{2,1,0:T(8,128)(2,1)S(1)} %fusion.26), channel_id=1, source_target_pairs={{0,2},{1,5},{2,0},{3,7},{4,6},{5,1},{6,4},{7,3},{8,10},{9,13},{10,... | collective-permute-start | bytes 589832 | tf_op jit(solution)/shard_map/ppermute | solution.py:76
  10.7 26.1 %collective-permute-start = (bf16[64,6144]{1,0:T(8,128)(2,1)}, bf16[64,6144]{1,0:T(8,128)(2,1)S(1)}, u32[]{:S(2)}, u32[]{:S(2)}) collective-permute-start(bf16[64,6144]{1,0:T(8,128)(2,1)} %get-tuple-element.23), channel_id=1, source_target_pairs={{0,16},{16,0},{1,17},{17,1},{2,18},{18,2},{3,19},{19,3},{4,20},{20... | collective-permute-start | bytes 2359304 | tf_op jit(solution)/shard_map/ppermute | solution.py:12
  17.0 4.7 %collective-permute-start.4 = (bf16[1,8,6144]{2,1,0:T(8,128)(2,1)S(1)}, bf16[1,8,6144]{2,1,0:T(8,128)(2,1)S(1)}, u32[]{:S(2)}, u32[]{:S(2)}) collective-permute-start(bf16[1,8,6144]{2,1,0:T(8,128)(2,1)S(1)} %get-tuple-element.33), channel_id=1, source_target_pairs={{0,2},{1,5},{2,0},{3,7},{4,6},{5,1},{6,4},{7,3},{8,10},{9,13},{10,... | collective-permute-start | bytes 294920 | tf_op jit(solution)/shard_map/ppermute | solution.py:76
  18.6 5.3 %collective-permute-start.7 = (bf16[1,8,6144]{2,1,0:T(8,128)(2,1)S(1)}, bf16[1,8,6144]{2,1,0:T(8,128)(2,1)S(1)}, u32[]{:S(2)}, u32[]{:S(2)}) collective-permute-start(bf16[1,8,6144]{2,1,0:T(8,128)(2,1)S(1)} %get-tuple-element.34), channel_id=1, source_target_pairs={{0,2},{1,5},{2,0},{3,7},{4,6},{5,1},{6,4},{7,3},{8,10},{9,13},{10,... | collective-permute-start | bytes 294920 | tf_op jit(solution)/shard_map/ppermute | solution.py:76
  21.7 5.7 %collective-permute-start.5 = (bf16[2,8,6144]{2,1,0:T(8,128)(2,1)S(1)}, bf16[2,8,6144]{2,1,0:T(8,128)(2,1)S(1)}, u32[]{:S(2)}, u32[]{:S(2)}) collective-permute-start(bf16[2,8,6144]{2,1,0:T(8,128)(2,1)S(1)} %pad_maximum_fusion.3), channel_id=1, source_target_pairs={{0,4},{1,3},{2,6},{3,1},{4,0},{5,7},{6,2},{7,5},{8,12},{9,11},{10,... | collective-permute-start | bytes 589832 | tf_op jit(solution)/shard_map/ppermute | solution.py:76
  24.0 5.7 %collective-permute-start.8 = (bf16[2,8,6144]{2,1,0:T(8,128)(2,1)S(1)}, bf16[2,8,6144]{2,1,0:T(8,128)(2,1)S(1)}, u32[]{:S(2)}, u32[]{:S(2)}) collective-permute-start(bf16[2,8,6144]{2,1,0:T(8,128)(2,1)S(1)} %pad_maximum_fusion.4), channel_id=1, source_target_pairs={{0,4},{1,3},{2,6},{3,1},{4,0},{5,7},{6,2},{7,5},{8,12},{9,11},{10,... | collective-permute-start | bytes 589832 | tf_op jit(solution)/shard_map/ppermute | solution.py:76
  24.1 9.8 %collective-permute-start.2 = (bf16[2,16,6144]{2,1,0:T(8,128)(2,1)S(1)}, bf16[2,16,6144]{2,1,0:T(8,128)(2,1)S(1)}, u32[]{:S(2)}, u32[]{:S(2)}) collective-permute-start(bf16[2,16,6144]{2,1,0:T(8,128)(2,1)S(1)} %pad_maximum_fusion.2), channel_id=1, source_target_pairs={{0,4},{1,3},{2,6},{3,1},{4,0},{5,7},{6,2},{7,5},{8,12},{9,11},{10,... | collective-permute-start | bytes 1179656 | tf_op jit(solution)/shard_map/ppermute | solution.py:76
  29.8 6.5 %collective-permute-start.10 = (bf16[4,16,6144]{2,1,0:T(8,128)(2,1)S(1)}, bf16[4,16,6144]{2,1,0:T(8,128)(2,1)S(1)}, u32[]{:S(2)}, u32[]{:S(2)}) collective-permute-start(bf16[4,16,6144]{2,1,0:T(8,128)(2,1)S(1)} %maximum_maximum_fusion), channel_id=1, source_target_pairs={{0,1},{1,0},{2,3},{3,2},{4,5},{5,4},{6,7},{7,6},{8,9},{9,8},{10,11... | collective-permute-start | bytes 2359304 | tf_op jit(solution)/shard_map/ppermute | solution.py:12
  34.0 2.4 %collective-permute-start.9 = (bf16[4,16,6144]{2,1,0:T(8,128)(2,1)S(1)}, bf16[4,16,6144]{2,1,0:T(8,128)(2,1)S(1)}, u32[]{:S(2)}, u32[]{:S(2)}) collective-permute-start(bf16[4,16,6144]{2,1,0:T(8,128)(2,1)S(1)} %get-tuple-element.26), channel_id=1, source_target_pairs={{0,1},{1,0},{2,3},{3,2},{4,5},{5,4},{6,7},{7,6},{8,9},{9,8},{10,11... | collective-permute-start | bytes 2359304 | tf_op jit(solution)/shard_map/ppermute | solution.py:12
  34.2 34.6 %collective-permute-start.12 = (f32[2,16,128]{2,1,0:T(8,128)S(1)}, f32[2,16,128]{2,1,0:T(8,128)S(1)}, u32[]{:S(2)}, u32[]{:S(2)}) collective-permute-start(f32[2,16,128]{2,1,0:T(8,128)S(1)} %broadcast_select_fusion), channel_id=1, source_target_pairs={{0,16},{16,0},{1,17},{17,1},{2,18},{18,2},{3,19},{19,3},{4,20},{20... | collective-permute-start | bytes 49160 | tf_op jit(solution)/shard_map/ppermute | solution.py:12
  35.8 33.0 %collective-permute-start.11 = (bf16[64,6144]{1,0:T(8,128)(2,1)S(1)}, bf16[64,6144]{1,0:T(8,128)(2,1)S(1)}, u32[]{:S(2)}, u32[]{:S(2)}) collective-permute-start(bf16[64,6144]{1,0:T(8,128)(2,1)S(1)} %get-tuple-element.24), channel_id=1, source_target_pairs={{0,16},{16,0},{1,17},{17,1},{2,18},{18,2},{3,19},{19,3},{4,20},{20... | collective-permute-start | bytes 2359304 | tf_op jit(solution)/shard_map/ppermute | solution.py:12
  68.9 2.4 %collective-permute-start.13 = (bf16[4,2,16,3072]{3,2,1,0:T(8,128)(2,1)S(1)}, bf16[4,2,16,3072]{3,2,1,0:T(8,128)(2,1)S(1)}, u32[]{:S(2)}, u32[]{:S(2)}) collective-permute-start(bf16[4,2,16,3072]{3,2,1,0:T(8,128)(2,1)S(1)} %bitcast.92), channel_id=1, source_target_pairs={{0,1},{1,0},{2,3},{3,2},{4,5},{5,4},{6,7},{7,6},{8,9},{9,8},{10,11... | collective-permute-start | bytes 2359304 | tf_op jit(solution)/shard_map/ppermute | solution.py:12
  71.5 9.5 %collective-permute-start.14 = (bf16[2,2,16,3072]{3,2,1,0:T(8,128)(2,1)S(1)}, bf16[2,2,16,3072]{3,2,1,0:T(8,128)(2,1)S(1)}, u32[]{:S(2)}, u32[]{:S(2)}) collective-permute-start(bf16[2,2,16,3072]{3,2,1,0:T(8,128)(2,1)S(1)} %slice.164), channel_id=1, source_target_pairs={{0,4},{1,3},{2,6},{3,1},{4,0},{5,7},{6,2},{7,5},{8,12},{9,11},{10,... | collective-permute-start | bytes 1179656 | tf_op jit(solution)/shard_map/ppermute | solution.py:123
  80.3 2.7 %collective-permute-start.17 = (bf16[4,2,16,3072]{3,2,1,0:T(8,128)(2,1)S(1)}, bf16[4,2,16,3072]{3,2,1,0:T(8,128)(2,1)S(1)}, u32[]{:S(2)}, u32[]{:S(2)}) collective-permute-start(bf16[4,2,16,3072]{3,2,1,0:T(8,128)(2,1)S(1)} %bitcast.91), channel_id=1, source_target_pairs={{0,1},{1,0},{2,3},{3,2},{4,5},{5,4},{6,7},{7,6},{8,9},{9,8},{10,11... | collective-permute-start | bytes 2359304 | tf_op jit(solution)/shard_map/ppermute | solution.py:12
  81.2 6.3 %collective-permute-start.15 = (bf16[1,2,16,3072]{3,2,1,0:T(8,128)(2,1)S(1)}, bf16[1,2,16,3072]{3,2,1,0:T(8,128)(2,1)S(1)}, u32[]{:S(2)}, u32[]{:S(2)}) collective-permute-start(bf16[1,2,16,3072]{3,2,1,0:T(8,128)(2,1)S(1)} %slice.166), channel_id=1, source_target_pairs={{0,2},{1,5},{2,0},{3,7},{4,6},{5,1},{6,4},{7,3},{8,10},{9,13},{10,... | collective-permute-start | bytes 589832 | tf_op jit(solution)/shard_map/ppermute | solution.py:123
  83.2 7.8 %collective-permute-start.18 = (bf16[2,2,16,3072]{3,2,1,0:T(8,128)(2,1)S(1)}, bf16[2,2,16,3072]{3,2,1,0:T(8,128)(2,1)S(1)}, u32[]{:S(2)}, u32[]{:S(2)}) collective-permute-start(bf16[2,2,16,3072]{3,2,1,0:T(8,128)(2,1)S(1)} %slice.163), channel_id=1, source_target_pairs={{0,4},{1,3},{2,6},{3,1},{4,0},{5,7},{6,2},{7,5},{8,12},{9,11},{10,... | collective-permute-start | bytes 1179656 | tf_op jit(solution)/shard_map/ppermute | solution.py:123
  91.2 5.7 %collective-permute-start.19 = (bf16[1,2,16,3072]{3,2,1,0:T(8,128)(2,1)S(1)}, bf16[1,2,16,3072]{3,2,1,0:T(8,128)(2,1)S(1)}, u32[]{:S(2)}, u32[]{:S(2)}) collective-permute-start(bf16[1,2,16,3072]{3,2,1,0:T(8,128)(2,1)S(1)} %slice.165), channel_id=1, source_target_pairs={{0,2},{1,5},{2,0},{3,7},{4,6},{5,1},{6,4},{7,3},{8,10},{9,13},{10,... | collective-permute-start | bytes 589832 | tf_op jit(solution)/shard_map/ppermute | solution.py:123
  92.4 9.9 %collective-permute-start.16 = (bf16[16,3072]{1,0:T(8,128)(2,1)S(1)}, bf16[16,3072]{1,0:T(8,128)(2,1)S(1)}, u32[]{:S(2)}, u32[]{:S(2)}) collective-permute-start(bf16[16,3072]{1,0:T(8,128)(2,1)S(1)} %get-tuple-element.29), channel_id=1, source_target_pairs={{0,16},{16,0},{1,17},{17,1},{2,18},{18,2},{3,19},{19,3},{4,20},{20... | collective-permute-start | bytes 294920 | tf_op jit(solution)/shard_map/ppermute | solution.py:12
  97.0 5.4 %collective-permute-start.20 = (bf16[16,3072]{1,0:T(8,128)(2,1)S(1)}, bf16[16,3072]{1,0:T(8,128)(2,1)S(1)}, u32[]{:S(2)}, u32[]{:S(2)}) collective-permute-start(bf16[16,3072]{1,0:T(8,128)(2,1)S(1)} %get-tuple-element.31), channel_id=1, source_target_pairs={{0,16},{16,0},{1,17},{17,1},{2,18},{18,2},{3,19},{19,3},{4,20},{20... | collective-permute-start | bytes 294920 | tf_op jit(solution)/shard_map/ppermute | solution.py:12
  98.5 10.4 %collective-permute-start.21 = (bf16[16,3072]{1,0:T(8,128)(2,1)S(1)}, bf16[16,3072]{1,0:T(8,128)(2,1)S(1)}, u32[]{:S(2)}, u32[]{:S(2)}) collective-permute-start(bf16[16,3072]{1,0:T(8,128)(2,1)S(1)} %get-tuple-element.30), channel_id=1, source_target_pairs={{0,24},{8,16},{16,8},{24,0},{1,25},{9,17},{17,9},{25,1},{2,26},{10... | collective-permute-start | bytes 294920 | tf_op jit(solution)/shard_map/ppermute | solution.py:136
  101.5 8.8 %collective-permute-start.22 = (bf16[16,3072]{1,0:T(8,128)(2,1)S(1)}, bf16[16,3072]{1,0:T(8,128)(2,1)S(1)}, u32[]{:S(2)}, u32[]{:S(2)}) collective-permute-start(bf16[16,3072]{1,0:T(8,128)(2,1)S(1)} %get-tuple-element.32), channel_id=1, source_target_pairs={{0,24},{8,16},{16,8},{24,0},{1,25},{9,17},{17,9},{25,1},{2,26},{10... | collective-permute-start | bytes 294920 | tf_op jit(solution)/shard_map/ppermute | solution.py:136

commit v11 on v8

--- a/solution.py
+++ b/solution.py
@@ -4,7 +4,7 @@
 from jax.sharding import Mesh, PartitionSpec as P
 
 SUM_DTYPE = jnp.bfloat16
-PIECES = 1
+PIECES = 3
 
 
 def shifted(block, axes, size, distance):

time: 114 us -> 116 us (1.018)
  waiting for transfers between devices: 45.2 us -> 31.2 us
  starting transfers between devices: 20.6 us -> 32.3 us
  matrix products: 40.7 us -> 45.6 us
  local copies, waits for them, and re-layouts: 4.7 us -> 3.53 us
    dot_general x0 -> x1, matrix products: none -> 12.4 us  [body(): up_part = jnp.dot(flat_rows, up_cols, preferred_element_type=jnp.float32)]
    ppermute x2 -> x6, waiting for transfers between devices: 17.8 us -> 9.87 us  [body(): lax.ppermute(sent, ('chip', 'core'), chip_route(n_chip, n_core, stage, le...]
    ppermute x2 -> x6, starting transfers between devices: 2.11 us -> 7.24 us  [body(): lax.ppermute(sent, ('chip', 'core'), chip_route(n_chip, n_core, stage, le...]
    dot_general x1 -> x3, matrix products: 22.1 us -> 17.1 us  [body(): jnp.dot(activated, cols, preferred_element_type=jnp.float32)]
    ppermute x9 -> x13, waiting for transfers between devices: 9.17 us -> 4.7 us  [shifted(): return lax.ppermute(block, axes, route)]
    ppermute x1 -> x3, starting transfers between devices: 1.78 us -> 5.6 us  [body(): got[k].append(lax.ppermute(outgoing, ('section', 'ex'), route))]
    ppermute x9 -> x13, starting transfers between devices: 9.73 us -> 12.4 us  [shifted(): return lax.ppermute(block, axes, route)]
    unnamed x16 -> x10, local copies, waits for them, and re-layouts: 1.87 us -> 0.03 us
  transfers between devices with their start and end apart: 18 -> 28, of which waited for: 13 -> 16; matrix products, arithmetic and copies ran while one was open for 34% -> 39% of each run, Pallas kernels for 0% -> 0%
where the time goes in v11:
time: 116 us; the launch traced here: 115 us
  matrix products  45.6 us (39%)
  starting transfers between devices  32.3 us (28%)
  waiting for transfers between devices  31.2 us (27%)
  local copies, waits for them, and re-layouts  3.53 us (3%)
  other arithmetic  2.39 us (2%)
    dot_general x3, matrix products, body(): jnp.dot(activated, cols, preferred_element_type=jnp.float32)  17.1 us
    ppermute x13, starting transfers between devices, shifted(): return lax.ppermute(block, axes, route)  12.4 us
    dot_general x1, matrix products, body(): up_part = jnp.dot(flat_rows, up_cols, preferred_element_type=jnp.float32)  12.4 us
    dot_general x1, matrix products, body(): jnp.dot(flat_rows, gate_cols, preferred_element_type=jnp.float32)  11.7 us
    ppermute x6, waiting for transfers between devices, doubled(): lax.ppermute(held, ('chip', 'core'), chip_route(n_chip, n_core, stage, le...  11.6 us
    ppermute x6, waiting for transfers between devices, body(): lax.ppermute(sent, ('chip', 'core'), chip_route(n_chip, n_core, stage, le...  9.87 us
    ppermute x6, starting transfers between devices, body(): lax.ppermute(sent, ('chip', 'core'), chip_route(n_chip, n_core, stage, le...  7.24 us
    ppermute x6, starting transfers between devices, doubled(): lax.ppermute(held, ('chip', 'core'), chip_route(n_chip, n_core, stage, le...  6.99 us
  transfers between devices with their start and end apart: 28, of which 16 were waited for; matrix products, arithmetic and copies ran while one was open for 39% of the time, Pallas kernels for 0%

profile of v11, /device:TPU:0, one launch (start us, length us, event | category | flops | bytes accessed | tf_op | source)
XLA Modules:
  0.0 115.4 jit_solution(6730914746799634156)
XLA Ops:
  0.0 0.9 eq.34
  0.9 1.8 %convolution_convert_fusion = bf16[32,6144]{1,0:T(8,128)(2,1)S(1)} fusion(bf16[1,128,6144]{2,1,0:T(8,128)(2,1)} %param.8, s32[32]{0:T(128)S(1)} %eq.34), kind=kOutput, calls=%fused_computation.15 | convolution fusion | flops 50532352 | bytes 1966208 | tf_op jit(solution)/shard_map/dot_general | solution.py:63
  2.7 0.7 dynamic-slice_bitcast_fusion.1
  3.4 4.0 %collective-permute-start.6 = (bf16[8,6144]{1,0:T(8,128)(2,1)}, bf16[8,6144]{1,0:T(8,128)(2,1)S(1)}, u32[]{:S(2)}, u32[]{:S(2)}) collective-permute-start(bf16[8,6144]{1,0:T(8,128)(2,1)} %get-tuple-element.26), channel_id=1, source_target_pairs={{0,8},{8,0},{1,9},{9,1},{2,10},{10,2},{3,11},{11,3},{4,12},{12,4},... | collective-permute-start | bytes 294920 | tf_op jit(solution)/shard_map/ppermute | solution.py:12
  7.5 0.2 fusion.29
  7.7 0.1 fusion.31
  7.8 1.9 %collective-permute-start.1 = (bf16[1,16,6144]{2,1,0:T(8,128)(2,1)S(1)}, bf16[1,16,6144]{2,1,0:T(8,128)(2,1)S(1)}, u32[]{:S(2)}, u32[]{:S(2)}) collective-permute-start(bf16[1,16,6144]{2,1,0:T(8,128)(2,1)S(1)} %fusion.31), channel_id=1, source_target_pairs={{0,2},{1,5},{2,0},{3,7},{4,6},{5,1},{6,4},{7,3},{8,10},{9,13},{10,... | collective-permute-start | bytes 589832 | tf_op jit(solution)/shard_map/ppermute | solution.py:76
  9.7 1.0 slice_bitcast_fusion.1
  10.7 1.5 %collective-permute-start = (bf16[64,6144]{1,0:T(8,128)(2,1)}, bf16[64,6144]{1,0:T(8,128)(2,1)S(1)}, u32[]{:S(2)}, u32[]{:S(2)}) collective-permute-start(bf16[64,6144]{1,0:T(8,128)(2,1)} %get-tuple-element.15), channel_id=1, source_target_pairs={{0,16},{16,0},{1,17},{17,1},{2,18},{18,2},{3,19},{19,3},{4,20},{20... | collective-permute-start | bytes 2359304 | tf_op jit(solution)/shard_map/ppermute | solution.py:12
  12.4 0.5 gather_fusion
  12.9 2.5 %collective-permute-done.6 = bf16[8,6144]{1,0:T(8,128)(2,1)S(1)} collective-permute-done((bf16[8,6144]{1,0:T(8,128)(2,1)}, bf16[8,6144]{1,0:T(8,128)(2,1)S(1)}, u32[]{:S(2)}, u32[]{:S(2)}) %collective-permute-start.6) | collective-permute-done | bytes 98336 | tf_op jit(solution)/shard_map/ppermute | solution.py:12
  15.5 0.2 fusion.41
  15.6 1.1 collective-permute-done.3
  16.7 0.2 fusion.38
  16.9 0.1 fusion.45
  17.0 1.6 %collective-permute-start.4 = (bf16[1,8,6144]{2,1,0:T(8,128)(2,1)S(1)}, bf16[1,8,6144]{2,1,0:T(8,128)(2,1)S(1)}, u32[]{:S(2)}, u32[]{:S(2)}) collective-permute-start(bf16[1,8,6144]{2,1,0:T(8,128)(2,1)S(1)} %get-tuple-element.33), channel_id=1, source_target_pairs={{0,2},{1,5},{2,0},{3,7},{4,6},{5,1},{6,4},{7,3},{8,10},{9,13},{10,... | collective-permute-start | bytes 294920 | tf_op jit(solution)/shard_map/ppermute | solution.py:76
  18.7 0.5 collective-permute-start.7
  19.2 2.5 %collective-permute-done.4 = bf16[1,8,6144]{2,1,0:T(8,128)(2,1)S(1)} collective-permute-done((bf16[1,8,6144]{2,1,0:T(8,128)(2,1)S(1)}, bf16[1,8,6144]{2,1,0:T(8,128)(2,1)S(1)}, u32[]{:S(2)}, u32[]{:S(2)}) %collective-permute-start.4) | collective-permute-done | bytes 98336 | tf_op jit(solution)/shard_map/ppermute | solution.py:76
  21.7 0.8 collective-permute-start.5
  22.5 1.4 %collective-permute-done.7 = bf16[1,8,6144]{2,1,0:T(8,128)(2,1)S(1)} collective-permute-done((bf16[1,8,6144]{2,1,0:T(8,128)(2,1)S(1)}, bf16[1,8,6144]{2,1,0:T(8,128)(2,1)S(1)}, u32[]{:S(2)}, u32[]{:S(2)}) %collective-permute-start.7) | collective-permute-done | bytes 98336 | tf_op jit(solution)/shard_map/ppermute | solution.py:76
  24.0 0.1 collective-permute-start.8
  24.2 2.0 %collective-permute-start.2 = (bf16[2,16,6144]{2,1,0:T(8,128)(2,1)S(1)}, bf16[2,16,6144]{2,1,0:T(8,128)(2,1)S(1)}, u32[]{:S(2)}, u32[]{:S(2)}) collective-permute-start(bf16[2,16,6144]{2,1,0:T(8,128)(2,1)S(1)} %pad_maximum_fusion.2), channel_id=1, source_target_pairs={{0,4},{1,3},{2,6},{3,1},{4,0},{5,7},{6,2},{7,5},{8,12},{9,11},{10,... | collective-permute-start | bytes 1179656 | tf_op jit(solution)/shard_map/ppermute | solution.py:76
  26.2 1.3 %collective-permute-done.5 = bf16[2,8,6144]{2,1,0:T(8,128)(2,1)S(1)} collective-permute-done((bf16[2,8,6144]{2,1,0:T(8,128)(2,1)S(1)}, bf16[2,8,6144]{2,1,0:T(8,128)(2,1)S(1)}, u32[]{:S(2)}, u32[]{:S(2)}) %collective-permute-start.5) | collective-permute-done | bytes 196640 | tf_op jit(solution)/shard_map/ppermute | solution.py:76
  27.5 2.3 %collective-permute-done.8 = bf16[2,8,6144]{2,1,0:T(8,128)(2,1)S(1)} collective-permute-done((bf16[2,8,6144]{2,1,0:T(8,128)(2,1)S(1)}, bf16[2,8,6144]{2,1,0:T(8,128)(2,1)S(1)}, u32[]{:S(2)}, u32[]{:S(2)}) %collective-permute-start.8) | collective-permute-done | bytes 196640 | tf_op jit(solution)/shard_map/ppermute | solution.py:76
  29.9 4.1 %collective-permute-done.2 = bf16[2,16,6144]{2,1,0:T(8,128)(2,1)S(1)} collective-permute-done((bf16[2,16,6144]{2,1,0:T(8,128)(2,1)S(1)}, bf16[2,16,6144]{2,1,0:T(8,128)(2,1)S(1)}, u32[]{:S(2)}, u32[]{:S(2)}) %collective-permute-start.2) | collective-permute-done | bytes 393248 | tf_op jit(solution)/shard_map/ppermute | solution.py:76
  34.0 0.1 fusion.52
  34.2 1.6 %collective-permute-start.12 = (f32[2,16,128]{2,1,0:T(8,128)S(1)}, f32[2,16,128]{2,1,0:T(8,128)S(1)}, u32[]{:S(2)}, u32[]{:S(2)}) collective-permute-start(f32[2,16,128]{2,1,0:T(8,128)S(1)} %broadcast_select_fusion), channel_id=1, source_target_pairs={{0,16},{16,0},{1,17},{17,1},{2,18},{18,2},{3,19},{19,3},{4,20},{20... | collective-permute-start | bytes 49160 | tf_op jit(solution)/shard_map/ppermute | solution.py:12
  35.9 0.4 collective-permute-start.11
  36.3 0.1 collective-permute-done.9
  36.4 0.1 maximum_bitcast_fusion.1
  36.6 0.2 pad_maximum_fusion
  36.8 11.7 %fusion.2 = f32[256,2048]{1,0:T(8,128)S(1)} fusion(bf16[256,6144]{1,0:T(8,128)(2,1)S(1)} %bitcast.90, bf16[1,6144,2048]{2,1,0:T(8,128)(2,1)} %param.10), kind=kOutput, calls=%fused_computation.3 | convolution fusion | flops 6442450944 | bytes 30408704 | tf_op jit(solution)/shard_map/dot_general | solution.py:97
  48.5 12.4 %fusion.16 = bf16[256,2048]{1,0:T(8,128)(2,1)S(1)} fusion(bf16[256,6144]{1,0:T(8,128)(2,1)S(1)} %bitcast.91, bf16[1,6144,2048]{2,1,0:T(8,128)(2,1)} %param.11, f32[256,2048]{1,0:T(8,128)S(1)} %fusion.2), kind=kOutput, calls=%fused_computation.18 | convolution fusion | flops 6445596672 | bytes 31457280 | tf_op jit(solution)/shard_map/dot_general | solution.py:98
  60.9 5.7 %fusion.19 = bf16[256,2048]{1,0:T(8,128)(2,1)S(1)} fusion(bf16[256,2048]{1,0:T(8,128)(2,1)S(1)} %fusion.16, bf16[2048,6144]{1,0:T(8,128)(2,1)} %bitcast.107), kind=kOutput, calls=%fused_computation.19 | convolution fusion | flops 2148007936 | bytes 10485760 | tf_op jit(solution)/shard_map/dot_general | solution.py:106
  66.6 5.7 %fusion.22 = bf16[256,2048]{1,0:T(8,128)(2,1)S(1)} fusion(bf16[256,2048]{1,0:T(8,128)(2,1)S(1)} %fusion.16, bf16[2048,6144]{1,0:T(8,128)(2,1)} %bitcast.108), kind=kOutput, calls=%fused_computation.20 | convolution fusion | flops 2148007936 | bytes 10485760 | tf_op jit(solution)/shard_map/dot_general | solution.py:106
  72.3 5.7 %fusion.25 = bf16[256,2048]{1,0:T(8,128)(2,1)S(1)} fusion(bf16[256,2048]{1,0:T(8,128)(2,1)S(1)} %fusion.16, bf16[2048,6144]{1,0:T(8,128)(2,1)} %bitcast.109), kind=kOutput, calls=%fused_computation.21 | convolution fusion | flops 2148007936 | bytes 10485760 | tf_op jit(solution)/shard_map/dot_general | solution.py:106
  78.0 0.1 fusion.53
  78.1 0.2 collective-permute-start.13
  78.4 0.4 collective-permute-start.17
  78.9 0.2 collective-permute-start.21
  79.1 1.0 collective-permute-done.13
  80.1 0.1 convert_add_fusion.2
  80.3 0.6 collective-permute-start.14
  80.9 0.1 convert_add_fusion.1
  81.1 1.5 %collective-permute-start.18 = (bf16[2,2,16,2048]{3,2,1,0:T(8,128)(2,1)S(1)}, bf16[2,2,16,2048]{3,2,1,0:T(8,128)(2,1)S(1)}, u32[]{:S(2)}, u32[]{:S(2)}) collective-permute-start(bf16[2,2,16,2048]{3,2,1,0:T(8,128)(2,1)S(1)} %slice.230), channel_id=1, source_target_pairs={{0,4},{1,3},{2,6},{3,1},{4,0},{5,7},{6,2},{7,5},{8,12},{9,11},{10,... | collective-permute-start | bytes 786440 | tf_op jit(solution)/shard_map/ppermute | solution.py:121
  82.6 0.1 convert_add_fusion
  82.8 0.6 collective-permute-start.22
  83.4 3.3 %collective-permute-done.14 = bf16[2,2,16,2048]{3,2,1,0:T(8,128)(2,1)S(1)} collective-permute-done((bf16[2,2,16,2048]{3,2,1,0:T(8,128)(2,1)S(1)}, bf16[2,2,16,2048]{3,2,1,0:T(8,128)(2,1)S(1)}, u32[]{:S(2)}, u32[]{:S(2)}) %collective-permute-start.14) | collective-permute-done | bytes 262176 | tf_op jit(solution)/shard_map/ppermute | solution.py:121
  86.8 1.5 %collective-permute-start.15 = (bf16[1,2,16,2048]{3,2,1,0:T(8,128)(2,1)S(1)}, bf16[1,2,16,2048]{3,2,1,0:T(8,128)(2,1)S(1)}, u32[]{:S(2)}, u32[]{:S(2)}) collective-permute-start(bf16[1,2,16,2048]{3,2,1,0:T(8,128)(2,1)S(1)} %slice.234), channel_id=1, source_target_pairs={{0,2},{1,5},{2,0},{3,7},{4,6},{5,1},{6,4},{7,3},{8,10},{9,13},{10,... | collective-permute-start | bytes 393224 | tf_op jit(solution)/shard_map/ppermute | solution.py:121
  88.3 1.9 %collective-permute-done.18 = bf16[2,2,16,2048]{3,2,1,0:T(8,128)(2,1)S(1)} collective-permute-done((bf16[2,2,16,2048]{3,2,1,0:T(8,128)(2,1)S(1)}, bf16[2,2,16,2048]{3,2,1,0:T(8,128)(2,1)S(1)}, u32[]{:S(2)}, u32[]{:S(2)}) %collective-permute-start.18) | collective-permute-done | bytes 262176 | tf_op jit(solution)/shard_map/ppermute | solution.py:121
  90.3 1.5 %collective-permute-start.19 = (bf16[1,2,16,2048]{3,2,1,0:T(8,128)(2,1)S(1)}, bf16[1,2,16,2048]{3,2,1,0:T(8,128)(2,1)S(1)}, u32[]{:S(2)}, u32[]{:S(2)}) collective-permute-start(bf16[1,2,16,2048]{3,2,1,0:T(8,128)(2,1)S(1)} %slice.233), channel_id=1, source_target_pairs={{0,2},{1,5},{2,0},{3,7},{4,6},{5,1},{6,4},{7,3},{8,10},{9,13},{10,... | collective-permute-start | bytes 393224 | tf_op jit(solution)/shard_map/ppermute | solution.py:121
  91.8 3.3 %collective-permute-done.22 = bf16[2,2,16,2048]{3,2,1,0:T(8,128)(2,1)S(1)} collective-permute-done((bf16[2,2,16,2048]{3,2,1,0:T(8,128)(2,1)S(1)}, bf16[2,2,16,2048]{3,2,1,0:T(8,128)(2,1)S(1)}, u32[]{:S(2)}, u32[]{:S(2)}) %collective-permute-start.22) | collective-permute-done | bytes 262176 | tf_op jit(solution)/shard_map/ppermute | solution.py:121
  95.2 1.5 %collective-permute-start.23 = (bf16[1,2,16,2048]{3,2,1,0:T(8,128)(2,1)S(1)}, bf16[1,2,16,2048]{3,2,1,0:T(8,128)(2,1)S(1)}, u32[]{:S(2)}, u32[]{:S(2)}) collective-permute-start(bf16[1,2,16,2048]{3,2,1,0:T(8,128)(2,1)S(1)} %slice.232), channel_id=1, source_target_pairs={{0,2},{1,5},{2,0},{3,7},{4,6},{5,1},{6,4},{7,3},{8,10},{9,13},{10,... | collective-permute-start | bytes 393224 | tf_op jit(solution)/shard_map/ppermute | solution.py:121
  96.8 1.6 %collective-permute-start.16 = (bf16[16,2048]{1,0:T(8,128)(2,1)S(1)}, bf16[16,2048]{1,0:T(8,128)(2,1)S(1)}, u32[]{:S(2)}, u32[]{:S(2)}) collective-permute-start(bf16[16,2048]{1,0:T(8,128)(2,1)S(1)} %get-tuple-element.27), channel_id=1, source_target_pairs={{0,16},{16,0},{1,17},{17,1},{2,18},{18,2},{3,19},{19,3},{4,20},{20... | collective-permute-start | bytes 196616 | tf_op jit(solution)/shard_map/ppermute | solution.py:12
  98.4 0.6 collective-permute-start.20
  99.0 1.3 %collective-permute-done.23 = bf16[1,2,16,2048]{3,2,1,0:T(8,128)(2,1)S(1)} collective-permute-done((bf16[1,2,16,2048]{3,2,1,0:T(8,128)(2,1)S(1)}, bf16[1,2,16,2048]{3,2,1,0:T(8,128)(2,1)S(1)}, u32[]{:S(2)}, u32[]{:S(2)}) %collective-permute-start.23) | collective-permute-done | bytes 131104 | tf_op jit(solution)/shard_map/ppermute | solution.py:121
  100.3 1.7 %collective-permute-start.24 = (bf16[16,2048]{1,0:T(8,128)(2,1)S(1)}, bf16[16,2048]{1,0:T(8,128)(2,1)S(1)}, u32[]{:S(2)}, u32[]{:S(2)}) collective-permute-start(bf16[16,2048]{1,0:T(8,128)(2,1)S(1)} %get-tuple-element.31), channel_id=1, source_target_pairs={{0,16},{16,0},{1,17},{17,1},{2,18},{18,2},{3,19},{19,3},{4,20},{20... | collective-permute-start | bytes 196616 | tf_op jit(solution)/shard_map/ppermute | solution.py:12
  102.0 1.8 %collective-permute-start.25 = (bf16[16,2048]{1,0:T(8,128)(2,1)S(1)}, bf16[16,2048]{1,0:T(8,128)(2,1)S(1)}, u32[]{:S(2)}, u32[]{:S(2)}) collective-permute-start(bf16[16,2048]{1,0:T(8,128)(2,1)S(1)} %get-tuple-element.28), channel_id=1, source_target_pairs={{0,24},{8,16},{16,8},{24,0},{1,25},{9,17},{17,9},{25,1},{2,26},{10... | collective-permute-start | bytes 196616 | tf_op jit(solution)/shard_map/ppermute | solution.py:134
  103.8 2.0 %collective-permute-start.26 = (bf16[16,2048]{1,0:T(8,128)(2,1)S(1)}, bf16[16,2048]{1,0:T(8,128)(2,1)S(1)}, u32[]{:S(2)}, u32[]{:S(2)}) collective-permute-start(bf16[16,2048]{1,0:T(8,128)(2,1)S(1)} %get-tuple-element.30), channel_id=1, source_target_pairs={{0,24},{8,16},{16,8},{24,0},{1,25},{9,17},{17,9},{25,1},{2,26},{10... | collective-permute-start | bytes 196616 | tf_op jit(solution)/shard_map/ppermute | solution.py:134
  105.8 1.8 %collective-permute-start.27 = (bf16[16,2048]{1,0:T(8,128)(2,1)S(1)}, bf16[16,2048]{1,0:T(8,128)(2,1)S(1)}, u32[]{:S(2)}, u32[]{:S(2)}) collective-permute-start(bf16[16,2048]{1,0:T(8,128)(2,1)S(1)} %get-tuple-element.32), channel_id=1, source_target_pairs={{0,24},{8,16},{16,8},{24,0},{1,25},{9,17},{17,9},{25,1},{2,26},{10... | collective-permute-start | bytes 196616 | tf_op jit(solution)/shard_map/ppermute | solution.py:134
  107.6 1.3 %collective-permute-done.25 = bf16[16,2048]{1,0:T(8,128)(2,1)S(1)} collective-permute-done((bf16[16,2048]{1,0:T(8,128)(2,1)S(1)}, bf16[16,2048]{1,0:T(8,128)(2,1)S(1)}, u32[]{:S(2)}, u32[]{:S(2)}) %collective-permute-start.25) | collective-permute-done | bytes 65568 | tf_op jit(solution)/shard_map/ppermute | solution.py:134
  108.9 0.9 collective-permute-done.26
  109.8 2.9 %collective-permute-done.27 = bf16[16,2048]{1,0:T(8,128)(2,1)S(1)} collective-permute-done((bf16[16,2048]{1,0:T(8,128)(2,1)S(1)}, bf16[16,2048]{1,0:T(8,128)(2,1)S(1)}, u32[]{:S(2)}, u32[]{:S(2)}) %collective-permute-start.27) | collective-permute-done | bytes 65568 | tf_op jit(solution)/shard_map/ppermute | solution.py:134
  112.7 2.7 %fusion.12 = bf16[1,128,6144]{2,1,0:T(8,128)(2,1)} fusion(f32[2,16,128]{2,1,0:T(8,128)S(1)} %collective-permute-done.12, bf16[64,6144]{1,0:T(8,128)(2,1)S(1)} %collective-permute-done.11, bf16[64,6144]{1,0:T(8,128)(2,1)S(1)} %collective-permute-done, bf16[1,16,6144]{2,1,0:T(8,128)(2,1)S(1)} %maximum_bitcast_fusion.3, ...), kind=kOutput, calls=%fused_computation.14 | convolution fusion | flops 306905088 | bytes 3555328 | tf_op jit(solution)/shard_map/ect,ecd->td/dot_general | solution.py:138
  (59 shorter events, 1.4 us)
Async XLA Ops:
  0.0 9.7 %copy-start = (bf16[1,128,6144]{2,1,0:T(8,128)(2,1)S(1)}, bf16[1,128,6144]{2,1,0:T(8,128)(2,1)}, u32[]{:S(2)}) copy-start(bf16[1,128,6144]{2,1,0:T(8,128)(2,1)} %param.8) | copy-start | bytes 4718596
  0.0 7.5 %copy-start.1 = (bf16[1,6144]{1,0:T(2,128)(2,1)S(1)}, bf16[1,6144]{1,0:T(2,128)(2,1)}, u32[]{:S(2)}) copy-start(bf16[1,6144]{1,0:T(2,128)(2,1)} %param.9) | copy-start | bytes 36868
  2.7 9.5 %copy-start.3 = (f32[1,1,2,16]{3,2,1,0:T(2,128)S(1)}, f32[1,1,2,16]{3,2,1,0:T(2,128)}, u32[]{:S(2)}) copy-start(f32[1,1,2,16]{3,2,1,0:T(2,128)} %param.15) | copy-start | bytes 388
  2.7 9.5 %copy-start.4 = (s32[1,1,2]{2,1,0:T(1,128)S(1)}, s32[1,1,2]{2,1,0:T(1,128)}, u32[]{:S(2)}) copy-start(s32[1,1,2]{2,1,0:T(1,128)} %param.14) | copy-start | bytes 28
  2.7 9.6 %copy-start.2 = (s32[1,1,2,16]{3,2,1,0:T(2,128)S(1)}, s32[1,1,2,16]{3,2,1,0:T(2,128)}, u32[]{:S(2)}) copy-start(s32[1,1,2,16]{3,2,1,0:T(2,128)} %param.13) | copy-start | bytes 388
  3.4 12.1 %collective-permute-start.6 = (bf16[8,6144]{1,0:T(8,128)(2,1)}, bf16[8,6144]{1,0:T(8,128)(2,1)S(1)}, u32[]{:S(2)}, u32[]{:S(2)}) collective-permute-start(bf16[8,6144]{1,0:T(8,128)(2,1)} %get-tuple-element.26), channel_id=1, source_target_pairs={{0,8},{8,0},{1,9},{9,1},{2,10},{10,2},{3,11},{11,3},{4,12},{12,4},... | collective-permute-start | bytes 294920 | tf_op jit(solution)/shard_map/ppermute | solution.py:12
  7.4 9.3 %collective-permute-start.3 = (bf16[8,6144]{1,0:T(8,128)(2,1)S(1)}, bf16[8,6144]{1,0:T(8,128)(2,1)S(1)}, u32[]{:S(2)}, u32[]{:S(2)}) collective-permute-start(bf16[8,6144]{1,0:T(8,128)(2,1)S(1)} %get-tuple-element.25), channel_id=1, source_target_pairs={{0,8},{8,0},{1,9},{9,1},{2,10},{10,2},{3,11},{11,3},{4,12},{12,4},... | collective-permute-start | bytes 294920 | tf_op jit(solution)/shard_map/ppermute | solution.py:12
  7.8 16.3 %collective-permute-start.1 = (bf16[1,16,6144]{2,1,0:T(8,128)(2,1)S(1)}, bf16[1,16,6144]{2,1,0:T(8,128)(2,1)S(1)}, u32[]{:S(2)}, u32[]{:S(2)}) collective-permute-start(bf16[1,16,6144]{2,1,0:T(8,128)(2,1)S(1)} %fusion.31), channel_id=1, source_target_pairs={{0,2},{1,5},{2,0},{3,7},{4,6},{5,1},{6,4},{7,3},{8,10},{9,13},{10,... | collective-permute-start | bytes 589832 | tf_op jit(solution)/shard_map/ppermute | solution.py:76
  10.7 26.1 %collective-permute-start = (bf16[64,6144]{1,0:T(8,128)(2,1)}, bf16[64,6144]{1,0:T(8,128)(2,1)S(1)}, u32[]{:S(2)}, u32[]{:S(2)}) collective-permute-start(bf16[64,6144]{1,0:T(8,128)(2,1)} %get-tuple-element.15), channel_id=1, source_target_pairs={{0,16},{16,0},{1,17},{17,1},{2,18},{18,2},{3,19},{19,3},{4,20},{20... | collective-permute-start | bytes 2359304 | tf_op jit(solution)/shard_map/ppermute | solution.py:12
  17.0 4.7 %collective-permute-start.4 = (bf16[1,8,6144]{2,1,0:T(8,128)(2,1)S(1)}, bf16[1,8,6144]{2,1,0:T(8,128)(2,1)S(1)}, u32[]{:S(2)}, u32[]{:S(2)}) collective-permute-start(bf16[1,8,6144]{2,1,0:T(8,128)(2,1)S(1)} %get-tuple-element.33), channel_id=1, source_target_pairs={{0,2},{1,5},{2,0},{3,7},{4,6},{5,1},{6,4},{7,3},{8,10},{9,13},{10,... | collective-permute-start | bytes 294920 | tf_op jit(solution)/shard_map/ppermute | solution.py:76
  18.7 5.3 %collective-permute-start.7 = (bf16[1,8,6144]{2,1,0:T(8,128)(2,1)S(1)}, bf16[1,8,6144]{2,1,0:T(8,128)(2,1)S(1)}, u32[]{:S(2)}, u32[]{:S(2)}) collective-permute-start(bf16[1,8,6144]{2,1,0:T(8,128)(2,1)S(1)} %get-tuple-element.34), channel_id=1, source_target_pairs={{0,2},{1,5},{2,0},{3,7},{4,6},{5,1},{6,4},{7,3},{8,10},{9,13},{10,... | collective-permute-start | bytes 294920 | tf_op jit(solution)/shard_map/ppermute | solution.py:76
  21.7 5.7 %collective-permute-start.5 = (bf16[2,8,6144]{2,1,0:T(8,128)(2,1)S(1)}, bf16[2,8,6144]{2,1,0:T(8,128)(2,1)S(1)}, u32[]{:S(2)}, u32[]{:S(2)}) collective-permute-start(bf16[2,8,6144]{2,1,0:T(8,128)(2,1)S(1)} %pad_maximum_fusion.3), channel_id=1, source_target_pairs={{0,4},{1,3},{2,6},{3,1},{4,0},{5,7},{6,2},{7,5},{8,12},{9,11},{10,... | collective-permute-start | bytes 589832 | tf_op jit(solution)/shard_map/ppermute | solution.py:76
  24.0 5.7 %collective-permute-start.8 = (bf16[2,8,6144]{2,1,0:T(8,128)(2,1)S(1)}, bf16[2,8,6144]{2,1,0:T(8,128)(2,1)S(1)}, u32[]{:S(2)}, u32[]{:S(2)}) collective-permute-start(bf16[2,8,6144]{2,1,0:T(8,128)(2,1)S(1)} %pad_maximum_fusion.4), channel_id=1, source_target_pairs={{0,4},{1,3},{2,6},{3,1},{4,0},{5,7},{6,2},{7,5},{8,12},{9,11},{10,... | collective-permute-start | bytes 589832 | tf_op jit(solution)/shard_map/ppermute | solution.py:76
  24.2 9.8 %collective-permute-start.2 = (bf16[2,16,6144]{2,1,0:T(8,128)(2,1)S(1)}, bf16[2,16,6144]{2,1,0:T(8,128)(2,1)S(1)}, u32[]{:S(2)}, u32[]{:S(2)}) collective-permute-start(bf16[2,16,6144]{2,1,0:T(8,128)(2,1)S(1)} %pad_maximum_fusion.2), channel_id=1, source_target_pairs={{0,4},{1,3},{2,6},{3,1},{4,0},{5,7},{6,2},{7,5},{8,12},{9,11},{10,... | collective-permute-start | bytes 1179656 | tf_op jit(solution)/shard_map/ppermute | solution.py:76
  29.8 6.5 %collective-permute-start.10 = (bf16[4,16,6144]{2,1,0:T(8,128)(2,1)S(1)}, bf16[4,16,6144]{2,1,0:T(8,128)(2,1)S(1)}, u32[]{:S(2)}, u32[]{:S(2)}) collective-permute-start(bf16[4,16,6144]{2,1,0:T(8,128)(2,1)S(1)} %maximum_maximum_fusion), channel_id=1, source_target_pairs={{0,1},{1,0},{2,3},{3,2},{4,5},{5,4},{6,7},{7,6},{8,9},{9,8},{10,11... | collective-permute-start | bytes 2359304 | tf_op jit(solution)/shard_map/ppermute | solution.py:12
  34.1 2.4 %collective-permute-start.9 = (bf16[4,16,6144]{2,1,0:T(8,128)(2,1)S(1)}, bf16[4,16,6144]{2,1,0:T(8,128)(2,1)S(1)}, u32[]{:S(2)}, u32[]{:S(2)}) collective-permute-start(bf16[4,16,6144]{2,1,0:T(8,128)(2,1)S(1)} %get-tuple-element.24), channel_id=1, source_target_pairs={{0,1},{1,0},{2,3},{3,2},{4,5},{5,4},{6,7},{7,6},{8,9},{9,8},{10,11... | collective-permute-start | bytes 2359304 | tf_op jit(solution)/shard_map/ppermute | solution.py:12
  34.2 43.8 %collective-permute-start.12 = (f32[2,16,128]{2,1,0:T(8,128)S(1)}, f32[2,16,128]{2,1,0:T(8,128)S(1)}, u32[]{:S(2)}, u32[]{:S(2)}) collective-permute-start(f32[2,16,128]{2,1,0:T(8,128)S(1)} %broadcast_select_fusion), channel_id=1, source_target_pairs={{0,16},{16,0},{1,17},{17,1},{2,18},{18,2},{3,19},{19,3},{4,20},{20... | collective-permute-start | bytes 49160 | tf_op jit(solution)/shard_map/ppermute | solution.py:12
  35.9 42.2 %collective-permute-start.11 = (bf16[64,6144]{1,0:T(8,128)(2,1)S(1)}, bf16[64,6144]{1,0:T(8,128)(2,1)S(1)}, u32[]{:S(2)}, u32[]{:S(2)}) collective-permute-start(bf16[64,6144]{1,0:T(8,128)(2,1)S(1)} %get-tuple-element.16), channel_id=1, source_target_pairs={{0,16},{16,0},{1,17},{17,1},{2,18},{18,2},{3,19},{19,3},{4,20},{20... | collective-permute-start | bytes 2359304 | tf_op jit(solution)/shard_map/ppermute | solution.py:12
  78.1 2.0 %collective-permute-start.13 = (bf16[4,2,16,2048]{3,2,1,0:T(8,128)(2,1)S(1)}, bf16[4,2,16,2048]{3,2,1,0:T(8,128)(2,1)S(1)}, u32[]{:S(2)}, u32[]{:S(2)}) collective-permute-start(bf16[4,2,16,2048]{3,2,1,0:T(8,128)(2,1)S(1)} %bitcast.102), channel_id=1, source_target_pairs={{0,1},{1,0},{2,3},{3,2},{4,5},{5,4},{6,7},{7,6},{8,9},{9,8},{10,11... | collective-permute-start | bytes 1572872 | tf_op jit(solution)/shard_map/ppermute | solution.py:12
  78.4 2.5 %collective-permute-start.17 = (bf16[4,2,16,2048]{3,2,1,0:T(8,128)(2,1)S(1)}, bf16[4,2,16,2048]{3,2,1,0:T(8,128)(2,1)S(1)}, u32[]{:S(2)}, u32[]{:S(2)}) collective-permute-start(bf16[4,2,16,2048]{3,2,1,0:T(8,128)(2,1)S(1)} %bitcast.101), channel_id=1, source_target_pairs={{0,1},{1,0},{2,3},{3,2},{4,5},{5,4},{6,7},{7,6},{8,9},{9,8},{10,11... | collective-permute-start | bytes 1572872 | tf_op jit(solution)/shard_map/ppermute | solution.py:12
  78.9 3.7 %collective-permute-start.21 = (bf16[4,2,16,2048]{3,2,1,0:T(8,128)(2,1)S(1)}, bf16[4,2,16,2048]{3,2,1,0:T(8,128)(2,1)S(1)}, u32[]{:S(2)}, u32[]{:S(2)}) collective-permute-start(bf16[4,2,16,2048]{3,2,1,0:T(8,128)(2,1)S(1)} %bitcast.100), channel_id=1, source_target_pairs={{0,1},{1,0},{2,3},{3,2},{4,5},{5,4},{6,7},{7,6},{8,9},{9,8},{10,11... | collective-permute-start | bytes 1572872 | tf_op jit(solution)/shard_map/ppermute | solution.py:12
  80.3 6.4 %collective-permute-start.14 = (bf16[2,2,16,2048]{3,2,1,0:T(8,128)(2,1)S(1)}, bf16[2,2,16,2048]{3,2,1,0:T(8,128)(2,1)S(1)}, u32[]{:S(2)}, u32[]{:S(2)}) collective-permute-start(bf16[2,2,16,2048]{3,2,1,0:T(8,128)(2,1)S(1)} %slice.231), channel_id=1, source_target_pairs={{0,4},{1,3},{2,6},{3,1},{4,0},{5,7},{6,2},{7,5},{8,12},{9,11},{10,... | collective-permute-start | bytes 786440 | tf_op jit(solution)/shard_map/ppermute | solution.py:121
  81.1 9.1 %collective-permute-start.18 = (bf16[2,2,16,2048]{3,2,1,0:T(8,128)(2,1)S(1)}, bf16[2,2,16,2048]{3,2,1,0:T(8,128)(2,1)S(1)}, u32[]{:S(2)}, u32[]{:S(2)}) collective-permute-start(bf16[2,2,16,2048]{3,2,1,0:T(8,128)(2,1)S(1)} %slice.230), channel_id=1, source_target_pairs={{0,4},{1,3},{2,6},{3,1},{4,0},{5,7},{6,2},{7,5},{8,12},{9,11},{10,... | collective-permute-start | bytes 786440 | tf_op jit(solution)/shard_map/ppermute | solution.py:121
  82.8 12.4 %collective-permute-start.22 = (bf16[2,2,16,2048]{3,2,1,0:T(8,128)(2,1)S(1)}, bf16[2,2,16,2048]{3,2,1,0:T(8,128)(2,1)S(1)}, u32[]{:S(2)}, u32[]{:S(2)}) collective-permute-start(bf16[2,2,16,2048]{3,2,1,0:T(8,128)(2,1)S(1)} %slice.229), channel_id=1, source_target_pairs={{0,4},{1,3},{2,6},{3,1},{4,0},{5,7},{6,2},{7,5},{8,12},{9,11},{10,... | collective-permute-start | bytes 786440 | tf_op jit(solution)/shard_map/ppermute | solution.py:121
  86.8 9.9 %collective-permute-start.15 = (bf16[1,2,16,2048]{3,2,1,0:T(8,128)(2,1)S(1)}, bf16[1,2,16,2048]{3,2,1,0:T(8,128)(2,1)S(1)}, u32[]{:S(2)}, u32[]{:S(2)}) collective-permute-start(bf16[1,2,16,2048]{3,2,1,0:T(8,128)(2,1)S(1)} %slice.234), channel_id=1, source_target_pairs={{0,2},{1,5},{2,0},{3,7},{4,6},{5,1},{6,4},{7,3},{8,10},{9,13},{10,... | collective-permute-start | bytes 393224 | tf_op jit(solution)/shard_map/ppermute | solution.py:121
  90.3 8.0 %collective-permute-start.19 = (bf16[1,2,16,2048]{3,2,1,0:T(8,128)(2,1)S(1)}, bf16[1,2,16,2048]{3,2,1,0:T(8,128)(2,1)S(1)}, u32[]{:S(2)}, u32[]{:S(2)}) collective-permute-start(bf16[1,2,16,2048]{3,2,1,0:T(8,128)(2,1)S(1)} %slice.233), channel_id=1, source_target_pairs={{0,2},{1,5},{2,0},{3,7},{4,6},{5,1},{6,4},{7,3},{8,10},{9,13},{10,... | collective-permute-start | bytes 393224 | tf_op jit(solution)/shard_map/ppermute | solution.py:121
  95.2 5.0 %collective-permute-start.23 = (bf16[1,2,16,2048]{3,2,1,0:T(8,128)(2,1)S(1)}, bf16[1,2,16,2048]{3,2,1,0:T(8,128)(2,1)S(1)}, u32[]{:S(2)}, u32[]{:S(2)}) collective-permute-start(bf16[1,2,16,2048]{3,2,1,0:T(8,128)(2,1)S(1)} %slice.232), channel_id=1, source_target_pairs={{0,2},{1,5},{2,0},{3,7},{4,6},{5,1},{6,4},{7,3},{8,10},{9,13},{10,... | collective-permute-start | bytes 393224 | tf_op jit(solution)/shard_map/ppermute | solution.py:121
  96.8 9.1 %collective-permute-start.16 = (bf16[16,2048]{1,0:T(8,128)(2,1)S(1)}, bf16[16,2048]{1,0:T(8,128)(2,1)S(1)}, u32[]{:S(2)}, u32[]{:S(2)}) collective-permute-start(bf16[16,2048]{1,0:T(8,128)(2,1)S(1)} %get-tuple-element.27), channel_id=1, source_target_pairs={{0,16},{16,0},{1,17},{17,1},{2,18},{18,2},{3,19},{19,3},{4,20},{20... | collective-permute-start | bytes 196616 | tf_op jit(solution)/shard_map/ppermute | solution.py:12
  98.4 9.2 %collective-permute-start.20 = (bf16[16,2048]{1,0:T(8,128)(2,1)S(1)}, bf16[16,2048]{1,0:T(8,128)(2,1)S(1)}, u32[]{:S(2)}, u32[]{:S(2)}) collective-permute-start(bf16[16,2048]{1,0:T(8,128)(2,1)S(1)} %get-tuple-element.29), channel_id=1, source_target_pairs={{0,16},{16,0},{1,17},{17,1},{2,18},{18,2},{3,19},{19,3},{4,20},{20... | collective-permute-start | bytes 196616 | tf_op jit(solution)/shard_map/ppermute | solution.py:12
  100.3 7.3 %collective-permute-start.24 = (bf16[16,2048]{1,0:T(8,128)(2,1)S(1)}, bf16[16,2048]{1,0:T(8,128)(2,1)S(1)}, u32[]{:S(2)}, u32[]{:S(2)}) collective-permute-start(bf16[16,2048]{1,0:T(8,128)(2,1)S(1)} %get-tuple-element.31), channel_id=1, source_target_pairs={{0,16},{16,0},{1,17},{17,1},{2,18},{18,2},{3,19},{19,3},{4,20},{20... | collective-permute-start | bytes 196616 | tf_op jit(solution)/shard_map/ppermute | solution.py:12
  102.0 6.9 %collective-permute-start.25 = (bf16[16,2048]{1,0:T(8,128)(2,1)S(1)}, bf16[16,2048]{1,0:T(8,128)(2,1)S(1)}, u32[]{:S(2)}, u32[]{:S(2)}) collective-permute-start(bf16[16,2048]{1,0:T(8,128)(2,1)S(1)} %get-tuple-element.28), channel_id=1, source_target_pairs={{0,24},{8,16},{16,8},{24,0},{1,25},{9,17},{17,9},{25,1},{2,26},{10... | collective-permute-start | bytes 196616 | tf_op jit(solution)/shard_map/ppermute | solution.py:134
  103.8 6.1 %collective-permute-start.26 = (bf16[16,2048]{1,0:T(8,128)(2,1)S(1)}, bf16[16,2048]{1,0:T(8,128)(2,1)S(1)}, u32[]{:S(2)}, u32[]{:S(2)}) collective-permute-start(bf16[16,2048]{1,0:T(8,128)(2,1)S(1)} %get-tuple-element.30), channel_id=1, source_target_pairs={{0,24},{8,16},{16,8},{24,0},{1,25},{9,17},{17,9},{25,1},{2,26},{10... | collective-permute-start | bytes 196616 | tf_op jit(solution)/shard_map/ppermute | solution.py:134
  105.8 6.9 %collective-permute-start.27 = (bf16[16,2048]{1,0:T(8,128)(2,1)S(1)}, bf16[16,2048]{1,0:T(8,128)(2,1)S(1)}, u32[]{:S(2)}, u32[]{:S(2)}) collective-permute-start(bf16[16,2048]{1,0:T(8,128)(2,1)S(1)} %get-tuple-element.32), channel_id=1, source_target_pairs={{0,24},{8,16},{16,8},{24,0},{1,25},{9,17},{17,9},{25,1},{2,26},{10... | collective-permute-start | bytes 196616 | tf_op jit(solution)/shard_map/ppermute | solution.py:134

commit v12 on v7

--- a/solution.py
+++ b/solution.py
@@ -77,7 +77,7 @@
             held = jnp.concatenate([held, arrived])
         return held
 
-    splits = 2 if capacity % 2 == 0 else 1
+    splits = 1
     chip_rows = [doubled(normalized(lax.dynamic_index_in_dim(raw, ex_me, 0, keepdims=False)))]
     for k in range(1, n_ex):
         outgoing = lax.dynamic_index_in_dim(raw, (ex_me + k) % n_ex, 0, keepdims=False)

time: 111 us -> 114 us (1.027)
  starting transfers between devices: 26.7 us -> 22.2 us
  waiting for transfers between devices: 33.5 us -> 37.5 us
  other arithmetic: 2.35 us -> 6.12 us
    ppermute x11 -> x10, waiting for transfers between devices: 5.19 us -> 8.03 us  [shifted(): return lax.ppermute(block, axes, route)]
    ppermute x6 -> x4, starting transfers between devices: 6.99 us -> 4.76 us  [doubled(): lax.ppermute(held, ('chip', 'core'), chip_route(n_chip, n_core, stage, le...]
    another operation x2, other arithmetic: 0.18 us -> 2.02 us  [body(): jnp.stack(core_rows[q], axis=1)]
    ppermute x11 -> x10, starting transfers between devices: 11.6 us -> 9.99 us  [shifted(): return lax.ppermute(block, axes, route)]
    another operation x2, other arithmetic: 0.35 us -> 1.78 us  [body(): jnp.stack([jnp.stack(core_rows[q], axis=1) for q in range(n_core)])]
    ppermute x6 -> x4, waiting for transfers between devices: 11.6 us -> 12.9 us  [doubled(): lax.ppermute(held, ('chip', 'core'), chip_route(n_chip, n_core, stage, le...]
  transfers between devices with their start and end apart: 23 -> 20, of which waited for: 15 -> 10; matrix products, arithmetic and copies ran while one was open for 40% -> 42% of each run, Pallas kernels for 0% -> 0%
where the time goes in v12:
time: 114 us
  matrix products  44.5 us (39%)
  waiting for transfers between devices  37.5 us (33%)
  starting transfers between devices  22.2 us (19%)
  other arithmetic  6.12 us (5%)
  local copies, waits for them, and re-layouts  2.86 us (3%)
    dot_general x2, matrix products, body(): jnp.dot(activated, cols, preferred_element_type=jnp.float32)  16 us
    ppermute x4, waiting for transfers between devices, doubled(): lax.ppermute(held, ('chip', 'core'), chip_route(n_chip, n_core, stage, le...  12.9 us
    ppermute x4, waiting for transfers between devices, body(): lax.ppermute(sent, ('chip', 'core'), chip_route(n_chip, n_core, stage, le...  12.7 us
    dot_general x1, matrix products, body(): up_part = jnp.dot(flat_rows, up_cols, preferred_element_type=jnp.float32)  12.4 us
    dot_general x1, matrix products, body(): jnp.dot(flat_rows, gate_cols, preferred_element_type=jnp.float32)  11.7 us
    ppermute x10, starting transfers between devices, shifted(): return lax.ppermute(block, axes, route)  9.99 us
    ppermute x10, waiting for transfers between devices, shifted(): return lax.ppermute(block, axes, route)  8.03 us
    ppermute x4, starting transfers between devices, doubled(): lax.ppermute(held, ('chip', 'core'), chip_route(n_chip, n_core, stage, le...  4.76 us
  transfers between devices with their start and end apart: 20, of which 10 were waited for; matrix products, arithmetic and copies ran while one was open for 42% of the time, Pallas kernels for 0%

profile of v12, /device:TPU:0, one launch (start us, length us, event | category | flops | bytes accessed | tf_op | source)
XLA Modules:
  0.0 113.5 jit_solution(7261873381633688349)
XLA Ops:
  0.0 0.9 eq.34
  0.9 1.8 %convolution_convert_fusion = bf16[32,6144]{1,0:T(8,128)(2,1)S(1)} fusion(bf16[1,128,6144]{2,1,0:T(8,128)(2,1)} %param.8, s32[32]{0:T(128)S(1)} %eq.34), kind=kOutput, calls=%fused_computation.13 | convolution fusion | flops 50532352 | bytes 1966208 | tf_op jit(solution)/shard_map/dot_general | solution.py:63
  2.7 0.2 fusion.24
  2.9 0.1 fusion.26
  3.0 3.0 %collective-permute-start.1 = (bf16[1,16,6144]{2,1,0:T(8,128)(2,1)S(1)}, bf16[1,16,6144]{2,1,0:T(8,128)(2,1)S(1)}, u32[]{:S(2)}, u32[]{:S(2)}) collective-permute-start(bf16[1,16,6144]{2,1,0:T(8,128)(2,1)S(1)} %fusion.26), channel_id=1, source_target_pairs={{0,2},{1,5},{2,0},{3,7},{4,6},{5,1},{6,4},{7,3},{8,10},{9,13},{10,... | collective-permute-start | bytes 589832 | tf_op jit(solution)/shard_map/ppermute | solution.py:76
  6.1 2.7 %collective-permute-start.3 = (bf16[16,6144]{1,0:T(8,128)(2,1)S(1)}, bf16[16,6144]{1,0:T(8,128)(2,1)S(1)}, u32[]{:S(2)}, u32[]{:S(2)}) collective-permute-start(bf16[16,6144]{1,0:T(8,128)(2,1)S(1)} %dynamic-slice_bitcast_fusion), channel_id=1, source_target_pairs={{0,8},{8,0},{1,9},{9,1},{2,10},{10,2},{3,11},{11,3},{4,12},{12,4},... | collective-permute-start | bytes 589832 | tf_op jit(solution)/shard_map/ppermute | solution.py:12
  8.7 1.0 slice_bitcast_fusion.1
  9.8 1.5 %collective-permute-start = (bf16[64,6144]{1,0:T(8,128)(2,1)}, bf16[64,6144]{1,0:T(8,128)(2,1)S(1)}, u32[]{:S(2)}, u32[]{:S(2)}) collective-permute-start(bf16[64,6144]{1,0:T(8,128)(2,1)} %get-tuple-element.19), channel_id=1, source_target_pairs={{0,16},{16,0},{1,17},{17,1},{2,18},{18,2},{3,19},{19,3},{4,20},{20... | collective-permute-start | bytes 2359304 | tf_op jit(solution)/shard_map/ppermute | solution.py:12
  11.3 6.4 %collective-permute-done.3 = bf16[16,6144]{1,0:T(8,128)(2,1)S(1)} collective-permute-done((bf16[16,6144]{1,0:T(8,128)(2,1)S(1)}, bf16[16,6144]{1,0:T(8,128)(2,1)S(1)}, u32[]{:S(2)}, u32[]{:S(2)}) %collective-permute-start.3) | collective-permute-done | bytes 196640 | tf_op jit(solution)/shard_map/ppermute | solution.py:12
  17.7 0.2 fusion.27
  17.9 0.9 fusion.35
  18.7 1.6 %collective-permute-start.4 = (bf16[1,16,6144]{2,1,0:T(8,128)(2,1)S(1)}, bf16[1,16,6144]{2,1,0:T(8,128)(2,1)S(1)}, u32[]{:S(2)}, u32[]{:S(2)}) collective-permute-start(bf16[1,16,6144]{2,1,0:T(8,128)(2,1)S(1)} %fusion.35), channel_id=1, source_target_pairs={{0,2},{1,5},{2,0},{3,7},{4,6},{5,1},{6,4},{7,3},{8,10},{9,13},{10,... | collective-permute-start | bytes 589832 | tf_op jit(solution)/shard_map/ppermute | solution.py:76
  20.3 0.0 collective-permute-done.1
  20.4 0.1 collective-permute-start.2
  20.4 6.1 %collective-permute-done.4 = bf16[1,16,6144]{2,1,0:T(8,128)(2,1)S(1)} collective-permute-done((bf16[1,16,6144]{2,1,0:T(8,128)(2,1)S(1)}, bf16[1,16,6144]{2,1,0:T(8,128)(2,1)S(1)}, u32[]{:S(2)}, u32[]{:S(2)}) %collective-permute-start.4) | collective-permute-done | bytes 196640 | tf_op jit(solution)/shard_map/ppermute | solution.py:76
  26.6 0.0 copy-start.4
  26.6 0.0 copy-start.5
  26.6 0.0 copy-start.3
  26.6 0.1 collective-permute-start.5
  26.7 1.5 %collective-permute-done.2 = bf16[2,16,6144]{2,1,0:T(8,128)(2,1)S(1)} collective-permute-done((bf16[2,16,6144]{2,1,0:T(8,128)(2,1)S(1)}, bf16[2,16,6144]{2,1,0:T(8,128)(2,1)S(1)}, u32[]{:S(2)}, u32[]{:S(2)}) %collective-permute-start.2) | collective-permute-done | bytes 393248 | tf_op jit(solution)/shard_map/ppermute | solution.py:76
  28.2 1.0 fusion.43
  29.2 0.0 collective-permute-start.6
  29.2 5.3 %collective-permute-done.5 = bf16[2,16,6144]{2,1,0:T(8,128)(2,1)S(1)} collective-permute-done((bf16[2,16,6144]{2,1,0:T(8,128)(2,1)S(1)}, bf16[2,16,6144]{2,1,0:T(8,128)(2,1)S(1)}, u32[]{:S(2)}, u32[]{:S(2)}) %collective-permute-start.5) | collective-permute-done | bytes 393248 | tf_op jit(solution)/shard_map/ppermute | solution.py:76
  34.5 1.0 fusion.42
  35.5 0.0 collective-permute-start.7
  35.5 0.1 compare_select_fusion.6
  35.6 0.1 fusion.36
  35.7 0.6 gather_fusion
  36.3 0.1 broadcast_select_fusion
  36.3 1.5 %collective-permute-start.9 = (f32[2,16,128]{2,1,0:T(8,128)S(1)}, f32[2,16,128]{2,1,0:T(8,128)S(1)}, u32[]{:S(2)}, u32[]{:S(2)}) collective-permute-start(f32[2,16,128]{2,1,0:T(8,128)S(1)} %broadcast_select_fusion), channel_id=1, source_target_pairs={{0,16},{16,0},{1,17},{17,1},{2,18},{18,2},{3,19},{19,3},{4,20},{20... | collective-permute-start | bytes 49160 | tf_op jit(solution)/shard_map/ppermute | solution.py:12
  37.9 0.5 collective-permute-start.8
  38.4 0.0 collective-permute-done.6
  38.4 0.0 collective-permute-done.7
  38.4 1.5 %maximum_bitcast_fusion.1 = bf16[1,4,2,16,6144]{4,3,2,1,0:T(8,128)(2,1)S(1)} fusion(bf16[4,1,16,6144]{3,2,1,0:T(8,128)(2,1)} %bitcast.11, bf16[4,1,16,6144]{3,2,1,0:T(8,128)(2,1)} %bitcast.10), kind=kLoop, calls=%fused_computation.20 | loop fusion | flops 786432 | bytes 3145728 | tf_op jit(solution)/shard_map/stack | solution.py:93
  39.9 0.3 pad_maximum_fusion
  40.2 0.0 collective-permute-done
  40.2 11.7 %fusion.2 = f32[256,2048]{1,0:T(8,128)S(1)} fusion(bf16[256,6144]{1,0:T(8,128)(2,1)S(1)} %bitcast.78, bf16[1,6144,2048]{2,1,0:T(8,128)(2,1)} %param.10), kind=kOutput, calls=%fused_computation.3 | convolution fusion | flops 6442450944 | bytes 30408704 | tf_op jit(solution)/shard_map/dot_general | solution.py:97
  51.8 12.4 %fusion.20 = bf16[256,2048]{1,0:T(8,128)(2,1)S(1)} fusion(bf16[256,6144]{1,0:T(8,128)(2,1)S(1)} %bitcast.79, bf16[1,6144,2048]{2,1,0:T(8,128)(2,1)} %param.11, f32[256,2048]{1,0:T(8,128)S(1)} %fusion.2), kind=kOutput, calls=%fused_computation.18 | convolution fusion | flops 6445596672 | bytes 31457280 | tf_op jit(solution)/shard_map/dot_general | solution.py:98
  64.2 8.0 %fusion.11 = bf16[256,3072]{1,0:T(8,128)(2,1)S(1)} fusion(bf16[256,2048]{1,0:T(8,128)(2,1)S(1)} %fusion.20, bf16[2048,6144]{1,0:T(8,128)(2,1)} %bitcast.91), kind=kOutput, calls=%fused_computation.14 | convolution fusion | flops 3222011904 | bytes 15204352 | tf_op jit(solution)/shard_map/dot_general | solution.py:106
  72.2 0.0 collective-permute-done.9
  72.3 0.1 fusion.44
  72.4 0.1 collective-permute-start.10
  72.5 8.0 %fusion.14 = bf16[256,3072]{1,0:T(8,128)(2,1)S(1)} fusion(bf16[256,2048]{1,0:T(8,128)(2,1)S(1)} %fusion.20, bf16[2048,6144]{1,0:T(8,128)(2,1)} %bitcast.92), kind=kOutput, calls=%fused_computation.15 | convolution fusion | flops 3222011904 | bytes 15204352 | tf_op jit(solution)/shard_map/dot_general | solution.py:106
  80.5 0.1 fusion.45
  80.6 0.6 collective-permute-start.14
  81.1 0.2 convert_add_fusion.1
  81.4 0.1 collective-permute-start.11
  81.5 1.6 %collective-permute-done.14 = bf16[4,2,16,3072]{3,2,1,0:T(8,128)(2,1)S(1)} collective-permute-done((bf16[4,2,16,3072]{3,2,1,0:T(8,128)(2,1)S(1)}, bf16[4,2,16,3072]{3,2,1,0:T(8,128)(2,1)S(1)}, u32[]{:S(2)}, u32[]{:S(2)}) %collective-permute-start.14) | collective-permute-done | bytes 786464 | tf_op jit(solution)/shard_map/ppermute | solution.py:12
  83.1 0.2 convert_add_fusion
  83.3 0.5 collective-permute-start.15
  83.8 5.4 %collective-permute-done.11 = bf16[2,2,16,3072]{3,2,1,0:T(8,128)(2,1)S(1)} collective-permute-done((bf16[2,2,16,3072]{3,2,1,0:T(8,128)(2,1)S(1)}, bf16[2,2,16,3072]{3,2,1,0:T(8,128)(2,1)S(1)}, u32[]{:S(2)}, u32[]{:S(2)}) %collective-permute-start.11) | collective-permute-done | bytes 393248 | tf_op jit(solution)/shard_map/ppermute | solution.py:121
  89.2 0.1 slice_add_fusion.1
  89.3 1.6 %collective-permute-start.12 = (bf16[1,2,16,3072]{3,2,1,0:T(8,128)(2,1)S(1)}, bf16[1,2,16,3072]{3,2,1,0:T(8,128)(2,1)S(1)}, u32[]{:S(2)}, u32[]{:S(2)}) collective-permute-start(bf16[1,2,16,3072]{3,2,1,0:T(8,128)(2,1)S(1)} %slice.151), channel_id=1, source_target_pairs={{0,2},{1,5},{2,0},{3,7},{4,6},{5,1},{6,4},{7,3},{8,10},{9,13},{10,... | collective-permute-start | bytes 589832 | tf_op jit(solution)/shard_map/ppermute | solution.py:121
  90.9 4.8 %collective-permute-done.15 = bf16[2,2,16,3072]{3,2,1,0:T(8,128)(2,1)S(1)} collective-permute-done((bf16[2,2,16,3072]{3,2,1,0:T(8,128)(2,1)S(1)}, bf16[2,2,16,3072]{3,2,1,0:T(8,128)(2,1)S(1)}, u32[]{:S(2)}, u32[]{:S(2)}) %collective-permute-start.15) | collective-permute-done | bytes 393248 | tf_op jit(solution)/shard_map/ppermute | solution.py:121
  95.7 0.1 slice_add_fusion
  95.8 1.6 %collective-permute-start.16 = (bf16[1,2,16,3072]{3,2,1,0:T(8,128)(2,1)S(1)}, bf16[1,2,16,3072]{3,2,1,0:T(8,128)(2,1)S(1)}, u32[]{:S(2)}, u32[]{:S(2)}) collective-permute-start(bf16[1,2,16,3072]{3,2,1,0:T(8,128)(2,1)S(1)} %slice.150), channel_id=1, source_target_pairs={{0,2},{1,5},{2,0},{3,7},{4,6},{5,1},{6,4},{7,3},{8,10},{9,13},{10,... | collective-permute-start | bytes 589832 | tf_op jit(solution)/shard_map/ppermute | solution.py:121
  97.4 1.6 %collective-permute-start.13 = (bf16[16,3072]{1,0:T(8,128)(2,1)S(1)}, bf16[16,3072]{1,0:T(8,128)(2,1)S(1)}, u32[]{:S(2)}, u32[]{:S(2)}) collective-permute-start(bf16[16,3072]{1,0:T(8,128)(2,1)S(1)} %get-tuple-element.25), channel_id=1, source_target_pairs={{0,16},{16,0},{1,17},{17,1},{2,18},{18,2},{3,19},{19,3},{4,20},{20... | collective-permute-start | bytes 294920 | tf_op jit(solution)/shard_map/ppermute | solution.py:12
  99.0 2.5 %collective-permute-done.16 = bf16[1,2,16,3072]{3,2,1,0:T(8,128)(2,1)S(1)} collective-permute-done((bf16[1,2,16,3072]{3,2,1,0:T(8,128)(2,1)S(1)}, bf16[1,2,16,3072]{3,2,1,0:T(8,128)(2,1)S(1)}, u32[]{:S(2)}, u32[]{:S(2)}) %collective-permute-start.16) | collective-permute-done | bytes 196640 | tf_op jit(solution)/shard_map/ppermute | solution.py:121
  101.6 1.6 %collective-permute-start.17 = (bf16[16,3072]{1,0:T(8,128)(2,1)S(1)}, bf16[16,3072]{1,0:T(8,128)(2,1)S(1)}, u32[]{:S(2)}, u32[]{:S(2)}) collective-permute-start(bf16[16,3072]{1,0:T(8,128)(2,1)S(1)} %get-tuple-element.27), channel_id=1, source_target_pairs={{0,16},{16,0},{1,17},{17,1},{2,18},{18,2},{3,19},{19,3},{4,20},{20... | collective-permute-start | bytes 294920 | tf_op jit(solution)/shard_map/ppermute | solution.py:12
  103.2 0.8 collective-permute-start.18
  104.0 3.0 %collective-permute-start.19 = (bf16[16,3072]{1,0:T(8,128)(2,1)S(1)}, bf16[16,3072]{1,0:T(8,128)(2,1)S(1)}, u32[]{:S(2)}, u32[]{:S(2)}) collective-permute-start(bf16[16,3072]{1,0:T(8,128)(2,1)S(1)} %get-tuple-element.28), channel_id=1, source_target_pairs={{0,24},{8,16},{16,8},{24,0},{1,25},{9,17},{17,9},{25,1},{2,26},{10... | collective-permute-start | bytes 294920 | tf_op jit(solution)/shard_map/ppermute | solution.py:134
  107.0 2.8 %collective-permute-done.18 = bf16[16,3072]{1,0:T(8,128)(2,1)S(1)} collective-permute-done((bf16[16,3072]{1,0:T(8,128)(2,1)S(1)}, bf16[16,3072]{1,0:T(8,128)(2,1)S(1)}, u32[]{:S(2)}, u32[]{:S(2)}) %collective-permute-start.18) | collective-permute-done | bytes 98336 | tf_op jit(solution)/shard_map/ppermute | solution.py:134
  109.8 1.1 collective-permute-done.19
  110.9 2.7 %fusion.10 = bf16[1,128,6144]{2,1,0:T(8,128)(2,1)} fusion(f32[2,16,128]{2,1,0:T(8,128)S(1)} %collective-permute-done.9, bf16[64,6144]{1,0:T(8,128)(2,1)S(1)} %collective-permute-done.8, bf16[64,6144]{1,0:T(8,128)(2,1)S(1)} %collective-permute-done, bf16[1,16,6144]{2,1,0:T(8,128)(2,1)S(1)} %maximum_bitcast_fusion.3, ...), kind=kOutput, calls=%fused_computation.12 | convolution fusion | flops 306905088 | bytes 3555328 | tf_op jit(solution)/shard_map/ect,ecd->td/dot_general | solution.py:138
  (33 shorter events, 0.5 us)
Async XLA Ops:
  0.0 8.7 %copy-start = (bf16[1,128,6144]{2,1,0:T(8,128)(2,1)S(1)}, bf16[1,128,6144]{2,1,0:T(8,128)(2,1)}, u32[]{:S(2)}) copy-start(bf16[1,128,6144]{2,1,0:T(8,128)(2,1)} %param.8) | copy-start | bytes 4718596
  0.0 2.9 %copy-start.2 = (bf16[1,6144]{1,0:T(2,128)(2,1)S(1)}, bf16[1,6144]{1,0:T(2,128)(2,1)}, u32[]{:S(2)}) copy-start(bf16[1,6144]{1,0:T(2,128)(2,1)} %param.9) | copy-start | bytes 36868
  2.9 6.8 %copy-start.1 = (f32[1,6144]{1,0:T(1,128)}, f32[1,6144]{1,0:T(1,128)S(1)}, u32[]{:S(2)}) copy-start(f32[1,6144]{1,0:T(1,128)S(1)} %mul.76) | copy-start | bytes 73732
  3.0 17.3 %collective-permute-start.1 = (bf16[1,16,6144]{2,1,0:T(8,128)(2,1)S(1)}, bf16[1,16,6144]{2,1,0:T(8,128)(2,1)S(1)}, u32[]{:S(2)}, u32[]{:S(2)}) collective-permute-start(bf16[1,16,6144]{2,1,0:T(8,128)(2,1)S(1)} %fusion.26), channel_id=1, source_target_pairs={{0,2},{1,5},{2,0},{3,7},{4,6},{5,1},{6,4},{7,3},{8,10},{9,13},{10,... | collective-permute-start | bytes 589832 | tf_op jit(solution)/shard_map/ppermute | solution.py:76
  6.1 11.6 %collective-permute-start.3 = (bf16[16,6144]{1,0:T(8,128)(2,1)S(1)}, bf16[16,6144]{1,0:T(8,128)(2,1)S(1)}, u32[]{:S(2)}, u32[]{:S(2)}) collective-permute-start(bf16[16,6144]{1,0:T(8,128)(2,1)S(1)} %dynamic-slice_bitcast_fusion), channel_id=1, source_target_pairs={{0,8},{8,0},{1,9},{9,1},{2,10},{10,2},{3,11},{11,3},{4,12},{12,4},... | collective-permute-start | bytes 589832 | tf_op jit(solution)/shard_map/ppermute | solution.py:12
  9.8 30.4 %collective-permute-start = (bf16[64,6144]{1,0:T(8,128)(2,1)}, bf16[64,6144]{1,0:T(8,128)(2,1)S(1)}, u32[]{:S(2)}, u32[]{:S(2)}) collective-permute-start(bf16[64,6144]{1,0:T(8,128)(2,1)} %get-tuple-element.19), channel_id=1, source_target_pairs={{0,16},{16,0},{1,17},{17,1},{2,18},{18,2},{3,19},{19,3},{4,20},{20... | collective-permute-start | bytes 2359304 | tf_op jit(solution)/shard_map/ppermute | solution.py:12
  18.7 7.8 %collective-permute-start.4 = (bf16[1,16,6144]{2,1,0:T(8,128)(2,1)S(1)}, bf16[1,16,6144]{2,1,0:T(8,128)(2,1)S(1)}, u32[]{:S(2)}, u32[]{:S(2)}) collective-permute-start(bf16[1,16,6144]{2,1,0:T(8,128)(2,1)S(1)} %fusion.35), channel_id=1, source_target_pairs={{0,2},{1,5},{2,0},{3,7},{4,6},{5,1},{6,4},{7,3},{8,10},{9,13},{10,... | collective-permute-start | bytes 589832 | tf_op jit(solution)/shard_map/ppermute | solution.py:76
  20.4 7.8 %collective-permute-start.2 = (bf16[2,16,6144]{2,1,0:T(8,128)(2,1)S(1)}, bf16[2,16,6144]{2,1,0:T(8,128)(2,1)S(1)}, u32[]{:S(2)}, u32[]{:S(2)}) collective-permute-start(bf16[2,16,6144]{2,1,0:T(8,128)(2,1)S(1)} %pad_maximum_fusion.3), channel_id=1, source_target_pairs={{0,4},{1,3},{2,6},{3,1},{4,0},{5,7},{6,2},{7,5},{8,12},{9,11},{10,... | collective-permute-start | bytes 1179656 | tf_op jit(solution)/shard_map/ppermute | solution.py:76
  26.6 8.9 %copy-start.4 = (f32[1,1,2,16]{3,2,1,0:T(2,128)S(1)}, f32[1,1,2,16]{3,2,1,0:T(2,128)}, u32[]{:S(2)}) copy-start(f32[1,1,2,16]{3,2,1,0:T(2,128)} %param.15) | copy-start | bytes 388
  26.6 8.9 %copy-start.5 = (s32[1,1,2]{2,1,0:T(1,128)S(1)}, s32[1,1,2]{2,1,0:T(1,128)}, u32[]{:S(2)}) copy-start(s32[1,1,2]{2,1,0:T(1,128)} %param.14) | copy-start | bytes 28
  26.6 9.0 %copy-start.3 = (s32[1,1,2,16]{3,2,1,0:T(2,128)S(1)}, s32[1,1,2,16]{3,2,1,0:T(2,128)}, u32[]{:S(2)}) copy-start(s32[1,1,2,16]{3,2,1,0:T(2,128)} %param.13) | copy-start | bytes 388
  26.6 7.8 %collective-permute-start.5 = (bf16[2,16,6144]{2,1,0:T(8,128)(2,1)S(1)}, bf16[2,16,6144]{2,1,0:T(8,128)(2,1)S(1)}, u32[]{:S(2)}, u32[]{:S(2)}) collective-permute-start(bf16[2,16,6144]{2,1,0:T(8,128)(2,1)S(1)} %pad_maximum_fusion.4), channel_id=1, source_target_pairs={{0,4},{1,3},{2,6},{3,1},{4,0},{5,7},{6,2},{7,5},{8,12},{9,11},{10,... | collective-permute-start | bytes 1179656 | tf_op jit(solution)/shard_map/ppermute | solution.py:76
  29.2 9.2 %collective-permute-start.6 = (bf16[4,16,6144]{2,1,0:T(8,128)(2,1)}, bf16[4,16,6144]{2,1,0:T(8,128)(2,1)}, u32[]{:S(2)}, u32[]{:S(2)}) collective-permute-start(bf16[4,16,6144]{2,1,0:T(8,128)(2,1)} %get-tuple-element.22), channel_id=1, source_target_pairs={{0,1},{1,0},{2,3},{3,2},{4,5},{5,4},{6,7},{7,6},{8,9},{9,8},{10,11... | collective-permute-start | bytes 2359304 | tf_op jit(solution)/shard_map/ppermute | solution.py:12
  35.5 2.9 %collective-permute-start.7 = (bf16[4,16,6144]{2,1,0:T(8,128)(2,1)}, bf16[4,16,6144]{2,1,0:T(8,128)(2,1)}, u32[]{:S(2)}, u32[]{:S(2)}) collective-permute-start(bf16[4,16,6144]{2,1,0:T(8,128)(2,1)} %get-tuple-element.24), channel_id=1, source_target_pairs={{0,1},{1,0},{2,3},{3,2},{4,5},{5,4},{6,7},{7,6},{8,9},{9,8},{10,11... | collective-permute-start | bytes 2359304 | tf_op jit(solution)/shard_map/ppermute | solution.py:12
  36.3 35.9 %collective-permute-start.9 = (f32[2,16,128]{2,1,0:T(8,128)S(1)}, f32[2,16,128]{2,1,0:T(8,128)S(1)}, u32[]{:S(2)}, u32[]{:S(2)}) collective-permute-start(f32[2,16,128]{2,1,0:T(8,128)S(1)} %broadcast_select_fusion), channel_id=1, source_target_pairs={{0,16},{16,0},{1,17},{17,1},{2,18},{18,2},{3,19},{19,3},{4,20},{20... | collective-permute-start | bytes 49160 | tf_op jit(solution)/shard_map/ppermute | solution.py:12
  37.9 34.4 %collective-permute-start.8 = (bf16[64,6144]{1,0:T(8,128)(2,1)S(1)}, bf16[64,6144]{1,0:T(8,128)(2,1)S(1)}, u32[]{:S(2)}, u32[]{:S(2)}) collective-permute-start(bf16[64,6144]{1,0:T(8,128)(2,1)S(1)} %get-tuple-element.20), channel_id=1, source_target_pairs={{0,16},{16,0},{1,17},{17,1},{2,18},{18,2},{3,19},{19,3},{4,20},{20... | collective-permute-start | bytes 2359304 | tf_op jit(solution)/shard_map/ppermute | solution.py:12
  72.4 8.8 %collective-permute-start.10 = (bf16[4,2,16,3072]{3,2,1,0:T(8,128)(2,1)S(1)}, bf16[4,2,16,3072]{3,2,1,0:T(8,128)(2,1)S(1)}, u32[]{:S(2)}, u32[]{:S(2)}) collective-permute-start(bf16[4,2,16,3072]{3,2,1,0:T(8,128)(2,1)S(1)} %bitcast.86), channel_id=1, source_target_pairs={{0,1},{1,0},{2,3},{3,2},{4,5},{5,4},{6,7},{7,6},{8,9},{9,8},{10,11... | collective-permute-start | bytes 2359304 | tf_op jit(solution)/shard_map/ppermute | solution.py:12
  80.6 2.5 %collective-permute-start.14 = (bf16[4,2,16,3072]{3,2,1,0:T(8,128)(2,1)S(1)}, bf16[4,2,16,3072]{3,2,1,0:T(8,128)(2,1)S(1)}, u32[]{:S(2)}, u32[]{:S(2)}) collective-permute-start(bf16[4,2,16,3072]{3,2,1,0:T(8,128)(2,1)S(1)} %bitcast.85), channel_id=1, source_target_pairs={{0,1},{1,0},{2,3},{3,2},{4,5},{5,4},{6,7},{7,6},{8,9},{9,8},{10,11... | collective-permute-start | bytes 2359304 | tf_op jit(solution)/shard_map/ppermute | solution.py:12
  81.4 7.8 %collective-permute-start.11 = (bf16[2,2,16,3072]{3,2,1,0:T(8,128)(2,1)S(1)}, bf16[2,2,16,3072]{3,2,1,0:T(8,128)(2,1)S(1)}, u32[]{:S(2)}, u32[]{:S(2)}) collective-permute-start(bf16[2,2,16,3072]{3,2,1,0:T(8,128)(2,1)S(1)} %slice.149), channel_id=1, source_target_pairs={{0,4},{1,3},{2,6},{3,1},{4,0},{5,7},{6,2},{7,5},{8,12},{9,11},{10,... | collective-permute-start | bytes 1179656 | tf_op jit(solution)/shard_map/ppermute | solution.py:121
  83.3 12.4 %collective-permute-start.15 = (bf16[2,2,16,3072]{3,2,1,0:T(8,128)(2,1)S(1)}, bf16[2,2,16,3072]{3,2,1,0:T(8,128)(2,1)S(1)}, u32[]{:S(2)}, u32[]{:S(2)}) collective-permute-start(bf16[2,2,16,3072]{3,2,1,0:T(8,128)(2,1)S(1)} %slice.148), channel_id=1, source_target_pairs={{0,4},{1,3},{2,6},{3,1},{4,0},{5,7},{6,2},{7,5},{8,12},{9,11},{10,... | collective-permute-start | bytes 1179656 | tf_op jit(solution)/shard_map/ppermute | solution.py:121
  89.3 8.0 %collective-permute-start.12 = (bf16[1,2,16,3072]{3,2,1,0:T(8,128)(2,1)S(1)}, bf16[1,2,16,3072]{3,2,1,0:T(8,128)(2,1)S(1)}, u32[]{:S(2)}, u32[]{:S(2)}) collective-permute-start(bf16[1,2,16,3072]{3,2,1,0:T(8,128)(2,1)S(1)} %slice.151), channel_id=1, source_target_pairs={{0,2},{1,5},{2,0},{3,7},{4,6},{5,1},{6,4},{7,3},{8,10},{9,13},{10,... | collective-permute-start | bytes 589832 | tf_op jit(solution)/shard_map/ppermute | solution.py:121
  95.8 5.7 %collective-permute-start.16 = (bf16[1,2,16,3072]{3,2,1,0:T(8,128)(2,1)S(1)}, bf16[1,2,16,3072]{3,2,1,0:T(8,128)(2,1)S(1)}, u32[]{:S(2)}, u32[]{:S(2)}) collective-permute-start(bf16[1,2,16,3072]{3,2,1,0:T(8,128)(2,1)S(1)} %slice.150), channel_id=1, source_target_pairs={{0,2},{1,5},{2,0},{3,7},{4,6},{5,1},{6,4},{7,3},{8,10},{9,13},{10,... | collective-permute-start | bytes 589832 | tf_op jit(solution)/shard_map/ppermute | solution.py:121
  97.4 9.6 %collective-permute-start.13 = (bf16[16,3072]{1,0:T(8,128)(2,1)S(1)}, bf16[16,3072]{1,0:T(8,128)(2,1)S(1)}, u32[]{:S(2)}, u32[]{:S(2)}) collective-permute-start(bf16[16,3072]{1,0:T(8,128)(2,1)S(1)} %get-tuple-element.25), channel_id=1, source_target_pairs={{0,16},{16,0},{1,17},{17,1},{2,18},{18,2},{3,19},{19,3},{4,20},{20... | collective-permute-start | bytes 294920 | tf_op jit(solution)/shard_map/ppermute | solution.py:12
  101.6 5.4 %collective-permute-start.17 = (bf16[16,3072]{1,0:T(8,128)(2,1)S(1)}, bf16[16,3072]{1,0:T(8,128)(2,1)S(1)}, u32[]{:S(2)}, u32[]{:S(2)}) collective-permute-start(bf16[16,3072]{1,0:T(8,128)(2,1)S(1)} %get-tuple-element.27), channel_id=1, source_target_pairs={{0,16},{16,0},{1,17},{17,1},{2,18},{18,2},{3,19},{19,3},{4,20},{20... | collective-permute-start | bytes 294920 | tf_op jit(solution)/shard_map/ppermute | solution.py:12
  103.2 6.6 %collective-permute-start.18 = (bf16[16,3072]{1,0:T(8,128)(2,1)S(1)}, bf16[16,3072]{1,0:T(8,128)(2,1)S(1)}, u32[]{:S(2)}, u32[]{:S(2)}) collective-permute-start(bf16[16,3072]{1,0:T(8,128)(2,1)S(1)} %get-tuple-element.26), channel_id=1, source_target_pairs={{0,24},{8,16},{16,8},{24,0},{1,25},{9,17},{17,9},{25,1},{2,26},{10... | collective-permute-start | bytes 294920 | tf_op jit(solution)/shard_map/ppermute | solution.py:134
  104.0 6.9 %collective-permute-start.19 = (bf16[16,3072]{1,0:T(8,128)(2,1)S(1)}, bf16[16,3072]{1,0:T(8,128)(2,1)S(1)}, u32[]{:S(2)}, u32[]{:S(2)}) collective-permute-start(bf16[16,3072]{1,0:T(8,128)(2,1)S(1)} %get-tuple-element.28), channel_id=1, source_target_pairs={{0,24},{8,16},{16,8},{24,0},{1,25},{9,17},{17,9},{25,1},{2,26},{10... | collective-permute-start | bytes 294920 | tf_op jit(solution)/shard_map/ppermute | solution.py:134

commit v13 on v7

--- a/solution.py
+++ b/solution.py
@@ -132,13 +132,16 @@
                     for e in range(n_ex):
                         route.append((s * n_ex + e, ((s + 1) % sections) * n_ex + (e - k) % n_ex))
                 got[k].append(lax.ppermute(outgoing, ("section", "ex"), route))
-    expert_out = jnp.stack([jnp.concatenate(pieces_k, axis=-1) for pieces_k in got])
     states_in = jnp.concatenate([early_in, late_in])
-
-    branch = jnp.einsum(
-        "ect,ecd->td", selector_in, expert_out.astype(jnp.float32), precision=lax.Precision.HIGHEST
-    )
-    layer_out = (states_in.astype(jnp.float32) + branch).astype(jnp.bfloat16)
+    outs = []
+    for piece in range(pieces):
+        expert_out = jnp.stack([got[k][piece] for k in range(n_ex)]).astype(jnp.float32)
+        branch = jnp.einsum(
+            "ect,ecd->td", selector_in, expert_out, precision=lax.Precision.HIGHEST
+        )
+        base = states_in[:, piece * span:(piece + 1) * span].astype(jnp.float32)
+        outs.append((base + branch).astype(jnp.bfloat16))
+    layer_out = jnp.concatenate(outs, axis=-1)
     return layer_out[None]
 
 

time: 111 us -> 110 us (level)
  other arithmetic: 2.35 us -> 3.54 us
    ppermute x4, waiting for transfers between devices: 12.7 us -> 11 us  [body(): lax.ppermute(sent, ('chip', 'core'), chip_route(n_chip, n_core, stage, le...]
    broadcast_in_dim x0 -> x1, other arithmetic: none -> 1.25 us  [body(): return layer_out[None]]
    dot_general x1 -> x2, matrix products: 2.67 us -> 1.7 us  [body(): jnp.einsum('ect,ecd->td', selector_in, expert_out, precision=lax.Precisio...]
  transfers between devices with their start and end apart: 23 -> 23, of which waited for: 15 -> 15; matrix products, arithmetic and copies ran while one was open for 40% -> 41% of each run, Pallas kernels for 0% -> 0%
where the time goes in v13:
time: 110 us
  matrix products  43.5 us (40%)
  waiting for transfers between devices  32.9 us (30%)
  starting transfers between devices  26.8 us (24%)
  other arithmetic  3.54 us (3%)
  local copies, waits for them, and re-layouts  2.96 us (3%)
    dot_general x2, matrix products, body(): jnp.dot(activated, cols, preferred_element_type=jnp.float32)  16 us
    dot_general x1, matrix products, body(): up_part = jnp.dot(flat_rows, up_cols, preferred_element_type=jnp.float32)  12.4 us
    ppermute x11, starting transfers between devices, shifted(): return lax.ppermute(block, axes, route)  11.7 us
    dot_general x1, matrix products, body(): jnp.dot(flat_rows, gate_cols, preferred_element_type=jnp.float32)  11.7 us
    ppermute x6, waiting for transfers between devices, doubled(): lax.ppermute(held, ('chip', 'core'), chip_route(n_chip, n_core, stage, le...  11.6 us
    ppermute x4, waiting for transfers between devices, body(): lax.ppermute(sent, ('chip', 'core'), chip_route(n_chip, n_core, stage, le...  11 us
    ppermute x6, starting transfers between devices, doubled(): lax.ppermute(held, ('chip', 'core'), chip_route(n_chip, n_core, stage, le...  6.94 us
    ppermute x11, waiting for transfers between devices, shifted(): return lax.ppermute(block, axes, route)  5.22 us
  transfers between devices with their start and end apart: 23, of which 15 were waited for; matrix products, arithmetic and copies ran while one was open for 41% of the time, Pallas kernels for 0%

profile of v13, /device:TPU:0, one launch (start us, length us, event | category | flops | bytes accessed | tf_op | source)
XLA Modules:
  0.0 110.1 jit_solution(15632504808056130287)
XLA Ops:
  0.0 0.9 eq.34
  0.9 1.8 %convolution_convert_fusion = bf16[32,6144]{1,0:T(8,128)(2,1)S(1)} fusion(bf16[1,128,6144]{2,1,0:T(8,128)(2,1)} %param.8, s32[32]{0:T(128)S(1)} %eq.34), kind=kOutput, calls=%fused_computation.9 | convolution fusion | flops 50532352 | bytes 1966208 | tf_op jit(solution)/shard_map/dot_general | solution.py:63
  2.7 4.1 %collective-permute-start.6 = (bf16[8,6144]{1,0:T(8,128)(2,1)S(1)}, bf16[8,6144]{1,0:T(8,128)(2,1)S(1)}, u32[]{:S(2)}, u32[]{:S(2)}) collective-permute-start(bf16[8,6144]{1,0:T(8,128)(2,1)S(1)} %get-tuple-element.24), channel_id=1, source_target_pairs={{0,8},{8,0},{1,9},{9,1},{2,10},{10,2},{3,11},{11,3},{4,12},{12,4},... | collective-permute-start | bytes 294920 | tf_op jit(solution)/shard_map/ppermute | solution.py:12
  6.8 0.1 collective-permute-start.3
  6.9 0.2 fusion.25
  7.1 0.1 fusion.27
  7.3 1.8 %collective-permute-start.1 = (bf16[1,16,6144]{2,1,0:T(8,128)(2,1)S(1)}, bf16[1,16,6144]{2,1,0:T(8,128)(2,1)S(1)}, u32[]{:S(2)}, u32[]{:S(2)}) collective-permute-start(bf16[1,16,6144]{2,1,0:T(8,128)(2,1)S(1)} %fusion.27), channel_id=1, source_target_pairs={{0,2},{1,5},{2,0},{3,7},{4,6},{5,1},{6,4},{7,3},{8,10},{9,13},{10,... | collective-permute-start | bytes 589832 | tf_op jit(solution)/shard_map/ppermute | solution.py:76
  9.1 1.0 slice_bitcast_fusion.1
  10.1 1.5 %collective-permute-start = (bf16[64,6144]{1,0:T(8,128)(2,1)}, bf16[64,6144]{1,0:T(8,128)(2,1)S(1)}, u32[]{:S(2)}, u32[]{:S(2)}) collective-permute-start(bf16[64,6144]{1,0:T(8,128)(2,1)} %get-tuple-element.19), channel_id=1, source_target_pairs={{0,16},{16,0},{1,17},{17,1},{2,18},{18,2},{3,19},{19,3},{4,20},{20... | collective-permute-start | bytes 2359304 | tf_op jit(solution)/shard_map/ppermute | solution.py:12
  11.7 0.1 compare_select_fusion.6
  11.7 0.1 fusion.44
  11.8 0.5 gather_fusion
  12.4 2.3 %collective-permute-done.6 = bf16[8,6144]{1,0:T(8,128)(2,1)S(1)} collective-permute-done((bf16[8,6144]{1,0:T(8,128)(2,1)S(1)}, bf16[8,6144]{1,0:T(8,128)(2,1)S(1)}, u32[]{:S(2)}, u32[]{:S(2)}) %collective-permute-start.6) | collective-permute-done | bytes 98336 | tf_op jit(solution)/shard_map/ppermute | solution.py:12
  14.7 0.2 fusion.33
  14.8 1.1 %collective-permute-done.3 = bf16[8,6144]{1,0:T(8,128)(2,1)S(1)} collective-permute-done((bf16[8,6144]{1,0:T(8,128)(2,1)S(1)}, bf16[8,6144]{1,0:T(8,128)(2,1)S(1)}, u32[]{:S(2)}, u32[]{:S(2)}) %collective-permute-start.3) | collective-permute-done | bytes 98336 | tf_op jit(solution)/shard_map/ppermute | solution.py:12
  15.9 0.2 fusion.30
  16.1 0.1 fusion.43
  16.2 1.6 %collective-permute-start.4 = (bf16[1,8,6144]{2,1,0:T(8,128)(2,1)S(1)}, bf16[1,8,6144]{2,1,0:T(8,128)(2,1)S(1)}, u32[]{:S(2)}, u32[]{:S(2)}) collective-permute-start(bf16[1,8,6144]{2,1,0:T(8,128)(2,1)S(1)} %get-tuple-element.29), channel_id=1, source_target_pairs={{0,2},{1,5},{2,0},{3,7},{4,6},{5,1},{6,4},{7,3},{8,10},{9,13},{10,... | collective-permute-start | bytes 294920 | tf_op jit(solution)/shard_map/ppermute | solution.py:76
  17.9 0.5 collective-permute-start.7
  18.4 2.5 %collective-permute-done.4 = bf16[1,8,6144]{2,1,0:T(8,128)(2,1)S(1)} collective-permute-done((bf16[1,8,6144]{2,1,0:T(8,128)(2,1)S(1)}, bf16[1,8,6144]{2,1,0:T(8,128)(2,1)S(1)}, u32[]{:S(2)}, u32[]{:S(2)}) %collective-permute-start.4) | collective-permute-done | bytes 98336 | tf_op jit(solution)/shard_map/ppermute | solution.py:76
  20.9 0.8 collective-permute-start.5
  21.7 1.4 %collective-permute-done.7 = bf16[1,8,6144]{2,1,0:T(8,128)(2,1)S(1)} collective-permute-done((bf16[1,8,6144]{2,1,0:T(8,128)(2,1)S(1)}, bf16[1,8,6144]{2,1,0:T(8,128)(2,1)S(1)}, u32[]{:S(2)}, u32[]{:S(2)}) %collective-permute-start.7) | collective-permute-done | bytes 98336 | tf_op jit(solution)/shard_map/ppermute | solution.py:76
  23.2 0.1 collective-permute-start.8
  23.4 2.0 %collective-permute-start.2 = (bf16[2,16,6144]{2,1,0:T(8,128)(2,1)S(1)}, bf16[2,16,6144]{2,1,0:T(8,128)(2,1)S(1)}, u32[]{:S(2)}, u32[]{:S(2)}) collective-permute-start(bf16[2,16,6144]{2,1,0:T(8,128)(2,1)S(1)} %pad_maximum_fusion.2), channel_id=1, source_target_pairs={{0,4},{1,3},{2,6},{3,1},{4,0},{5,7},{6,2},{7,5},{8,12},{9,11},{10,... | collective-permute-start | bytes 1179656 | tf_op jit(solution)/shard_map/ppermute | solution.py:76
  25.4 1.3 %collective-permute-done.5 = bf16[2,8,6144]{2,1,0:T(8,128)(2,1)S(1)} collective-permute-done((bf16[2,8,6144]{2,1,0:T(8,128)(2,1)S(1)}, bf16[2,8,6144]{2,1,0:T(8,128)(2,1)S(1)}, u32[]{:S(2)}, u32[]{:S(2)}) %collective-permute-start.5) | collective-permute-done | bytes 196640 | tf_op jit(solution)/shard_map/ppermute | solution.py:76
  26.7 2.2 %collective-permute-done.8 = bf16[2,8,6144]{2,1,0:T(8,128)(2,1)S(1)} collective-permute-done((bf16[2,8,6144]{2,1,0:T(8,128)(2,1)S(1)}, bf16[2,8,6144]{2,1,0:T(8,128)(2,1)S(1)}, u32[]{:S(2)}, u32[]{:S(2)}) %collective-permute-start.8) | collective-permute-done | bytes 196640 | tf_op jit(solution)/shard_map/ppermute | solution.py:76
  29.0 0.1 collective-permute-start.10
  29.1 4.1 %collective-permute-done.2 = bf16[2,16,6144]{2,1,0:T(8,128)(2,1)S(1)} collective-permute-done((bf16[2,16,6144]{2,1,0:T(8,128)(2,1)S(1)}, bf16[2,16,6144]{2,1,0:T(8,128)(2,1)S(1)}, u32[]{:S(2)}, u32[]{:S(2)}) %collective-permute-start.2) | collective-permute-done | bytes 393248 | tf_op jit(solution)/shard_map/ppermute | solution.py:76
  33.1 0.1 fusion.51
  33.3 0.1 collective-permute-start.9
  33.3 0.1 broadcast_select_fusion
  33.4 1.6 %collective-permute-start.12 = (f32[2,16,128]{2,1,0:T(8,128)S(1)}, f32[2,16,128]{2,1,0:T(8,128)S(1)}, u32[]{:S(2)}, u32[]{:S(2)}) collective-permute-start(f32[2,16,128]{2,1,0:T(8,128)S(1)} %broadcast_select_fusion), channel_id=1, source_target_pairs={{0,16},{16,0},{1,17},{17,1},{2,18},{18,2},{3,19},{19,3},{4,20},{20... | collective-permute-start | bytes 49160 | tf_op jit(solution)/shard_map/ppermute | solution.py:12
  35.0 0.4 collective-permute-start.11
  35.5 0.1 collective-permute-done.9
  35.6 0.1 maximum_bitcast_fusion.1
  35.8 0.2 pad_maximum_fusion
  36.0 11.7 %fusion.2 = f32[256,2048]{1,0:T(8,128)S(1)} fusion(bf16[256,6144]{1,0:T(8,128)(2,1)S(1)} %bitcast.87, bf16[1,6144,2048]{2,1,0:T(8,128)(2,1)} %param.10), kind=kOutput, calls=%fused_computation.3 | convolution fusion | flops 6442450944 | bytes 30408704 | tf_op jit(solution)/shard_map/dot_general | solution.py:97
  47.6 12.4 %fusion.21 = bf16[256,2048]{1,0:T(8,128)(2,1)S(1)} fusion(bf16[256,6144]{1,0:T(8,128)(2,1)S(1)} %bitcast.88, bf16[1,6144,2048]{2,1,0:T(8,128)(2,1)} %param.11, f32[256,2048]{1,0:T(8,128)S(1)} %fusion.2), kind=kOutput, calls=%fused_computation.20 | convolution fusion | flops 6445596672 | bytes 31457280 | tf_op jit(solution)/shard_map/dot_general | solution.py:98
  60.0 8.0 %fusion.8 = bf16[256,3072]{1,0:T(8,128)(2,1)S(1)} fusion(bf16[256,2048]{1,0:T(8,128)(2,1)S(1)} %fusion.21, bf16[2048,6144]{1,0:T(8,128)(2,1)} %bitcast.106), kind=kOutput, calls=%fused_computation.10 | convolution fusion | flops 3222011904 | bytes 15204352 | tf_op jit(solution)/shard_map/dot_general | solution.py:106
  68.0 8.0 %fusion.11 = bf16[256,3072]{1,0:T(8,128)(2,1)S(1)} fusion(bf16[256,2048]{1,0:T(8,128)(2,1)S(1)} %fusion.21, bf16[2048,6144]{1,0:T(8,128)(2,1)} %bitcast.107), kind=kOutput, calls=%fused_computation.11 | convolution fusion | flops 3222011904 | bytes 15204352 | tf_op jit(solution)/shard_map/dot_general | solution.py:106
  76.1 0.1 fusion.52
  76.2 0.2 collective-permute-start.13
  76.4 0.1 fusion.53
  76.6 0.4 collective-permute-start.18
  77.1 1.5 %collective-permute-done.13 = bf16[4,2,16,3072]{3,2,1,0:T(8,128)(2,1)S(1)} collective-permute-done((bf16[4,2,16,3072]{3,2,1,0:T(8,128)(2,1)S(1)}, bf16[4,2,16,3072]{3,2,1,0:T(8,128)(2,1)S(1)}, u32[]{:S(2)}, u32[]{:S(2)}) %collective-permute-start.13) | collective-permute-done | bytes 786464 | tf_op jit(solution)/shard_map/ppermute | solution.py:12
  78.5 0.2 convert_add_fusion.1
  78.8 0.6 collective-permute-start.14
  79.4 0.2 collective-permute-done.18
  79.7 0.2 convert_add_fusion
  79.9 1.3 %collective-permute-start.19 = (bf16[2,2,16,3072]{3,2,1,0:T(8,128)(2,1)S(1)}, bf16[2,2,16,3072]{3,2,1,0:T(8,128)(2,1)S(1)}, u32[]{:S(2)}, u32[]{:S(2)}) collective-permute-start(bf16[2,2,16,3072]{3,2,1,0:T(8,128)(2,1)S(1)} %slice.176), channel_id=1, source_target_pairs={{0,4},{1,3},{2,6},{3,1},{4,0},{5,7},{6,2},{7,5},{8,12},{9,11},{10,... | collective-permute-start | bytes 1179656 | tf_op jit(solution)/shard_map/ppermute | solution.py:121
  81.2 5.4 %collective-permute-done.14 = bf16[2,2,16,3072]{3,2,1,0:T(8,128)(2,1)S(1)} collective-permute-done((bf16[2,2,16,3072]{3,2,1,0:T(8,128)(2,1)S(1)}, bf16[2,2,16,3072]{3,2,1,0:T(8,128)(2,1)S(1)}, u32[]{:S(2)}, u32[]{:S(2)}) %collective-permute-start.14) | collective-permute-done | bytes 393248 | tf_op jit(solution)/shard_map/ppermute | solution.py:121
  86.7 1.5 %collective-permute-start.15 = (bf16[1,2,16,3072]{3,2,1,0:T(8,128)(2,1)S(1)}, bf16[1,2,16,3072]{3,2,1,0:T(8,128)(2,1)S(1)}, u32[]{:S(2)}, u32[]{:S(2)}) collective-permute-start(bf16[1,2,16,3072]{3,2,1,0:T(8,128)(2,1)S(1)} %slice.179), channel_id=1, source_target_pairs={{0,2},{1,5},{2,0},{3,7},{4,6},{5,1},{6,4},{7,3},{8,10},{9,13},{10,... | collective-permute-start | bytes 589832 | tf_op jit(solution)/shard_map/ppermute | solution.py:121
  88.2 4.7 %collective-permute-done.19 = bf16[2,2,16,3072]{3,2,1,0:T(8,128)(2,1)S(1)} collective-permute-done((bf16[2,2,16,3072]{3,2,1,0:T(8,128)(2,1)S(1)}, bf16[2,2,16,3072]{3,2,1,0:T(8,128)(2,1)S(1)}, u32[]{:S(2)}, u32[]{:S(2)}) %collective-permute-start.19) | collective-permute-done | bytes 393248 | tf_op jit(solution)/shard_map/ppermute | solution.py:121
  93.1 1.5 %collective-permute-start.20 = (bf16[1,2,16,3072]{3,2,1,0:T(8,128)(2,1)S(1)}, bf16[1,2,16,3072]{3,2,1,0:T(8,128)(2,1)S(1)}, u32[]{:S(2)}, u32[]{:S(2)}) collective-permute-start(bf16[1,2,16,3072]{3,2,1,0:T(8,128)(2,1)S(1)} %slice.178), channel_id=1, source_target_pairs={{0,2},{1,5},{2,0},{3,7},{4,6},{5,1},{6,4},{7,3},{8,10},{9,13},{10,... | collective-permute-start | bytes 589832 | tf_op jit(solution)/shard_map/ppermute | solution.py:121
  94.6 1.6 %collective-permute-start.16 = (bf16[16,3072]{1,0:T(8,128)(2,1)S(1)}, bf16[16,3072]{1,0:T(8,128)(2,1)S(1)}, u32[]{:S(2)}, u32[]{:S(2)}) collective-permute-start(bf16[16,3072]{1,0:T(8,128)(2,1)S(1)} %get-tuple-element.25), channel_id=1, source_target_pairs={{0,16},{16,0},{1,17},{17,1},{2,18},{18,2},{3,19},{19,3},{4,20},{20... | collective-permute-start | bytes 294920 | tf_op jit(solution)/shard_map/ppermute | solution.py:12
  96.2 1.7 %collective-permute-start.17 = (bf16[16,3072]{1,0:T(8,128)(2,1)S(1)}, bf16[16,3072]{1,0:T(8,128)(2,1)S(1)}, u32[]{:S(2)}, u32[]{:S(2)}) collective-permute-start(bf16[16,3072]{1,0:T(8,128)(2,1)S(1)} %get-tuple-element.26), channel_id=1, source_target_pairs={{0,24},{8,16},{16,8},{24,0},{1,25},{9,17},{17,9},{25,1},{2,26},{10... | collective-permute-start | bytes 294920 | tf_op jit(solution)/shard_map/ppermute | solution.py:134
  97.9 0.9 collective-permute-done.20
  98.9 1.7 %collective-permute-start.21 = (bf16[16,3072]{1,0:T(8,128)(2,1)S(1)}, bf16[16,3072]{1,0:T(8,128)(2,1)S(1)}, u32[]{:S(2)}, u32[]{:S(2)}) collective-permute-start(bf16[16,3072]{1,0:T(8,128)(2,1)S(1)} %get-tuple-element.27), channel_id=1, source_target_pairs={{0,16},{16,0},{1,17},{17,1},{2,18},{18,2},{3,19},{19,3},{4,20},{20... | collective-permute-start | bytes 294920 | tf_op jit(solution)/shard_map/ppermute | solution.py:12
  100.6 1.5 %collective-permute-start.22 = (bf16[16,3072]{1,0:T(8,128)(2,1)S(1)}, bf16[16,3072]{1,0:T(8,128)(2,1)S(1)}, u32[]{:S(2)}, u32[]{:S(2)}) collective-permute-start(bf16[16,3072]{1,0:T(8,128)(2,1)S(1)} %get-tuple-element.28), channel_id=1, source_target_pairs={{0,24},{8,16},{16,8},{24,0},{1,25},{9,17},{17,9},{25,1},{2,26},{10... | collective-permute-start | bytes 294920 | tf_op jit(solution)/shard_map/ppermute | solution.py:134
  102.1 3.7 %collective-permute-done.17 = bf16[16,3072]{1,0:T(8,128)(2,1)S(1)} collective-permute-done((bf16[16,3072]{1,0:T(8,128)(2,1)S(1)}, bf16[16,3072]{1,0:T(8,128)(2,1)S(1)}, u32[]{:S(2)}, u32[]{:S(2)}) %collective-permute-start.17) | collective-permute-done | bytes 98336 | tf_op jit(solution)/shard_map/ppermute | solution.py:134
  105.7 0.8 fusion.17
  106.6 1.4 %collective-permute-done.22 = bf16[16,3072]{1,0:T(8,128)(2,1)S(1)} collective-permute-done((bf16[16,3072]{1,0:T(8,128)(2,1)S(1)}, bf16[16,3072]{1,0:T(8,128)(2,1)S(1)}, u32[]{:S(2)}, u32[]{:S(2)}) %collective-permute-start.22) | collective-permute-done | bytes 98336 | tf_op jit(solution)/shard_map/ppermute | solution.py:134
  108.0 0.8 fusion.16
  108.9 1.3 %maximum_bitcast_fusion.2 = bf16[1,128,6144]{2,1,0:T(8,128)(2,1)} fusion(bf16[128,3072]{1,0:T(8,128)(2,1)S(1)} %fusion.16, bf16[128,3072]{1,0:T(8,128)(2,1)S(1)} %fusion.17), kind=kLoop, calls=%fused_computation.23 | loop fusion | flops 3145728 | bytes 3145728 | tf_op jit(solution)/shard_map/broadcast_in_dim | solution.py:145
  (43 shorter events, 0.8 us)
Async XLA Ops:
  0.0 9.1 %copy-start = (bf16[1,128,6144]{2,1,0:T(8,128)(2,1)S(1)}, bf16[1,128,6144]{2,1,0:T(8,128)(2,1)}, u32[]{:S(2)}) copy-start(bf16[1,128,6144]{2,1,0:T(8,128)(2,1)} %param.8) | copy-start | bytes 4718596
  0.0 6.9 %copy-start.1 = (bf16[1,6144]{1,0:T(2,128)(2,1)S(1)}, bf16[1,6144]{1,0:T(2,128)(2,1)}, u32[]{:S(2)}) copy-start(bf16[1,6144]{1,0:T(2,128)(2,1)} %param.9) | copy-start | bytes 36868
  2.7 11.9 %collective-permute-start.6 = (bf16[8,6144]{1,0:T(8,128)(2,1)S(1)}, bf16[8,6144]{1,0:T(8,128)(2,1)S(1)}, u32[]{:S(2)}, u32[]{:S(2)}) collective-permute-start(bf16[8,6144]{1,0:T(8,128)(2,1)S(1)} %get-tuple-element.24), channel_id=1, source_target_pairs={{0,8},{8,0},{1,9},{9,1},{2,10},{10,2},{3,11},{11,3},{4,12},{12,4},... | collective-permute-start | bytes 294920 | tf_op jit(solution)/shard_map/ppermute | solution.py:12
  6.8 9.1 %collective-permute-start.3 = (bf16[8,6144]{1,0:T(8,128)(2,1)S(1)}, bf16[8,6144]{1,0:T(8,128)(2,1)S(1)}, u32[]{:S(2)}, u32[]{:S(2)}) collective-permute-start(bf16[8,6144]{1,0:T(8,128)(2,1)S(1)} %get-tuple-element.23), channel_id=1, source_target_pairs={{0,8},{8,0},{1,9},{9,1},{2,10},{10,2},{3,11},{11,3},{4,12},{12,4},... | collective-permute-start | bytes 294920 | tf_op jit(solution)/shard_map/ppermute | solution.py:12
  7.2 4.4 %copy-start.3 = (f32[1,1,2,16]{3,2,1,0:T(2,128)S(1)}, f32[1,1,2,16]{3,2,1,0:T(2,128)}, u32[]{:S(2)}) copy-start(f32[1,1,2,16]{3,2,1,0:T(2,128)} %param.15) | copy-start | bytes 388
  7.3 4.4 %copy-start.4 = (s32[1,1,2]{2,1,0:T(1,128)S(1)}, s32[1,1,2]{2,1,0:T(1,128)}, u32[]{:S(2)}) copy-start(s32[1,1,2]{2,1,0:T(1,128)} %param.14) | copy-start | bytes 28
  7.3 4.5 %copy-start.2 = (s32[1,1,2,16]{3,2,1,0:T(2,128)S(1)}, s32[1,1,2,16]{3,2,1,0:T(2,128)}, u32[]{:S(2)}) copy-start(s32[1,1,2,16]{3,2,1,0:T(2,128)} %param.13) | copy-start | bytes 388
  7.3 16.0 %collective-permute-start.1 = (bf16[1,16,6144]{2,1,0:T(8,128)(2,1)S(1)}, bf16[1,16,6144]{2,1,0:T(8,128)(2,1)S(1)}, u32[]{:S(2)}, u32[]{:S(2)}) collective-permute-start(bf16[1,16,6144]{2,1,0:T(8,128)(2,1)S(1)} %fusion.27), channel_id=1, source_target_pairs={{0,2},{1,5},{2,0},{3,7},{4,6},{5,1},{6,4},{7,3},{8,10},{9,13},{10,... | collective-permute-start | bytes 589832 | tf_op jit(solution)/shard_map/ppermute | solution.py:76
  10.1 25.8 %collective-permute-start = (bf16[64,6144]{1,0:T(8,128)(2,1)}, bf16[64,6144]{1,0:T(8,128)(2,1)S(1)}, u32[]{:S(2)}, u32[]{:S(2)}) collective-permute-start(bf16[64,6144]{1,0:T(8,128)(2,1)} %get-tuple-element.19), channel_id=1, source_target_pairs={{0,16},{16,0},{1,17},{17,1},{2,18},{18,2},{3,19},{19,3},{4,20},{20... | collective-permute-start | bytes 2359304 | tf_op jit(solution)/shard_map/ppermute | solution.py:12
  16.2 4.7 %collective-permute-start.4 = (bf16[1,8,6144]{2,1,0:T(8,128)(2,1)S(1)}, bf16[1,8,6144]{2,1,0:T(8,128)(2,1)S(1)}, u32[]{:S(2)}, u32[]{:S(2)}) collective-permute-start(bf16[1,8,6144]{2,1,0:T(8,128)(2,1)S(1)} %get-tuple-element.29), channel_id=1, source_target_pairs={{0,2},{1,5},{2,0},{3,7},{4,6},{5,1},{6,4},{7,3},{8,10},{9,13},{10,... | collective-permute-start | bytes 294920 | tf_op jit(solution)/shard_map/ppermute | solution.py:76
  17.9 5.3 %collective-permute-start.7 = (bf16[1,8,6144]{2,1,0:T(8,128)(2,1)S(1)}, bf16[1,8,6144]{2,1,0:T(8,128)(2,1)S(1)}, u32[]{:S(2)}, u32[]{:S(2)}) collective-permute-start(bf16[1,8,6144]{2,1,0:T(8,128)(2,1)S(1)} %get-tuple-element.30), channel_id=1, source_target_pairs={{0,2},{1,5},{2,0},{3,7},{4,6},{5,1},{6,4},{7,3},{8,10},{9,13},{10,... | collective-permute-start | bytes 294920 | tf_op jit(solution)/shard_map/ppermute | solution.py:76
  20.9 5.7 %collective-permute-start.5 = (bf16[2,8,6144]{2,1,0:T(8,128)(2,1)S(1)}, bf16[2,8,6144]{2,1,0:T(8,128)(2,1)S(1)}, u32[]{:S(2)}, u32[]{:S(2)}) collective-permute-start(bf16[2,8,6144]{2,1,0:T(8,128)(2,1)S(1)} %pad_maximum_fusion.3), channel_id=1, source_target_pairs={{0,4},{1,3},{2,6},{3,1},{4,0},{5,7},{6,2},{7,5},{8,12},{9,11},{10,... | collective-permute-start | bytes 589832 | tf_op jit(solution)/shard_map/ppermute | solution.py:76
  23.2 5.7 %collective-permute-start.8 = (bf16[2,8,6144]{2,1,0:T(8,128)(2,1)S(1)}, bf16[2,8,6144]{2,1,0:T(8,128)(2,1)S(1)}, u32[]{:S(2)}, u32[]{:S(2)}) collective-permute-start(bf16[2,8,6144]{2,1,0:T(8,128)(2,1)S(1)} %pad_maximum_fusion.4), channel_id=1, source_target_pairs={{0,4},{1,3},{2,6},{3,1},{4,0},{5,7},{6,2},{7,5},{8,12},{9,11},{10,... | collective-permute-start | bytes 589832 | tf_op jit(solution)/shard_map/ppermute | solution.py:76
  23.4 9.8 %collective-permute-start.2 = (bf16[2,16,6144]{2,1,0:T(8,128)(2,1)S(1)}, bf16[2,16,6144]{2,1,0:T(8,128)(2,1)S(1)}, u32[]{:S(2)}, u32[]{:S(2)}) collective-permute-start(bf16[2,16,6144]{2,1,0:T(8,128)(2,1)S(1)} %pad_maximum_fusion.2), channel_id=1, source_target_pairs={{0,4},{1,3},{2,6},{3,1},{4,0},{5,7},{6,2},{7,5},{8,12},{9,11},{10,... | collective-permute-start | bytes 1179656 | tf_op jit(solution)/shard_map/ppermute | solution.py:76
  29.0 6.5 %collective-permute-start.10 = (bf16[4,16,6144]{2,1,0:T(8,128)(2,1)S(1)}, bf16[4,16,6144]{2,1,0:T(8,128)(2,1)S(1)}, u32[]{:S(2)}, u32[]{:S(2)}) collective-permute-start(bf16[4,16,6144]{2,1,0:T(8,128)(2,1)S(1)} %maximum_maximum_fusion), channel_id=1, source_target_pairs={{0,1},{1,0},{2,3},{3,2},{4,5},{5,4},{6,7},{7,6},{8,9},{9,8},{10,11... | collective-permute-start | bytes 2359304 | tf_op jit(solution)/shard_map/ppermute | solution.py:12
  33.3 2.4 %collective-permute-start.9 = (bf16[4,16,6144]{2,1,0:T(8,128)(2,1)S(1)}, bf16[4,16,6144]{2,1,0:T(8,128)(2,1)S(1)}, u32[]{:S(2)}, u32[]{:S(2)}) collective-permute-start(bf16[4,16,6144]{2,1,0:T(8,128)(2,1)S(1)} %get-tuple-element.22), channel_id=1, source_target_pairs={{0,1},{1,0},{2,3},{3,2},{4,5},{5,4},{6,7},{7,6},{8,9},{9,8},{10,11... | collective-permute-start | bytes 2359304 | tf_op jit(solution)/shard_map/ppermute | solution.py:12
  33.4 42.7 %collective-permute-start.12 = (f32[2,16,128]{2,1,0:T(8,128)S(1)}, f32[2,16,128]{2,1,0:T(8,128)S(1)}, u32[]{:S(2)}, u32[]{:S(2)}) collective-permute-start(f32[2,16,128]{2,1,0:T(8,128)S(1)} %broadcast_select_fusion), channel_id=1, source_target_pairs={{0,16},{16,0},{1,17},{17,1},{2,18},{18,2},{3,19},{19,3},{4,20},{20... | collective-permute-start | bytes 49160 | tf_op jit(solution)/shard_map/ppermute | solution.py:12
  35.0 41.0 %collective-permute-start.11 = (bf16[64,6144]{1,0:T(8,128)(2,1)S(1)}, bf16[64,6144]{1,0:T(8,128)(2,1)S(1)}, u32[]{:S(2)}, u32[]{:S(2)}) collective-permute-start(bf16[64,6144]{1,0:T(8,128)(2,1)S(1)} %get-tuple-element.20), channel_id=1, source_target_pairs={{0,16},{16,0},{1,17},{17,1},{2,18},{18,2},{3,19},{19,3},{4,20},{20... | collective-permute-start | bytes 2359304 | tf_op jit(solution)/shard_map/ppermute | solution.py:12
  76.2 2.4 %collective-permute-start.13 = (bf16[4,2,16,3072]{3,2,1,0:T(8,128)(2,1)S(1)}, bf16[4,2,16,3072]{3,2,1,0:T(8,128)(2,1)S(1)}, u32[]{:S(2)}, u32[]{:S(2)}) collective-permute-start(bf16[4,2,16,3072]{3,2,1,0:T(8,128)(2,1)S(1)} %bitcast.97), channel_id=1, source_target_pairs={{0,1},{1,0},{2,3},{3,2},{4,5},{5,4},{6,7},{7,6},{8,9},{9,8},{10,11... | collective-permute-start | bytes 2359304 | tf_op jit(solution)/shard_map/ppermute | solution.py:12
  76.6 3.1 %collective-permute-start.18 = (bf16[4,2,16,3072]{3,2,1,0:T(8,128)(2,1)S(1)}, bf16[4,2,16,3072]{3,2,1,0:T(8,128)(2,1)S(1)}, u32[]{:S(2)}, u32[]{:S(2)}) collective-permute-start(bf16[4,2,16,3072]{3,2,1,0:T(8,128)(2,1)S(1)} %bitcast.96), channel_id=1, source_target_pairs={{0,1},{1,0},{2,3},{3,2},{4,5},{5,4},{6,7},{7,6},{8,9},{9,8},{10,11... | collective-permute-start | bytes 2359304 | tf_op jit(solution)/shard_map/ppermute | solution.py:12
  78.8 7.8 %collective-permute-start.14 = (bf16[2,2,16,3072]{3,2,1,0:T(8,128)(2,1)S(1)}, bf16[2,2,16,3072]{3,2,1,0:T(8,128)(2,1)S(1)}, u32[]{:S(2)}, u32[]{:S(2)}) collective-permute-start(bf16[2,2,16,3072]{3,2,1,0:T(8,128)(2,1)S(1)} %slice.177), channel_id=1, source_target_pairs={{0,4},{1,3},{2,6},{3,1},{4,0},{5,7},{6,2},{7,5},{8,12},{9,11},{10,... | collective-permute-start | bytes 1179656 | tf_op jit(solution)/shard_map/ppermute | solution.py:121
  79.9 13.0 %collective-permute-start.19 = (bf16[2,2,16,3072]{3,2,1,0:T(8,128)(2,1)S(1)}, bf16[2,2,16,3072]{3,2,1,0:T(8,128)(2,1)S(1)}, u32[]{:S(2)}, u32[]{:S(2)}) collective-permute-start(bf16[2,2,16,3072]{3,2,1,0:T(8,128)(2,1)S(1)} %slice.176), channel_id=1, source_target_pairs={{0,4},{1,3},{2,6},{3,1},{4,0},{5,7},{6,2},{7,5},{8,12},{9,11},{10,... | collective-permute-start | bytes 1179656 | tf_op jit(solution)/shard_map/ppermute | solution.py:121
  86.7 7.8 %collective-permute-start.15 = (bf16[1,2,16,3072]{3,2,1,0:T(8,128)(2,1)S(1)}, bf16[1,2,16,3072]{3,2,1,0:T(8,128)(2,1)S(1)}, u32[]{:S(2)}, u32[]{:S(2)}) collective-permute-start(bf16[1,2,16,3072]{3,2,1,0:T(8,128)(2,1)S(1)} %slice.179), channel_id=1, source_target_pairs={{0,2},{1,5},{2,0},{3,7},{4,6},{5,1},{6,4},{7,3},{8,10},{9,13},{10,... | collective-permute-start | bytes 589832 | tf_op jit(solution)/shard_map/ppermute | solution.py:121
  93.1 5.7 %collective-permute-start.20 = (bf16[1,2,16,3072]{3,2,1,0:T(8,128)(2,1)S(1)}, bf16[1,2,16,3072]{3,2,1,0:T(8,128)(2,1)S(1)}, u32[]{:S(2)}, u32[]{:S(2)}) collective-permute-start(bf16[1,2,16,3072]{3,2,1,0:T(8,128)(2,1)S(1)} %slice.178), channel_id=1, source_target_pairs={{0,2},{1,5},{2,0},{3,7},{4,6},{5,1},{6,4},{7,3},{8,10},{9,13},{10,... | collective-permute-start | bytes 589832 | tf_op jit(solution)/shard_map/ppermute | solution.py:121
  94.6 7.5 %collective-permute-start.16 = (bf16[16,3072]{1,0:T(8,128)(2,1)S(1)}, bf16[16,3072]{1,0:T(8,128)(2,1)S(1)}, u32[]{:S(2)}, u32[]{:S(2)}) collective-permute-start(bf16[16,3072]{1,0:T(8,128)(2,1)S(1)} %get-tuple-element.25), channel_id=1, source_target_pairs={{0,16},{16,0},{1,17},{17,1},{2,18},{18,2},{3,19},{19,3},{4,20},{20... | collective-permute-start | bytes 294920 | tf_op jit(solution)/shard_map/ppermute | solution.py:12
  96.2 9.6 %collective-permute-start.17 = (bf16[16,3072]{1,0:T(8,128)(2,1)S(1)}, bf16[16,3072]{1,0:T(8,128)(2,1)S(1)}, u32[]{:S(2)}, u32[]{:S(2)}) collective-permute-start(bf16[16,3072]{1,0:T(8,128)(2,1)S(1)} %get-tuple-element.26), channel_id=1, source_target_pairs={{0,24},{8,16},{16,8},{24,0},{1,25},{9,17},{17,9},{25,1},{2,26},{10... | collective-permute-start | bytes 294920 | tf_op jit(solution)/shard_map/ppermute | solution.py:134
  98.9 7.7 %collective-permute-start.21 = (bf16[16,3072]{1,0:T(8,128)(2,1)S(1)}, bf16[16,3072]{1,0:T(8,128)(2,1)S(1)}, u32[]{:S(2)}, u32[]{:S(2)}) collective-permute-start(bf16[16,3072]{1,0:T(8,128)(2,1)S(1)} %get-tuple-element.27), channel_id=1, source_target_pairs={{0,16},{16,0},{1,17},{17,1},{2,18},{18,2},{3,19},{19,3},{4,20},{20... | collective-permute-start | bytes 294920 | tf_op jit(solution)/shard_map/ppermute | solution.py:12
  100.6 7.5 %collective-permute-start.22 = (bf16[16,3072]{1,0:T(8,128)(2,1)S(1)}, bf16[16,3072]{1,0:T(8,128)(2,1)S(1)}, u32[]{:S(2)}, u32[]{:S(2)}) collective-permute-start(bf16[16,3072]{1,0:T(8,128)(2,1)S(1)} %get-tuple-element.28), channel_id=1, source_target_pairs={{0,24},{8,16},{16,8},{24,0},{1,25},{9,17},{17,9},{25,1},{2,26},{10... | collective-permute-start | bytes 294920 | tf_op jit(solution)/shard_map/ppermute | solution.py:134

commit v14 on v13

--- a/solution.py
+++ b/solution.py
@@ -53,8 +53,7 @@
     selector_out = (slot_rows[..., None] == jnp.arange(tok_count)[None, None, :]).astype(
         jnp.float32
     ) * weighting[..., None]
-    order = (ex_me + jnp.arange(n_ex)) % n_ex
-    selector_out = jnp.take(selector_out, order, axis=0)
+    selector_out = jnp.roll(selector_out, -ex_me, axis=0)
     early_in = shifted(states[: tok_count // 2], "section", sections, 1)
     late_in = shifted(states[tok_count // 2 :], "section", sections, 1)
     selector_in = shifted(selector_out, "section", sections, 1)

time: 110 us -> 110 us (level)
  transfers between devices with their start and end apart: 23 -> 23, of which waited for: 15 -> 15; matrix products, arithmetic and copies ran while one was open for 41% -> 40% of each run, Pallas kernels for 0% -> 0%
where the time goes in v14:
time: 110 us
  matrix products  43.5 us (40%)
  waiting for transfers between devices  33.8 us (31%)
  starting transfers between devices  26.6 us (24%)
  other arithmetic  3.45 us (3%)
  local copies, waits for them, and re-layouts  2.41 us (2%)
    dot_general x2, matrix products, body(): jnp.dot(activated, cols, preferred_element_type=jnp.float32)  16 us
    dot_general x1, matrix products, body(): up_part = jnp.dot(flat_rows, up_cols, preferred_element_type=jnp.float32)  12.4 us
    ppermute x11, starting transfers between devices, shifted(): return lax.ppermute(block, axes, route)  11.8 us
    dot_general x1, matrix products, body(): jnp.dot(flat_rows, gate_cols, preferred_element_type=jnp.float32)  11.7 us
    ppermute x6, waiting for transfers between devices, doubled(): lax.ppermute(held, ('chip', 'core'), chip_route(n_chip, n_core, stage, le...  11.6 us
    ppermute x4, waiting for transfers between devices, body(): lax.ppermute(sent, ('chip', 'core'), chip_route(n_chip, n_core, stage, le...  11.1 us
    ppermute x6, starting transfers between devices, doubled(): lax.ppermute(held, ('chip', 'core'), chip_route(n_chip, n_core, stage, le...  6.9 us
    ppermute x11, waiting for transfers between devices, shifted(): return lax.ppermute(block, axes, route)  5.94 us
  transfers between devices with their start and end apart: 23, of which 15 were waited for; matrix products, arithmetic and copies ran while one was open for 40% of the time, Pallas kernels for 0%

profile of v14, /device:TPU:0, one launch (start us, length us, event | category | flops | bytes accessed | tf_op | source)
XLA Modules:
  0.0 110.2 jit_solution(8355171303694011335)
XLA Ops:
  0.0 0.9 eq.35
  0.9 1.8 %convolution_convert_fusion = bf16[32,6144]{1,0:T(8,128)(2,1)S(1)} fusion(bf16[1,128,6144]{2,1,0:T(8,128)(2,1)} %param.8, s32[32]{0:T(128)S(1)} %eq.35), kind=kOutput, calls=%fused_computation.8 | convolution fusion | flops 50532352 | bytes 1966208 | tf_op jit(solution)/shard_map/dot_general | solution.py:62
  2.7 4.1 %collective-permute-start.6 = (bf16[8,6144]{1,0:T(8,128)(2,1)S(1)}, bf16[8,6144]{1,0:T(8,128)(2,1)S(1)}, u32[]{:S(2)}, u32[]{:S(2)}) collective-permute-start(bf16[8,6144]{1,0:T(8,128)(2,1)S(1)} %get-tuple-element.24), channel_id=1, source_target_pairs={{0,8},{8,0},{1,9},{9,1},{2,10},{10,2},{3,11},{11,3},{4,12},{12,4},... | collective-permute-start | bytes 294920 | tf_op jit(solution)/shard_map/ppermute | solution.py:12
  6.8 0.1 collective-permute-start.3
  6.9 0.2 fusion.25
  7.1 0.1 fusion.27
  7.3 1.8 %collective-permute-start.1 = (bf16[1,16,6144]{2,1,0:T(8,128)(2,1)S(1)}, bf16[1,16,6144]{2,1,0:T(8,128)(2,1)S(1)}, u32[]{:S(2)}, u32[]{:S(2)}) collective-permute-start(bf16[1,16,6144]{2,1,0:T(8,128)(2,1)S(1)} %fusion.27), channel_id=1, source_target_pairs={{0,2},{1,5},{2,0},{3,7},{4,6},{5,1},{6,4},{7,3},{8,10},{9,13},{10,... | collective-permute-start | bytes 589832 | tf_op jit(solution)/shard_map/ppermute | solution.py:75
  9.1 1.0 slice_bitcast_fusion.1
  10.1 1.5 %collective-permute-start = (bf16[64,6144]{1,0:T(8,128)(2,1)}, bf16[64,6144]{1,0:T(8,128)(2,1)S(1)}, u32[]{:S(2)}, u32[]{:S(2)}) collective-permute-start(bf16[64,6144]{1,0:T(8,128)(2,1)} %get-tuple-element.19), channel_id=1, source_target_pairs={{0,16},{16,0},{1,17},{17,1},{2,18},{18,2},{3,19},{19,3},{4,20},{20... | collective-permute-start | bytes 2359304 | tf_op jit(solution)/shard_map/ppermute | solution.py:12
  11.6 0.1 compare_select_fusion
  11.7 3.0 %collective-permute-done.6 = bf16[8,6144]{1,0:T(8,128)(2,1)S(1)} collective-permute-done((bf16[8,6144]{1,0:T(8,128)(2,1)S(1)}, bf16[8,6144]{1,0:T(8,128)(2,1)S(1)}, u32[]{:S(2)}, u32[]{:S(2)}) %collective-permute-start.6) | collective-permute-done | bytes 98336 | tf_op jit(solution)/shard_map/ppermute | solution.py:12
  14.7 0.2 fusion.33
  14.8 1.1 %collective-permute-done.3 = bf16[8,6144]{1,0:T(8,128)(2,1)S(1)} collective-permute-done((bf16[8,6144]{1,0:T(8,128)(2,1)S(1)}, bf16[8,6144]{1,0:T(8,128)(2,1)S(1)}, u32[]{:S(2)}, u32[]{:S(2)}) %collective-permute-start.3) | collective-permute-done | bytes 98336 | tf_op jit(solution)/shard_map/ppermute | solution.py:12
  15.9 0.2 fusion.30
  16.1 0.1 fusion.43
  16.2 1.6 %collective-permute-start.4 = (bf16[1,8,6144]{2,1,0:T(8,128)(2,1)S(1)}, bf16[1,8,6144]{2,1,0:T(8,128)(2,1)S(1)}, u32[]{:S(2)}, u32[]{:S(2)}) collective-permute-start(bf16[1,8,6144]{2,1,0:T(8,128)(2,1)S(1)} %get-tuple-element.29), channel_id=1, source_target_pairs={{0,2},{1,5},{2,0},{3,7},{4,6},{5,1},{6,4},{7,3},{8,10},{9,13},{10,... | collective-permute-start | bytes 294920 | tf_op jit(solution)/shard_map/ppermute | solution.py:75
  17.9 0.1 fusion.45
  17.9 0.5 collective-permute-start.7
  18.4 2.5 %collective-permute-done.4 = bf16[1,8,6144]{2,1,0:T(8,128)(2,1)S(1)} collective-permute-done((bf16[1,8,6144]{2,1,0:T(8,128)(2,1)S(1)}, bf16[1,8,6144]{2,1,0:T(8,128)(2,1)S(1)}, u32[]{:S(2)}, u32[]{:S(2)}) %collective-permute-start.4) | collective-permute-done | bytes 98336 | tf_op jit(solution)/shard_map/ppermute | solution.py:75
  20.9 0.8 collective-permute-start.5
  21.7 1.5 %collective-permute-done.7 = bf16[1,8,6144]{2,1,0:T(8,128)(2,1)S(1)} collective-permute-done((bf16[1,8,6144]{2,1,0:T(8,128)(2,1)S(1)}, bf16[1,8,6144]{2,1,0:T(8,128)(2,1)S(1)}, u32[]{:S(2)}, u32[]{:S(2)}) %collective-permute-start.7) | collective-permute-done | bytes 98336 | tf_op jit(solution)/shard_map/ppermute | solution.py:75
  23.2 0.1 collective-permute-start.8
  23.4 2.0 %collective-permute-start.2 = (bf16[2,16,6144]{2,1,0:T(8,128)(2,1)S(1)}, bf16[2,16,6144]{2,1,0:T(8,128)(2,1)S(1)}, u32[]{:S(2)}, u32[]{:S(2)}) collective-permute-start(bf16[2,16,6144]{2,1,0:T(8,128)(2,1)S(1)} %pad_maximum_fusion.2), channel_id=1, source_target_pairs={{0,4},{1,3},{2,6},{3,1},{4,0},{5,7},{6,2},{7,5},{8,12},{9,11},{10,... | collective-permute-start | bytes 1179656 | tf_op jit(solution)/shard_map/ppermute | solution.py:75
  25.4 1.2 %collective-permute-done.5 = bf16[2,8,6144]{2,1,0:T(8,128)(2,1)S(1)} collective-permute-done((bf16[2,8,6144]{2,1,0:T(8,128)(2,1)S(1)}, bf16[2,8,6144]{2,1,0:T(8,128)(2,1)S(1)}, u32[]{:S(2)}, u32[]{:S(2)}) %collective-permute-start.5) | collective-permute-done | bytes 196640 | tf_op jit(solution)/shard_map/ppermute | solution.py:75
  26.7 2.3 %collective-permute-done.8 = bf16[2,8,6144]{2,1,0:T(8,128)(2,1)S(1)} collective-permute-done((bf16[2,8,6144]{2,1,0:T(8,128)(2,1)S(1)}, bf16[2,8,6144]{2,1,0:T(8,128)(2,1)S(1)}, u32[]{:S(2)}, u32[]{:S(2)}) %collective-permute-start.8) | collective-permute-done | bytes 196640 | tf_op jit(solution)/shard_map/ppermute | solution.py:75
  29.0 0.1 collective-permute-start.10
  29.1 4.1 %collective-permute-done.2 = bf16[2,16,6144]{2,1,0:T(8,128)(2,1)S(1)} collective-permute-done((bf16[2,16,6144]{2,1,0:T(8,128)(2,1)S(1)}, bf16[2,16,6144]{2,1,0:T(8,128)(2,1)S(1)}, u32[]{:S(2)}, u32[]{:S(2)}) %collective-permute-start.2) | collective-permute-done | bytes 393248 | tf_op jit(solution)/shard_map/ppermute | solution.py:75
  33.2 0.1 fusion.49
  33.3 0.1 collective-permute-start.9
  33.4 1.7 %collective-permute-start.12 = (f32[2,16,128]{2,1,0:T(8,128)S(1)}, f32[2,16,128]{2,1,0:T(8,128)S(1)}, u32[]{:S(2)}, u32[]{:S(2)}) collective-permute-start(f32[2,16,128]{2,1,0:T(8,128)S(1)} %fusion.44), channel_id=1, source_target_pairs={{0,16},{16,0},{1,17},{17,1},{2,18},{18,2},{3,19},{19,3},{4,20},{20... | collective-permute-start | bytes 49160 | tf_op jit(solution)/shard_map/ppermute | solution.py:12
  35.1 0.4 collective-permute-start.11
  35.6 0.1 collective-permute-done.9
  35.7 0.1 maximum_bitcast_fusion.1
  35.8 0.2 pad_maximum_fusion
  36.0 11.7 %fusion.2 = f32[256,2048]{1,0:T(8,128)S(1)} fusion(bf16[256,6144]{1,0:T(8,128)(2,1)S(1)} %bitcast.85, bf16[1,6144,2048]{2,1,0:T(8,128)(2,1)} %param.10), kind=kOutput, calls=%fused_computation.2 | convolution fusion | flops 6442450944 | bytes 30408704 | tf_op jit(solution)/shard_map/dot_general | solution.py:96
  47.7 12.4 %fusion.21 = bf16[256,2048]{1,0:T(8,128)(2,1)S(1)} fusion(bf16[256,6144]{1,0:T(8,128)(2,1)S(1)} %bitcast.86, bf16[1,6144,2048]{2,1,0:T(8,128)(2,1)} %param.11, f32[256,2048]{1,0:T(8,128)S(1)} %fusion.2), kind=kOutput, calls=%fused_computation.19 | convolution fusion | flops 6445596672 | bytes 31457280 | tf_op jit(solution)/shard_map/dot_general | solution.py:97
  60.1 8.0 %fusion.8 = bf16[256,3072]{1,0:T(8,128)(2,1)S(1)} fusion(bf16[256,2048]{1,0:T(8,128)(2,1)S(1)} %fusion.21, bf16[2048,6144]{1,0:T(8,128)(2,1)} %bitcast.104), kind=kOutput, calls=%fused_computation.9 | convolution fusion | flops 3222011904 | bytes 15204352 | tf_op jit(solution)/shard_map/dot_general | solution.py:105
  68.1 8.0 %fusion.11 = bf16[256,3072]{1,0:T(8,128)(2,1)S(1)} fusion(bf16[256,2048]{1,0:T(8,128)(2,1)S(1)} %fusion.21, bf16[2048,6144]{1,0:T(8,128)(2,1)} %bitcast.105), kind=kOutput, calls=%fused_computation.10 | convolution fusion | flops 3222011904 | bytes 15204352 | tf_op jit(solution)/shard_map/dot_general | solution.py:105
  76.1 0.1 fusion.50
  76.2 0.2 collective-permute-start.13
  76.5 0.1 fusion.51
  76.6 0.4 collective-permute-start.18
  77.1 1.5 %collective-permute-done.13 = bf16[4,2,16,3072]{3,2,1,0:T(8,128)(2,1)S(1)} collective-permute-done((bf16[4,2,16,3072]{3,2,1,0:T(8,128)(2,1)S(1)}, bf16[4,2,16,3072]{3,2,1,0:T(8,128)(2,1)S(1)}, u32[]{:S(2)}, u32[]{:S(2)}) %collective-permute-start.13) | collective-permute-done | bytes 786464 | tf_op jit(solution)/shard_map/ppermute | solution.py:12
  78.6 0.2 convert_add_fusion.1
  78.8 0.6 collective-permute-start.14
  79.4 0.3 collective-permute-done.18
  79.7 0.2 convert_add_fusion
  80.0 1.3 %collective-permute-start.19 = (bf16[2,2,16,3072]{3,2,1,0:T(8,128)(2,1)S(1)}, bf16[2,2,16,3072]{3,2,1,0:T(8,128)(2,1)S(1)}, u32[]{:S(2)}, u32[]{:S(2)}) collective-permute-start(bf16[2,2,16,3072]{3,2,1,0:T(8,128)(2,1)S(1)} %slice.174), channel_id=1, source_target_pairs={{0,4},{1,3},{2,6},{3,1},{4,0},{5,7},{6,2},{7,5},{8,12},{9,11},{10,... | collective-permute-start | bytes 1179656 | tf_op jit(solution)/shard_map/ppermute | solution.py:120
  81.3 5.4 %collective-permute-done.14 = bf16[2,2,16,3072]{3,2,1,0:T(8,128)(2,1)S(1)} collective-permute-done((bf16[2,2,16,3072]{3,2,1,0:T(8,128)(2,1)S(1)}, bf16[2,2,16,3072]{3,2,1,0:T(8,128)(2,1)S(1)}, u32[]{:S(2)}, u32[]{:S(2)}) %collective-permute-start.14) | collective-permute-done | bytes 393248 | tf_op jit(solution)/shard_map/ppermute | solution.py:120
  86.7 0.1 slice_add_fusion.1
  86.8 1.4 %collective-permute-start.15 = (bf16[1,2,16,3072]{3,2,1,0:T(8,128)(2,1)S(1)}, bf16[1,2,16,3072]{3,2,1,0:T(8,128)(2,1)S(1)}, u32[]{:S(2)}, u32[]{:S(2)}) collective-permute-start(bf16[1,2,16,3072]{3,2,1,0:T(8,128)(2,1)S(1)} %slice.177), channel_id=1, source_target_pairs={{0,2},{1,5},{2,0},{3,7},{4,6},{5,1},{6,4},{7,3},{8,10},{9,13},{10,... | collective-permute-start | bytes 589832 | tf_op jit(solution)/shard_map/ppermute | solution.py:120
  88.2 4.8 %collective-permute-done.19 = bf16[2,2,16,3072]{3,2,1,0:T(8,128)(2,1)S(1)} collective-permute-done((bf16[2,2,16,3072]{3,2,1,0:T(8,128)(2,1)S(1)}, bf16[2,2,16,3072]{3,2,1,0:T(8,128)(2,1)S(1)}, u32[]{:S(2)}, u32[]{:S(2)}) %collective-permute-start.19) | collective-permute-done | bytes 393248 | tf_op jit(solution)/shard_map/ppermute | solution.py:120
  93.0 0.1 slice_add_fusion
  93.1 1.4 %collective-permute-start.20 = (bf16[1,2,16,3072]{3,2,1,0:T(8,128)(2,1)S(1)}, bf16[1,2,16,3072]{3,2,1,0:T(8,128)(2,1)S(1)}, u32[]{:S(2)}, u32[]{:S(2)}) collective-permute-start(bf16[1,2,16,3072]{3,2,1,0:T(8,128)(2,1)S(1)} %slice.176), channel_id=1, source_target_pairs={{0,2},{1,5},{2,0},{3,7},{4,6},{5,1},{6,4},{7,3},{8,10},{9,13},{10,... | collective-permute-start | bytes 589832 | tf_op jit(solution)/shard_map/ppermute | solution.py:120
  94.6 1.6 %collective-permute-start.16 = (bf16[16,3072]{1,0:T(8,128)(2,1)S(1)}, bf16[16,3072]{1,0:T(8,128)(2,1)S(1)}, u32[]{:S(2)}, u32[]{:S(2)}) collective-permute-start(bf16[16,3072]{1,0:T(8,128)(2,1)S(1)} %get-tuple-element.25), channel_id=1, source_target_pairs={{0,16},{16,0},{1,17},{17,1},{2,18},{18,2},{3,19},{19,3},{4,20},{20... | collective-permute-start | bytes 294920 | tf_op jit(solution)/shard_map/ppermute | solution.py:12
  96.2 1.7 %collective-permute-start.17 = (bf16[16,3072]{1,0:T(8,128)(2,1)S(1)}, bf16[16,3072]{1,0:T(8,128)(2,1)S(1)}, u32[]{:S(2)}, u32[]{:S(2)}) collective-permute-start(bf16[16,3072]{1,0:T(8,128)(2,1)S(1)} %get-tuple-element.26), channel_id=1, source_target_pairs={{0,24},{8,16},{16,8},{24,0},{1,25},{9,17},{17,9},{25,1},{2,26},{10... | collective-permute-start | bytes 294920 | tf_op jit(solution)/shard_map/ppermute | solution.py:133
  97.9 0.9 collective-permute-done.20
  98.9 1.7 %collective-permute-start.21 = (bf16[16,3072]{1,0:T(8,128)(2,1)S(1)}, bf16[16,3072]{1,0:T(8,128)(2,1)S(1)}, u32[]{:S(2)}, u32[]{:S(2)}) collective-permute-start(bf16[16,3072]{1,0:T(8,128)(2,1)S(1)} %get-tuple-element.27), channel_id=1, source_target_pairs={{0,16},{16,0},{1,17},{17,1},{2,18},{18,2},{3,19},{19,3},{4,20},{20... | collective-permute-start | bytes 294920 | tf_op jit(solution)/shard_map/ppermute | solution.py:12
  100.6 1.5 %collective-permute-start.22 = (bf16[16,3072]{1,0:T(8,128)(2,1)S(1)}, bf16[16,3072]{1,0:T(8,128)(2,1)S(1)}, u32[]{:S(2)}, u32[]{:S(2)}) collective-permute-start(bf16[16,3072]{1,0:T(8,128)(2,1)S(1)} %get-tuple-element.28), channel_id=1, source_target_pairs={{0,24},{8,16},{16,8},{24,0},{1,25},{9,17},{17,9},{25,1},{2,26},{10... | collective-permute-start | bytes 294920 | tf_op jit(solution)/shard_map/ppermute | solution.py:133
  102.1 3.7 %collective-permute-done.17 = bf16[16,3072]{1,0:T(8,128)(2,1)S(1)} collective-permute-done((bf16[16,3072]{1,0:T(8,128)(2,1)S(1)}, bf16[16,3072]{1,0:T(8,128)(2,1)S(1)}, u32[]{:S(2)}, u32[]{:S(2)}) %collective-permute-start.17) | collective-permute-done | bytes 98336 | tf_op jit(solution)/shard_map/ppermute | solution.py:133
  105.7 0.8 fusion.17
  106.6 1.5 %collective-permute-done.22 = bf16[16,3072]{1,0:T(8,128)(2,1)S(1)} collective-permute-done((bf16[16,3072]{1,0:T(8,128)(2,1)S(1)}, bf16[16,3072]{1,0:T(8,128)(2,1)S(1)}, u32[]{:S(2)}, u32[]{:S(2)}) %collective-permute-start.22) | collective-permute-done | bytes 98336 | tf_op jit(solution)/shard_map/ppermute | solution.py:133
  108.1 0.9 fusion.16
  108.9 1.3 %maximum_bitcast_fusion.2 = bf16[1,128,6144]{2,1,0:T(8,128)(2,1)} fusion(bf16[128,3072]{1,0:T(8,128)(2,1)S(1)} %fusion.16, bf16[128,3072]{1,0:T(8,128)(2,1)S(1)} %fusion.17), kind=kLoop, calls=%fused_computation.22 | loop fusion | flops 3145728 | bytes 3145728 | tf_op jit(solution)/shard_map/broadcast_in_dim | solution.py:144
  (39 shorter events, 0.7 us)
Async XLA Ops:
  0.0 9.1 %copy-start = (bf16[1,128,6144]{2,1,0:T(8,128)(2,1)S(1)}, bf16[1,128,6144]{2,1,0:T(8,128)(2,1)}, u32[]{:S(2)}) copy-start(bf16[1,128,6144]{2,1,0:T(8,128)(2,1)} %param.8) | copy-start | bytes 4718596
  0.0 6.9 %copy-start.1 = (bf16[1,6144]{1,0:T(2,128)(2,1)S(1)}, bf16[1,6144]{1,0:T(2,128)(2,1)}, u32[]{:S(2)}) copy-start(bf16[1,6144]{1,0:T(2,128)(2,1)} %param.9) | copy-start | bytes 36868
  2.7 11.9 %collective-permute-start.6 = (bf16[8,6144]{1,0:T(8,128)(2,1)S(1)}, bf16[8,6144]{1,0:T(8,128)(2,1)S(1)}, u32[]{:S(2)}, u32[]{:S(2)}) collective-permute-start(bf16[8,6144]{1,0:T(8,128)(2,1)S(1)} %get-tuple-element.24), channel_id=1, source_target_pairs={{0,8},{8,0},{1,9},{9,1},{2,10},{10,2},{3,11},{11,3},{4,12},{12,4},... | collective-permute-start | bytes 294920 | tf_op jit(solution)/shard_map/ppermute | solution.py:12
  6.8 9.1 %collective-permute-start.3 = (bf16[8,6144]{1,0:T(8,128)(2,1)S(1)}, bf16[8,6144]{1,0:T(8,128)(2,1)S(1)}, u32[]{:S(2)}, u32[]{:S(2)}) collective-permute-start(bf16[8,6144]{1,0:T(8,128)(2,1)S(1)} %get-tuple-element.23), channel_id=1, source_target_pairs={{0,8},{8,0},{1,9},{9,1},{2,10},{10,2},{3,11},{11,3},{4,12},{12,4},... | collective-permute-start | bytes 294920 | tf_op jit(solution)/shard_map/ppermute | solution.py:12
  7.2 4.4 %copy-start.3 = (f32[1,1,2,16]{3,2,1,0:T(2,128)S(1)}, f32[1,1,2,16]{3,2,1,0:T(2,128)}, u32[]{:S(2)}) copy-start(f32[1,1,2,16]{3,2,1,0:T(2,128)} %param.15) | copy-start | bytes 388
  7.3 4.4 %copy-start.4 = (s32[1,1,2]{2,1,0:T(1,128)S(1)}, s32[1,1,2]{2,1,0:T(1,128)}, u32[]{:S(2)}) copy-start(s32[1,1,2]{2,1,0:T(1,128)} %param.14) | copy-start | bytes 28
  7.3 10.6 %copy-start.2 = (s32[1,1,2,16]{3,2,1,0:T(2,128)S(1)}, s32[1,1,2,16]{3,2,1,0:T(2,128)}, u32[]{:S(2)}) copy-start(s32[1,1,2,16]{3,2,1,0:T(2,128)} %param.13) | copy-start | bytes 388
  7.3 16.1 %collective-permute-start.1 = (bf16[1,16,6144]{2,1,0:T(8,128)(2,1)S(1)}, bf16[1,16,6144]{2,1,0:T(8,128)(2,1)S(1)}, u32[]{:S(2)}, u32[]{:S(2)}) collective-permute-start(bf16[1,16,6144]{2,1,0:T(8,128)(2,1)S(1)} %fusion.27), channel_id=1, source_target_pairs={{0,2},{1,5},{2,0},{3,7},{4,6},{5,1},{6,4},{7,3},{8,10},{9,13},{10,... | collective-permute-start | bytes 589832 | tf_op jit(solution)/shard_map/ppermute | solution.py:75
  10.1 25.9 %collective-permute-start = (bf16[64,6144]{1,0:T(8,128)(2,1)}, bf16[64,6144]{1,0:T(8,128)(2,1)S(1)}, u32[]{:S(2)}, u32[]{:S(2)}) collective-permute-start(bf16[64,6144]{1,0:T(8,128)(2,1)} %get-tuple-element.19), channel_id=1, source_target_pairs={{0,16},{16,0},{1,17},{17,1},{2,18},{18,2},{3,19},{19,3},{4,20},{20... | collective-permute-start | bytes 2359304 | tf_op jit(solution)/shard_map/ppermute | solution.py:12
  16.2 4.7 %collective-permute-start.4 = (bf16[1,8,6144]{2,1,0:T(8,128)(2,1)S(1)}, bf16[1,8,6144]{2,1,0:T(8,128)(2,1)S(1)}, u32[]{:S(2)}, u32[]{:S(2)}) collective-permute-start(bf16[1,8,6144]{2,1,0:T(8,128)(2,1)S(1)} %get-tuple-element.29), channel_id=1, source_target_pairs={{0,2},{1,5},{2,0},{3,7},{4,6},{5,1},{6,4},{7,3},{8,10},{9,13},{10,... | collective-permute-start | bytes 294920 | tf_op jit(solution)/shard_map/ppermute | solution.py:75
  17.9 5.3 %collective-permute-start.7 = (bf16[1,8,6144]{2,1,0:T(8,128)(2,1)S(1)}, bf16[1,8,6144]{2,1,0:T(8,128)(2,1)S(1)}, u32[]{:S(2)}, u32[]{:S(2)}) collective-permute-start(bf16[1,8,6144]{2,1,0:T(8,128)(2,1)S(1)} %get-tuple-element.30), channel_id=1, source_target_pairs={{0,2},{1,5},{2,0},{3,7},{4,6},{5,1},{6,4},{7,3},{8,10},{9,13},{10,... | collective-permute-start | bytes 294920 | tf_op jit(solution)/shard_map/ppermute | solution.py:75
  20.9 5.7 %collective-permute-start.5 = (bf16[2,8,6144]{2,1,0:T(8,128)(2,1)S(1)}, bf16[2,8,6144]{2,1,0:T(8,128)(2,1)S(1)}, u32[]{:S(2)}, u32[]{:S(2)}) collective-permute-start(bf16[2,8,6144]{2,1,0:T(8,128)(2,1)S(1)} %pad_maximum_fusion.3), channel_id=1, source_target_pairs={{0,4},{1,3},{2,6},{3,1},{4,0},{5,7},{6,2},{7,5},{8,12},{9,11},{10,... | collective-permute-start | bytes 589832 | tf_op jit(solution)/shard_map/ppermute | solution.py:75
  23.2 5.7 %collective-permute-start.8 = (bf16[2,8,6144]{2,1,0:T(8,128)(2,1)S(1)}, bf16[2,8,6144]{2,1,0:T(8,128)(2,1)S(1)}, u32[]{:S(2)}, u32[]{:S(2)}) collective-permute-start(bf16[2,8,6144]{2,1,0:T(8,128)(2,1)S(1)} %pad_maximum_fusion.4), channel_id=1, source_target_pairs={{0,4},{1,3},{2,6},{3,1},{4,0},{5,7},{6,2},{7,5},{8,12},{9,11},{10,... | collective-permute-start | bytes 589832 | tf_op jit(solution)/shard_map/ppermute | solution.py:75
  23.4 9.8 %collective-permute-start.2 = (bf16[2,16,6144]{2,1,0:T(8,128)(2,1)S(1)}, bf16[2,16,6144]{2,1,0:T(8,128)(2,1)S(1)}, u32[]{:S(2)}, u32[]{:S(2)}) collective-permute-start(bf16[2,16,6144]{2,1,0:T(8,128)(2,1)S(1)} %pad_maximum_fusion.2), channel_id=1, source_target_pairs={{0,4},{1,3},{2,6},{3,1},{4,0},{5,7},{6,2},{7,5},{8,12},{9,11},{10,... | collective-permute-start | bytes 1179656 | tf_op jit(solution)/shard_map/ppermute | solution.py:75
  29.0 6.5 %collective-permute-start.10 = (bf16[4,16,6144]{2,1,0:T(8,128)(2,1)S(1)}, bf16[4,16,6144]{2,1,0:T(8,128)(2,1)S(1)}, u32[]{:S(2)}, u32[]{:S(2)}) collective-permute-start(bf16[4,16,6144]{2,1,0:T(8,128)(2,1)S(1)} %maximum_maximum_fusion), channel_id=1, source_target_pairs={{0,1},{1,0},{2,3},{3,2},{4,5},{5,4},{6,7},{7,6},{8,9},{9,8},{10,11... | collective-permute-start | bytes 2359304 | tf_op jit(solution)/shard_map/ppermute | solution.py:12
  33.3 2.4 %collective-permute-start.9 = (bf16[4,16,6144]{2,1,0:T(8,128)(2,1)S(1)}, bf16[4,16,6144]{2,1,0:T(8,128)(2,1)S(1)}, u32[]{:S(2)}, u32[]{:S(2)}) collective-permute-start(bf16[4,16,6144]{2,1,0:T(8,128)(2,1)S(1)} %get-tuple-element.22), channel_id=1, source_target_pairs={{0,1},{1,0},{2,3},{3,2},{4,5},{5,4},{6,7},{7,6},{8,9},{9,8},{10,11... | collective-permute-start | bytes 2359304 | tf_op jit(solution)/shard_map/ppermute | solution.py:12
  33.4 42.7 %collective-permute-start.12 = (f32[2,16,128]{2,1,0:T(8,128)S(1)}, f32[2,16,128]{2,1,0:T(8,128)S(1)}, u32[]{:S(2)}, u32[]{:S(2)}) collective-permute-start(f32[2,16,128]{2,1,0:T(8,128)S(1)} %fusion.44), channel_id=1, source_target_pairs={{0,16},{16,0},{1,17},{17,1},{2,18},{18,2},{3,19},{19,3},{4,20},{20... | collective-permute-start | bytes 49160 | tf_op jit(solution)/shard_map/ppermute | solution.py:12
  35.1 41.0 %collective-permute-start.11 = (bf16[64,6144]{1,0:T(8,128)(2,1)S(1)}, bf16[64,6144]{1,0:T(8,128)(2,1)S(1)}, u32[]{:S(2)}, u32[]{:S(2)}) collective-permute-start(bf16[64,6144]{1,0:T(8,128)(2,1)S(1)} %get-tuple-element.20), channel_id=1, source_target_pairs={{0,16},{16,0},{1,17},{17,1},{2,18},{18,2},{3,19},{19,3},{4,20},{20... | collective-permute-start | bytes 2359304 | tf_op jit(solution)/shard_map/ppermute | solution.py:12
  76.2 2.4 %collective-permute-start.13 = (bf16[4,2,16,3072]{3,2,1,0:T(8,128)(2,1)S(1)}, bf16[4,2,16,3072]{3,2,1,0:T(8,128)(2,1)S(1)}, u32[]{:S(2)}, u32[]{:S(2)}) collective-permute-start(bf16[4,2,16,3072]{3,2,1,0:T(8,128)(2,1)S(1)} %bitcast.95), channel_id=1, source_target_pairs={{0,1},{1,0},{2,3},{3,2},{4,5},{5,4},{6,7},{7,6},{8,9},{9,8},{10,11... | collective-permute-start | bytes 2359304 | tf_op jit(solution)/shard_map/ppermute | solution.py:12
  76.6 3.1 %collective-permute-start.18 = (bf16[4,2,16,3072]{3,2,1,0:T(8,128)(2,1)S(1)}, bf16[4,2,16,3072]{3,2,1,0:T(8,128)(2,1)S(1)}, u32[]{:S(2)}, u32[]{:S(2)}) collective-permute-start(bf16[4,2,16,3072]{3,2,1,0:T(8,128)(2,1)S(1)} %bitcast.94), channel_id=1, source_target_pairs={{0,1},{1,0},{2,3},{3,2},{4,5},{5,4},{6,7},{7,6},{8,9},{9,8},{10,11... | collective-permute-start | bytes 2359304 | tf_op jit(solution)/shard_map/ppermute | solution.py:12
  78.8 7.8 %collective-permute-start.14 = (bf16[2,2,16,3072]{3,2,1,0:T(8,128)(2,1)S(1)}, bf16[2,2,16,3072]{3,2,1,0:T(8,128)(2,1)S(1)}, u32[]{:S(2)}, u32[]{:S(2)}) collective-permute-start(bf16[2,2,16,3072]{3,2,1,0:T(8,128)(2,1)S(1)} %slice.175), channel_id=1, source_target_pairs={{0,4},{1,3},{2,6},{3,1},{4,0},{5,7},{6,2},{7,5},{8,12},{9,11},{10,... | collective-permute-start | bytes 1179656 | tf_op jit(solution)/shard_map/ppermute | solution.py:120
  80.0 13.0 %collective-permute-start.19 = (bf16[2,2,16,3072]{3,2,1,0:T(8,128)(2,1)S(1)}, bf16[2,2,16,3072]{3,2,1,0:T(8,128)(2,1)S(1)}, u32[]{:S(2)}, u32[]{:S(2)}) collective-permute-start(bf16[2,2,16,3072]{3,2,1,0:T(8,128)(2,1)S(1)} %slice.174), channel_id=1, source_target_pairs={{0,4},{1,3},{2,6},{3,1},{4,0},{5,7},{6,2},{7,5},{8,12},{9,11},{10,... | collective-permute-start | bytes 1179656 | tf_op jit(solution)/shard_map/ppermute | solution.py:120
  86.8 7.8 %collective-permute-start.15 = (bf16[1,2,16,3072]{3,2,1,0:T(8,128)(2,1)S(1)}, bf16[1,2,16,3072]{3,2,1,0:T(8,128)(2,1)S(1)}, u32[]{:S(2)}, u32[]{:S(2)}) collective-permute-start(bf16[1,2,16,3072]{3,2,1,0:T(8,128)(2,1)S(1)} %slice.177), channel_id=1, source_target_pairs={{0,2},{1,5},{2,0},{3,7},{4,6},{5,1},{6,4},{7,3},{8,10},{9,13},{10,... | collective-permute-start | bytes 589832 | tf_op jit(solution)/shard_map/ppermute | solution.py:120
  93.1 5.7 %collective-permute-start.20 = (bf16[1,2,16,3072]{3,2,1,0:T(8,128)(2,1)S(1)}, bf16[1,2,16,3072]{3,2,1,0:T(8,128)(2,1)S(1)}, u32[]{:S(2)}, u32[]{:S(2)}) collective-permute-start(bf16[1,2,16,3072]{3,2,1,0:T(8,128)(2,1)S(1)} %slice.176), channel_id=1, source_target_pairs={{0,2},{1,5},{2,0},{3,7},{4,6},{5,1},{6,4},{7,3},{8,10},{9,13},{10,... | collective-permute-start | bytes 589832 | tf_op jit(solution)/shard_map/ppermute | solution.py:120
  94.6 7.5 %collective-permute-start.16 = (bf16[16,3072]{1,0:T(8,128)(2,1)S(1)}, bf16[16,3072]{1,0:T(8,128)(2,1)S(1)}, u32[]{:S(2)}, u32[]{:S(2)}) collective-permute-start(bf16[16,3072]{1,0:T(8,128)(2,1)S(1)} %get-tuple-element.25), channel_id=1, source_target_pairs={{0,16},{16,0},{1,17},{17,1},{2,18},{18,2},{3,19},{19,3},{4,20},{20... | collective-permute-start | bytes 294920 | tf_op jit(solution)/shard_map/ppermute | solution.py:12
  96.2 9.6 %collective-permute-start.17 = (bf16[16,3072]{1,0:T(8,128)(2,1)S(1)}, bf16[16,3072]{1,0:T(8,128)(2,1)S(1)}, u32[]{:S(2)}, u32[]{:S(2)}) collective-permute-start(bf16[16,3072]{1,0:T(8,128)(2,1)S(1)} %get-tuple-element.26), channel_id=1, source_target_pairs={{0,24},{8,16},{16,8},{24,0},{1,25},{9,17},{17,9},{25,1},{2,26},{10... | collective-permute-start | bytes 294920 | tf_op jit(solution)/shard_map/ppermute | solution.py:133
  98.9 7.7 %collective-permute-start.21 = (bf16[16,3072]{1,0:T(8,128)(2,1)S(1)}, bf16[16,3072]{1,0:T(8,128)(2,1)S(1)}, u32[]{:S(2)}, u32[]{:S(2)}) collective-permute-start(bf16[16,3072]{1,0:T(8,128)(2,1)S(1)} %get-tuple-element.27), channel_id=1, source_target_pairs={{0,16},{16,0},{1,17},{17,1},{2,18},{18,2},{3,19},{19,3},{4,20},{20... | collective-permute-start | bytes 294920 | tf_op jit(solution)/shard_map/ppermute | solution.py:12
  100.6 7.5 %collective-permute-start.22 = (bf16[16,3072]{1,0:T(8,128)(2,1)S(1)}, bf16[16,3072]{1,0:T(8,128)(2,1)S(1)}, u32[]{:S(2)}, u32[]{:S(2)}) collective-permute-start(bf16[16,3072]{1,0:T(8,128)(2,1)S(1)} %get-tuple-element.28), channel_id=1, source_target_pairs={{0,24},{8,16},{16,8},{24,0},{1,25},{9,17},{17,9},{25,1},{2,26},{10... | collective-permute-start | bytes 294920 | tf_op jit(solution)/shard_map/ppermute | solution.py:133
